TPU v7x, 128 devices: a whole 4x4x4 slice. The times are simulated.
128 devices in a mesh: tile: 8 (over x, core), orient: 16 (over z, y).
Axes of the slice: x: 4, y: 4, z: 4, core: 2. Of those that a mesh axis runs over, the one named last changes fastest.
Arguments:
- micrograph: float32 [4096, 512], P('tile'), may hold values from -40 to 40
- templates: float32 [16, 256, 256], P('orient', 'tile'), may hold values from -6 to 6
- defocus_values: float32 [4], replicated, may hold values from 5000 to 20000
- defocus_group: int32 [8], P('tile'), may hold values from 0 to 3, as said below
Outputs:
- best_score: float32 [4096, 512], P(('tile', 'orient'))
- second_score: float32 [4096, 512], P(('tile', 'orient'))
- mean_score: float32 [4096, 512], P(('tile', 'orient'))
- score_variance: float32 [4096, 512], P(('tile', 'orient'))
Inputs may be any that keep to these rules, and one draw needn't show every extreme that they name: `defocus_group`: every group is used by some tile.
All inputs are finite; a program needn't handle non-finite values.
Results may differ from a plain program's by a relative error of at most 0.0003.
Values sent between devices are 32-bit elements; how exact they have to be, the bound alone decides.
No kernel may reach another device: no remote copies, remote signals or barrier semaphores. Data moves between devices by JAX's collectives and lax.ppermute only.
A program may use at most 128 MiB of HBM per device.

v0:
```python
import math

import jax
import jax.numpy as jnp
from jax import lax
from jax.sharding import PartitionSpec as P

TPL = 256


WAVELENGTH = 0.0197
AMPLITUDE = 0.07
exact_mode = lax.Precision.HIGHEST


def padded(shard, sides, width):
    for axis, dim in sides:
        size, length = (lax.axis_size(axis), shard.shape[dim])
        up = [(i, (i + 1) % size) for i in range(size - 1)]
        down = [(j, i) for i, j in up]
        last = lax.slice_in_dim(shard, length - width, length, axis=dim)
        initial = lax.slice_in_dim(shard, 0, width, axis=dim)
        before = lax.ppermute(last, axis, up)
        after = lax.ppermute(initial, axis, down)
        shard = jnp.concatenate([before, shard, after], axis=dim)
    return shard


def merged_2(shard, axis, combine):
    everything = jax.tree.map(lambda part: lax.all_gather(part, axis), shard)
    initial = jax.tree.map(lambda part: part[0], everything)

    def turn(k, so_far):
        return combine(so_far, jax.tree.map(lambda part: part[k], everything))

    return lax.fori_loop(1, lax.axis_size(axis), turn, initial)


def product(former, latter):
    return jnp.dot(former, latter, precision=exact_mode, preferred_element_type=jnp.float32)


def fourier_tables(rows_out, cols_out, period):
    row_ids = lax.broadcasted_iota(jnp.int32, (rows_out, cols_out), 0)
    col_ids = lax.broadcasted_iota(jnp.int32, (rows_out, cols_out), 1)
    angles = (row_ids * col_ids % period).astype(jnp.float32) * (2.0 * math.pi / period)
    return (jnp.cos(angles), jnp.sin(angles))


def extend(plane, margin):
    rows_ext = padded(plane, (("tile", 0),), margin)
    return jnp.pad(rows_ext, ((0, 0), (margin, margin)))


def transform(plane, cos_rows, sin_rows, cosine, sine_table):
    left_real = product(cos_rows, plane)
    left_imag = -product(sin_rows, plane)
    spec_real = product(left_real, cosine) + product(left_imag, sine_table)
    spec_imag = product(left_imag, cosine) - product(left_real, sine_table)
    return (spec_real, spec_imag)


def full_spectrum(plane, cosine, sine_table):
    return transform(plane, cosine, sine_table, cosine, sine_table)


def combine(former, latter):
    top_value = jnp.maximum(former[0], latter[0])
    second = jnp.maximum(jnp.minimum(former[0], latter[0]), jnp.maximum(former[1], latter[1]))
    return (top_value, second, former[2] + latter[2], former[3] + latter[3])


def per_device(micrograph, templates, defocus_values, defocus_group):
    tile_rows, tile_width = micrograph.shape
    margin = TPL // 2
    ext_size = tile_width + 2 * margin
    tile_count = lax.axis_size("tile")
    cosine, sine_table = fourier_tables(ext_size, ext_size, ext_size)
    pixel_count = float(tile_rows * tile_width * tile_count)
    local_sums = (jnp.sum(micrograph), jnp.sum(micrograph * micrograph))
    totals = lax.psum((local_sums[0], local_sums[1]), "tile")
    centre = totals[0] / pixel_count
    spread = jnp.sqrt(totals[1] / pixel_count - centre * centre + 1e-05)
    centre, spread = (centre, spread)
    spec_real, spec_imag = full_spectrum(
        extend((micrograph - centre) / spread, margin), cosine, sine_table
    )
    gathered = lax.all_gather(templates, "tile", axis=1, tiled=True)
    centred = gathered - jnp.mean(gathered, axis=(1, 2), keepdims=True)
    root_mean = jnp.sqrt(jnp.mean(centred * centred, axis=(1, 2), keepdims=True) + 1e-06)
    normed = centred / (root_mean * TPL)
    extent = normed.shape[1]
    positions_f = lax.iota(jnp.int32, ext_size)
    signed_freq = (
        jnp.where(positions_f < ext_size // 2, positions_f, positions_f - ext_size).astype(
            jnp.float32
        )
        / ext_size
    )
    freq_square = signed_freq[:, None] ** 2 + signed_freq[None, :] ** 2
    group_ids = lax.iota(jnp.int32, defocus_values.shape[0])
    defocus = jnp.sum(jnp.where(group_ids == defocus_group[0], defocus_values, 0.0))
    phase_shift = math.pi * WAVELENGTH * defocus * freq_square
    contrast = -(
        math.sqrt(1.0 - AMPLITUDE * AMPLITUDE) * jnp.sin(phase_shift)
        + AMPLITUDE * jnp.cos(phase_shift)
    )
    partial_real = product(cosine[:, :extent], normed[0])
    partial_imag = -product(sine_table[:, :extent], normed[0])
    template_real = product(partial_real, cosine[:extent]) + product(
        partial_imag, sine_table[:extent]
    )
    template_imag = product(partial_imag, cosine[:extent]) - product(
        partial_real, sine_table[:extent]
    )
    product_real = (spec_real * template_real + spec_imag * template_imag) * contrast
    product_imag = (spec_imag * template_real - spec_real * template_imag) * contrast
    back_real = product(product_real, cosine[:, :tile_width]) - product(
        product_imag, sine_table[:, :tile_width]
    )
    back_imag = product(product_imag, cosine[:, :tile_width]) + product(
        product_real, sine_table[:, :tile_width]
    )
    scores = (
        product(cosine[:tile_width], back_real) - product(sine_table[:tile_width], back_imag)
    ) / (ext_size * ext_size)
    entry = (scores, jnp.full_like(scores, -jnp.inf), scores, scores * scores)
    orient_count = lax.axis_size("orient")
    share_rows = tile_rows // orient_count
    merged = merged_2((entry[0], entry[1], entry[2], entry[3]), "orient", combine)
    row_start = lax.axis_index("orient") * share_rows
    own_rows = tuple((lax.dynamic_slice_in_dim(item, row_start, share_rows, 0) for item in merged))
    total_orients = normed.shape[0] * orient_count
    mean_map = own_rows[2] / total_orients
    variance = own_rows[3] / total_orients - mean_map * mean_map
    return (own_rows[0], own_rows[1], mean_map, variance)


def solution(mesh):
    placed = (P("tile", None), P("orient", "tile", None), P(), P("tile"))
    return jax.shard_map(
        per_device,
        mesh=mesh,
        in_specs=placed,
        out_specs=(
            P(("tile", "orient"), None),
            P(("tile", "orient"), None),
            P(("tile", "orient"), None),
            P(("tile", "orient"), None),
        ),
        check_vma=False,
    )
```

profile of v0, /device:TPU:1, one launch (start us, length us, event | category | flops | bytes accessed | tf_op | source)
XLA Modules:
  0.0 510.2 jit_solution(16587215460453781528)
XLA Ops:
  7.2 0.0 all-gather.5.cloned.1.call-start
  7.2 2.1 fusion.101
  9.3 13.8 %all-reduce.1 = (f32[]{:T(128)}, f32[]{:T(128)}) all-reduce(f32[]{:T(128)} %get-tuple-element.242, f32[]{:T(128)} %get-tuple-element.241), channel_id=1, replica_groups=mesh['tile'=8,'orient'=16] {'tile'}, use_global_device_ids=true, to_apply=%region_3.4 | all-reduce | flops 2 | bytes 16 | tf_op jit(solution)/shard_map/psum | solution.py:81
  25.8 1.4 subtract_divide_fusion
  27.1 0.0 copy-start.2
  27.1 0.9 fusion.102
  28.1 3.0 collective-permute-start
  31.1 0.0 copy-start.4
  31.1 4.0 collective-permute-start.1
  35.0 9.8 %fusion.7 = f32[768,768]{1,0:T(8,128)} fusion(), kind=kLoop, calls=%fused_computation.19 | loop fusion | flops 5308416 | bytes 2359296 | tf_op jit(solution)/shard_map/cos | solution.py:47
  44.8 8.9 %fusion.6 = f32[768,768]{1,0:T(8,128)S(1)} fusion(), kind=kLoop, calls=%fused_computation.18 | loop fusion | flops 5308416 | bytes 2359296 | tf_op jit(solution)/shard_map/sin | solution.py:47
  53.7 0.0 copy-done.2
  53.7 12.3 %all_gather.18 = f32[1,256,256]{2,1,0:T(8,128)S(1)} all-gather(f32[1,32,256]{2,1,0:T(8,128)S(1)} %copy-done.4), channel_id=1, replica_groups=mesh['tile'=8,'orient'=16] {'tile'}, dimensions={1}, use_global_device_ids=true | all-gather | bytes 294912 | tf_op jit(solution)/shard_map/all_gather | solution.py:88
  66.0 0.7 reduce_sum.47
  67.3 0.7 multiply_reduce_fusion.1
  68.7 1.9 fusion.61
  70.6 3.3 fusion.67
  73.9 0.8 convolution_negate_fusion
  74.8 4.6 fusion.65
  79.4 3.6 convolution_add_fusion
  83.7 0.0 copy-done.5
  83.7 0.6 fusion.80
  85.0 4.0 convolution_subtract_fusion
  89.0 0.0 collective-permute-done
  89.0 0.0 collective-permute-done.1
  89.0 0.0 copy-done.3
  89.0 16.2 %fusion.44 = f32[768,768]{1,0:T(8,128)S(1)} fusion(f32[128,512]{1,0:T(8,128)} %collective-permute-done.1, f32[512,512]{1,0:T(8,128)S(1)} %copy-done.3, f32[128,512]{1,0:T(8,128)} %collective-permute-done), kind=kOutput, calls=%fused_computation.47 | convolution fusion | flops 5445844992 | bytes 3932160 | tf_op jit(solution)/shard_map/dot_general | solution.py:40
  105.2 15.8 %fusion.53 = f32[768,768]{1,0:T(8,128)S(1)} fusion(f32[768,768]{1,0:T(8,128)S(1)} %fusion.44), kind=kOutput, calls=%fused_computation.55 | convolution fusion | flops 5441126400 | bytes 4718592 | tf_op jit(solution)/shard_map/dot_general | solution.py:40
  121.0 16.0 %fusion.56 = f32[768,768]{1,0:T(8,128)S(1)} fusion(f32[768,768]{1,0:T(8,128)S(1)} %fusion.44), kind=kOutput, calls=%fused_computation.56 | convolution fusion | flops 5441126400 | bytes 4718592 | tf_op jit(solution)/shard_map/dot_general | solution.py:40
  137.1 16.1 %fusion.45 = f32[768,768]{1,0:T(8,128)S(1)} fusion(f32[128,512]{1,0:T(8,128)} %collective-permute-done.1, f32[512,512]{1,0:T(8,128)S(1)} %copy-done.3, f32[128,512]{1,0:T(8,128)} %collective-permute-done), kind=kOutput, calls=%fused_computation.48 | convolution fusion | flops 5445844992 | bytes 3932160 | tf_op jit(solution)/shard_map/dot_general | solution.py:40
  153.2 15.9 %fusion.14 = f32[768,768]{1,0:T(8,128)S(1)} fusion(f32[768,768]{1,0:T(8,128)S(1)} %fusion.53, f32[768,768]{1,0:T(8,128)S(1)} %fusion.45), kind=kOutput, calls=%fused_computation.26 | convolution fusion | flops 5442306048 | bytes 7077888 | tf_op jit(solution)/shard_map/dot_general | solution.py:40
  169.2 26.0 %fusion.3 = (f32[768,768]{1,0:T(8,128)S(1)}, f32[768,768]{1,0:T(8,128)S(1)}) fusion(f32[768,768]{1,0:T(8,128)S(1)} %convolution_subtract_fusion, f32[768,768]{1,0:T(8,128)S(1)} %fusion.14, f32[768,768]{1,0:T(8,128)S(1)} %copy-done.1, f32[768]{0:T(1024)S(1)} %fusion.73, f32[]{:T(128)S(6)} %mul_shard_map.3, f32[768,768]{1,0:T(8,128)S(1)} %fusion.56, ...), kind=kOutput, calls=%fused_computation.14 | convolution fusion | flops 5450563584 | bytes 16518148 | tf_op jit(solution)/shard_map/dot_general | solution.py:40
  195.2 3.9 fusion.30
  199.0 3.9 fusion.28
  202.9 3.9 fusion.26
  206.8 3.9 fusion.32
  210.7 3.0 fusion.20
  213.7 4.1 fusion.103
  217.8 0.0 all-gather.5.cloned.1.call-update
  217.9 0.0 all-gather.7.cloned.1.call-start
  217.9 0.7 all-gather.7.cloned.1.call-update
  218.6 111.2 %all-gather.5.cloned.1.call-done = f32[8192,512]{1,0:T(8,128)} async-done(((f32[512,512]{1,0:T(8,128)}), f32[8192,512]{1,0:T(8,128)}) %all-gather.5.cloned.1.call-update) | async-done | bytes 16777232 | tf_op jit(solution)/shard_map/all_gather | solution.py:30
  329.8 1.3 slice.74
  331.1 0.1 copy.11
  331.2 111.8 %all-gather.7.cloned.1.call-done = f32[8192,512]{1,0:T(8,128)} async-done(((f32[512,512]{1,0:T(8,128)}), f32[8192,512]{1,0:T(8,128)}) %all-gather.7.cloned.1.call-update) | async-done | bytes 16777232 | tf_op jit(solution)/shard_map/all_gather | solution.py:30
  443.0 1.3 slice.75
  444.3 56.5 %while.23 = (s32[]{:T(128)}, f32[512,512]{1,0:T(8,128)S(1)}, f32[512,512]{1,0:T(8,128)}, f32[512,512]{1,0:T(8,128)S(1)}, f32[512,512]{1,0:T(8,128)S(1)}, /*index...) while((s32[]{:T(128)}, f32[512,512]{1,0:T(8,128)S(1)}, ...), condition=%wide.region_8.9_spmd.clone, body=%wide.region_7.8_spmd.clone.sunk | while | flops 1572870 | bytes 10485917 | solution.py:36
  444.3 3.5 fusion.115
  447.8 3.8 fusion.115
  451.6 3.8 fusion.115
  455.4 3.8 fusion.115
  459.1 3.8 fusion.115
  462.9 3.8 fusion.115
  466.7 3.8 fusion.115
  470.5 3.8 fusion.115
  474.3 3.8 fusion.115
  478.1 3.8 fusion.115
  481.9 3.8 fusion.115
  485.6 3.8 fusion.115
  489.4 3.8 fusion.115
  493.2 3.8 fusion.115
  497.0 3.8 fusion.115
  500.8 0.6 constant_dynamic-slice_fusion.1
  501.4 1.5 multiply_subtract_fusion
  (9 shorter events, 0.0 us)
Async XLA Ops:
  7.2 322.6 %all-gather.5.cloned.1.call-start = ((), (), s32[]{:S(2)}) async-start(), calls=%async_computation | async-start | bytes 17825792 | tf_op jit(solution)/shard_map/all_gather | solution.py:30
  27.1 26.5 %copy-start.2 = (f32[512,512]{1,0:T(8,128)}, f32[512,512]{1,0:T(8,128)S(1)}, u32[]{:S(2)}) copy-start(f32[512,512]{1,0:T(8,128)S(1)} %subtract_divide_fusion) | copy-start | bytes 3145732
  28.1 60.9 %collective-permute-start = (f32[128,512]{1,0:T(8,128)}, f32[128,512]{1,0:T(8,128)}, u32[]{:S(2)}, u32[]{:S(2)}) collective-permute-start(f32[128,512]{1,0:T(8,128)} %get-tuple-element.267), channel_id=1, source_target_pairs={{0,16},{16,32},{32,48},{48,64},{64,80},{80,96},{96,112},{1,17},{17... | collective-permute-start | bytes 786440 | tf_op jit(solution)/shard_map/ppermute | solution.py:23
  31.1 22.6 %copy-start.4 = (f32[1,32,256]{2,1,0:T(8,128)S(1)}, f32[1,32,256]{2,1,0:T(8,128)}, u32[]{:S(2)}) copy-start(f32[1,32,256]{2,1,0:T(8,128)} %param.7) | copy-start | bytes 98308
  31.1 57.9 %collective-permute-start.1 = (f32[128,512]{1,0:T(8,128)}, f32[128,512]{1,0:T(8,128)}, u32[]{:S(2)}, u32[]{:S(2)}) collective-permute-start(f32[128,512]{1,0:T(8,128)} %get-tuple-element.268), channel_id=1, source_target_pairs={{16,0},{32,16},{48,32},{64,48},{80,64},{96,80},{112,96},{17,1},{33... | collective-permute-start | bytes 786440 | tf_op jit(solution)/shard_map/ppermute | solution.py:24
  79.4 4.3 copy-start.5
  85.0 4.0 copy-start.3
  153.2 15.9 %copy-start.1 = (f32[768,768]{1,0:T(8,128)S(1)}, f32[768,768]{1,0:T(8,128)}, u32[]{:S(2)}) copy-start(f32[768,768]{1,0:T(8,128)} %convolution_add_fusion) | copy-start | bytes 7077892
  169.1 26.0 %copy-start = (f32[768,768]{1,0:T(8,128)S(1)}, f32[768,768]{1,0:T(8,128)}, u32[]{:S(2)}) copy-start(f32[768,768]{1,0:T(8,128)} %fusion.7) | copy-start | bytes 7077892
  217.9 225.1 %all-gather.7.cloned.1.call-start = ((), (), s32[]{:S(2)}) async-start(), calls=%async_computation.1 | async-start | bytes 17825792 | tf_op jit(solution)/shard_map/all_gather | solution.py:30
Sparse Core Ops, SparseCore 0:
  218.0 111.7 all-gather.4
  331.9 111.0 all-gather.6
where the time goes:
time: 519 us; the launch traced here: 510 us
  waiting for transfers between devices  224 us (43%)
  matrix products  147 us (28%)
  other arithmetic  82 us (16%)
  blocking collectives  26.1 us (5%)
  between operations  20 us (4%)
  starting transfers between devices  7.01 us (1%)
    all_gather x2, waiting for transfers between devices, merged_2(): everything = jax.tree.map(lambda part: lax.all_gather(part, axis), shard)  223 us
    dot_general x18, matrix products, product(): jnp.dot(former, latter, precision=exact_mode, preferred_element_type=jnp....  147 us
    max x15, other arithmetic, combine(): jnp.maximum(jnp.minimum(former[0], latter[0]), jnp.maximum(former[1], lat...  56.5 us
    psum x1, blocking collectives, per_device(): totals = lax.psum((local_sums[0], local_sums[1]), 'tile')  13.8 us
    all_gather x1, blocking collectives, per_device(): gathered = lax.all_gather(templates, 'tile', axis=1, tiled=True)  12.3 us
  transfers between devices with their start and end apart: 4, of which 2 were waited for; matrix products, arithmetic and copies ran while one was open for 8% of the time, Pallas kernels for 0%

commit v1 on v0

v1 whole, which is shorter than its diff:
```python
import math

import numpy as np
import jax
import jax.numpy as jnp
from jax import lax
from jax.sharding import PartitionSpec as P

TPL = 256


WAVELENGTH = 0.0197
AMPLITUDE = 0.07
mode = lax.Precision.HIGH


def padded(shard, sides, width):
    for axis, dim in sides:
        size, length = (lax.axis_size(axis), shard.shape[dim])
        up = [(i, (i + 1) % size) for i in range(size - 1)]
        down = [(j, i) for i, j in up]
        last = lax.slice_in_dim(shard, length - width, length, axis=dim)
        initial = lax.slice_in_dim(shard, 0, width, axis=dim)
        before = lax.ppermute(last, axis, up)
        after = lax.ppermute(initial, axis, down)
        shard = jnp.concatenate([before, shard, after], axis=dim)
    return shard


def product(former, latter):
    return jnp.dot(former, latter, precision=mode, preferred_element_type=jnp.float32)


def tables(tile_width, margin, extent):
    n = tile_width + 2 * margin
    h = n // 2 + 1
    idx = np.arange(n)
    angles = 2.0 * np.pi * ((idx[:, None] * idx[None, :]) % n) / n
    cos, sin = np.cos(angles), np.sin(angles)
    left = np.concatenate([cos[:h], sin[:h]], axis=0)
    left_t = left[:, :extent]
    right_w = np.concatenate([cos[margin:margin + tile_width], sin[margin:margin + tile_width]], axis=1)
    right_t = np.concatenate([cos[:extent], sin[:extent]], axis=1)
    back = np.concatenate([cos[:, :tile_width], sin[:, :tile_width]], axis=1)
    weight = np.full(h, 2.0)
    weight[0] = 1.0
    weight[-1] = 1.0
    final = np.concatenate(
        [cos[:tile_width, :h] * weight, -2.0 * sin[:tile_width, 1:h - 1]], axis=1
    ) / (n * n)
    as32 = lambda a: jnp.asarray(a.astype(np.float32))
    return tuple(as32(a) for a in (left, left_t, right_w, right_t, back, final))


def per_device(micrograph, templates, defocus_values, defocus_group):
    tile_rows, tile_width = micrograph.shape
    margin = TPL // 2
    n = tile_width + 2 * margin
    h = n // 2 + 1
    tile_count = lax.axis_size("tile")
    pixel_count = float(tile_rows * tile_width * tile_count)
    local_sums = (jnp.sum(micrograph), jnp.sum(micrograph * micrograph))
    totals = lax.psum((local_sums[0], local_sums[1]), "tile")
    centre = totals[0] / pixel_count
    spread = jnp.sqrt(totals[1] / pixel_count - centre * centre + 1e-05)
    rows_ext = padded((micrograph - centre) / spread, (("tile", 0),), margin)

    gathered = lax.all_gather(templates, "tile", axis=1, tiled=True)[0]
    extent = gathered.shape[0]
    left, left_t, right_w, right_t, back, final = tables(tile_width, margin, extent)

    centred = gathered - jnp.mean(gathered)
    root_mean = jnp.sqrt(jnp.mean(centred * centred) + 1e-06)
    normed = centred / (root_mean * TPL)

    stage = product(left, rows_ext)
    spec = product(stage, right_w)
    a_c, a_s = spec[:h, :n], spec[:h, n:]
    b_c, b_s = spec[h:, :n], spec[h:, n:]
    spec_real = a_c - b_s
    spec_imag = -(a_s + b_c)

    stage_t = product(left_t, normed)
    spec_t = product(stage_t, right_t)
    ta_c, ta_s = spec_t[:h, :n], spec_t[:h, n:]
    tb_c, tb_s = spec_t[h:, :n], spec_t[h:, n:]
    template_real = ta_c - tb_s
    template_imag = -(ta_s + tb_c)

    positions = lax.iota(jnp.int32, n)
    signed_freq = (
        jnp.where(positions < n // 2, positions, positions - n).astype(jnp.float32) / n
    )
    freq_square = signed_freq[:h, None] ** 2 + signed_freq[None, :] ** 2
    group_ids = lax.iota(jnp.int32, defocus_values.shape[0])
    defocus = jnp.sum(jnp.where(group_ids == defocus_group[0], defocus_values, 0.0))
    phase_shift = math.pi * WAVELENGTH * defocus * freq_square
    contrast = -(
        math.sqrt(1.0 - AMPLITUDE * AMPLITUDE) * jnp.sin(phase_shift)
        + AMPLITUDE * jnp.cos(phase_shift)
    )
    product_real = (spec_real * template_real + spec_imag * template_imag) * contrast
    product_imag = (spec_imag * template_real - spec_real * template_imag) * contrast

    inner = product(jnp.concatenate([product_real, product_imag], axis=0), back)
    pr_c, pr_s = inner[:h, :tile_width], inner[:h, tile_width:]
    pi_c, pi_s = inner[h:, :tile_width], inner[h:, tile_width:]
    back_real = pr_c - pi_s
    back_imag = pr_s + pi_c
    scores = product(final, jnp.concatenate([back_real, back_imag[1:h - 1]], axis=0))

    orient_count = lax.axis_size("orient")
    share_rows = tile_rows // orient_count
    pieces = lax.all_to_all(scores, "orient", 0, 0, tiled=True).reshape(
        orient_count, share_rows, tile_width
    )
    top = pieces[0]
    second = jnp.full_like(top, -jnp.inf)
    total = pieces[0]
    squares = pieces[0] * pieces[0]
    for k in range(1, orient_count):
        value = pieces[k]
        second = jnp.maximum(second, jnp.minimum(top, value))
        top = jnp.maximum(top, value)
        total = total + value
        squares = squares + value * value
    mean_map = total / orient_count
    variance = squares / orient_count - mean_map * mean_map
    return (top, second, mean_map, variance)


def solution(mesh):
    placed = (P("tile", None), P("orient", "tile", None), P(), P("tile"))
    return jax.shard_map(
        per_device,
        mesh=mesh,
        in_specs=placed,
        out_specs=(
            P(("tile", "orient"), None),
            P(("tile", "orient"), None),
            P(("tile", "orient"), None),
            P(("tile", "orient"), None),
        ),
        check_vma=False,
    )
```

time: 519 us -> 103 us (0.20); the launches traced: 510 us -> 102 us
  waiting for transfers between devices: 224 us -> 0.01 us
  matrix products: 147 us -> 25 us
  other arithmetic: 82 us -> 12.3 us
  blocking collectives: 26.1 us -> 50.1 us
  between operations: 20 us -> 6.25 us
    all_gather x2 -> x0, waiting for transfers between devices: 223 us -> none  [merged_2(): everything = jax.tree.map(lambda part: lax.all_gather(part, axis), shard)]
    dot_general x18 -> x9, matrix products: 147 us -> 25 us  [product(): jnp.dot(former, latter, precision=mode, preferred_element_type=jnp.float32)]
    max x15 -> x2, other arithmetic: 56.5 us -> 1.44 us  [the longest x1 0.73 us: per_device(): second = jnp.maximum(second, jnp.minimum(top, value))]
    all_to_all x0 -> x1, blocking collectives: none -> 24.1 us  [per_device(): lax.all_to_all(scores, 'orient', 0, 0, tiled=True)]
    cos x1 -> x0, other arithmetic: 9.75 us -> none  [fourier_tables(): return (jnp.cos(angles), jnp.sin(angles))]
    sin x1 -> x0, other arithmetic: 8.88 us -> none  [fourier_tables(): return (jnp.cos(angles), jnp.sin(angles))]
    mul x0 -> x1, other arithmetic: none -> 5.83 us  [per_device(): (spec_real * template_real + spec_imag * template_imag) * contrast]
  transfers between devices with their start and end apart: 4 -> 2, of which waited for: 2 -> 0; matrix products, arithmetic and copies ran while one was open for 8% -> 15% of each run, Pallas kernels for 0% -> 0%
where the time goes in v1:
time: 103 us; the launch traced here: 102 us
  blocking collectives  50.1 us (49%)
  matrix products  25 us (24%)
  other arithmetic  12.3 us (12%)
  between operations  6.25 us (6%)
  starting transfers between devices  6.12 us (6%)
  local copies, waits for them, and re-layouts  2.18 us (2%)
    dot_general x9, matrix products, product(): jnp.dot(former, latter, precision=mode, preferred_element_type=jnp.float32)  25 us
    all_to_all x1, blocking collectives, per_device(): lax.all_to_all(scores, 'orient', 0, 0, tiled=True)  24.1 us
    psum x1, blocking collectives, per_device(): totals = lax.psum((local_sums[0], local_sums[1]), 'tile')  13.8 us
    all_gather x1, blocking collectives, per_device(): gathered = lax.all_gather(templates, 'tile', axis=1, tiled=True)[0]  12.2 us
    mul x1, other arithmetic, per_device(): (spec_real * template_real + spec_imag * template_imag) * contrast  5.83 us
    ppermute x1, starting transfers between devices, padded(): after = lax.ppermute(initial, axis, down)  3.15 us
    ppermute x1, starting transfers between devices, padded(): before = lax.ppermute(last, axis, up)  2.97 us
    reduce_sum x1, other arithmetic, per_device(): local_sums = (jnp.sum(micrograph), jnp.sum(micrograph * micrograph))  2.19 us
  transfers between devices with their start and end apart: 2, of which 0 were waited for; matrix products, arithmetic and copies ran while one was open for 15% of the time, Pallas kernels for 0%

profile of v1, /device:TPU:1, one launch (start us, length us, event | category | flops | bytes accessed | tf_op | source)
XLA Modules:
  0.0 102.0 jit_solution(1610078001904721976)
XLA Ops:
  0.6 0.0 copy-start
  0.6 2.2 %fusion.23 = (f32[]{:T(128)}, f32[]{:T(128)}) fusion(f32[512,512]{1,0:T(8,128)} %param.10), kind=kLoop, calls=%fused_computation.45 | loop fusion | flops 786430 | bytes 1048584 | tf_op jit(solution)/shard_map/reduce_sum | solution.py:62
  2.8 13.8 %all-reduce = (f32[]{:T(128)}, f32[]{:T(128)}) all-reduce(f32[]{:T(128)} %get-tuple-element.5, f32[]{:T(128)} %get-tuple-element.4), channel_id=1, replica_groups=mesh['tile'=8,'orient'=16] {'tile'}, use_global_device_ids=true, to_apply=%region_3.0 | all-reduce | flops 2 | bytes 16 | tf_op jit(solution)/shard_map/psum | solution.py:63
  19.3 0.0 copy-done
  19.3 0.0 copy-start.8
  19.3 0.1 subtract_divide_fusion
  19.4 0.8 fusion.25
  20.3 3.0 %collective-permute-start = (f32[128,512]{1,0:T(8,128)}, f32[128,512]{1,0:T(8,128)S(1)}, u32[]{:S(2)}, u32[]{:S(2)}) collective-permute-start(f32[128,512]{1,0:T(8,128)} %get-tuple-element.14), channel_id=1, source_target_pairs={{0,16},{16,32},{32,48},{48,64},{64,80},{80,96},{96,112},{1,17},{17... | collective-permute-start | bytes 786440 | tf_op jit(solution)/shard_map/ppermute | solution.py:24
  23.3 3.1 %collective-permute-start.1 = (f32[128,512]{1,0:T(8,128)}, f32[128,512]{1,0:T(8,128)}, u32[]{:S(2)}, u32[]{:S(2)}) collective-permute-start(f32[128,512]{1,0:T(8,128)} %get-tuple-element.15), channel_id=1, source_target_pairs={{16,0},{32,16},{48,32},{64,48},{80,64},{96,80},{112,96},{17,1},{33... | collective-permute-start | bytes 786440 | tf_op jit(solution)/shard_map/ppermute | solution.py:25
  27.1 0.0 copy-done.8
  27.1 12.2 %all_gather.3 = f32[1,256,256]{2,1,0:T(8,128)S(1)} all-gather(f32[1,32,256]{2,1,0:T(8,128)S(1)} %copy-done.8), channel_id=1, replica_groups=mesh['tile'=8,'orient'=16] {'tile'}, dimensions={1}, use_global_device_ids=true | all-gather | bytes 294912 | tf_op jit(solution)/shard_map/all_gather | solution.py:68
  39.3 0.7 reduce_sum.47
  40.6 0.7 multiply_reduce_fusion.1
  42.0 0.0 copy-start.9
  42.0 4.8 %fusion.27 = f32[512,770]{1,0:T(8,128)S(1)} fusion(f32[512,512]{1,0:T(8,128)S(1)} %subtract_divide_fusion, f32[770,512]{1,0:T(8,128)} %constant.58), kind=kOutput, calls=%fused_computation.49 | convolution fusion | flops 1211105280 | bytes 4202496 | tf_op jit(solution)/shard_map/dot_general | solution.py:31
  46.8 0.0 copy-done.9
  46.8 0.6 fusion.21
  47.4 0.0 copy-start.3
  47.4 2.3 %fusion.11 = f32[256,770]{1,0:T(8,128)S(1)} fusion(f32[770,256]{1,0:T(8,128)} %constant.50.clone, f32[1,256,256]{2,1,0:T(8,128)S(1)} %all_gather.3, f32[]{:T(128)S(6)} %mul.113, f32[]{:T(128)S(6)} %div.43), kind=kOutput, calls=%fused_computation.22 | convolution fusion | flops 302907392 | bytes 1839112 | tf_op jit(solution)/shard_map/dot_general | solution.py:31
  49.7 0.0 copy-done.3
  49.7 0.0 copy-start.7
  49.7 4.3 %fusion.29 = f32[770,1536]{1,0:T(8,128)} fusion(f32[256,770]{1,0:T(8,128)S(1)} %fusion.11, f32[256,1536]{1,0:T(8,128)S(1)} %copy-done.3), kind=kOutput, calls=%fused_computation.51 | convolution fusion | flops 1816657920 | bytes 7092224 | tf_op jit(solution)/shard_map/dot_general | solution.py:31
  54.0 0.0 copy-start.6
  54.8 0.0 collective-permute-done.1
  54.8 0.0 copy-done.7
  54.8 0.0 copy-start.2
  54.8 2.2 %fusion.28 = f32[512,770]{1,0:T(8,128)S(1)} fusion(f32[128,512]{1,0:T(8,128)} %collective-permute-done.1, f32[770,128]{1,0:T(8,128)S(1)} %copy-done.7), kind=kOutput, calls=%fused_computation.50 | convolution fusion | flops 302776320 | bytes 2233344 | tf_op jit(solution)/shard_map/dot_general | solution.py:31
  57.0 0.0 collective-permute-done
  57.0 0.0 copy-done.6
  57.0 0.0 slice-start
  57.0 1.1 %fusion.26 = f32[512,770]{1,0:T(8,128)S(1)} fusion(f32[128,512]{1,0:T(8,128)S(1)} %collective-permute-done, f32[770,128]{1,0:T(8,128)S(1)} %copy-done.6), kind=kOutput, calls=%fused_computation.48 | convolution fusion | flops 302776320 | bytes 2233344 | tf_op jit(solution)/shard_map/dot_general | solution.py:31
  58.1 0.0 copy-done.2
  58.1 0.0 slice-start.1
  58.1 4.2 %fusion.4 = f32[770,1536]{1,0:T(8,128)S(1)} fusion(f32[512,1536]{1,0:T(8,128)S(1)} %copy-done.2, f32[512,770]{1,0:T(8,128)S(1)} %fusion.28, f32[512,770]{1,0:T(8,128)S(1)} %fusion.26, f32[512,770]{1,0:T(8,128)S(1)} %fusion.27), kind=kOutput, calls=%fused_computation.4 | convolution fusion | flops 3634104320 | bytes 12607488 | tf_op jit(solution)/shard_map/dot_general | solution.py:31
  62.3 0.0 slice-done
  62.4 0.0 slice-done.1
  62.4 0.0 copy-start.1
  62.4 5.8 %fusion.7 = (f32[385,768]{1,0:T(8,128)S(1)}, f32[385,768]{1,0:T(8,128)S(1)}) fusion(f32[768]{0:T(1024)S(1)} %fusion.20, f32[385]{0:T(512)S(1)} %slice_multiply_fusion, f32[]{:T(128)S(6)} %mul_shard_map.3, f32[770,1536]{1,0:T(8,128)S(1)} %fusion.4, f32[770,1536]{1,0:T(8,128)S(1)} %bitcast.33), kind=kLoop, calls=%fused_computation.14 | loop fusion | flops 5913600 | bytes 11831816 | tf_op jit(solution)/shard_map/mul | solution.py:102
  68.2 0.0 copy-done.1
  68.2 4.0 %fusion = f32[770,1024]{1,0:T(8,128)S(1)} fusion(f32[768,1024]{1,0:T(8,128)S(1)} %copy-done.1, f32[385,768]{1,0:T(8,128)S(1)} %get-tuple-element.11, f32[385,768]{1,0:T(8,128)S(1)} %get-tuple-element.10), kind=kOutput, calls=%fused_computation | convolution fusion | flops 3633907200 | bytes 8665088 | tf_op jit(solution)/shard_map/dot_general | solution.py:31
  72.2 0.0 copy-start.4
  72.3 0.2 fusion.24
  72.4 1.0 %copy-done.4 = f32[512,385]{1,0:T(8,128)S(1)} copy-done((f32[512,385]{1,0:T(8,128)S(1)}, f32[512,385]{1,0:T(8,128)}, u32[]{:S(2)}) %copy-start.4) | copy-done | bytes 788504
  73.5 0.0 copy-start.5
  73.5 1.0 %fusion.8 = f32[512,512]{0,1:T(8,128)S(1)} fusion(f32[512,385]{1,0:T(8,128)S(1)} %copy-done.4, f32[770,1024]{1,0:T(8,128)S(1)} %fusion), kind=kOutput, calls=%fused_computation.18 | convolution fusion | flops 605749760 | bytes 3702784 | tf_op jit(solution)/shard_map/dot_general | solution.py:31
  74.5 0.1 copy-done.5
  74.6 1.1 %convolution_add_fusion = f32[512,512]{0,1:T(8,128)S(1)} fusion(f32[512,512]{0,1:T(8,128)S(1)} %fusion.8, f32[512,383]{1,0:T(8,128)S(1)} %copy-done.5, f32[385,512]{1,0:T(8,128)S(1)} %get-tuple-element.13, f32[385,512]{1,0:T(8,128)S(1)} %get-tuple-element.12), kind=kOutput, calls=%fused_computation.7 | convolution fusion | flops 602865152 | bytes 4456448 | tf_op jit(solution)/shard_map/dot_general | solution.py:31
  75.7 24.1 %all_to_all.9 = f32[16,32,512]{2,1,0:T(8,128)S(1)} all-to-all(f32[16,32,512]{2,1,0:T(8,128)S(1)} %bitcast.34), channel_id=1, replica_groups=mesh['tile'=8,'orient'=16] {'orient'}, dimensions={0} | all-to-all | bytes 2097152 | tf_op jit(solution)/shard_map/all_to_all | solution.py:114
  99.8 0.7 maximum_bitcast_fusion.1
  100.5 0.7 maximum_bitcast_fusion
  101.2 0.8 fusion.17
  (4 shorter events, 0.0 us)
Async XLA Ops:
  0.6 18.7 %copy-start = (f32[512,512]{1,0:T(8,128)S(1)}, f32[512,512]{1,0:T(8,128)}, u32[]{:S(2)}) copy-start(f32[512,512]{1,0:T(8,128)} %param.10) | copy-start | bytes 3145732
  19.3 7.8 %copy-start.8 = (f32[1,32,256]{2,1,0:T(8,128)S(1)}, f32[1,32,256]{2,1,0:T(8,128)}, u32[]{:S(2)}) copy-start(f32[1,32,256]{2,1,0:T(8,128)} %param.11) | copy-start | bytes 98308
  20.3 36.7 %collective-permute-start = (f32[128,512]{1,0:T(8,128)}, f32[128,512]{1,0:T(8,128)S(1)}, u32[]{:S(2)}, u32[]{:S(2)}) collective-permute-start(f32[128,512]{1,0:T(8,128)} %get-tuple-element.14), channel_id=1, source_target_pairs={{0,16},{16,32},{32,48},{48,64},{64,80},{80,96},{96,112},{1,17},{17... | collective-permute-start | bytes 786440 | tf_op jit(solution)/shard_map/ppermute | solution.py:24
  23.3 31.5 %collective-permute-start.1 = (f32[128,512]{1,0:T(8,128)}, f32[128,512]{1,0:T(8,128)}, u32[]{:S(2)}, u32[]{:S(2)}) collective-permute-start(f32[128,512]{1,0:T(8,128)} %get-tuple-element.15), channel_id=1, source_target_pairs={{16,0},{32,16},{48,32},{64,48},{80,64},{96,80},{112,96},{17,1},{33... | collective-permute-start | bytes 786440 | tf_op jit(solution)/shard_map/ppermute | solution.py:25
  42.0 4.9 %copy-start.9 = (f32[4]{0:T(128)S(1)}, f32[4]{0:T(128)}, u32[]{:S(2)}) copy-start(f32[4]{0:T(128)} %param.12) | copy-start | bytes 52
  47.4 2.3 %copy-start.3 = (f32[256,1536]{1,0:T(8,128)S(1)}, f32[256,1536]{1,0:T(8,128)}, u32[]{:S(2)}) copy-start(f32[256,1536]{1,0:T(8,128)} %constant.52.clone) | copy-start | bytes 4718596
  49.7 5.1 %copy-start.7 = (f32[770,128]{1,0:T(8,128)S(1)}, f32[770,128]{1,0:T(8,128)}, u32[]{:S(2)}) copy-start(f32[770,128]{1,0:T(8,128)} %constant.59) | copy-start | bytes 1182724
  54.0 2.9 %copy-start.6 = (f32[770,128]{1,0:T(8,128)S(1)}, f32[770,128]{1,0:T(8,128)}, u32[]{:S(2)}) copy-start(f32[770,128]{1,0:T(8,128)} %constant.57) | copy-start | bytes 1182724
  54.8 3.3 %copy-start.2 = (f32[512,1536]{1,0:T(8,128)S(1)}, f32[512,1536]{1,0:T(8,128)}, u32[]{:S(2)}) copy-start(f32[512,1536]{1,0:T(8,128)} %constant.51.clone) | copy-start | bytes 9437188
  57.0 5.4 %slice-start = ((s8[4767744]{0:T(1024)(128)(4,1)}), s8[4194304]{0:T(1024)(128)(4,1)S(1)}, s32[]{:S(2)}) async-start(s8[4767744]{0:T(1024)(128)(4,1)} %bitcast.32), calls=%async_computation.1 | async-start | bytes 8388608
  58.1 4.3 %slice-start.1 = ((s8[4767744]{0:T(1024)(128)(4,1)}), s8[573440]{0:T(1024)(128)(4,1)S(1)}, s32[]{:S(2)}) async-start(s8[4767744]{0:T(1024)(128)(4,1)} %bitcast.32), calls=%async_computation.2 | async-start | bytes 1146880
  62.4 5.9 %copy-start.1 = (f32[768,1024]{1,0:T(8,128)S(1)}, f32[768,1024]{1,0:T(8,128)}, u32[]{:S(2)}) copy-start(f32[768,1024]{1,0:T(8,128)} %constant.53.clone) | copy-start | bytes 9437188
  72.2 1.2 %copy-start.4 = (f32[512,385]{1,0:T(8,128)S(1)}, f32[512,385]{1,0:T(8,128)}, u32[]{:S(2)}) copy-start(f32[512,385]{1,0:T(8,128)} %constant.60) | copy-start | bytes 2365444
  73.5 1.1 %copy-start.5 = (f32[512,383]{1,0:T(8,128)S(1)}, f32[512,383]{1,0:T(8,128)}, u32[]{:S(2)}) copy-start(f32[512,383]{1,0:T(8,128)} %constant.61) | copy-start | bytes 2353156

commit v2 on v1

--- a/solution.py
+++ b/solution.py
@@ -4,7 +4,7 @@
 import jax
 import jax.numpy as jnp
 from jax import lax
-from jax.sharding import PartitionSpec as P
+from jax.sharding import Mesh, PartitionSpec as P
 
 TPL = 256
 
@@ -59,13 +59,17 @@
     h = n // 2 + 1
     tile_count = lax.axis_size("tile")
     pixel_count = float(tile_rows * tile_width * tile_count)
-    local_sums = (jnp.sum(micrograph), jnp.sum(micrograph * micrograph))
-    totals = lax.psum((local_sums[0], local_sums[1]), "tile")
+    own_rows, tpl_width = templates.shape[1], templates.shape[2]
+    sums = jnp.stack([jnp.sum(micrograph), jnp.sum(micrograph * micrograph)])
+    payload = jnp.concatenate(
+        [templates[0], jnp.pad(sums, (0, tpl_width - 2))[None]], axis=0
+    )
+    everything = lax.all_gather(payload, "tile")
+    totals = jnp.sum(everything[:, own_rows, :2], axis=0)
+    gathered = everything[:, :own_rows].reshape(tile_count * own_rows, tpl_width)
     centre = totals[0] / pixel_count
     spread = jnp.sqrt(totals[1] / pixel_count - centre * centre + 1e-05)
     rows_ext = padded((micrograph - centre) / spread, (("tile", 0),), margin)
-
-    gathered = lax.all_gather(templates, "tile", axis=1, tiled=True)[0]
     extent = gathered.shape[0]
     left, left_t, right_w, right_t, back, final = tables(tile_width, margin, extent)
 
@@ -109,37 +113,52 @@
     back_imag = pr_s + pi_c
     scores = product(final, jnp.concatenate([back_real, back_imag[1:h - 1]], axis=0))
 
-    orient_count = lax.axis_size("orient")
-    share_rows = tile_rows // orient_count
-    pieces = lax.all_to_all(scores, "orient", 0, 0, tiled=True).reshape(
-        orient_count, share_rows, tile_width
-    )
+    outer, inner_count = lax.axis_size("oz"), lax.axis_size("oy")
+    orient_count = outer * inner_count
+    block = tile_rows // outer
+    share_rows = block // inner_count
+    pieces = lax.all_to_all(scores, "oz", 0, 0, tiled=True).reshape(outer, block, tile_width)
     top = pieces[0]
     second = jnp.full_like(top, -jnp.inf)
     total = pieces[0]
     squares = pieces[0] * pieces[0]
-    for k in range(1, orient_count):
+    for k in range(1, outer):
         value = pieces[k]
         second = jnp.maximum(second, jnp.minimum(top, value))
         top = jnp.maximum(top, value)
         total = total + value
         squares = squares + value * value
+    partial = jnp.stack([top, second, total, squares], axis=0)
+    partial = partial.reshape(4, inner_count, share_rows, tile_width).transpose(1, 0, 2, 3)
+    parts = lax.all_to_all(
+        partial.reshape(inner_count * 4, share_rows, tile_width), "oy", 0, 0, tiled=True
+    ).reshape(inner_count, 4, share_rows, tile_width)
+    top, second, total, squares = parts[0, 0], parts[0, 1], parts[0, 2], parts[0, 3]
+    for k in range(1, inner_count):
+        other_top, other_second = parts[k, 0], parts[k, 1]
+        second = jnp.maximum(
+            jnp.minimum(top, other_top), jnp.maximum(second, other_second)
+        )
+        top = jnp.maximum(top, other_top)
+        total = total + parts[k, 2]
+        squares = squares + parts[k, 3]
     mean_map = total / orient_count
     variance = squares / orient_count - mean_map * mean_map
     return (top, second, mean_map, variance)
 
 
 def solution(mesh):
-    placed = (P("tile", None), P("orient", "tile", None), P(), P("tile"))
+    tile_size, orient_size = mesh.devices.shape
+    outer = 4 if orient_size % 4 == 0 else 1
+    split = Mesh(
+        mesh.devices.reshape(tile_size, outer, orient_size // outer), ("tile", "oz", "oy")
+    )
+    rows = P(("tile", "oz", "oy"), None)
+    placed = (P("tile", None), P(("oz", "oy"), "tile", None), P(), P("tile"))
     return jax.shard_map(
         per_device,
-        mesh=mesh,
+        mesh=split,
         in_specs=placed,
-        out_specs=(
-            P(("tile", "orient"), None),
-            P(("tile", "orient"), None),
-            P(("tile", "orient"), None),
-            P(("tile", "orient"), None),
-        ),
+        out_specs=(rows, rows, rows, rows),
         check_vma=False,
     )

time: 103 us -> 105 us (1.019)
  blocking collectives: 50.1 us -> 52.7 us
  other arithmetic: 12.3 us -> 13.9 us
  starting transfers between devices: 6.12 us -> 4.79 us
    all_to_all x1 -> x2, blocking collectives: 24.1 us -> 38.1 us  [the longest x1 19.9 us: per_device(): lax.all_to_all(scores, 'oz', 0, 0, tiled=True)]
    psum x1 -> x0, blocking collectives: 13.8 us -> none  [per_device(): totals = lax.psum((local_sums[0], local_sums[1]), 'tile')]
    all_gather x1, blocking collectives: 12.2 us -> 14.6 us  [per_device(): everything = lax.all_gather(payload, 'tile')]
    another operation x0 -> x1, other arithmetic: none -> 1.37 us  [per_device(): sums = jnp.stack([jnp.sum(micrograph), jnp.sum(micrograph * micrograph)])]
    ppermute x1, starting transfers between devices: 3.15 us -> 1.92 us  [padded(): after = lax.ppermute(initial, axis, down)]
    reduce_sum x1 -> x2, other arithmetic: 2.19 us -> 2.22 us  [the longest x1 2.19 us: per_device(): sums = jnp.stack([jnp.sum(micrograph), jnp.sum(micrograph * micrograph)])]
  transfers between devices with their start and end apart: 2 -> 2, of which waited for: 0 -> 0; matrix products, arithmetic and copies ran while one was open for 15% -> 14% of each run, Pallas kernels for 0% -> 0%
where the time goes in v2:
time: 105 us
  blocking collectives  52.7 us (50%)
  matrix products  24 us (23%)
  other arithmetic  13.9 us (13%)
  between operations  6.28 us (6%)
  starting transfers between devices  4.79 us (5%)
  local copies, waits for them, and re-layouts  2.83 us (3%)
    dot_general x9, matrix products, product(): jnp.dot(former, latter, precision=mode, preferred_element_type=jnp.float32)  24 us
    all_to_all x1, blocking collectives, per_device(): lax.all_to_all(scores, 'oz', 0, 0, tiled=True)  19.9 us
    all_to_all x1, blocking collectives, per_device(): lax.all_to_all(partial.reshape(inner_count * 4, share_rows, tile_width),...  18.2 us
    all_gather x1, blocking collectives, per_device(): everything = lax.all_gather(payload, 'tile')  14.6 us
    mul x1, other arithmetic, per_device(): (spec_real * template_real + spec_imag * template_imag) * contrast  5.83 us
    ppermute x1, starting transfers between devices, padded(): before = lax.ppermute(last, axis, up)  2.86 us
    reduce_sum x1, other arithmetic, per_device(): sums = jnp.stack([jnp.sum(micrograph), jnp.sum(micrograph * micrograph)])  2.19 us
  transfers between devices with their start and end apart: 2, of which 0 were waited for; matrix products, arithmetic and copies ran while one was open for 14% of the time, Pallas kernels for 0%

profile of v2, /device:TPU:1, one launch (start us, length us, event | category | flops | bytes accessed | tf_op | source)
XLA Modules:
  0.0 104.6 jit_solution(10299307920945019112)
XLA Ops:
  0.6 0.0 copy-start
  0.6 2.2 %fusion.26 = (f32[]{:T(128)}, f32[]{:T(128)}) fusion(f32[512,512]{1,0:T(8,128)} %param.10), kind=kLoop, calls=%fused_computation.65 | loop fusion | flops 786430 | bytes 1048584 | tf_op jit(solution)/shard_map/reduce_sum | solution.py:63
  2.8 1.4 %select_maximum_fusion = f32[256]{0:T(256)S(1)} fusion(f32[1]{0:T(128)} %bitcast.2, f32[1]{0:T(128)} %bitcast.1), kind=kLoop, calls=%fused_computation.62 | loop fusion | flops 1024 | bytes 1032 | tf_op jit(solution)/shard_map/stack | solution.py:63
  4.2 0.8 maximum_bitcast_fusion.2
  5.0 14.6 %all-gather.1 = f32[8,33,256]{2,1,0:T(8,128)S(1)} all-gather(f32[1,33,256]{2,1,0:T(8,128)S(1)} %maximum_bitcast_fusion.2), channel_id=2, replica_groups=mesh['tile'=8,'oz'=4,'oy'=4] {'tile'}, dimensions={0}, use_global_device_ids=true | all-gather | bytes 304128 | tf_op jit(solution)/shard_map/all_gather | solution.py:67
  19.6 0.6 fusion.30
  22.8 0.0 copy-done
  22.8 0.1 subtract_divide_fusion
  22.9 0.8 fusion.29
  23.8 2.9 %collective-permute-start = (f32[128,512]{1,0:T(8,128)}, f32[128,512]{1,0:T(8,128)S(1)}, u32[]{:S(2)}, u32[]{:S(2)}) collective-permute-start(f32[128,512]{1,0:T(8,128)} %get-tuple-element.18), channel_id=1, source_target_pairs={{0,16},{16,32},{32,48},{48,64},{64,80},{80,96},{96,112},{1,17},{17... | collective-permute-start | bytes 786440 | tf_op jit(solution)/shard_map/ppermute | solution.py:24
  26.6 1.9 %collective-permute-start.1 = (f32[128,512]{1,0:T(8,128)}, f32[128,512]{1,0:T(8,128)}, u32[]{:S(2)}, u32[]{:S(2)}) collective-permute-start(f32[128,512]{1,0:T(8,128)} %get-tuple-element.19), channel_id=1, source_target_pairs={{16,0},{32,16},{48,32},{64,48},{80,64},{96,80},{112,96},{17,1},{33... | collective-permute-start | bytes 786440 | tf_op jit(solution)/shard_map/ppermute | solution.py:25
  28.6 0.7 slice_reduce_fusion
  30.5 0.7 multiply_reduce_fusion.1
  32.0 0.0 copy-start.9
  32.0 0.0 copy-start.5
  32.0 4.9 %fusion.32 = f32[512,770]{1,0:T(8,128)S(1)} fusion(f32[512,512]{1,0:T(8,128)S(1)} %subtract_divide_fusion, f32[770,512]{1,0:T(8,128)} %constant.66), kind=kOutput, calls=%fused_computation.70 | convolution fusion | flops 1211105280 | bytes 4202496 | tf_op jit(solution)/shard_map/dot_general | solution.py:31
  36.9 0.0 copy-start.3
  36.9 0.0 copy-done.9
  36.9 0.6 fusion.24
  37.5 0.0 copy-done.5
  37.5 1.0 fusion.34
  38.5 0.0 copy-done.3
  38.5 0.0 copy-start.8
  38.6 4.3 %fusion.35 = f32[770,1536]{1,0:T(8,128)} fusion(f32[256,770]{1,0:T(8,128)S(1)} %fusion.34, f32[256,1536]{1,0:T(8,128)S(1)} %copy-done.3), kind=kOutput, calls=%fused_computation.73 | convolution fusion | flops 1816657920 | bytes 7092224 | tf_op jit(solution)/shard_map/dot_general | solution.py:31
  42.9 0.0 copy-start.7
  43.6 0.0 collective-permute-done.1
  43.6 0.0 copy-done.8
  43.6 0.0 copy-start.2
  43.6 2.2 %fusion.33 = f32[512,770]{1,0:T(8,128)S(1)} fusion(f32[128,512]{1,0:T(8,128)} %collective-permute-done.1, f32[770,128]{1,0:T(8,128)S(1)} %copy-done.8), kind=kOutput, calls=%fused_computation.71 | convolution fusion | flops 302776320 | bytes 2233344 | tf_op jit(solution)/shard_map/dot_general | solution.py:31
  45.8 0.0 collective-permute-done
  45.8 0.0 copy-done.7
  45.8 0.0 slice-start
  45.8 1.1 %fusion.31 = f32[512,770]{1,0:T(8,128)S(1)} fusion(f32[128,512]{1,0:T(8,128)S(1)} %collective-permute-done, f32[770,128]{1,0:T(8,128)S(1)} %copy-done.7), kind=kOutput, calls=%fused_computation.69 | convolution fusion | flops 302776320 | bytes 2233344 | tf_op jit(solution)/shard_map/dot_general | solution.py:31
  46.9 0.0 copy-done.2
  46.9 0.0 slice-start.1
  46.9 4.2 %fusion.4 = f32[770,1536]{1,0:T(8,128)S(1)} fusion(f32[512,1536]{1,0:T(8,128)S(1)} %copy-done.2, f32[512,770]{1,0:T(8,128)S(1)} %fusion.33, f32[512,770]{1,0:T(8,128)S(1)} %fusion.31, f32[512,770]{1,0:T(8,128)S(1)} %fusion.32), kind=kOutput, calls=%fused_computation.4 | convolution fusion | flops 3634104320 | bytes 12607488 | tf_op jit(solution)/shard_map/dot_general | solution.py:31
  51.2 0.0 slice-done
  51.2 0.0 slice-done.1
  51.2 0.0 copy-start.1
  51.2 5.8 %fusion.7 = (f32[385,768]{1,0:T(8,128)S(1)}, f32[385,768]{1,0:T(8,128)S(1)}) fusion(f32[768]{0:T(1024)S(1)} %fusion.23, f32[385]{0:T(512)S(1)} %slice_multiply_fusion, f32[]{:T(128)S(6)} %mul_shard_map.3, f32[770,1536]{1,0:T(8,128)S(1)} %fusion.4, f32[770,1536]{1,0:T(8,128)S(1)} %bitcast.48), kind=kLoop, calls=%fused_computation.14 | loop fusion | flops 5913600 | bytes 11831816 | tf_op jit(solution)/shard_map/mul | solution.py:106
  57.1 0.0 copy-done.1
  57.1 4.1 %fusion = f32[770,1024]{1,0:T(8,128)S(1)} fusion(f32[768,1024]{1,0:T(8,128)S(1)} %copy-done.1, f32[385,768]{1,0:T(8,128)S(1)} %get-tuple-element.9, f32[385,768]{1,0:T(8,128)S(1)} %get-tuple-element.8), kind=kOutput, calls=%fused_computation | convolution fusion | flops 3633907200 | bytes 8665088 | tf_op jit(solution)/shard_map/dot_general | solution.py:31
  61.2 0.0 copy-start.4
  61.2 0.2 fusion.28
  61.4 1.0 %copy-done.4 = f32[512,385]{1,0:T(8,128)S(1)} copy-done((f32[512,385]{1,0:T(8,128)S(1)}, f32[512,385]{1,0:T(8,128)}, u32[]{:S(2)}) %copy-start.4) | copy-done | bytes 788504
  62.4 0.0 copy-start.6
  62.4 1.1 %fusion.8 = f32[512,512]{0,1:T(8,128)S(1)} fusion(f32[512,385]{1,0:T(8,128)S(1)} %copy-done.4, f32[770,1024]{1,0:T(8,128)S(1)} %fusion), kind=kOutput, calls=%fused_computation.19 | convolution fusion | flops 605749760 | bytes 3702784 | tf_op jit(solution)/shard_map/dot_general | solution.py:31
  63.5 0.0 copy-done.6
  63.6 1.1 %convolution_add_fusion = f32[512,512]{0,1:T(8,128)S(1)} fusion(f32[512,512]{0,1:T(8,128)S(1)} %fusion.8, f32[512,383]{1,0:T(8,128)S(1)} %copy-done.6, f32[385,512]{1,0:T(8,128)S(1)} %get-tuple-element.11, f32[385,512]{1,0:T(8,128)S(1)} %get-tuple-element.10), kind=kOutput, calls=%fused_computation.7 | convolution fusion | flops 602865152 | bytes 4456448 | tf_op jit(solution)/shard_map/dot_general | solution.py:31
  64.7 19.9 %all_to_all.14 = f32[4,128,512]{2,1,0:T(8,128)S(1)} all-to-all(f32[4,128,512]{2,1,0:T(8,128)S(1)} %bitcast.51), channel_id=1, replica_groups=mesh['tile'=8,'oz'=4,'oy'=4] {'oz'}, dimensions={0} | all-to-all | bytes 2097152 | tf_op jit(solution)/shard_map/all_to_all | solution.py:120
  84.6 0.2 slice_maximum_fusion
  84.8 0.1 maximum_bitcast_fusion
  84.9 0.1 copy.15
  84.9 18.2 %all_to_all.15 = f32[16,32,512]{2,1,0:T(8,128)S(1)} all-to-all(f32[16,32,512]{2,1,0:T(8,128)S(1)} %bitcast.52), channel_id=1, replica_groups=mesh['tile'=8,'oz'=4,'oy'=4] {'oy'}, dimensions={0} | all-to-all | bytes 2097152 | tf_op jit(solution)/shard_map/all_to_all | solution.py:133
  103.2 0.7 fusion.18
  103.9 0.7 fusion.14
  (6 shorter events, 0.1 us)
Async XLA Ops:
  0.6 22.2 %copy-start = (f32[512,512]{1,0:T(8,128)S(1)}, f32[512,512]{1,0:T(8,128)}, u32[]{:S(2)}) copy-start(f32[512,512]{1,0:T(8,128)} %param.10) | copy-start | bytes 3145732
  23.8 22.0 %collective-permute-start = (f32[128,512]{1,0:T(8,128)}, f32[128,512]{1,0:T(8,128)S(1)}, u32[]{:S(2)}, u32[]{:S(2)}) collective-permute-start(f32[128,512]{1,0:T(8,128)} %get-tuple-element.18), channel_id=1, source_target_pairs={{0,16},{16,32},{32,48},{48,64},{64,80},{80,96},{96,112},{1,17},{17... | collective-permute-start | bytes 786440 | tf_op jit(solution)/shard_map/ppermute | solution.py:24
  26.6 17.0 %collective-permute-start.1 = (f32[128,512]{1,0:T(8,128)}, f32[128,512]{1,0:T(8,128)}, u32[]{:S(2)}, u32[]{:S(2)}) collective-permute-start(f32[128,512]{1,0:T(8,128)} %get-tuple-element.19), channel_id=1, source_target_pairs={{16,0},{32,16},{48,32},{64,48},{80,64},{96,80},{112,96},{17,1},{33... | collective-permute-start | bytes 786440 | tf_op jit(solution)/shard_map/ppermute | solution.py:25
  32.0 5.0 %copy-start.9 = (f32[4]{0:T(128)S(1)}, f32[4]{0:T(128)}, u32[]{:S(2)}) copy-start(f32[4]{0:T(128)} %param.12) | copy-start | bytes 52
  32.0 5.6 %copy-start.5 = (f32[770,256]{1,0:T(8,128)S(1)}, f32[770,256]{1,0:T(8,128)}, u32[]{:S(2)}) copy-start(f32[770,256]{1,0:T(8,128)} %constant.56.clone) | copy-start | bytes 2365444
  36.9 1.6 %copy-start.3 = (f32[256,1536]{1,0:T(8,128)S(1)}, f32[256,1536]{1,0:T(8,128)}, u32[]{:S(2)}) copy-start(f32[256,1536]{1,0:T(8,128)} %constant.58.clone) | copy-start | bytes 4718596
  38.5 5.1 %copy-start.8 = (f32[770,128]{1,0:T(8,128)S(1)}, f32[770,128]{1,0:T(8,128)}, u32[]{:S(2)}) copy-start(f32[770,128]{1,0:T(8,128)} %constant.67) | copy-start | bytes 1182724
  42.9 2.9 %copy-start.7 = (f32[770,128]{1,0:T(8,128)S(1)}, f32[770,128]{1,0:T(8,128)}, u32[]{:S(2)}) copy-start(f32[770,128]{1,0:T(8,128)} %constant.65) | copy-start | bytes 1182724
  43.6 3.3 %copy-start.2 = (f32[512,1536]{1,0:T(8,128)S(1)}, f32[512,1536]{1,0:T(8,128)}, u32[]{:S(2)}) copy-start(f32[512,1536]{1,0:T(8,128)} %constant.57.clone) | copy-start | bytes 9437188
  45.8 5.4 %slice-start = ((s8[4767744]{0:T(1024)(128)(4,1)}), s8[4194304]{0:T(1024)(128)(4,1)S(1)}, s32[]{:S(2)}) async-start(s8[4767744]{0:T(1024)(128)(4,1)} %bitcast.47), calls=%async_computation.2 | async-start | bytes 8388608
  46.9 4.3 %slice-start.1 = ((s8[4767744]{0:T(1024)(128)(4,1)}), s8[573440]{0:T(1024)(128)(4,1)S(1)}, s32[]{:S(2)}) async-start(s8[4767744]{0:T(1024)(128)(4,1)} %bitcast.47), calls=%async_computation.3 | async-start | bytes 1146880
  51.2 5.9 %copy-start.1 = (f32[768,1024]{1,0:T(8,128)S(1)}, f32[768,1024]{1,0:T(8,128)}, u32[]{:S(2)}) copy-start(f32[768,1024]{1,0:T(8,128)} %constant.59.clone) | copy-start | bytes 9437188
  61.2 1.2 %copy-start.4 = (f32[512,385]{1,0:T(8,128)S(1)}, f32[512,385]{1,0:T(8,128)}, u32[]{:S(2)}) copy-start(f32[512,385]{1,0:T(8,128)} %constant.68) | copy-start | bytes 2365444
  62.4 1.1 %copy-start.6 = (f32[512,383]{1,0:T(8,128)S(1)}, f32[512,383]{1,0:T(8,128)}, u32[]{:S(2)}) copy-start(f32[512,383]{1,0:T(8,128)} %constant.69) | copy-start | bytes 2353156

commit v3 on v1

--- a/solution.py
+++ b/solution.py
@@ -59,13 +59,23 @@
     h = n // 2 + 1
     tile_count = lax.axis_size("tile")
     pixel_count = float(tile_rows * tile_width * tile_count)
-    local_sums = (jnp.sum(micrograph), jnp.sum(micrograph * micrograph))
-    totals = lax.psum((local_sums[0], local_sums[1]), "tile")
+    own_rows, tpl_width = templates.shape[1], templates.shape[2]
+    halo = padded(micrograph, (("tile", 0),), margin)
+    sums = jnp.stack([jnp.sum(micrograph), jnp.sum(micrograph * micrograph)])
+    payload = jnp.concatenate(
+        [templates[0], jnp.pad(sums, (0, tpl_width - 2))[None]], axis=0
+    )
+    everything = lax.all_gather(payload, "tile")
+    totals = jnp.sum(everything[:, own_rows, :2], axis=0)
+    gathered = everything[:, :own_rows].reshape(tile_count * own_rows, tpl_width)
     centre = totals[0] / pixel_count
     spread = jnp.sqrt(totals[1] / pixel_count - centre * centre + 1e-05)
-    rows_ext = padded((micrograph - centre) / spread, (("tile", 0),), margin)
-
-    gathered = lax.all_gather(templates, "tile", axis=1, tiled=True)[0]
+    tile_index = lax.axis_index("tile")
+    row_ids = lax.broadcasted_iota(jnp.int32, (n, 1), 0)
+    valid = ((row_ids >= margin) | (tile_index > 0)) & (
+        (row_ids < margin + tile_rows) | (tile_index < tile_count - 1)
+    )
+    rows_ext = lax.optimization_barrier(jnp.where(valid, (halo - centre) / spread, 0.0))
     extent = gathered.shape[0]
     left, left_t, right_w, right_t, back, final = tables(tile_width, margin, extent)
 
@@ -91,14 +101,17 @@
     signed_freq = (
         jnp.where(positions < n // 2, positions, positions - n).astype(jnp.float32) / n
     )
-    freq_square = signed_freq[:h, None] ** 2 + signed_freq[None, :] ** 2
     group_ids = lax.iota(jnp.int32, defocus_values.shape[0])
     defocus = jnp.sum(jnp.where(group_ids == defocus_group[0], defocus_values, 0.0))
-    phase_shift = math.pi * WAVELENGTH * defocus * freq_square
-    contrast = -(
-        math.sqrt(1.0 - AMPLITUDE * AMPLITUDE) * jnp.sin(phase_shift)
-        + AMPLITUDE * jnp.cos(phase_shift)
-    )
+    scale = math.pi * WAVELENGTH * defocus
+    row_phase = scale * signed_freq[:h, None] ** 2
+    col_phase = scale * signed_freq[None, :] ** 2
+    sin_r, cos_r = jnp.sin(row_phase), jnp.cos(row_phase)
+    sin_c, cos_c = jnp.sin(col_phase), jnp.cos(col_phase)
+    weight_sin = math.sqrt(1.0 - AMPLITUDE * AMPLITUDE)
+    col_u = weight_sin * cos_c - AMPLITUDE * sin_c
+    col_v = weight_sin * sin_c + AMPLITUDE * cos_c
+    contrast = -(sin_r * col_u + cos_r * col_v)
     product_real = (spec_real * template_real + spec_imag * template_imag) * contrast
     product_imag = (spec_imag * template_real - spec_real * template_imag) * contrast
 

time: 103 us -> 84.3 us (0.82)
  blocking collectives: 50.1 us -> 37.8 us
  matrix products: 25 us -> 19.3 us
  other arithmetic: 12.3 us -> 8.5 us
  local copies, waits for them, and re-layouts: 2.18 us -> 5.48 us
    psum x1 -> x0, blocking collectives: 13.8 us -> none  [per_device(): totals = lax.psum((local_sums[0], local_sums[1]), 'tile')]
    dot_general x9 -> x7, matrix products: 25 us -> 19.3 us  [product(): jnp.dot(former, latter, precision=mode, preferred_element_type=jnp.float32)]
    mul x1, other arithmetic: 5.83 us -> 0.82 us  [per_device(): (spec_real * template_real + spec_imag * template_imag) * contrast]
    unnamed x24 -> x20, local copies, waits for them, and re-layouts: 1.19 us -> 3.58 us
    ppermute x1, starting transfers between devices: 2.97 us -> 4.51 us  [padded(): before = lax.ppermute(last, axis, up)]
    all_gather x1, blocking collectives: 12.2 us -> 13.7 us  [per_device(): everything = lax.all_gather(payload, 'tile')]
    another operation x0 -> x1, other arithmetic: none -> 1.37 us  [per_device(): sums = jnp.stack([jnp.sum(micrograph), jnp.sum(micrograph * micrograph)])]
    reduce_sum x1 -> x2, other arithmetic: 2.19 us -> 0.9 us  [the longest x1 0.87 us: per_device(): sums = jnp.stack([jnp.sum(micrograph), jnp.sum(micrograph * micrograph)])]
  transfers between devices with their start and end apart: 2 -> 2, of which waited for: 0 -> 0; matrix products, arithmetic and copies ran while one was open for 15% -> 10% of each run, Pallas kernels for 0% -> 0%
where the time goes in v3:
time: 84.3 us; the launch traced here: 83.7 us
  blocking collectives  37.8 us (45%)
  matrix products  19.3 us (23%)
  other arithmetic  8.5 us (10%)
  starting transfers between devices  6.43 us (8%)
  between operations  6.14 us (7%)
  local copies, waits for them, and re-layouts  5.48 us (7%)
    all_to_all x1, blocking collectives, per_device(): lax.all_to_all(scores, 'orient', 0, 0, tiled=True)  24.1 us
    dot_general x7, matrix products, product(): jnp.dot(former, latter, precision=mode, preferred_element_type=jnp.float32)  19.3 us
    all_gather x1, blocking collectives, per_device(): everything = lax.all_gather(payload, 'tile')  13.7 us
    ppermute x1, starting transfers between devices, padded(): before = lax.ppermute(last, axis, up)  4.51 us
    unnamed x20, local copies, waits for them, and re-layouts  3.58 us
    ppermute x1, starting transfers between devices, padded(): after = lax.ppermute(initial, axis, down)  1.92 us
  transfers between devices with their start and end apart: 2, of which 0 were waited for; matrix products, arithmetic and copies ran while one was open for 10% of the time, Pallas kernels for 0%

profile of v3, /device:TPU:1, one launch (start us, length us, event | category | flops | bytes accessed | tf_op | source)
XLA Modules:
  0.0 83.7 jit_solution(16342607028115220148)
XLA Ops:
  0.6 0.0 copy-start
  0.6 0.0 copy-start.8
  0.7 0.0 copy-start.9
  0.7 1.1 %fusion.25 = (f32[128,512]{1,0:T(8,128)S(1)}, f32[128,512]{1,0:T(8,128)S(1)}) fusion(f32[512,512]{1,0:T(8,128)} %param.10), kind=kLoop, calls=%fused_computation.57 | loop fusion | bytes 1048576 | tf_op jit(solution)/shard_map/slice | solution.py:22
  1.8 4.5 %collective-permute-start = (f32[128,512]{1,0:T(8,128)S(1)}, f32[128,512]{1,0:T(8,128)S(1)}, u32[]{:S(2)}, u32[]{:S(2)}) collective-permute-start(f32[128,512]{1,0:T(8,128)S(1)} %get-tuple-element.10), channel_id=1, source_target_pairs={{0,16},{16,32},{32,48},{48,64},{64,80},{80,96},{96,112},{1,17},{17... | collective-permute-start | bytes 786440 | tf_op jit(solution)/shard_map/ppermute | solution.py:24
  6.3 1.9 %collective-permute-start.1 = (f32[128,512]{1,0:T(8,128)S(1)}, f32[128,512]{1,0:T(8,128)S(1)}, u32[]{:S(2)}, u32[]{:S(2)}) collective-permute-start(f32[128,512]{1,0:T(8,128)S(1)} %get-tuple-element.11), channel_id=1, source_target_pairs={{16,0},{32,16},{48,32},{64,48},{80,64},{96,80},{112,96},{17,1},{33... | collective-permute-start | bytes 786440 | tf_op jit(solution)/shard_map/ppermute | solution.py:25
  8.3 0.0 copy-done
  8.3 0.0 copy-start.6
  8.3 0.9 %fusion.23 = (f32[]{:T(128)}, f32[]{:T(128)}) fusion(f32[512,512]{1,0:T(8,128)S(1)} %copy-done), kind=kLoop, calls=%fused_computation.55 | loop fusion | flops 786430 | bytes 1048584 | tf_op jit(solution)/shard_map/reduce_sum | solution.py:64
  9.2 1.4 %select_maximum_fusion = f32[256]{0:T(256)S(1)} fusion(f32[1]{0:T(128)} %bitcast.2, f32[1]{0:T(128)} %bitcast.1), kind=kLoop, calls=%fused_computation.52 | loop fusion | flops 1024 | bytes 1032 | tf_op jit(solution)/shard_map/stack | solution.py:64
  10.5 0.0 copy-done.8
  10.5 13.7 %all-gather.1 = f32[8,33,256]{2,1,0:T(8,128)S(1)} all-gather(f32[1,33,256]{2,1,0:T(8,128)S(1)} %maximum_bitcast_fusion.2), channel_id=2, replica_groups=mesh['tile'=8,'orient'=16] {'tile'}, dimensions={0}, use_global_device_ids=true | all-gather | bytes 304128 | tf_op jit(solution)/shard_map/all_gather | solution.py:68
  24.3 0.7 slice_reduce_fusion
  25.6 0.0 copy-done.9
  25.6 0.6 fusion.21
  27.6 0.7 multiply_reduce_fusion.1
  28.9 0.0 copy-start.4
  29.0 0.6 fusion.26
  29.6 0.0 copy-done.6
  29.6 1.0 %fusion.29 = f32[256,770]{1,0:T(8,128)S(1)} fusion(f32[256,256]{1,0:T(8,128)S(1)} %bitcast.37, f32[770,256]{1,0:T(8,128)S(1)} %copy-done.6), kind=kOutput, calls=%fused_computation.61 | convolution fusion | flops 302776320 | bytes 1839104 | tf_op jit(solution)/shard_map/dot_general | solution.py:31
  30.6 0.0 copy-done.4
  30.6 2.3 %fusion.30 = f32[770,1536]{1,0:T(8,128)S(1)} fusion(f32[256,770]{1,0:T(8,128)S(1)} %fusion.29, f32[256,1536]{1,0:T(8,128)S(1)} %copy-done.4), kind=kOutput, calls=%fused_computation.62 | convolution fusion | flops 1816657920 | bytes 7092224 | tf_op jit(solution)/shard_map/dot_general | solution.py:31
  35.6 0.0 collective-permute-done
  35.6 0.0 collective-permute-done.1
  35.6 0.0 copy-start.3
  35.6 0.2 fusion.5
  35.8 1.4 %copy-done.3 = f32[770,768]{1,0:T(8,128)S(1)} copy-done((f32[770,768]{1,0:T(8,128)S(1)}, f32[770,768]{1,0:T(8,128)}, u32[]{:S(2)}) %copy-start.3) | copy-done | bytes 2365464
  37.3 0.0 copy-start.2
  37.3 5.1 %fusion.27 = f32[512,770]{1,0:T(8,128)S(1)} fusion(f32[768,512]{1,0:T(8,128)S(1)} %fusion.5, f32[770,768]{1,0:T(8,128)S(1)} %copy-done.3), kind=kOutput, calls=%fused_computation.59 | convolution fusion | flops 1816657920 | bytes 5515264 | tf_op jit(solution)/shard_map/dot_general | solution.py:31
  42.4 0.0 copy-done.2
  42.4 4.6 %fusion.28 = f32[770,1536]{1,0:T(8,128)S(1)} fusion(f32[512,770]{1,0:T(8,128)S(1)} %fusion.27, f32[512,1536]{1,0:T(8,128)S(1)} %copy-done.2), kind=kOutput, calls=%fused_computation.60 | convolution fusion | flops 3633315840 | bytes 9453568 | tf_op jit(solution)/shard_map/dot_general | solution.py:31
  47.1 0.8 fusion.6
  47.9 0.0 copy-start.1
  47.9 0.9 %subtract_multiply_fusion = f32[385,768]{1,0:T(8,128)S(1)} fusion(f32[768]{0:T(1024)S(1)} %get-tuple-element.16, f32[385]{0:T(512)S(1)} %get-tuple-element.13, f32[768]{0:T(1024)S(1)} %get-tuple-element.17, f32[385]{0:T(512)S(1)} %get-tuple-element.12, f32[770,1536]{1,0:T(8,128)S(1)} %fusion.28, f32[770,1536]{1,0:T(8,128)S(1)} %fusion.30), kind=kLoop, calls=%fused_computation.12 | loop fusion | flops 4139520 | bytes 10653704 | tf_op jit(solution)/shard_map/mul | solution.py:116
  48.8 1.0 %copy-done.1 = f32[768,1024]{1,0:T(8,128)S(1)} copy-done((f32[768,1024]{1,0:T(8,128)S(1)}, f32[768,1024]{1,0:T(8,128)}, u32[]{:S(2)}) %copy-start.1) | copy-done | bytes 3145752
  49.8 4.1 %fusion = f32[770,1024]{1,0:T(8,128)S(1)} fusion(f32[768,1024]{1,0:T(8,128)S(1)} %copy-done.1, f32[385,768]{1,0:T(8,128)S(1)} %subtract_multiply_fusion, f32[385,768]{1,0:T(8,128)S(1)} %fusion.6), kind=kOutput, calls=%fused_computation | convolution fusion | flops 3633907200 | bytes 8665088 | tf_op jit(solution)/shard_map/dot_general | solution.py:31
  53.9 0.0 copy-start.5
  53.9 0.2 fusion.24
  54.1 1.0 %copy-done.5 = f32[512,385]{1,0:T(8,128)S(1)} copy-done((f32[512,385]{1,0:T(8,128)S(1)}, f32[512,385]{1,0:T(8,128)}, u32[]{:S(2)}) %copy-start.5) | copy-done | bytes 788504
  55.1 0.0 copy-start.7
  55.1 1.0 %fusion.7 = f32[512,512]{0,1:T(8,128)S(1)} fusion(f32[512,385]{1,0:T(8,128)S(1)} %copy-done.5, f32[770,1024]{1,0:T(8,128)S(1)} %fusion), kind=kOutput, calls=%fused_computation.17 | convolution fusion | flops 605749760 | bytes 3702784 | tf_op jit(solution)/shard_map/dot_general | solution.py:31
  56.2 0.1 copy-done.7
  56.3 1.1 %convolution_add_fusion = f32[512,512]{0,1:T(8,128)S(1)} fusion(f32[512,512]{0,1:T(8,128)S(1)} %fusion.7, f32[512,383]{1,0:T(8,128)S(1)} %copy-done.7, f32[385,512]{1,0:T(8,128)S(1)} %get-tuple-element.9, f32[385,512]{1,0:T(8,128)S(1)} %get-tuple-element.8), kind=kOutput, calls=%fused_computation.7 | convolution fusion | flops 602865152 | bytes 4456448 | tf_op jit(solution)/shard_map/dot_general | solution.py:31
  57.4 24.1 %all_to_all.9 = f32[16,32,512]{2,1,0:T(8,128)S(1)} all-to-all(f32[16,32,512]{2,1,0:T(8,128)S(1)} %bitcast.36), channel_id=1, replica_groups=mesh['tile'=8,'orient'=16] {'orient'}, dimensions={0} | all-to-all | bytes 2097152 | tf_op jit(solution)/shard_map/all_to_all | solution.py:127
  81.5 0.7 maximum_bitcast_fusion.1
  82.2 0.7 maximum_bitcast_fusion
  82.9 0.8 fusion.11
  (7 shorter events, 0.2 us)
Async XLA Ops:
  0.6 7.6 %copy-start = (f32[512,512]{1,0:T(8,128)S(1)}, f32[512,512]{1,0:T(8,128)}, u32[]{:S(2)}) copy-start(f32[512,512]{1,0:T(8,128)} %param.10) | copy-start | bytes 3145732
  0.6 9.9 %copy-start.8 = (f32[1,32,256]{2,1,0:T(8,128)S(1)}, f32[1,32,256]{2,1,0:T(8,128)}, u32[]{:S(2)}) copy-start(f32[1,32,256]{2,1,0:T(8,128)} %param.11) | copy-start | bytes 98308
  0.7 25.0 %copy-start.9 = (f32[4]{0:T(128)S(1)}, f32[4]{0:T(128)}, u32[]{:S(2)}) copy-start(f32[4]{0:T(128)} %param.12) | copy-start | bytes 52
  1.8 33.8 %collective-permute-start = (f32[128,512]{1,0:T(8,128)S(1)}, f32[128,512]{1,0:T(8,128)S(1)}, u32[]{:S(2)}, u32[]{:S(2)}) collective-permute-start(f32[128,512]{1,0:T(8,128)S(1)} %get-tuple-element.10), channel_id=1, source_target_pairs={{0,16},{16,32},{32,48},{48,64},{64,80},{80,96},{96,112},{1,17},{17... | collective-permute-start | bytes 786440 | tf_op jit(solution)/shard_map/ppermute | solution.py:24
  6.3 29.3 %collective-permute-start.1 = (f32[128,512]{1,0:T(8,128)S(1)}, f32[128,512]{1,0:T(8,128)S(1)}, u32[]{:S(2)}, u32[]{:S(2)}) collective-permute-start(f32[128,512]{1,0:T(8,128)S(1)} %get-tuple-element.11), channel_id=1, source_target_pairs={{16,0},{32,16},{48,32},{64,48},{80,64},{96,80},{112,96},{17,1},{33... | collective-permute-start | bytes 786440 | tf_op jit(solution)/shard_map/ppermute | solution.py:25
  8.3 21.3 %copy-start.6 = (f32[770,256]{1,0:T(8,128)S(1)}, f32[770,256]{1,0:T(8,128)}, u32[]{:S(2)}) copy-start(f32[770,256]{1,0:T(8,128)} %constant.69.clone) | copy-start | bytes 2365444
  28.9 1.7 %copy-start.4 = (f32[256,1536]{1,0:T(8,128)S(1)}, f32[256,1536]{1,0:T(8,128)}, u32[]{:S(2)}) copy-start(f32[256,1536]{1,0:T(8,128)} %constant.71.clone) | copy-start | bytes 4718596
  35.6 1.7 %copy-start.3 = (f32[770,768]{1,0:T(8,128)S(1)}, f32[770,768]{1,0:T(8,128)}, u32[]{:S(2)}) copy-start(f32[770,768]{1,0:T(8,128)} %constant.68.clone) | copy-start | bytes 7096324
  37.3 5.1 %copy-start.2 = (f32[512,1536]{1,0:T(8,128)S(1)}, f32[512,1536]{1,0:T(8,128)}, u32[]{:S(2)}) copy-start(f32[512,1536]{1,0:T(8,128)} %constant.70.clone) | copy-start | bytes 9437188
  47.9 1.9 %copy-start.1 = (f32[768,1024]{1,0:T(8,128)S(1)}, f32[768,1024]{1,0:T(8,128)}, u32[]{:S(2)}) copy-start(f32[768,1024]{1,0:T(8,128)} %constant.72.clone) | copy-start | bytes 9437188
  53.9 1.2 %copy-start.5 = (f32[512,385]{1,0:T(8,128)S(1)}, f32[512,385]{1,0:T(8,128)}, u32[]{:S(2)}) copy-start(f32[512,385]{1,0:T(8,128)} %constant.78) | copy-start | bytes 2365444
  55.1 1.1 %copy-start.7 = (f32[512,383]{1,0:T(8,128)S(1)}, f32[512,383]{1,0:T(8,128)}, u32[]{:S(2)}) copy-start(f32[512,383]{1,0:T(8,128)} %constant.79) | copy-start | bytes 2353156

commit v4 on v3

--- a/solution.py
+++ b/solution.py
@@ -37,7 +37,7 @@
     idx = np.arange(n)
     angles = 2.0 * np.pi * ((idx[:, None] * idx[None, :]) % n) / n
     cos, sin = np.cos(angles), np.sin(angles)
-    left = np.concatenate([cos[:h], sin[:h]], axis=0)
+    left = np.concatenate([cos[:h], sin[1:h - 1]], axis=0)
     left_t = left[:, :extent]
     right_w = np.concatenate([cos[margin:margin + tile_width], sin[margin:margin + tile_width]], axis=1)
     right_t = np.concatenate([cos[:extent], sin[:extent]], axis=1)
@@ -85,15 +85,16 @@
 
     stage = product(left, rows_ext)
     spec = product(stage, right_w)
+    edge = ((1, 1), (0, 0))
     a_c, a_s = spec[:h, :n], spec[:h, n:]
-    b_c, b_s = spec[h:, :n], spec[h:, n:]
+    b_c, b_s = jnp.pad(spec[h:, :n], edge), jnp.pad(spec[h:, n:], edge)
     spec_real = a_c - b_s
     spec_imag = -(a_s + b_c)
 
     stage_t = product(left_t, normed)
     spec_t = product(stage_t, right_t)
     ta_c, ta_s = spec_t[:h, :n], spec_t[:h, n:]
-    tb_c, tb_s = spec_t[h:, :n], spec_t[h:, n:]
+    tb_c, tb_s = jnp.pad(spec_t[h:, :n], edge), jnp.pad(spec_t[h:, n:], edge)
     template_real = ta_c - tb_s
     template_imag = -(ta_s + tb_c)
 

time: 84.3 us -> 84.9 us (level)
  other arithmetic: 8.5 us -> 9.68 us
    select_n x1, other arithmetic: 0.21 us -> 1.39 us  [per_device(): jnp.where(valid, (halo - centre) / spread, 0.0)]
    unnamed x20 -> x18, local copies, waits for them, and re-layouts: 3.58 us -> 2.6 us
  transfers between devices with their start and end apart: 2 -> 2, of which waited for: 0 -> 0; matrix products, arithmetic and copies ran while one was open for 10% -> 11% of each run, Pallas kernels for 0% -> 0%
where the time goes in v4:
time: 84.9 us; the launch traced here: 84.2 us
  blocking collectives  37.8 us (45%)
  matrix products  18.9 us (22%)
  other arithmetic  9.68 us (11%)
  starting transfers between devices  6.43 us (8%)
  between operations  6.26 us (7%)
  local copies, waits for them, and re-layouts  5.1 us (6%)
    all_to_all x1, blocking collectives, per_device(): lax.all_to_all(scores, 'orient', 0, 0, tiled=True)  24.1 us
    dot_general x7, matrix products, product(): jnp.dot(former, latter, precision=mode, preferred_element_type=jnp.float32)  18.9 us
    all_gather x1, blocking collectives, per_device(): everything = lax.all_gather(payload, 'tile')  13.7 us
    ppermute x1, starting transfers between devices, padded(): before = lax.ppermute(last, axis, up)  4.51 us
    unnamed x18, local copies, waits for them, and re-layouts  2.6 us
    ppermute x1, starting transfers between devices, padded(): after = lax.ppermute(initial, axis, down)  1.92 us
  transfers between devices with their start and end apart: 2, of which 0 were waited for; matrix products, arithmetic and copies ran while one was open for 11% of the time, Pallas kernels for 0%

profile of v4, /device:TPU:1, one launch (start us, length us, event | category | flops | bytes accessed | tf_op | source)
XLA Modules:
  0.0 84.2 jit_solution(2725400818046567988)
XLA Ops:
  0.6 0.0 copy-start
  0.6 0.0 copy-start.7
  0.7 0.0 copy-start.8
  0.7 1.1 %fusion.27 = (f32[128,512]{1,0:T(8,128)S(1)}, f32[128,512]{1,0:T(8,128)S(1)}) fusion(f32[512,512]{1,0:T(8,128)} %param.10), kind=kLoop, calls=%fused_computation.59 | loop fusion | bytes 1048576 | tf_op jit(solution)/shard_map/slice | solution.py:22
  1.8 4.5 %collective-permute-start = (f32[128,512]{1,0:T(8,128)S(1)}, f32[128,512]{1,0:T(8,128)}, u32[]{:S(2)}, u32[]{:S(2)}) collective-permute-start(f32[128,512]{1,0:T(8,128)S(1)} %get-tuple-element.14), channel_id=1, source_target_pairs={{0,16},{16,32},{32,48},{48,64},{64,80},{80,96},{96,112},{1,17},{17... | collective-permute-start | bytes 786440 | tf_op jit(solution)/shard_map/ppermute | solution.py:24
  6.3 1.9 %collective-permute-start.1 = (f32[128,512]{1,0:T(8,128)S(1)}, f32[128,512]{1,0:T(8,128)}, u32[]{:S(2)}, u32[]{:S(2)}) collective-permute-start(f32[128,512]{1,0:T(8,128)S(1)} %get-tuple-element.15), channel_id=1, source_target_pairs={{16,0},{32,16},{48,32},{64,48},{80,64},{96,80},{112,96},{17,1},{33... | collective-permute-start | bytes 786440 | tf_op jit(solution)/shard_map/ppermute | solution.py:25
  8.3 0.0 copy-done
  8.3 0.9 %fusion.23 = (f32[]{:T(128)}, f32[]{:T(128)}) fusion(f32[512,512]{1,0:T(8,128)S(1)} %copy-done), kind=kLoop, calls=%fused_computation.55 | loop fusion | flops 786430 | bytes 1048584 | tf_op jit(solution)/shard_map/reduce_sum | solution.py:64
  9.2 1.4 %select_maximum_fusion = f32[256]{0:T(256)S(1)} fusion(f32[1]{0:T(128)} %bitcast.2, f32[1]{0:T(128)} %bitcast.1), kind=kLoop, calls=%fused_computation.52 | loop fusion | flops 1024 | bytes 1032 | tf_op jit(solution)/shard_map/stack | solution.py:64
  10.5 0.0 copy-done.7
  10.5 13.7 %all-gather.1 = f32[8,33,256]{2,1,0:T(8,128)S(1)} all-gather(f32[1,33,256]{2,1,0:T(8,128)S(1)} %maximum_bitcast_fusion.2), channel_id=2, replica_groups=mesh['tile'=8,'orient'=16] {'tile'}, dimensions={0}, use_global_device_ids=true | all-gather | bytes 304128 | tf_op jit(solution)/shard_map/all_gather | solution.py:68
  24.3 0.7 slice_reduce_fusion
  25.6 0.0 copy-done.8
  25.6 0.6 fusion.21
  27.6 0.7 multiply_reduce_fusion.1
  28.2 0.0 copy-start.4
  29.1 0.6 fusion.28
  29.7 2.0 %fusion.31 = f32[256,768]{1,0:T(8,128)S(1)} fusion(f32[256,256]{1,0:T(8,128)S(1)} %bitcast.37, f32[768,256]{1,0:T(8,128)} %constant.69.clone), kind=kOutput, calls=%fused_computation.63 | convolution fusion | flops 301989888 | bytes 1835008 | tf_op jit(solution)/shard_map/dot_general | solution.py:31
  31.7 0.0 copy-done.4
  31.7 2.2 %fusion.32 = f32[768,1536]{1,0:T(8,128)S(1)} fusion(f32[256,768]{1,0:T(8,128)S(1)} %fusion.31, f32[256,1536]{1,0:T(8,128)S(1)} %copy-done.4), kind=kOutput, calls=%fused_computation.64 | convolution fusion | flops 1811939328 | bytes 7077888 | tf_op jit(solution)/shard_map/dot_general | solution.py:31
  36.6 0.0 collective-permute-done
  36.6 0.0 collective-permute-done.1
  36.6 0.0 copy-start.3
  36.6 1.4 %fusion.5 = f32[768,512]{1,0:T(8,128)S(1)} fusion(f32[128,512]{1,0:T(8,128)} %collective-permute-done.1, f32[512,512]{1,0:T(8,128)S(1)} %copy-done, f32[128,512]{1,0:T(8,128)} %collective-permute-done, f32[]{:T(128)} %bitcast.6, f32[]{:T(128)} %bitcast.5, pred[768]{0:T(1024)(128)(4,1)S(1)} %fusion.15), kind=kLoop, calls=%fused_computation.6 | loop fusion | flops 1966080 | bytes 3146504 | tf_op jit(solution)/shard_map/jit(_where)/select_n | solution.py:78
  38.0 0.4 copy-done.3
  38.4 0.0 copy-start.2
  38.4 4.0 %fusion.29 = f32[512,768]{1,0:T(8,128)S(1)} fusion(f32[768,512]{1,0:T(8,128)S(1)} %fusion.5, f32[768,768]{1,0:T(8,128)S(1)} %copy-done.3), kind=kOutput, calls=%fused_computation.61 | convolution fusion | flops 1811939328 | bytes 5505024 | tf_op jit(solution)/shard_map/dot_general | solution.py:31
  42.5 0.0 copy-done.2
  42.5 4.4 %fusion.30 = f32[768,1536]{1,0:T(8,128)S(1)} fusion(f32[512,768]{1,0:T(8,128)S(1)} %fusion.29, f32[512,1536]{1,0:T(8,128)S(1)} %copy-done.2), kind=kOutput, calls=%fused_computation.62 | convolution fusion | flops 3623878656 | bytes 9437184 | tf_op jit(solution)/shard_map/dot_general | solution.py:31
  46.9 0.6 fusion.24
  47.5 0.9 %subtract_multiply_fusion = f32[385,768]{1,0:T(8,128)S(1)} fusion(f32[768]{0:T(1024)S(1)} %get-tuple-element.20, f32[385]{0:T(512)S(1)} %get-tuple-element.17, f32[768]{0:T(1024)S(1)} %get-tuple-element.21, f32[385]{0:T(512)S(1)} %get-tuple-element.16, f32[383,768]{1,0:T(8,128)S(1)} %get-tuple-element.22, f32[768,1536]{1,0:T(8,128)S(1)} %fusion.30, ...), kind=kLoop, calls=%fused_computation.12 | loop fusion | flops 4139520 | bytes 10629128 | tf_op jit(solution)/shard_map/mul | solution.py:117
  48.4 0.0 copy-start.1
  48.4 0.8 fusion.6
  49.3 1.1 %copy-done.1 = f32[768,1024]{1,0:T(8,128)S(1)} copy-done((f32[768,1024]{1,0:T(8,128)S(1)}, f32[768,1024]{1,0:T(8,128)}, u32[]{:S(2)}) %copy-start.1) | copy-done | bytes 3145752
  50.3 4.1 %fusion = f32[770,1024]{1,0:T(8,128)S(1)} fusion(f32[768,1024]{1,0:T(8,128)S(1)} %copy-done.1, f32[385,768]{1,0:T(8,128)S(1)} %subtract_multiply_fusion, f32[385,768]{1,0:T(8,128)S(1)} %fusion.6), kind=kOutput, calls=%fused_computation | convolution fusion | flops 3633907200 | bytes 8665088 | tf_op jit(solution)/shard_map/dot_general | solution.py:31
  54.4 0.0 copy-start.5
  54.4 0.2 fusion.26
  54.6 1.0 %copy-done.5 = f32[512,385]{1,0:T(8,128)S(1)} copy-done((f32[512,385]{1,0:T(8,128)S(1)}, f32[512,385]{1,0:T(8,128)}, u32[]{:S(2)}) %copy-start.5) | copy-done | bytes 788504
  55.7 0.0 copy-start.6
  55.7 1.1 %fusion.7 = f32[512,512]{0,1:T(8,128)S(1)} fusion(f32[512,385]{1,0:T(8,128)S(1)} %copy-done.5, f32[770,1024]{1,0:T(8,128)S(1)} %fusion), kind=kOutput, calls=%fused_computation.17 | convolution fusion | flops 605749760 | bytes 3702784 | tf_op jit(solution)/shard_map/dot_general | solution.py:31
  56.7 0.0 copy-done.6
  56.8 1.1 %convolution_add_fusion = f32[512,512]{0,1:T(8,128)S(1)} fusion(f32[512,512]{0,1:T(8,128)S(1)} %fusion.7, f32[512,383]{1,0:T(8,128)S(1)} %copy-done.6, f32[385,512]{1,0:T(8,128)S(1)} %get-tuple-element.13, f32[385,512]{1,0:T(8,128)S(1)} %get-tuple-element.12), kind=kOutput, calls=%fused_computation.7 | convolution fusion | flops 602865152 | bytes 4456448 | tf_op jit(solution)/shard_map/dot_general | solution.py:31
  57.9 24.1 %all_to_all.9 = f32[16,32,512]{2,1,0:T(8,128)S(1)} all-to-all(f32[16,32,512]{2,1,0:T(8,128)S(1)} %bitcast.36), channel_id=1, replica_groups=mesh['tile'=8,'orient'=16] {'orient'}, dimensions={0} | all-to-all | bytes 2097152 | tf_op jit(solution)/shard_map/all_to_all | solution.py:128
  82.0 0.7 maximum_bitcast_fusion.1
  82.7 0.7 maximum_bitcast_fusion
  83.5 0.8 fusion.11
  (7 shorter events, 0.2 us)
Async XLA Ops:
  0.6 7.6 %copy-start = (f32[512,512]{1,0:T(8,128)S(1)}, f32[512,512]{1,0:T(8,128)}, u32[]{:S(2)}) copy-start(f32[512,512]{1,0:T(8,128)} %param.10) | copy-start | bytes 3145732
  0.6 9.9 %copy-start.7 = (f32[1,32,256]{2,1,0:T(8,128)S(1)}, f32[1,32,256]{2,1,0:T(8,128)}, u32[]{:S(2)}) copy-start(f32[1,32,256]{2,1,0:T(8,128)} %param.11) | copy-start | bytes 98308
  0.7 25.0 %copy-start.8 = (f32[4]{0:T(128)S(1)}, f32[4]{0:T(128)}, u32[]{:S(2)}) copy-start(f32[4]{0:T(128)} %param.12) | copy-start | bytes 52
  1.8 34.8 %collective-permute-start = (f32[128,512]{1,0:T(8,128)S(1)}, f32[128,512]{1,0:T(8,128)}, u32[]{:S(2)}, u32[]{:S(2)}) collective-permute-start(f32[128,512]{1,0:T(8,128)S(1)} %get-tuple-element.14), channel_id=1, source_target_pairs={{0,16},{16,32},{32,48},{48,64},{64,80},{80,96},{96,112},{1,17},{17... | collective-permute-start | bytes 786440 | tf_op jit(solution)/shard_map/ppermute | solution.py:24
  6.3 30.2 %collective-permute-start.1 = (f32[128,512]{1,0:T(8,128)S(1)}, f32[128,512]{1,0:T(8,128)}, u32[]{:S(2)}, u32[]{:S(2)}) collective-permute-start(f32[128,512]{1,0:T(8,128)S(1)} %get-tuple-element.15), channel_id=1, source_target_pairs={{16,0},{32,16},{48,32},{64,48},{80,64},{96,80},{112,96},{17,1},{33... | collective-permute-start | bytes 786440 | tf_op jit(solution)/shard_map/ppermute | solution.py:25
  28.2 3.4 %copy-start.4 = (f32[256,1536]{1,0:T(8,128)S(1)}, f32[256,1536]{1,0:T(8,128)}, u32[]{:S(2)}) copy-start(f32[256,1536]{1,0:T(8,128)} %constant.71.clone) | copy-start | bytes 4718596
  36.6 1.8 %copy-start.3 = (f32[768,768]{1,0:T(8,128)S(1)}, f32[768,768]{1,0:T(8,128)}, u32[]{:S(2)}) copy-start(f32[768,768]{1,0:T(8,128)} %constant.68.clone) | copy-start | bytes 7077892
  38.4 4.0 %copy-start.2 = (f32[512,1536]{1,0:T(8,128)S(1)}, f32[512,1536]{1,0:T(8,128)}, u32[]{:S(2)}) copy-start(f32[512,1536]{1,0:T(8,128)} %constant.70.clone) | copy-start | bytes 9437188
  48.4 1.9 %copy-start.1 = (f32[768,1024]{1,0:T(8,128)S(1)}, f32[768,1024]{1,0:T(8,128)}, u32[]{:S(2)}) copy-start(f32[768,1024]{1,0:T(8,128)} %constant.72.clone) | copy-start | bytes 9437188
  54.4 1.2 %copy-start.5 = (f32[512,385]{1,0:T(8,128)S(1)}, f32[512,385]{1,0:T(8,128)}, u32[]{:S(2)}) copy-start(f32[512,385]{1,0:T(8,128)} %constant.86) | copy-start | bytes 2365444
  55.7 1.1 %copy-start.6 = (f32[512,383]{1,0:T(8,128)S(1)}, f32[512,383]{1,0:T(8,128)}, u32[]{:S(2)}) copy-start(f32[512,383]{1,0:T(8,128)} %constant.87) | copy-start | bytes 2353156

commit v5 on v4

--- a/solution.py
+++ b/solution.py
@@ -61,15 +61,27 @@
     pixel_count = float(tile_rows * tile_width * tile_count)
     own_rows, tpl_width = templates.shape[1], templates.shape[2]
     halo = padded(micrograph, (("tile", 0),), margin)
-    sums = jnp.stack([jnp.sum(micrograph), jnp.sum(micrograph * micrograph)])
-    payload = jnp.concatenate(
-        [templates[0], jnp.pad(sums, (0, tpl_width - 2))[None]], axis=0
-    )
+    own_tpl = templates[0]
+    own_count = float(own_rows * tpl_width)
+    own_mean = jnp.sum(own_tpl) / own_count
+    own_spread = jnp.sum((own_tpl - own_mean) ** 2)
+    lane = lax.broadcasted_iota(jnp.int32, (1, tpl_width), 1)
+    stats_row = jnp.where(lane == 0, jnp.sum(micrograph), 0.0)
+    stats_row = jnp.where(lane == 1, jnp.sum(micrograph * micrograph), stats_row)
+    stats_row = jnp.where(lane == 2, own_mean, stats_row)
+    stats_row = jnp.where(lane == 3, own_spread, stats_row)
+    payload = jnp.concatenate([own_tpl, stats_row], axis=0)
     everything = lax.all_gather(payload, "tile")
     totals = jnp.sum(everything[:, own_rows, :2], axis=0)
     gathered = everything[:, :own_rows].reshape(tile_count * own_rows, tpl_width)
     centre = totals[0] / pixel_count
     spread = jnp.sqrt(totals[1] / pixel_count - centre * centre + 1e-05)
+    part_means = everything[:, own_rows, 2]
+    tpl_mean = jnp.mean(part_means)
+    tpl_m2 = jnp.sum(everything[:, own_rows, 3]) + own_count * jnp.sum(
+        (part_means - tpl_mean) ** 2
+    )
+    root_mean = jnp.sqrt(tpl_m2 / (own_count * tile_count) + 1e-06)
     tile_index = lax.axis_index("tile")
     row_ids = lax.broadcasted_iota(jnp.int32, (n, 1), 0)
     valid = ((row_ids >= margin) | (tile_index > 0)) & (
@@ -79,9 +91,7 @@
     extent = gathered.shape[0]
     left, left_t, right_w, right_t, back, final = tables(tile_width, margin, extent)
 
-    centred = gathered - jnp.mean(gathered)
-    root_mean = jnp.sqrt(jnp.mean(centred * centred) + 1e-06)
-    normed = centred / (root_mean * TPL)
+    normed = (gathered - tpl_mean) / (root_mean * TPL)
 
     stage = product(left, rows_ext)
     spec = product(stage, right_w)

time: 84.9 us -> 88.2 us (1.039)
  other arithmetic: 9.68 us -> 11.5 us
  between operations: 6.26 us -> 7.62 us
    select_n x0 -> x1, other arithmetic: none -> 1.94 us  [per_device(): stats_row = jnp.where(lane == 3, own_spread, stats_row)]
    another operation x1 -> x0, other arithmetic: 1.37 us -> none  [per_device(): sums = jnp.stack([jnp.sum(micrograph), jnp.sum(micrograph * micrograph)])]
    reduce_sum x3 -> x5, other arithmetic: 2.2 us -> 3.45 us  [the longest x1 0.87 us: per_device(): jnp.sum(micrograph * micrograph)]
  transfers between devices with their start and end apart: 2 -> 2, of which waited for: 0 -> 0; matrix products, arithmetic and copies ran while one was open for 11% -> 13% of each run, Pallas kernels for 0% -> 0%
where the time goes in v5:
time: 88.2 us; the launch traced here: 87.5 us
  blocking collectives  37.8 us (43%)
  matrix products  18.9 us (21%)
  other arithmetic  11.5 us (13%)
  between operations  7.62 us (9%)
  starting transfers between devices  6.43 us (7%)
  local copies, waits for them, and re-layouts  5.19 us (6%)
    all_to_all x1, blocking collectives, per_device(): lax.all_to_all(scores, 'orient', 0, 0, tiled=True)  24.1 us
    dot_general x7, matrix products, product(): jnp.dot(former, latter, precision=mode, preferred_element_type=jnp.float32)  18.9 us
    all_gather x1, blocking collectives, per_device(): everything = lax.all_gather(payload, 'tile')  13.7 us
    ppermute x1, starting transfers between devices, padded(): before = lax.ppermute(last, axis, up)  4.51 us
    unnamed x18, local copies, waits for them, and re-layouts  2.61 us
    select_n x1, other arithmetic, per_device(): stats_row = jnp.where(lane == 3, own_spread, stats_row)  1.94 us
    ppermute x1, starting transfers between devices, padded(): after = lax.ppermute(initial, axis, down)  1.92 us
  transfers between devices with their start and end apart: 2, of which 0 were waited for; matrix products, arithmetic and copies ran while one was open for 13% of the time, Pallas kernels for 0%

profile of v5, /device:TPU:1, one launch (start us, length us, event | category | flops | bytes accessed | tf_op | source)
XLA Modules:
  0.0 87.5 jit_solution(13265344364732286895)
XLA Ops:
  0.6 0.0 copy-start
  0.6 0.0 copy-start.7
  0.7 0.0 copy-start.8
  0.7 1.1 %fusion.26 = (f32[128,512]{1,0:T(8,128)S(1)}, f32[128,512]{1,0:T(8,128)S(1)}) fusion(f32[512,512]{1,0:T(8,128)} %param.10), kind=kLoop, calls=%fused_computation.63 | loop fusion | bytes 1048576 | tf_op jit(solution)/shard_map/slice | solution.py:22
  1.8 4.5 %collective-permute-start = (f32[128,512]{1,0:T(8,128)S(1)}, f32[128,512]{1,0:T(8,128)}, u32[]{:S(2)}, u32[]{:S(2)}) collective-permute-start(f32[128,512]{1,0:T(8,128)S(1)} %get-tuple-element.16), channel_id=1, source_target_pairs={{0,16},{16,32},{32,48},{48,64},{64,80},{80,96},{96,112},{1,17},{17... | collective-permute-start | bytes 786440 | tf_op jit(solution)/shard_map/ppermute | solution.py:24
  6.3 1.9 %collective-permute-start.1 = (f32[128,512]{1,0:T(8,128)S(1)}, f32[128,512]{1,0:T(8,128)}, u32[]{:S(2)}, u32[]{:S(2)}) collective-permute-start(f32[128,512]{1,0:T(8,128)S(1)} %get-tuple-element.17), channel_id=1, source_target_pairs={{16,0},{32,16},{48,32},{64,48},{80,64},{96,80},{112,96},{17,1},{33... | collective-permute-start | bytes 786440 | tf_op jit(solution)/shard_map/ppermute | solution.py:25
  8.3 0.0 copy-done
  8.3 0.9 multiply_reduce_fusion
  9.2 0.0 copy-done.7
  9.2 0.6 reduce_sum.81
  10.4 0.6 multiply_reduce_fusion.1
  11.0 1.9 %compare_select_fusion.4 = f32[1,256]{1,0:T(1,128)S(1)} fusion(f32[]{:T(128)} %get-tuple-element.5, f32[]{:T(128)} %get-tuple-element.4, f32[]{:T(128)S(6)} %div.46, f32[]{:T(128)} %multiply_reduce_fusion.1), kind=kLoop, calls=%fused_computation.50 | loop fusion | flops 2048 | bytes 1040 | tf_op jit(solution)/shard_map/jit(_where)/select_n | solution.py:72
  13.0 13.7 %all-gather.1 = f32[8,33,256]{2,1,0:T(8,128)S(1)} all-gather(f32[1,33,256]{2,1,0:T(8,128)S(1)} %maximum_bitcast_fusion.2), channel_id=2, replica_groups=mesh['tile'=8,'orient'=16] {'tile'}, dimensions={0}, use_global_device_ids=true | all-gather | bytes 304128 | tf_op jit(solution)/shard_map/all_gather | solution.py:74
  26.7 0.7 slice_reduce_fusion.2
  27.4 0.0 copy-start.4
  28.2 0.0 copy-done.8
  28.2 0.6 fusion.21
  29.5 0.7 fusion.27
  30.8 0.7 multiply_reduce_fusion.2
  32.9 2.0 %fusion.30 = f32[256,768]{1,0:T(8,128)S(1)} fusion(f32[256,256]{1,0:T(8,128)S(1)} %bitcast.35, f32[768,256]{1,0:T(8,128)} %constant.82.clone), kind=kOutput, calls=%fused_computation.67 | convolution fusion | flops 301989888 | bytes 1835008 | tf_op jit(solution)/shard_map/dot_general | solution.py:31
  34.9 0.0 copy-done.4
  34.9 2.2 %fusion.31 = f32[768,1536]{1,0:T(8,128)S(1)} fusion(f32[256,768]{1,0:T(8,128)S(1)} %fusion.30, f32[256,1536]{1,0:T(8,128)S(1)} %copy-done.4), kind=kOutput, calls=%fused_computation.68 | convolution fusion | flops 1811939328 | bytes 7077888 | tf_op jit(solution)/shard_map/dot_general | solution.py:31
  39.8 0.0 collective-permute-done
  39.8 0.0 collective-permute-done.1
  39.9 0.0 copy-start.3
  39.9 1.4 %fusion.5 = f32[768,512]{1,0:T(8,128)S(1)} fusion(f32[128,512]{1,0:T(8,128)} %collective-permute-done.1, f32[512,512]{1,0:T(8,128)S(1)} %copy-done, f32[128,512]{1,0:T(8,128)} %collective-permute-done, f32[]{:T(128)} %bitcast.3, f32[]{:T(128)} %bitcast.2, pred[768]{0:T(1024)(128)(4,1)S(1)} %fusion.15), kind=kLoop, calls=%fused_computation.6 | loop fusion | flops 1966080 | bytes 3146504 | tf_op jit(solution)/shard_map/jit(_where)/select_n | solution.py:90
  41.3 0.4 copy-done.3
  41.7 0.0 copy-start.2
  41.7 4.0 %fusion.28 = f32[512,768]{1,0:T(8,128)S(1)} fusion(f32[768,512]{1,0:T(8,128)S(1)} %fusion.5, f32[768,768]{1,0:T(8,128)S(1)} %copy-done.3), kind=kOutput, calls=%fused_computation.65 | convolution fusion | flops 1811939328 | bytes 5505024 | tf_op jit(solution)/shard_map/dot_general | solution.py:31
  45.7 0.0 copy-done.2
  45.7 4.4 %fusion.29 = f32[768,1536]{1,0:T(8,128)S(1)} fusion(f32[512,768]{1,0:T(8,128)S(1)} %fusion.28, f32[512,1536]{1,0:T(8,128)S(1)} %copy-done.2), kind=kOutput, calls=%fused_computation.66 | convolution fusion | flops 3623878656 | bytes 9437184 | tf_op jit(solution)/shard_map/dot_general | solution.py:31
  50.2 0.6 fusion.23
  50.8 0.9 %subtract_multiply_fusion = f32[385,768]{1,0:T(8,128)S(1)} fusion(f32[768]{0:T(1024)S(1)} %get-tuple-element.22, f32[385]{0:T(512)S(1)} %get-tuple-element.19, f32[768]{0:T(1024)S(1)} %get-tuple-element.23, f32[385]{0:T(512)S(1)} %get-tuple-element.18, f32[383,768]{1,0:T(8,128)S(1)} %get-tuple-element.24, f32[768,1536]{1,0:T(8,128)S(1)} %fusion.29, ...), kind=kLoop, calls=%fused_computation.12 | loop fusion | flops 4139520 | bytes 10629128 | tf_op jit(solution)/shard_map/mul | solution.py:127
  51.7 0.0 copy-start.1
  51.7 0.8 fusion.6
  52.5 1.1 %copy-done.1 = f32[768,1024]{1,0:T(8,128)S(1)} copy-done((f32[768,1024]{1,0:T(8,128)S(1)}, f32[768,1024]{1,0:T(8,128)}, u32[]{:S(2)}) %copy-start.1) | copy-done | bytes 3145752
  53.6 4.1 %fusion = f32[770,1024]{1,0:T(8,128)S(1)} fusion(f32[768,1024]{1,0:T(8,128)S(1)} %copy-done.1, f32[385,768]{1,0:T(8,128)S(1)} %subtract_multiply_fusion, f32[385,768]{1,0:T(8,128)S(1)} %fusion.6), kind=kOutput, calls=%fused_computation | convolution fusion | flops 3633907200 | bytes 8665088 | tf_op jit(solution)/shard_map/dot_general | solution.py:31
  57.7 0.0 copy-start.5
  57.7 0.2 fusion.25
  57.9 1.0 %copy-done.5 = f32[512,385]{1,0:T(8,128)S(1)} copy-done((f32[512,385]{1,0:T(8,128)S(1)}, f32[512,385]{1,0:T(8,128)}, u32[]{:S(2)}) %copy-start.5) | copy-done | bytes 788504
  58.9 0.0 copy-start.6
  58.9 1.1 %fusion.7 = f32[512,512]{0,1:T(8,128)S(1)} fusion(f32[512,385]{1,0:T(8,128)S(1)} %copy-done.5, f32[770,1024]{1,0:T(8,128)S(1)} %fusion), kind=kOutput, calls=%fused_computation.17 | convolution fusion | flops 605749760 | bytes 3702784 | tf_op jit(solution)/shard_map/dot_general | solution.py:31
  60.0 0.1 copy-done.6
  60.1 1.1 %convolution_add_fusion = f32[512,512]{0,1:T(8,128)S(1)} fusion(f32[512,512]{0,1:T(8,128)S(1)} %fusion.7, f32[512,383]{1,0:T(8,128)S(1)} %copy-done.6, f32[385,512]{1,0:T(8,128)S(1)} %get-tuple-element.15, f32[385,512]{1,0:T(8,128)S(1)} %get-tuple-element.14), kind=kOutput, calls=%fused_computation.7 | convolution fusion | flops 602865152 | bytes 4456448 | tf_op jit(solution)/shard_map/dot_general | solution.py:31
  61.2 24.1 %all_to_all.9 = f32[16,32,512]{2,1,0:T(8,128)S(1)} all-to-all(f32[16,32,512]{2,1,0:T(8,128)S(1)} %bitcast.34), channel_id=1, replica_groups=mesh['tile'=8,'orient'=16] {'orient'}, dimensions={0} | all-to-all | bytes 2097152 | tf_op jit(solution)/shard_map/all_to_all | solution.py:138
  85.3 0.7 maximum_bitcast_fusion.1
  86.0 0.7 maximum_bitcast_fusion
  86.7 0.8 fusion.11
  (7 shorter events, 0.2 us)
Async XLA Ops:
  0.6 7.6 %copy-start = (f32[512,512]{1,0:T(8,128)S(1)}, f32[512,512]{1,0:T(8,128)}, u32[]{:S(2)}) copy-start(f32[512,512]{1,0:T(8,128)} %param.10) | copy-start | bytes 3145732
  0.6 8.5 %copy-start.7 = (f32[1,32,256]{2,1,0:T(8,128)S(1)}, f32[1,32,256]{2,1,0:T(8,128)}, u32[]{:S(2)}) copy-start(f32[1,32,256]{2,1,0:T(8,128)} %param.11) | copy-start | bytes 98308
  0.7 27.5 %copy-start.8 = (f32[4]{0:T(128)S(1)}, f32[4]{0:T(128)}, u32[]{:S(2)}) copy-start(f32[4]{0:T(128)} %param.12) | copy-start | bytes 52
  1.8 38.0 %collective-permute-start = (f32[128,512]{1,0:T(8,128)S(1)}, f32[128,512]{1,0:T(8,128)}, u32[]{:S(2)}, u32[]{:S(2)}) collective-permute-start(f32[128,512]{1,0:T(8,128)S(1)} %get-tuple-element.16), channel_id=1, source_target_pairs={{0,16},{16,32},{32,48},{48,64},{64,80},{80,96},{96,112},{1,17},{17... | collective-permute-start | bytes 786440 | tf_op jit(solution)/shard_map/ppermute | solution.py:24
  6.3 33.5 %collective-permute-start.1 = (f32[128,512]{1,0:T(8,128)S(1)}, f32[128,512]{1,0:T(8,128)}, u32[]{:S(2)}, u32[]{:S(2)}) collective-permute-start(f32[128,512]{1,0:T(8,128)S(1)} %get-tuple-element.17), channel_id=1, source_target_pairs={{16,0},{32,16},{48,32},{64,48},{80,64},{96,80},{112,96},{17,1},{33... | collective-permute-start | bytes 786440 | tf_op jit(solution)/shard_map/ppermute | solution.py:25
  27.4 7.5 %copy-start.4 = (f32[256,1536]{1,0:T(8,128)S(1)}, f32[256,1536]{1,0:T(8,128)}, u32[]{:S(2)}) copy-start(f32[256,1536]{1,0:T(8,128)} %constant.84.clone) | copy-start | bytes 4718596
  39.9 1.8 %copy-start.3 = (f32[768,768]{1,0:T(8,128)S(1)}, f32[768,768]{1,0:T(8,128)}, u32[]{:S(2)}) copy-start(f32[768,768]{1,0:T(8,128)} %constant.81.clone) | copy-start | bytes 7077892
  41.7 4.0 %copy-start.2 = (f32[512,1536]{1,0:T(8,128)S(1)}, f32[512,1536]{1,0:T(8,128)}, u32[]{:S(2)}) copy-start(f32[512,1536]{1,0:T(8,128)} %constant.83.clone) | copy-start | bytes 9437188
  51.7 1.9 %copy-start.1 = (f32[768,1024]{1,0:T(8,128)S(1)}, f32[768,1024]{1,0:T(8,128)}, u32[]{:S(2)}) copy-start(f32[768,1024]{1,0:T(8,128)} %constant.85.clone) | copy-start | bytes 9437188
  57.7 1.2 %copy-start.5 = (f32[512,385]{1,0:T(8,128)S(1)}, f32[512,385]{1,0:T(8,128)}, u32[]{:S(2)}) copy-start(f32[512,385]{1,0:T(8,128)} %constant.97) | copy-start | bytes 2365444
  58.9 1.1 %copy-start.6 = (f32[512,383]{1,0:T(8,128)S(1)}, f32[512,383]{1,0:T(8,128)}, u32[]{:S(2)}) copy-start(f32[512,383]{1,0:T(8,128)} %constant.98) | copy-start | bytes 2353156

commit v6 on v4

--- a/solution.py
+++ b/solution.py
@@ -39,9 +39,11 @@
     cos, sin = np.cos(angles), np.sin(angles)
     left = np.concatenate([cos[:h], sin[1:h - 1]], axis=0)
     left_t = left[:, :extent]
-    right_w = np.concatenate([cos[margin:margin + tile_width], sin[margin:margin + tile_width]], axis=1)
-    right_t = np.concatenate([cos[:extent], sin[:extent]], axis=1)
-    back = np.concatenate([cos[:, :tile_width], sin[:, :tile_width]], axis=1)
+    window_cols = slice(margin, margin + tile_width)
+    right_w = np.concatenate([cos[window_cols, :h], sin[window_cols, 1:h - 1]], axis=1)
+    right_t = np.concatenate([cos[:extent, :h], sin[:extent, 1:h - 1]], axis=1)
+    mirror = np.concatenate([np.arange(h), n - np.arange(1, h - 1)])
+    back = np.concatenate([cos[mirror, :tile_width], sin[mirror, :tile_width]], axis=1)
     weight = np.full(h, 2.0)
     weight[0] = 1.0
     weight[-1] = 1.0
@@ -83,30 +85,28 @@
     root_mean = jnp.sqrt(jnp.mean(centred * centred) + 1e-06)
     normed = centred / (root_mean * TPL)
 
-    stage = product(left, rows_ext)
-    spec = product(stage, right_w)
-    edge = ((1, 1), (0, 0))
-    a_c, a_s = spec[:h, :n], spec[:h, n:]
-    b_c, b_s = jnp.pad(spec[h:, :n], edge), jnp.pad(spec[h:, n:], edge)
-    spec_real = a_c - b_s
-    spec_imag = -(a_s + b_c)
+    def spectrum(packed):
+        edge_rows, edge_cols = ((1, 1), (0, 0)), ((0, 0), (1, 1))
+        ga, gb = packed[:h], jnp.pad(packed[h:], edge_rows)
+        ga_s = jnp.pad(ga[:, h:], edge_cols)
+        gb_s = jnp.pad(gb[:, h:], edge_cols)
+        real = jnp.concatenate([ga[:, :h] - gb_s, ga[:, 1:h - 1] + gb[:, h:]], axis=1)
+        imag = jnp.concatenate([-(ga_s + gb[:, :h]), ga[:, h:] - gb[:, 1:h - 1]], axis=1)
+        return real, imag
 
-    stage_t = product(left_t, normed)
-    spec_t = product(stage_t, right_t)
-    ta_c, ta_s = spec_t[:h, :n], spec_t[:h, n:]
-    tb_c, tb_s = jnp.pad(spec_t[h:, :n], edge), jnp.pad(spec_t[h:, n:], edge)
-    template_real = ta_c - tb_s
-    template_imag = -(ta_s + tb_c)
+    spec_real, spec_imag = spectrum(product(product(left, rows_ext), right_w))
+    template_real, template_imag = spectrum(product(product(left_t, normed), right_t))
 
     positions = lax.iota(jnp.int32, n)
     signed_freq = (
         jnp.where(positions < n // 2, positions, positions - n).astype(jnp.float32) / n
     )
+    packed_freq = jnp.where(positions < h, positions, positions - (h - 1)).astype(jnp.float32) / n
     group_ids = lax.iota(jnp.int32, defocus_values.shape[0])
     defocus = jnp.sum(jnp.where(group_ids == defocus_group[0], defocus_values, 0.0))
     scale = math.pi * WAVELENGTH * defocus
     row_phase = scale * signed_freq[:h, None] ** 2
-    col_phase = scale * signed_freq[None, :] ** 2
+    col_phase = scale * packed_freq[None, :] ** 2
     sin_r, cos_r = jnp.sin(row_phase), jnp.cos(row_phase)
     sin_c, cos_c = jnp.sin(col_phase), jnp.cos(col_phase)
     weight_sin = math.sqrt(1.0 - AMPLITUDE * AMPLITUDE)

time: 84.9 us -> 87.8 us (1.034)
  other arithmetic: 9.68 us -> 15.5 us
  matrix products: 18.9 us -> 14.9 us
  local copies, waits for them, and re-layouts: 5.1 us -> 6.04 us
    dot_general x7, matrix products: 18.9 us -> 14.9 us  [product(): jnp.dot(former, latter, precision=mode, preferred_element_type=jnp.float32)]
    add x0 -> x2, other arithmetic: none -> 3.11 us  [spectrum(): ga[:, 1:h - 1] + gb[:, h:]]
    neg x0 -> x2, other arithmetic: none -> 2.31 us  [spectrum(): -(ga_s + gb[:, :h])]
    unnamed x18 -> x26, local copies, waits for them, and re-layouts: 2.6 us -> 3.18 us
  transfers between devices with their start and end apart: 2 -> 2, of which waited for: 0 -> 0; matrix products, arithmetic and copies ran while one was open for 11% -> 13% of each run, Pallas kernels for 0% -> 0%
where the time goes in v6:
time: 87.8 us; the launch traced here: 87.1 us
  blocking collectives  37.8 us (43%)
  other arithmetic  15.5 us (18%)
  matrix products  14.9 us (17%)
  starting transfers between devices  6.55 us (7%)
  between operations  6.28 us (7%)
  local copies, waits for them, and re-layouts  6.04 us (7%)
    all_to_all x1, blocking collectives, per_device(): lax.all_to_all(scores, 'orient', 0, 0, tiled=True)  24.1 us
    dot_general x7, matrix products, product(): jnp.dot(former, latter, precision=mode, preferred_element_type=jnp.float32)  14.9 us
    all_gather x1, blocking collectives, per_device(): everything = lax.all_gather(payload, 'tile')  13.7 us
    ppermute x1, starting transfers between devices, padded(): before = lax.ppermute(last, axis, up)  4.5 us
    unnamed x26, local copies, waits for them, and re-layouts  3.18 us
    add x2, other arithmetic, spectrum(): ga[:, 1:h - 1] + gb[:, h:]  3.11 us
    neg x2, other arithmetic, spectrum(): -(ga_s + gb[:, :h])  2.31 us
    ppermute x1, starting transfers between devices, padded(): after = lax.ppermute(initial, axis, down)  2.05 us
  transfers between devices with their start and end apart: 2, of which 0 were waited for; matrix products, arithmetic and copies ran while one was open for 13% of the time, Pallas kernels for 0%

profile of v6, /device:TPU:1, one launch (start us, length us, event | category | flops | bytes accessed | tf_op | source)
XLA Modules:
  0.0 87.1 jit_solution(10606091369706284642)
XLA Ops:
  0.6 0.0 copy-start
  0.6 0.0 copy-start.11
  0.7 2.0 %fusion.35 = (f32[128,512]{1,0:T(8,128)}, f32[128,512]{1,0:T(8,128)}) fusion(f32[512,512]{1,0:T(8,128)} %param.10), kind=kLoop, calls=%fused_computation.77 | loop fusion | bytes 1048576 | tf_op jit(solution)/shard_map/slice | solution.py:22
  2.6 4.5 %collective-permute-start = (f32[128,512]{1,0:T(8,128)}, f32[128,512]{1,0:T(8,128)}, u32[]{:S(2)}, u32[]{:S(2)}) collective-permute-start(f32[128,512]{1,0:T(8,128)} %get-tuple-element.18), channel_id=1, source_target_pairs={{0,16},{16,32},{32,48},{48,64},{64,80},{80,96},{96,112},{1,17},{17... | collective-permute-start | bytes 786440 | tf_op jit(solution)/shard_map/ppermute | solution.py:24
  7.1 0.0 copy-start.8
  7.1 2.1 %collective-permute-start.1 = (f32[128,512]{1,0:T(8,128)}, f32[128,512]{1,0:T(8,128)}, u32[]{:S(2)}, u32[]{:S(2)}) collective-permute-start(f32[128,512]{1,0:T(8,128)} %get-tuple-element.19), channel_id=1, source_target_pairs={{16,0},{32,16},{48,32},{64,48},{80,64},{96,80},{112,96},{17,1},{33... | collective-permute-start | bytes 786440 | tf_op jit(solution)/shard_map/ppermute | solution.py:25
  9.2 0.0 copy-done
  9.2 0.9 %fusion.33 = (f32[]{:T(128)}, f32[]{:T(128)}) fusion(f32[512,512]{1,0:T(8,128)S(1)} %copy-done), kind=kLoop, calls=%fused_computation.75 | loop fusion | flops 786430 | bytes 1048584 | tf_op jit(solution)/shard_map/reduce_sum | solution.py:66
  10.1 1.4 %select_maximum_fusion = f32[256]{0:T(256)S(1)} fusion(f32[1]{0:T(128)} %bitcast.2, f32[1]{0:T(128)} %bitcast.1), kind=kLoop, calls=%fused_computation.72 | loop fusion | flops 1024 | bytes 1032 | tf_op jit(solution)/shard_map/stack | solution.py:66
  11.4 0.0 copy-done.11
  11.4 13.7 %all-gather.1 = f32[8,33,256]{2,1,0:T(8,128)S(1)} all-gather(f32[1,33,256]{2,1,0:T(8,128)S(1)} %maximum_bitcast_fusion.2), channel_id=2, replica_groups=mesh['tile'=8,'orient'=16] {'tile'}, dimensions={0}, use_global_device_ids=true | all-gather | bytes 304128 | tf_op jit(solution)/shard_map/all_gather | solution.py:70
  25.2 0.7 slice_reduce_fusion
  25.9 0.6 fusion.36
  29.7 0.7 multiply_reduce_fusion.1
  30.4 0.0 copy-start.10
  31.2 0.0 copy-done.8
  31.2 0.9 fusion.39
  32.1 0.0 copy-done.10
  32.1 1.3 %fusion.40 = f32[768,768]{1,0:T(8,128)S(1)} fusion(f32[256,768]{1,0:T(8,128)S(1)} %fusion.39, f32[256,768]{1,0:T(8,128)S(1)} %copy-done.10), kind=kOutput, calls=%fused_computation.82 | convolution fusion | flops 905969664 | bytes 3932160 | tf_op jit(solution)/shard_map/dot_general | solution.py:31
  33.4 0.1 slice.256
  33.5 0.0 copy-start.12
  33.5 2.3 %slice_add_fusion.2 = (f32[385,383]{1,0:T(8,128)}, f32[385,383]{1,0:T(8,128)}, f32[385,383]{1,0:T(8,128)}, f32[385,383]{1,0:T(8,128)}) fusion(f32[768,768]{1,0:T(8,128)S(1)} %fusion.40, f32[383,768]{1,0:T(8,128)S(1)} %slice.256), kind=kLoop, calls=%fused_computation.35 | loop fusion | flops 294910 | bytes 4715496 | tf_op jit(solution)/shard_map/add | solution.py:93
  36.4 0.0 copy-done.12
  36.4 0.6 fusion.31
  37.8 0.0 copy-start.1
  37.8 1.8 %fusion.10 = (f32[385,385]{1,0:T(8,128)S(1)}, f32[385,385]{1,0:T(8,128)S(1)}) fusion(f32[383,768]{1,0:T(8,128)S(1)} %slice.256, f32[385,383]{1,0:T(8,128)} %get-tuple-element.15, f32[385,383]{1,0:T(8,128)} %get-tuple-element.17, f32[768,768]{1,0:T(8,128)S(1)} %fusion.40), kind=kLoop, calls=%fused_computation.25 | loop fusion | flops 444675 | bytes 4134916 | tf_op jit(solution)/shard_map/neg | solution.py:94
  39.6 0.0 collective-permute-done
  39.6 0.0 collective-permute-done.1
  39.6 0.0 copy-done.1
  39.6 0.0 copy-start.5
  39.6 1.4 %fusion.5 = f32[768,512]{1,0:T(8,128)S(1)} fusion(f32[128,512]{1,0:T(8,128)} %collective-permute-done.1, f32[512,512]{1,0:T(8,128)S(1)} %copy-done.1, f32[128,512]{1,0:T(8,128)} %collective-permute-done, f32[]{:T(128)} %bitcast.6, f32[]{:T(128)} %bitcast.5, pred[768]{0:T(1024)(128)(4,1)S(1)} %fusion.27), kind=kLoop, calls=%fused_computation.6 | loop fusion | flops 1966080 | bytes 3146504 | tf_op jit(solution)/shard_map/jit(_where)/select_n | solution.py:80
  41.0 0.4 copy-done.5
  41.5 0.0 copy-start.6
  41.5 4.0 %fusion.37 = f32[512,768]{1,0:T(8,128)S(1)} fusion(f32[768,512]{1,0:T(8,128)S(1)} %fusion.5, f32[768,768]{1,0:T(8,128)S(1)} %copy-done.5), kind=kOutput, calls=%fused_computation.79 | convolution fusion | flops 1811939328 | bytes 5505024 | tf_op jit(solution)/shard_map/dot_general | solution.py:31
  45.4 0.0 copy-done.6
  45.5 2.5 %fusion.38 = f32[768,768]{1,0:T(8,128)S(1)} fusion(f32[512,768]{1,0:T(8,128)S(1)} %fusion.37, f32[512,768]{1,0:T(8,128)S(1)} %copy-done.6), kind=kOutput, calls=%fused_computation.80 | convolution fusion | flops 1811939328 | bytes 5505024 | tf_op jit(solution)/shard_map/dot_general | solution.py:31
  47.9 0.1 slice.252
  48.0 0.9 slice_add_fusion.3
  48.9 0.0 copy-start.2
  48.9 0.0 copy-start.3
  48.9 0.5 fusion.8
  49.4 0.5 copy-done.2
  50.0 0.2 copy-done.3
  50.1 1.1 %fusion.6 = f32[385,768]{1,0:T(8,128)S(1)} fusion(f32[385,383]{1,0:T(8,128)S(1)} %copy-done.3, f32[385,385]{1,0:T(8,128)S(1)} %get-tuple-element.24, f32[385,383]{1,0:T(8,128)S(1)} %get-tuple-element.9, f32[385,385]{1,0:T(8,128)S(1)} %get-tuple-element.26, f32[385,383]{1,0:T(8,128)S(1)} %copy-done.2, f32[385,385]{1,0:T(8,128)S(1)} %get-tuple-element.25, ...), kind=kLoop, calls=%fused_computation.14 | loop fusion | flops 3548160 | bytes 5922824 | tf_op jit(solution)/shard_map/mul | solution.py:116
  51.3 0.0 copy-start.4
  51.3 1.0 %subtract_multiply_fusion = f32[385,768]{1,0:T(8,128)S(1)} fusion(f32[385,383]{1,0:T(8,128)S(1)} %copy-done.3, f32[385,385]{1,0:T(8,128)S(1)} %get-tuple-element.24, f32[385,383]{1,0:T(8,128)S(1)} %get-tuple-element.9, f32[385,385]{1,0:T(8,128)S(1)} %get-tuple-element.26, f32[385,383]{1,0:T(8,128)S(1)} %copy-done.2, f32[385,385]{1,0:T(8,128)S(1)} %get-tuple-element.25, ...), kind=kLoop, calls=%fused_computation.12 | loop fusion | flops 3548160 | bytes 5922824 | tf_op jit(solution)/shard_map/mul | solution.py:117
  52.3 0.9 %copy-done.4 = f32[768,1024]{1,0:T(8,128)S(1)} copy-done((f32[768,1024]{1,0:T(8,128)S(1)}, f32[768,1024]{1,0:T(8,128)}, u32[]{:S(2)}) %copy-start.4) | copy-done | bytes 3145752
  53.2 4.1 %fusion = f32[770,1024]{1,0:T(8,128)S(1)} fusion(f32[768,1024]{1,0:T(8,128)S(1)} %copy-done.4, f32[385,768]{1,0:T(8,128)S(1)} %subtract_multiply_fusion, f32[385,768]{1,0:T(8,128)S(1)} %fusion.6), kind=kOutput, calls=%fused_computation | convolution fusion | flops 3633907200 | bytes 8665088 | tf_op jit(solution)/shard_map/dot_general | solution.py:31
  57.3 0.0 copy-start.7
  57.3 0.2 fusion.34
  57.5 1.0 %copy-done.7 = f32[512,385]{1,0:T(8,128)S(1)} copy-done((f32[512,385]{1,0:T(8,128)S(1)}, f32[512,385]{1,0:T(8,128)}, u32[]{:S(2)}) %copy-start.7) | copy-done | bytes 788504
  58.5 0.0 copy-start.9
  58.5 1.1 %fusion.11 = f32[512,512]{0,1:T(8,128)S(1)} fusion(f32[512,385]{1,0:T(8,128)S(1)} %copy-done.7, f32[770,1024]{1,0:T(8,128)S(1)} %fusion), kind=kOutput, calls=%fused_computation.27 | convolution fusion | flops 605749760 | bytes 3702784 | tf_op jit(solution)/shard_map/dot_general | solution.py:31
  59.6 0.0 copy-done.9
  59.6 1.1 %convolution_add_fusion = f32[512,512]{0,1:T(8,128)S(1)} fusion(f32[512,512]{0,1:T(8,128)S(1)} %fusion.11, f32[512,383]{1,0:T(8,128)S(1)} %copy-done.9, f32[385,512]{1,0:T(8,128)S(1)} %get-tuple-element.13, f32[385,512]{1,0:T(8,128)S(1)} %get-tuple-element.12), kind=kOutput, calls=%fused_computation.7 | convolution fusion | flops 602865152 | bytes 4456448 | tf_op jit(solution)/shard_map/dot_general | solution.py:31
  60.8 24.1 %all_to_all.9 = f32[16,32,512]{2,1,0:T(8,128)S(1)} all-to-all(f32[16,32,512]{2,1,0:T(8,128)S(1)} %bitcast.36), channel_id=1, replica_groups=mesh['tile'=8,'orient'=16] {'orient'}, dimensions={0} | all-to-all | bytes 2097152 | tf_op jit(solution)/shard_map/all_to_all | solution.py:128
  84.9 0.8 fusion.17
  85.6 0.7 maximum_bitcast_fusion
  86.4 0.7 maximum_bitcast_fusion.1
  (7 shorter events, 0.2 us)
Async XLA Ops:
  0.6 8.6 %copy-start = (f32[512,512]{1,0:T(8,128)S(1)}, f32[512,512]{1,0:T(8,128)}, u32[]{:S(2)}) copy-start(f32[512,512]{1,0:T(8,128)} %param.10) | copy-start | bytes 3145732
  0.6 10.8 %copy-start.11 = (f32[1,32,256]{2,1,0:T(8,128)S(1)}, f32[1,32,256]{2,1,0:T(8,128)}, u32[]{:S(2)}) copy-start(f32[1,32,256]{2,1,0:T(8,128)} %param.11) | copy-start | bytes 98308
  2.6 37.0 %collective-permute-start = (f32[128,512]{1,0:T(8,128)}, f32[128,512]{1,0:T(8,128)}, u32[]{:S(2)}, u32[]{:S(2)}) collective-permute-start(f32[128,512]{1,0:T(8,128)} %get-tuple-element.18), channel_id=1, source_target_pairs={{0,16},{16,32},{32,48},{48,64},{64,80},{80,96},{96,112},{1,17},{17... | collective-permute-start | bytes 786440 | tf_op jit(solution)/shard_map/ppermute | solution.py:24
  7.1 24.1 %copy-start.8 = (f32[768,256]{1,0:T(8,128)S(1)}, f32[768,256]{1,0:T(8,128)}, u32[]{:S(2)}) copy-start(f32[768,256]{1,0:T(8,128)} %constant.74.clone) | copy-start | bytes 2359300
  7.1 32.5 %collective-permute-start.1 = (f32[128,512]{1,0:T(8,128)}, f32[128,512]{1,0:T(8,128)}, u32[]{:S(2)}, u32[]{:S(2)}) collective-permute-start(f32[128,512]{1,0:T(8,128)} %get-tuple-element.19), channel_id=1, source_target_pairs={{16,0},{32,16},{48,32},{64,48},{80,64},{96,80},{112,96},{17,1},{33... | collective-permute-start | bytes 786440 | tf_op jit(solution)/shard_map/ppermute | solution.py:25
  30.4 1.7 %copy-start.10 = (f32[256,768]{1,0:T(8,128)S(1)}, f32[256,768]{1,0:T(8,128)}, u32[]{:S(2)}) copy-start(f32[256,768]{1,0:T(8,128)} %constant.76.clone) | copy-start | bytes 2359300
  33.5 2.9 %copy-start.12 = (f32[4]{0:T(128)S(1)}, f32[4]{0:T(128)}, u32[]{:S(2)}) copy-start(f32[4]{0:T(128)} %param.12) | copy-start | bytes 52
  37.8 1.9 %copy-start.1 = (f32[512,512]{1,0:T(8,128)S(1)}, f32[512,512]{1,0:T(8,128)}, u32[]{:S(2)}) copy-start(f32[512,512]{1,0:T(8,128)} %param.10) | copy-start | bytes 3145732
  39.6 1.8 %copy-start.5 = (f32[768,768]{1,0:T(8,128)S(1)}, f32[768,768]{1,0:T(8,128)}, u32[]{:S(2)}) copy-start(f32[768,768]{1,0:T(8,128)} %constant.73.clone) | copy-start | bytes 7077892
  41.5 4.0 %copy-start.6 = (f32[512,768]{1,0:T(8,128)S(1)}, f32[512,768]{1,0:T(8,128)}, u32[]{:S(2)}) copy-start(f32[512,768]{1,0:T(8,128)} %constant.75.clone) | copy-start | bytes 4718596
  48.9 1.1 %copy-start.2 = (f32[385,383]{1,0:T(8,128)S(1)}, f32[385,383]{1,0:T(8,128)}, u32[]{:S(2)}) copy-start(f32[385,383]{1,0:T(8,128)} %get-tuple-element.10) | copy-start | bytes 1769464
  48.9 1.2 %copy-start.3 = (f32[385,383]{1,0:T(8,128)S(1)}, f32[385,383]{1,0:T(8,128)}, u32[]{:S(2)}) copy-start(f32[385,383]{1,0:T(8,128)} %get-tuple-element.11) | copy-start | bytes 1769464
  51.3 1.9 %copy-start.4 = (f32[768,1024]{1,0:T(8,128)S(1)}, f32[768,1024]{1,0:T(8,128)}, u32[]{:S(2)}) copy-start(f32[768,1024]{1,0:T(8,128)} %constant.77.clone) | copy-start | bytes 9437188
  57.3 1.2 %copy-start.7 = (f32[512,385]{1,0:T(8,128)S(1)}, f32[512,385]{1,0:T(8,128)}, u32[]{:S(2)}) copy-start(f32[512,385]{1,0:T(8,128)} %constant.95) | copy-start | bytes 2365444
  58.5 1.1 %copy-start.9 = (f32[512,383]{1,0:T(8,128)S(1)}, f32[512,383]{1,0:T(8,128)}, u32[]{:S(2)}) copy-start(f32[512,383]{1,0:T(8,128)} %constant.96) | copy-start | bytes 2353156

commit v7 on v6

--- a/solution.py
+++ b/solution.py
@@ -85,17 +85,20 @@
     root_mean = jnp.sqrt(jnp.mean(centred * centred) + 1e-06)
     normed = centred / (root_mean * TPL)
 
-    def spectrum(packed):
-        edge_rows, edge_cols = ((1, 1), (0, 0)), ((0, 0), (1, 1))
-        ga, gb = packed[:h], jnp.pad(packed[h:], edge_rows)
-        ga_s = jnp.pad(ga[:, h:], edge_cols)
-        gb_s = jnp.pad(gb[:, h:], edge_cols)
-        real = jnp.concatenate([ga[:, :h] - gb_s, ga[:, 1:h - 1] + gb[:, h:]], axis=1)
-        imag = jnp.concatenate([-(ga_s + gb[:, :h]), ga[:, h:] - gb[:, 1:h - 1]], axis=1)
-        return real, imag
+    edge_rows, edge_cols = ((1, 1), (0, 0)), ((0, 0), (1, 1))
 
-    spec_real, spec_imag = spectrum(product(product(left, rows_ext), right_w))
-    template_real, template_imag = spectrum(product(product(left_t, normed), right_t))
+    def halves(packed):
+        return packed[:h], jnp.pad(packed[h:], edge_rows)
+
+    def direct(ga, gb):
+        ga_s, gb_s = jnp.pad(ga[:, h:], edge_cols), jnp.pad(gb[:, h:], edge_cols)
+        return ga[:, :h] - gb_s, -(ga_s + gb[:, :h])
+
+    def mirrored(ga, gb):
+        return ga[:, 1:h - 1] + gb[:, h:], ga[:, h:] - gb[:, 1:h - 1]
+
+    window_parts = halves(product(product(left, rows_ext), right_w))
+    template_parts = halves(product(product(left_t, normed), right_t))
 
     positions = lax.iota(jnp.int32, n)
     signed_freq = (
@@ -113,10 +116,21 @@
     col_u = weight_sin * cos_c - AMPLITUDE * sin_c
     col_v = weight_sin * sin_c + AMPLITUDE * cos_c
     contrast = -(sin_r * col_u + cos_r * col_v)
-    product_real = (spec_real * template_real + spec_imag * template_imag) * contrast
-    product_imag = (spec_imag * template_real - spec_real * template_imag) * contrast
+    def multiply(form, weight):
+        spec_real, spec_imag = form(*window_parts)
+        template_real, template_imag = form(*template_parts)
+        return (
+            (spec_real * template_real + spec_imag * template_imag) * weight,
+            (spec_imag * template_real - spec_real * template_imag) * weight,
+        )
 
-    inner = product(jnp.concatenate([product_real, product_imag], axis=0), back)
+    real_d, imag_d = multiply(direct, contrast[:, :h])
+    real_m, imag_m = multiply(mirrored, contrast[:, h:])
+    lhs = jnp.concatenate(
+        [jnp.concatenate([real_d, real_m], axis=1), jnp.concatenate([imag_d, imag_m], axis=1)],
+        axis=0,
+    )
+    inner = product(lhs, back)
     pr_c, pr_s = inner[:h, :tile_width], inner[:h, tile_width:]
     pi_c, pi_s = inner[h:, :tile_width], inner[h:, tile_width:]
     back_real = pr_c - pi_s

time: 87.8 us -> 82.1 us (0.935)
  other arithmetic: 15.5 us -> 11.8 us
  local copies, waits for them, and re-layouts: 6.04 us -> 4.37 us
    add x2 -> x0, other arithmetic: 3.11 us -> none  [spectrum(): ga[:, 1:h - 1] + gb[:, h:]]
    neg x2 -> x1, other arithmetic: 2.31 us -> 0.24 us  [per_device(): contrast = -(sin_r * col_u + cos_r * col_v)]
    mul x2, other arithmetic: 2.13 us -> 3.63 us  [multiply(): (spec_real * template_real + spec_imag * template_imag) * weight]
    unnamed x26 -> x20, local copies, waits for them, and re-layouts: 3.18 us -> 2.23 us
  transfers between devices with their start and end apart: 2 -> 2, of which waited for: 0 -> 0; matrix products, arithmetic and copies ran while one was open for 13% -> 9% of each run, Pallas kernels for 0% -> 0%
where the time goes in v7:
time: 82.1 us; the launch traced here: 81.5 us
  blocking collectives  38 us (46%)
  matrix products  14.7 us (18%)
  other arithmetic  11.8 us (14%)
  starting transfers between devices  6.43 us (8%)
  between operations  6.17 us (8%)
  local copies, waits for them, and re-layouts  4.37 us (5%)
    all_to_all x1, blocking collectives, per_device(): lax.all_to_all(scores, 'orient', 0, 0, tiled=True)  24.1 us
    dot_general x7, matrix products, product(): jnp.dot(former, latter, precision=mode, preferred_element_type=jnp.float32)  14.7 us
    all_gather x1, blocking collectives, per_device(): everything = lax.all_gather(payload, 'tile')  13.9 us
    ppermute x1, starting transfers between devices, padded(): before = lax.ppermute(last, axis, up)  4.51 us
    mul x2, other arithmetic, multiply(): (spec_real * template_real + spec_imag * template_imag) * weight  3.63 us
    unnamed x20, local copies, waits for them, and re-layouts  2.23 us
    ppermute x1, starting transfers between devices, padded(): after = lax.ppermute(initial, axis, down)  1.92 us
  transfers between devices with their start and end apart: 2, of which 0 were waited for; matrix products, arithmetic and copies ran while one was open for 9% of the time, Pallas kernels for 0%

profile of v7, /device:TPU:1, one launch (start us, length us, event | category | flops | bytes accessed | tf_op | source)
XLA Modules:
  0.0 81.5 jit_solution(1757498101080563974)
XLA Ops:
  0.6 0.0 copy-start
  0.6 0.0 copy-start.5
  0.7 0.0 copy-start.8
  0.7 0.0 copy-start.9
  0.7 1.2 %fusion.36 = (f32[128,512]{1,0:T(8,128)S(1)}, f32[128,512]{1,0:T(8,128)S(1)}) fusion(f32[512,512]{1,0:T(8,128)} %param.10), kind=kLoop, calls=%fused_computation.77 | loop fusion | bytes 1048576 | tf_op jit(solution)/shard_map/slice | solution.py:22
  1.9 4.5 %collective-permute-start = (f32[128,512]{1,0:T(8,128)S(1)}, f32[128,512]{1,0:T(8,128)}, u32[]{:S(2)}, u32[]{:S(2)}) collective-permute-start(f32[128,512]{1,0:T(8,128)S(1)} %get-tuple-element.18), channel_id=1, source_target_pairs={{0,16},{16,32},{32,48},{48,64},{64,80},{80,96},{96,112},{1,17},{17... | collective-permute-start | bytes 786440 | tf_op jit(solution)/shard_map/ppermute | solution.py:24
  6.4 1.9 %collective-permute-start.1 = (f32[128,512]{1,0:T(8,128)S(1)}, f32[128,512]{1,0:T(8,128)}, u32[]{:S(2)}, u32[]{:S(2)}) collective-permute-start(f32[128,512]{1,0:T(8,128)S(1)} %get-tuple-element.19), channel_id=1, source_target_pairs={{16,0},{32,16},{48,32},{64,48},{80,64},{96,80},{112,96},{17,1},{33... | collective-permute-start | bytes 786440 | tf_op jit(solution)/shard_map/ppermute | solution.py:25
  8.3 0.0 copy-done
  8.3 0.9 %fusion.34 = (f32[]{:T(128)}, f32[]{:T(128)}) fusion(f32[512,512]{1,0:T(8,128)S(1)} %copy-done), kind=kLoop, calls=%fused_computation.75 | loop fusion | flops 786430 | bytes 1048584 | tf_op jit(solution)/shard_map/reduce_sum | solution.py:66
  9.2 1.4 %select_maximum_fusion = f32[256]{0:T(256)S(1)} fusion(f32[1]{0:T(128)} %bitcast.2, f32[1]{0:T(128)} %bitcast.1), kind=kLoop, calls=%fused_computation.72 | loop fusion | flops 1024 | bytes 1032 | tf_op jit(solution)/shard_map/stack | solution.py:66
  10.6 0.0 copy-done.8
  10.6 0.0 copy-start.7
  10.6 13.9 %all-gather.1 = f32[8,33,256]{2,1,0:T(8,128)S(1)} all-gather(f32[1,33,256]{2,1,0:T(8,128)S(1)} %maximum_bitcast_fusion.2), channel_id=2, replica_groups=mesh['tile'=8,'orient'=16] {'tile'}, dimensions={0}, use_global_device_ids=true | all-gather | bytes 304128 | tf_op jit(solution)/shard_map/all_gather | solution.py:70
  24.5 0.7 slice_reduce_fusion
  25.8 0.0 copy-done.9
  25.8 0.6 fusion.32
  27.8 0.7 multiply_reduce_fusion.1
  29.2 0.6 fusion.37
  29.8 0.0 copy-done.5
  29.8 0.9 %fusion.40 = f32[256,768]{1,0:T(8,128)S(1)} fusion(f32[256,256]{1,0:T(8,128)S(1)} %bitcast.37, f32[768,256]{1,0:T(8,128)S(1)} %copy-done.5), kind=kOutput, calls=%fused_computation.81 | convolution fusion | flops 301989888 | bytes 1835008 | tf_op jit(solution)/shard_map/dot_general | solution.py:31
  30.7 0.0 copy-done.7
  30.7 1.3 %fusion.41 = f32[768,768]{1,0:T(8,128)S(1)} fusion(f32[256,768]{1,0:T(8,128)S(1)} %fusion.40, f32[256,768]{1,0:T(8,128)S(1)} %copy-done.7), kind=kOutput, calls=%fused_computation.82 | convolution fusion | flops 905969664 | bytes 3932160 | tf_op jit(solution)/shard_map/dot_general | solution.py:31
  34.6 0.1 slice.263
  34.7 0.2 add_negate_fusion
  35.0 0.0 collective-permute-done
  35.0 0.0 collective-permute-done.1
  35.0 0.0 copy-start.2
  35.0 1.4 %fusion.9 = f32[768,512]{1,0:T(8,128)S(1)} fusion(f32[128,512]{1,0:T(8,128)} %collective-permute-done.1, f32[512,512]{1,0:T(8,128)S(1)} %copy-done, f32[128,512]{1,0:T(8,128)} %collective-permute-done, f32[]{:T(128)} %bitcast.6, f32[]{:T(128)} %bitcast.5, pred[768]{0:T(1024)(128)(4,1)S(1)} %fusion.28), kind=kLoop, calls=%fused_computation.10 | loop fusion | flops 1966080 | bytes 3146504 | tf_op jit(solution)/shard_map/jit(_where)/select_n | solution.py:80
  36.4 0.4 copy-done.2
  36.8 0.0 copy-start.3
  36.8 4.0 %fusion.38 = f32[512,768]{1,0:T(8,128)S(1)} fusion(f32[768,512]{1,0:T(8,128)S(1)} %fusion.9, f32[768,768]{1,0:T(8,128)S(1)} %copy-done.2), kind=kOutput, calls=%fused_computation.79 | convolution fusion | flops 1811939328 | bytes 5505024 | tf_op jit(solution)/shard_map/dot_general | solution.py:31
  40.8 0.0 copy-done.3
  40.8 2.5 %fusion.39 = f32[768,768]{1,0:T(8,128)S(1)} fusion(f32[512,768]{1,0:T(8,128)S(1)} %fusion.38, f32[512,768]{1,0:T(8,128)S(1)} %copy-done.3), kind=kOutput, calls=%fused_computation.80 | convolution fusion | flops 1811939328 | bytes 5505024 | tf_op jit(solution)/shard_map/dot_general | solution.py:31
  43.3 0.1 slice.260
  43.4 2.4 %add_multiply_fusion.1 = (f32[385,383]{1,0:T(8,128)S(1)}, f32[385,383]{1,0:T(8,128)S(1)}, f32[385,383]{1,0:T(8,128)S(1)}, f32[385,383]{1,0:T(8,128)S(1)}, f32[385,383]{1,0:T(8,128)S(1)}, /*index=5*/f32[385,383]{1,0:T(8,128)S(1)}) fusion(f32[385,768]{1,0:T(8,128)S(1)} %add_negate_fusion, f32[768,768]{1,0:T(8,128)S(1)} %fusion.39, f32[768,768]{1,0:T(8,128)S(1)} %fusion.41, ...), kind=kLoop, calls=%fused_computation.36 | loop fusion | flops 2359280 | bytes 8841172 | tf_op jit(solution)/shard_map/mul | solution.py:123
  45.8 0.0 copy-start.1
  45.8 1.2 %add_multiply_fusion = (f32[385,385]{1,0:T(8,128)S(1)}, f32[385,385]{1,0:T(8,128)S(1)}) fusion(f32[385,768]{1,0:T(8,128)S(1)} %add_negate_fusion, f32[385,383]{1,0:T(8,128)S(1)} %get-tuple-element.16, f32[768,768]{1,0:T(8,128)S(1)} %fusion.39, f32[385,383]{1,0:T(8,128)S(1)} %get-tuple-element.17, f32[768,768]{1,0:T(8,128)S(1)} %fusion.41, ...), kind=kLoop, calls=%fused_computation.28 | loop fusion | flops 2371600 | bytes 7676932 | tf_op jit(solution)/shard_map/mul | solution.py:123
  47.0 0.7 copy-done.1
  47.7 4.0 %fusion = f32[770,1024]{1,0:T(8,128)S(1)} fusion(f32[768,1024]{1,0:T(8,128)S(1)} %copy-done.1, f32[385,383]{1,0:T(8,128)S(1)} %get-tuple-element.11, f32[385,385]{1,0:T(8,128)S(1)} %get-tuple-element.9, f32[385,383]{1,0:T(8,128)S(1)} %get-tuple-element.10, f32[385,385]{1,0:T(8,128)S(1)} %get-tuple-element.8), kind=kOutput, calls=%fused_computation | convolution fusion | flops 3635089920 | bytes 8665088 | tf_op jit(solution)/shard_map/dot_general | solution.py:31
  51.7 0.0 copy-start.4
  51.7 0.2 fusion.35
  51.9 1.0 %copy-done.4 = f32[512,385]{1,0:T(8,128)S(1)} copy-done((f32[512,385]{1,0:T(8,128)S(1)}, f32[512,385]{1,0:T(8,128)}, u32[]{:S(2)}) %copy-start.4) | copy-done | bytes 788504
  52.9 0.0 copy-start.6
  52.9 1.0 %fusion.12 = f32[512,512]{0,1:T(8,128)S(1)} fusion(f32[512,385]{1,0:T(8,128)S(1)} %copy-done.4, f32[770,1024]{1,0:T(8,128)S(1)} %fusion), kind=kOutput, calls=%fused_computation.23 | convolution fusion | flops 605749760 | bytes 3702784 | tf_op jit(solution)/shard_map/dot_general | solution.py:31
  54.0 0.1 copy-done.6
  54.1 1.1 %convolution_add_fusion = f32[512,512]{0,1:T(8,128)S(1)} fusion(f32[512,512]{0,1:T(8,128)S(1)} %fusion.12, f32[512,383]{1,0:T(8,128)S(1)} %copy-done.6, f32[385,512]{1,0:T(8,128)S(1)} %get-tuple-element.13, f32[385,512]{1,0:T(8,128)S(1)} %get-tuple-element.12), kind=kOutput, calls=%fused_computation.11 | convolution fusion | flops 602865152 | bytes 4456448 | tf_op jit(solution)/shard_map/dot_general | solution.py:31
  55.1 24.1 %all_to_all.9 = f32[16,32,512]{2,1,0:T(8,128)S(1)} all-to-all(f32[16,32,512]{2,1,0:T(8,128)S(1)} %bitcast.36), channel_id=1, replica_groups=mesh['tile'=8,'orient'=16] {'orient'}, dimensions={0} | all-to-all | bytes 2097152 | tf_op jit(solution)/shard_map/all_to_all | solution.py:142
  79.2 0.7 maximum_bitcast_fusion.1
  79.9 0.7 maximum_bitcast_fusion
  80.7 0.8 fusion.18
  (7 shorter events, 0.2 us)
Async XLA Ops:
  0.6 7.7 %copy-start = (f32[512,512]{1,0:T(8,128)S(1)}, f32[512,512]{1,0:T(8,128)}, u32[]{:S(2)}) copy-start(f32[512,512]{1,0:T(8,128)} %param.10) | copy-start | bytes 3145732
  0.6 29.2 %copy-start.5 = (f32[768,256]{1,0:T(8,128)S(1)}, f32[768,256]{1,0:T(8,128)}, u32[]{:S(2)}) copy-start(f32[768,256]{1,0:T(8,128)} %constant.74.clone) | copy-start | bytes 2359300
  0.7 9.9 %copy-start.8 = (f32[1,32,256]{2,1,0:T(8,128)S(1)}, f32[1,32,256]{2,1,0:T(8,128)}, u32[]{:S(2)}) copy-start(f32[1,32,256]{2,1,0:T(8,128)} %param.11) | copy-start | bytes 98308
  0.7 25.1 %copy-start.9 = (f32[4]{0:T(128)S(1)}, f32[4]{0:T(128)}, u32[]{:S(2)}) copy-start(f32[4]{0:T(128)} %param.12) | copy-start | bytes 52
  1.9 33.1 %collective-permute-start = (f32[128,512]{1,0:T(8,128)S(1)}, f32[128,512]{1,0:T(8,128)}, u32[]{:S(2)}, u32[]{:S(2)}) collective-permute-start(f32[128,512]{1,0:T(8,128)S(1)} %get-tuple-element.18), channel_id=1, source_target_pairs={{0,16},{16,32},{32,48},{48,64},{64,80},{80,96},{96,112},{1,17},{17... | collective-permute-start | bytes 786440 | tf_op jit(solution)/shard_map/ppermute | solution.py:24
  6.4 28.6 %collective-permute-start.1 = (f32[128,512]{1,0:T(8,128)S(1)}, f32[128,512]{1,0:T(8,128)}, u32[]{:S(2)}, u32[]{:S(2)}) collective-permute-start(f32[128,512]{1,0:T(8,128)S(1)} %get-tuple-element.19), channel_id=1, source_target_pairs={{16,0},{32,16},{48,32},{64,48},{80,64},{96,80},{112,96},{17,1},{33... | collective-permute-start | bytes 786440 | tf_op jit(solution)/shard_map/ppermute | solution.py:25
  10.6 20.1 %copy-start.7 = (f32[256,768]{1,0:T(8,128)S(1)}, f32[256,768]{1,0:T(8,128)}, u32[]{:S(2)}) copy-start(f32[256,768]{1,0:T(8,128)} %constant.76.clone) | copy-start | bytes 2359300
  35.0 1.8 %copy-start.2 = (f32[768,768]{1,0:T(8,128)S(1)}, f32[768,768]{1,0:T(8,128)}, u32[]{:S(2)}) copy-start(f32[768,768]{1,0:T(8,128)} %constant.73.clone) | copy-start | bytes 7077892
  36.8 4.0 %copy-start.3 = (f32[512,768]{1,0:T(8,128)S(1)}, f32[512,768]{1,0:T(8,128)}, u32[]{:S(2)}) copy-start(f32[512,768]{1,0:T(8,128)} %constant.75.clone) | copy-start | bytes 4718596
  45.8 1.9 %copy-start.1 = (f32[768,1024]{1,0:T(8,128)S(1)}, f32[768,1024]{1,0:T(8,128)}, u32[]{:S(2)}) copy-start(f32[768,1024]{1,0:T(8,128)} %constant.77.clone) | copy-start | bytes 9437188
  51.7 1.2 %copy-start.4 = (f32[512,385]{1,0:T(8,128)S(1)}, f32[512,385]{1,0:T(8,128)}, u32[]{:S(2)}) copy-start(f32[512,385]{1,0:T(8,128)} %constant.95) | copy-start | bytes 2365444
  52.9 1.1 %copy-start.6 = (f32[512,383]{1,0:T(8,128)S(1)}, f32[512,383]{1,0:T(8,128)}, u32[]{:S(2)}) copy-start(f32[512,383]{1,0:T(8,128)} %constant.96) | copy-start | bytes 2353156

commit v8 on v7

--- a/solution.py
+++ b/solution.py
@@ -63,15 +63,17 @@
     pixel_count = float(tile_rows * tile_width * tile_count)
     own_rows, tpl_width = templates.shape[1], templates.shape[2]
     halo = padded(micrograph, (("tile", 0),), margin)
-    sums = jnp.stack([jnp.sum(micrograph), jnp.sum(micrograph * micrograph)])
-    payload = jnp.concatenate(
-        [templates[0], jnp.pad(sums, (0, tpl_width - 2))[None]], axis=0
-    )
+    lane = lax.broadcasted_iota(jnp.int32, (1, tpl_width), 1)
+    half = tpl_width // 2
+    stats_row = jnp.where(lane < half, jnp.sum(micrograph), jnp.sum(micrograph * micrograph))
+    payload = jnp.concatenate([templates[0], stats_row], axis=0)
     everything = lax.all_gather(payload, "tile")
-    totals = jnp.sum(everything[:, own_rows, :2], axis=0)
+    totals = jnp.sum(everything[:, own_rows, :], axis=0)
     gathered = everything[:, :own_rows].reshape(tile_count * own_rows, tpl_width)
-    centre = totals[0] / pixel_count
-    spread = jnp.sqrt(totals[1] / pixel_count - centre * centre + 1e-05)
+    centre = totals[:half] / pixel_count
+    spread = jnp.sqrt(totals[half:] / pixel_count - centre * centre + 1e-05)
+    reps = tile_width // half
+    centre, spread = jnp.tile(centre, reps)[None, :], jnp.tile(spread, reps)[None, :]
     tile_index = lax.axis_index("tile")
     row_ids = lax.broadcasted_iota(jnp.int32, (n, 1), 0)
     valid = ((row_ids >= margin) | (tile_index > 0)) & (

time: 82.1 us -> 79.6 us (0.970)
  between operations: 6.17 us -> 3.58 us
  other arithmetic: 11.8 us -> 10.6 us
  local copies, waits for them, and re-layouts: 4.37 us -> 5.56 us
    another operation x1 -> x0, other arithmetic: 1.37 us -> none  [per_device(): sums = jnp.stack([jnp.sum(micrograph), jnp.sum(micrograph * micrograph)])]
    select_n x0 -> x1, other arithmetic: none -> 1.29 us  [per_device(): jnp.where(lane < half, jnp.sum(micrograph), jnp.sum(micrograph * microgra...]
    select_n x1, other arithmetic: 1.39 us -> 0.21 us  [per_device(): jnp.where(valid, (halo - centre) / spread, 0.0)]
    unnamed x20, local copies, waits for them, and re-layouts: 2.23 us -> 3.25 us
where the time goes in v8:
time: 79.6 us; the launch traced here: 79 us
  blocking collectives  38 us (48%)
  matrix products  14.7 us (18%)
  other arithmetic  10.6 us (13%)
  starting transfers between devices  6.55 us (8%)
  local copies, waits for them, and re-layouts  5.56 us (7%)
  between operations  3.58 us (4%)
    all_to_all x1, blocking collectives, per_device(): lax.all_to_all(scores, 'orient', 0, 0, tiled=True)  24.1 us
    dot_general x7, matrix products, product(): jnp.dot(former, latter, precision=mode, preferred_element_type=jnp.float32)  14.7 us
    all_gather x1, blocking collectives, per_device(): everything = lax.all_gather(payload, 'tile')  13.9 us
    ppermute x1, starting transfers between devices, padded(): before = lax.ppermute(last, axis, up)  4.63 us
    mul x2, other arithmetic, multiply(): (spec_real * template_real + spec_imag * template_imag) * weight  3.63 us
    unnamed x20, local copies, waits for them, and re-layouts  3.25 us
    slice x1, local copies, waits for them, and re-layouts, padded(): last = lax.slice_in_dim(shard, length - width, length, axis=dim)  1.95 us
    ppermute x1, starting transfers between devices, padded(): after = lax.ppermute(initial, axis, down)  1.92 us
  transfers between devices with their start and end apart: 2, of which 0 were waited for; matrix products, arithmetic and copies ran while one was open for 9% of the time, Pallas kernels for 0%

profile of v8, /device:TPU:1, one launch (start us, length us, event | category | flops | bytes accessed | tf_op | source)
XLA Modules:
  0.0 79.0 jit_solution(2598113434607144886)
XLA Ops:
  0.6 0.0 copy-start
  0.6 0.0 copy-start.8
  0.7 0.0 copy-start.9
  0.7 1.9 %fusion.36 = (f32[128,512]{1,0:T(8,128)}, f32[128,512]{1,0:T(8,128)}) fusion(f32[512,512]{1,0:T(8,128)} %param.10), kind=kLoop, calls=%fused_computation.81 | loop fusion | bytes 1048576 | tf_op jit(solution)/shard_map/slice | solution.py:22
  2.6 0.0 copy-start.5
  2.6 4.6 %collective-permute-start = (f32[128,512]{1,0:T(8,128)}, f32[128,512]{1,0:T(8,128)S(1)}, u32[]{:S(2)}, u32[]{:S(2)}) collective-permute-start(f32[128,512]{1,0:T(8,128)} %get-tuple-element.18), channel_id=1, source_target_pairs={{0,16},{16,32},{32,48},{48,64},{64,80},{80,96},{96,112},{1,17},{17... | collective-permute-start | bytes 786440 | tf_op jit(solution)/shard_map/ppermute | solution.py:24
  7.2 1.9 %collective-permute-start.1 = (f32[128,512]{1,0:T(8,128)}, f32[128,512]{1,0:T(8,128)S(1)}, u32[]{:S(2)}, u32[]{:S(2)}) collective-permute-start(f32[128,512]{1,0:T(8,128)} %get-tuple-element.19), channel_id=1, source_target_pairs={{16,0},{32,16},{48,32},{64,48},{80,64},{96,80},{112,96},{17,1},{33... | collective-permute-start | bytes 786440 | tf_op jit(solution)/shard_map/ppermute | solution.py:25
  9.2 0.0 copy-done
  9.2 0.9 %fusion.34 = (f32[]{:T(128)}, f32[]{:T(128)}) fusion(f32[512,512]{1,0:T(8,128)S(1)} %copy-done), kind=kLoop, calls=%fused_computation.79 | loop fusion | flops 786430 | bytes 1048584 | tf_op jit(solution)/shard_map/reduce_sum | solution.py:68
  10.1 1.3 %compare_select_fusion.2 = f32[1,256]{1,0:T(1,128)S(1)} fusion(f32[]{:T(128)} %get-tuple-element.5, f32[]{:T(128)} %get-tuple-element.4), kind=kLoop, calls=%fused_computation.68 | loop fusion | flops 512 | bytes 1032 | tf_op jit(solution)/shard_map/jit(_where)/select_n | solution.py:68
  11.4 0.0 copy-done.8
  11.4 0.0 copy-start.7
  11.4 13.9 %all-gather.1 = f32[8,33,256]{2,1,0:T(8,128)S(1)} all-gather(f32[1,33,256]{2,1,0:T(8,128)S(1)} %maximum_bitcast_fusion.2), channel_id=2, replica_groups=mesh['tile'=8,'orient'=16] {'tile'}, dimensions={0}, use_global_device_ids=true | all-gather | bytes 304128 | tf_op jit(solution)/shard_map/all_gather | solution.py:70
  25.3 0.7 slice_reduce_fusion
  26.6 0.0 copy-done.9
  26.6 0.6 fusion.32
  28.6 0.7 multiply_reduce_fusion.1
  30.1 0.0 copy-done.5
  30.1 0.9 %fusion.39 = f32[256,768]{1,0:T(8,128)S(1)} fusion(f32[256,256]{1,0:T(8,128)S(1)} %bitcast.36, f32[768,256]{1,0:T(8,128)S(1)} %copy-done.5), kind=kOutput, calls=%fused_computation.84 | convolution fusion | flops 301989888 | bytes 1835008 | tf_op jit(solution)/shard_map/dot_general | solution.py:31
  30.9 0.0 copy-done.7
  30.9 1.3 %fusion.40 = f32[768,768]{1,0:T(8,128)S(1)} fusion(f32[256,768]{1,0:T(8,128)S(1)} %fusion.39, f32[256,768]{1,0:T(8,128)S(1)} %copy-done.7), kind=kOutput, calls=%fused_computation.85 | convolution fusion | flops 905969664 | bytes 3932160 | tf_op jit(solution)/shard_map/dot_general | solution.py:31
  32.3 0.1 slice.263
  32.4 0.2 add_negate_fusion
  32.6 0.0 collective-permute-done
  32.6 0.0 collective-permute-done.1
  32.6 0.0 copy-start.2
  32.6 0.2 fusion.9
  32.8 1.4 %copy-done.2 = f32[768,768]{1,0:T(8,128)S(1)} copy-done((f32[768,768]{1,0:T(8,128)S(1)}, f32[768,768]{1,0:T(8,128)}, u32[]{:S(2)}) %copy-start.2) | copy-done | bytes 2359320
  34.3 0.0 copy-start.3
  34.3 4.0 %fusion.37 = f32[512,768]{1,0:T(8,128)S(1)} fusion(f32[768,512]{1,0:T(8,128)S(1)} %fusion.9, f32[768,768]{1,0:T(8,128)S(1)} %copy-done.2), kind=kOutput, calls=%fused_computation.82 | convolution fusion | flops 1811939328 | bytes 5505024 | tf_op jit(solution)/shard_map/dot_general | solution.py:31
  38.3 0.0 copy-done.3
  38.3 2.5 %fusion.38 = f32[768,768]{1,0:T(8,128)S(1)} fusion(f32[512,768]{1,0:T(8,128)S(1)} %fusion.37, f32[512,768]{1,0:T(8,128)S(1)} %copy-done.3), kind=kOutput, calls=%fused_computation.83 | convolution fusion | flops 1811939328 | bytes 5505024 | tf_op jit(solution)/shard_map/dot_general | solution.py:31
  40.8 0.1 slice.260
  40.9 2.4 %add_multiply_fusion.1 = (f32[385,383]{1,0:T(8,128)S(1)}, f32[385,383]{1,0:T(8,128)S(1)}, f32[385,383]{1,0:T(8,128)S(1)}, f32[385,383]{1,0:T(8,128)S(1)}, f32[385,383]{1,0:T(8,128)S(1)}, /*index=5*/f32[385,383]{1,0:T(8,128)S(1)}) fusion(f32[385,768]{1,0:T(8,128)S(1)} %add_negate_fusion, f32[768,768]{1,0:T(8,128)S(1)} %fusion.38, f32[768,768]{1,0:T(8,128)S(1)} %fusion.40, ...), kind=kLoop, calls=%fused_computation.36 | loop fusion | flops 2359280 | bytes 8841172 | tf_op jit(solution)/shard_map/mul | solution.py:125
  43.3 0.0 copy-start.1
  43.3 1.2 %add_multiply_fusion = (f32[385,385]{1,0:T(8,128)S(1)}, f32[385,385]{1,0:T(8,128)S(1)}) fusion(f32[385,768]{1,0:T(8,128)S(1)} %add_negate_fusion, f32[385,383]{1,0:T(8,128)S(1)} %get-tuple-element.16, f32[768,768]{1,0:T(8,128)S(1)} %fusion.38, f32[385,383]{1,0:T(8,128)S(1)} %get-tuple-element.17, f32[768,768]{1,0:T(8,128)S(1)} %fusion.40, ...), kind=kLoop, calls=%fused_computation.28 | loop fusion | flops 2371600 | bytes 7676932 | tf_op jit(solution)/shard_map/mul | solution.py:125
  44.5 0.7 copy-done.1
  45.2 4.0 %fusion = f32[770,1024]{1,0:T(8,128)S(1)} fusion(f32[768,1024]{1,0:T(8,128)S(1)} %copy-done.1, f32[385,383]{1,0:T(8,128)S(1)} %get-tuple-element.11, f32[385,385]{1,0:T(8,128)S(1)} %get-tuple-element.9, f32[385,383]{1,0:T(8,128)S(1)} %get-tuple-element.10, f32[385,385]{1,0:T(8,128)S(1)} %get-tuple-element.8), kind=kOutput, calls=%fused_computation | convolution fusion | flops 3635089920 | bytes 8665088 | tf_op jit(solution)/shard_map/dot_general | solution.py:31
  49.2 0.0 copy-start.4
  49.2 0.2 fusion.35
  49.4 1.0 %copy-done.4 = f32[512,385]{1,0:T(8,128)S(1)} copy-done((f32[512,385]{1,0:T(8,128)S(1)}, f32[512,385]{1,0:T(8,128)}, u32[]{:S(2)}) %copy-start.4) | copy-done | bytes 788504
  50.4 0.0 copy-start.6
  50.4 1.0 %fusion.12 = f32[512,512]{0,1:T(8,128)S(1)} fusion(f32[512,385]{1,0:T(8,128)S(1)} %copy-done.4, f32[770,1024]{1,0:T(8,128)S(1)} %fusion), kind=kOutput, calls=%fused_computation.23 | convolution fusion | flops 605749760 | bytes 3702784 | tf_op jit(solution)/shard_map/dot_general | solution.py:31
  51.5 0.1 copy-done.6
  51.5 1.1 %convolution_add_fusion = f32[512,512]{0,1:T(8,128)S(1)} fusion(f32[512,512]{0,1:T(8,128)S(1)} %fusion.12, f32[512,383]{1,0:T(8,128)S(1)} %copy-done.6, f32[385,512]{1,0:T(8,128)S(1)} %get-tuple-element.13, f32[385,512]{1,0:T(8,128)S(1)} %get-tuple-element.12), kind=kOutput, calls=%fused_computation.11 | convolution fusion | flops 602865152 | bytes 4456448 | tf_op jit(solution)/shard_map/dot_general | solution.py:31
  52.6 24.1 %all_to_all.9 = f32[16,32,512]{2,1,0:T(8,128)S(1)} all-to-all(f32[16,32,512]{2,1,0:T(8,128)S(1)} %bitcast.35), channel_id=1, replica_groups=mesh['tile'=8,'orient'=16] {'orient'}, dimensions={0} | all-to-all | bytes 2097152 | tf_op jit(solution)/shard_map/all_to_all | solution.py:144
  76.8 0.7 maximum_bitcast_fusion.1
  77.5 0.7 maximum_bitcast_fusion
  78.2 0.8 fusion.18
  (9 shorter events, 0.2 us)
Async XLA Ops:
  0.6 8.5 %copy-start = (f32[512,512]{1,0:T(8,128)S(1)}, f32[512,512]{1,0:T(8,128)}, u32[]{:S(2)}) copy-start(f32[512,512]{1,0:T(8,128)} %param.10) | copy-start | bytes 3145732
  0.6 10.7 %copy-start.8 = (f32[1,32,256]{2,1,0:T(8,128)S(1)}, f32[1,32,256]{2,1,0:T(8,128)}, u32[]{:S(2)}) copy-start(f32[1,32,256]{2,1,0:T(8,128)} %param.11) | copy-start | bytes 98308
  0.7 26.0 %copy-start.9 = (f32[4]{0:T(128)S(1)}, f32[4]{0:T(128)}, u32[]{:S(2)}) copy-start(f32[4]{0:T(128)} %param.12) | copy-start | bytes 52
  2.6 27.4 %copy-start.5 = (f32[768,256]{1,0:T(8,128)S(1)}, f32[768,256]{1,0:T(8,128)}, u32[]{:S(2)}) copy-start(f32[768,256]{1,0:T(8,128)} %constant.69.clone) | copy-start | bytes 2359300
  2.6 30.0 %collective-permute-start = (f32[128,512]{1,0:T(8,128)}, f32[128,512]{1,0:T(8,128)S(1)}, u32[]{:S(2)}, u32[]{:S(2)}) collective-permute-start(f32[128,512]{1,0:T(8,128)} %get-tuple-element.18), channel_id=1, source_target_pairs={{0,16},{16,32},{32,48},{48,64},{64,80},{80,96},{96,112},{1,17},{17... | collective-permute-start | bytes 786440 | tf_op jit(solution)/shard_map/ppermute | solution.py:24
  7.2 25.4 %collective-permute-start.1 = (f32[128,512]{1,0:T(8,128)}, f32[128,512]{1,0:T(8,128)S(1)}, u32[]{:S(2)}, u32[]{:S(2)}) collective-permute-start(f32[128,512]{1,0:T(8,128)} %get-tuple-element.19), channel_id=1, source_target_pairs={{16,0},{32,16},{48,32},{64,48},{80,64},{96,80},{112,96},{17,1},{33... | collective-permute-start | bytes 786440 | tf_op jit(solution)/shard_map/ppermute | solution.py:25
  11.4 19.5 %copy-start.7 = (f32[256,768]{1,0:T(8,128)S(1)}, f32[256,768]{1,0:T(8,128)}, u32[]{:S(2)}) copy-start(f32[256,768]{1,0:T(8,128)} %constant.71.clone) | copy-start | bytes 2359300
  32.6 1.7 %copy-start.2 = (f32[768,768]{1,0:T(8,128)S(1)}, f32[768,768]{1,0:T(8,128)}, u32[]{:S(2)}) copy-start(f32[768,768]{1,0:T(8,128)} %constant.68.clone) | copy-start | bytes 7077892
  34.3 4.0 %copy-start.3 = (f32[512,768]{1,0:T(8,128)S(1)}, f32[512,768]{1,0:T(8,128)}, u32[]{:S(2)}) copy-start(f32[512,768]{1,0:T(8,128)} %constant.70.clone) | copy-start | bytes 4718596
  43.3 1.9 %copy-start.1 = (f32[768,1024]{1,0:T(8,128)S(1)}, f32[768,1024]{1,0:T(8,128)}, u32[]{:S(2)}) copy-start(f32[768,1024]{1,0:T(8,128)} %constant.72.clone) | copy-start | bytes 9437188
  49.2 1.2 %copy-start.4 = (f32[512,385]{1,0:T(8,128)S(1)}, f32[512,385]{1,0:T(8,128)}, u32[]{:S(2)}) copy-start(f32[512,385]{1,0:T(8,128)} %constant.88) | copy-start | bytes 2365444
  50.4 1.1 %copy-start.6 = (f32[512,383]{1,0:T(8,128)S(1)}, f32[512,383]{1,0:T(8,128)}, u32[]{:S(2)}) copy-start(f32[512,383]{1,0:T(8,128)} %constant.89) | copy-start | bytes 2353156

commit v9 on v8

--- a/solution.py
+++ b/solution.py
@@ -83,8 +83,19 @@
     extent = gathered.shape[0]
     left, left_t, right_w, right_t, back, final = tables(tile_width, margin, extent)
 
-    centred = gathered - jnp.mean(gathered)
-    root_mean = jnp.sqrt(jnp.mean(centred * centred) + 1e-06)
+    def lane_total(columns):
+        width = columns.shape[0]
+        if width & (width - 1):
+            return jnp.full((1, width), jnp.sum(columns))
+        step = width // 2
+        while step:
+            columns = columns + jnp.roll(columns, step)
+            step //= 2
+        return columns[None, :]
+
+    tpl_count = float(gathered.shape[0] * gathered.shape[1])
+    centred = gathered - lane_total(jnp.sum(gathered, axis=0)) / tpl_count
+    root_mean = jnp.sqrt(lane_total(jnp.sum(centred * centred, axis=0)) / tpl_count + 1e-06)
     normed = centred / (root_mean * TPL)
 
     edge_rows, edge_cols = ((1, 1), (0, 0)), ((0, 0), (1, 1))

time: 79.6 us -> 81.4 us (1.023)
  local copies, waits for them, and re-layouts: 5.56 us -> 7.62 us
  between operations: 3.58 us -> 2.33 us
  other arithmetic: 10.6 us -> 11.8 us
    slice x0 -> x16, local copies, waits for them, and re-layouts: none -> 2.08 us  [lane_total(): columns = columns + jnp.roll(columns, step)]
    reduce_sum x2, other arithmetic: 1.33 us -> 0.11 us  [the longest x1 0.06 us: per_device(): jnp.sum(centred * centred, axis=0)]
    add x0 -> x14, other arithmetic: none -> 0.97 us  [lane_total(): columns = columns + jnp.roll(columns, step)]
  transfers between devices with their start and end apart: 2 -> 2, of which waited for: 0 -> 0; matrix products, arithmetic and copies ran while one was open for 9% -> 12% of each run, Pallas kernels for 0% -> 0%
where the time goes in v9:
time: 81.4 us; the launch traced here: 80.8 us
  blocking collectives  37.8 us (46%)
  matrix products  14.7 us (18%)
  other arithmetic  11.8 us (14%)
  local copies, waits for them, and re-layouts  7.62 us (9%)
  starting transfers between devices  6.55 us (8%)
  between operations  2.33 us (3%)
    all_to_all x1, blocking collectives, per_device(): lax.all_to_all(scores, 'orient', 0, 0, tiled=True)  24.1 us
    dot_general x7, matrix products, product(): jnp.dot(former, latter, precision=mode, preferred_element_type=jnp.float32)  14.7 us
    all_gather x1, blocking collectives, per_device(): everything = lax.all_gather(payload, 'tile')  13.7 us
    ppermute x1, starting transfers between devices, padded(): before = lax.ppermute(last, axis, up)  4.63 us
    mul x2, other arithmetic, multiply(): (spec_real * template_real + spec_imag * template_imag) * weight  3.63 us
    unnamed x20, local copies, waits for them, and re-layouts  3.25 us
    slice x16, local copies, waits for them, and re-layouts, lane_total(): columns = columns + jnp.roll(columns, step)  2.08 us
    slice x1, local copies, waits for them, and re-layouts, padded(): last = lax.slice_in_dim(shard, length - width, length, axis=dim)  1.94 us
  transfers between devices with their start and end apart: 2, of which 0 were waited for; matrix products, arithmetic and copies ran while one was open for 12% of the time, Pallas kernels for 0%

profile of v9, /device:TPU:1, one launch (start us, length us, event | category | flops | bytes accessed | tf_op | source)
XLA Modules:
  0.0 80.8 jit_solution(1915577417576301800)
XLA Ops:
  0.7 1.9 %fusion.41 = (f32[128,512]{1,0:T(8,128)}, f32[128,512]{1,0:T(8,128)}) fusion(f32[512,512]{1,0:T(8,128)} %param.10), kind=kLoop, calls=%fused_computation.102 | loop fusion | bytes 1048576 | tf_op jit(solution)/shard_map/slice | solution.py:22
  2.6 4.6 %collective-permute-start = (f32[128,512]{1,0:T(8,128)}, f32[128,512]{1,0:T(8,128)S(1)}, u32[]{:S(2)}, u32[]{:S(2)}) collective-permute-start(f32[128,512]{1,0:T(8,128)} %get-tuple-element.18), channel_id=1, source_target_pairs={{0,16},{16,32},{32,48},{48,64},{64,80},{80,96},{96,112},{1,17},{17... | collective-permute-start | bytes 786440 | tf_op jit(solution)/shard_map/ppermute | solution.py:24
  7.2 1.9 %collective-permute-start.1 = (f32[128,512]{1,0:T(8,128)}, f32[128,512]{1,0:T(8,128)S(1)}, u32[]{:S(2)}, u32[]{:S(2)}) collective-permute-start(f32[128,512]{1,0:T(8,128)} %get-tuple-element.19), channel_id=1, source_target_pairs={{16,0},{32,16},{48,32},{64,48},{80,64},{96,80},{112,96},{17,1},{33... | collective-permute-start | bytes 786440 | tf_op jit(solution)/shard_map/ppermute | solution.py:25
  9.2 0.9 %fusion.39 = (f32[]{:T(128)}, f32[]{:T(128)}) fusion(f32[512,512]{1,0:T(8,128)S(1)} %copy-done), kind=kLoop, calls=%fused_computation.100 | loop fusion | flops 786430 | bytes 1048584 | tf_op jit(solution)/shard_map/reduce_sum | solution.py:68
  10.1 1.3 %compare_select_fusion.2 = f32[1,256]{1,0:T(1,128)S(1)} fusion(f32[]{:T(128)} %get-tuple-element.5, f32[]{:T(128)} %get-tuple-element.4), kind=kLoop, calls=%fused_computation.67 | loop fusion | flops 512 | bytes 1032 | tf_op jit(solution)/shard_map/jit(_where)/select_n | solution.py:68
  11.4 13.7 %all-gather.1 = f32[8,33,256]{2,1,0:T(8,128)S(1)} all-gather(f32[1,33,256]{2,1,0:T(8,128)S(1)} %maximum_bitcast_fusion.2), channel_id=2, replica_groups=mesh['tile'=8,'orient'=16] {'tile'}, dimensions={0}, use_global_device_ids=true | all-gather | bytes 304128 | tf_op jit(solution)/shard_map/all_gather | solution.py:70
  25.2 0.0 copy-start.7
  25.9 0.6 fusion.37
  27.3 0.1 slice.324
  27.4 0.1 maximum_add_fusion.1
  27.5 0.1 slice.326
  27.5 0.1 maximum_add_fusion.2
  27.6 0.1 slice.328
  27.7 0.1 maximum_add_fusion.3
  27.8 0.1 slice.330
  27.9 0.1 maximum_add_fusion.4
  27.9 0.1 slice.332
  28.0 0.1 maximum_add_fusion.5
  28.1 0.1 slice.334
  28.2 0.1 maximum_add_fusion.6
  28.2 0.6 slice.336
  28.8 0.7 fusion.32
  29.6 0.1 multiply_reduce_fusion.1
  29.6 0.1 slice.340
  29.7 0.1 maximum_add_fusion.9
  29.8 0.1 slice.342
  29.9 0.1 maximum_add_fusion.10
  29.9 0.1 slice.344
  30.0 0.1 maximum_add_fusion.11
  30.1 0.1 slice.346
  30.2 0.1 maximum_add_fusion.12
  30.3 0.1 slice.348
  30.3 0.1 maximum_add_fusion.13
  30.4 0.1 slice.350
  30.5 0.1 maximum_add_fusion.14
  30.6 0.6 slice.352
  31.2 0.7 fusion.36
  31.9 0.9 %fusion.46 = f32[256,768]{1,0:T(8,128)S(1)} fusion(f32[256,256]{1,0:T(8,128)S(1)} %fusion.17, f32[768,256]{1,0:T(8,128)S(1)} %copy-done.5), kind=kOutput, calls=%fused_computation.107 | convolution fusion | flops 301989888 | bytes 1835008 | tf_op jit(solution)/shard_map/dot_general | solution.py:31
  32.8 1.3 %fusion.47 = f32[768,768]{1,0:T(8,128)S(1)} fusion(f32[256,768]{1,0:T(8,128)S(1)} %fusion.46, f32[256,768]{1,0:T(8,128)S(1)} %copy-done.7), kind=kOutput, calls=%fused_computation.108 | convolution fusion | flops 905969664 | bytes 3932160 | tf_op jit(solution)/shard_map/dot_general | solution.py:31
  34.1 0.1 slice.407
  34.2 0.2 add_negate_fusion
  34.5 0.0 collective-permute-done
  34.5 0.0 collective-permute-done.1
  34.5 0.0 copy-start.2
  34.5 0.2 fusion.9
  34.7 1.4 %copy-done.2 = f32[768,768]{1,0:T(8,128)S(1)} copy-done((f32[768,768]{1,0:T(8,128)S(1)}, f32[768,768]{1,0:T(8,128)}, u32[]{:S(2)}) %copy-start.2) | copy-done | bytes 2359320
  36.2 4.0 %fusion.44 = f32[512,768]{1,0:T(8,128)S(1)} fusion(f32[768,512]{1,0:T(8,128)S(1)} %fusion.9, f32[768,768]{1,0:T(8,128)S(1)} %copy-done.2), kind=kOutput, calls=%fused_computation.105 | convolution fusion | flops 1811939328 | bytes 5505024 | tf_op jit(solution)/shard_map/dot_general | solution.py:31
  40.2 2.5 %fusion.45 = f32[768,768]{1,0:T(8,128)S(1)} fusion(f32[512,768]{1,0:T(8,128)S(1)} %fusion.44, f32[512,768]{1,0:T(8,128)S(1)} %copy-done.3), kind=kOutput, calls=%fused_computation.106 | convolution fusion | flops 1811939328 | bytes 5505024 | tf_op jit(solution)/shard_map/dot_general | solution.py:31
  42.7 0.1 slice.404
  42.8 2.4 %add_multiply_fusion.1 = (f32[385,383]{1,0:T(8,128)S(1)}, f32[385,383]{1,0:T(8,128)S(1)}, f32[385,383]{1,0:T(8,128)S(1)}, f32[385,383]{1,0:T(8,128)S(1)}, f32[385,383]{1,0:T(8,128)S(1)}, /*index=5*/f32[385,383]{1,0:T(8,128)S(1)}) fusion(f32[385,768]{1,0:T(8,128)S(1)} %add_negate_fusion, f32[768,768]{1,0:T(8,128)S(1)} %fusion.45, f32[768,768]{1,0:T(8,128)S(1)} %fusion.47, ...), kind=kLoop, calls=%fused_computation.36 | loop fusion | flops 2359280 | bytes 8841172 | tf_op jit(solution)/shard_map/mul | solution.py:136
  45.2 0.0 copy-start.1
  45.2 1.2 %add_multiply_fusion = (f32[385,385]{1,0:T(8,128)S(1)}, f32[385,385]{1,0:T(8,128)S(1)}) fusion(f32[385,768]{1,0:T(8,128)S(1)} %add_negate_fusion, f32[385,383]{1,0:T(8,128)S(1)} %get-tuple-element.16, f32[768,768]{1,0:T(8,128)S(1)} %fusion.45, f32[385,383]{1,0:T(8,128)S(1)} %get-tuple-element.17, f32[768,768]{1,0:T(8,128)S(1)} %fusion.47, ...), kind=kLoop, calls=%fused_computation.28 | loop fusion | flops 2371600 | bytes 7676932 | tf_op jit(solution)/shard_map/mul | solution.py:136
  46.4 0.7 copy-done.1
  47.1 4.0 %fusion = f32[770,1024]{1,0:T(8,128)S(1)} fusion(f32[768,1024]{1,0:T(8,128)S(1)} %copy-done.1, f32[385,383]{1,0:T(8,128)S(1)} %get-tuple-element.11, f32[385,385]{1,0:T(8,128)S(1)} %get-tuple-element.9, f32[385,383]{1,0:T(8,128)S(1)} %get-tuple-element.10, f32[385,385]{1,0:T(8,128)S(1)} %get-tuple-element.8), kind=kOutput, calls=%fused_computation | convolution fusion | flops 3635089920 | bytes 8665088 | tf_op jit(solution)/shard_map/dot_general | solution.py:31
  51.1 0.0 copy-start.4
  51.1 0.2 fusion.40
  51.3 1.0 %copy-done.4 = f32[512,385]{1,0:T(8,128)S(1)} copy-done((f32[512,385]{1,0:T(8,128)S(1)}, f32[512,385]{1,0:T(8,128)}, u32[]{:S(2)}) %copy-start.4) | copy-done | bytes 788504
  52.3 1.0 %fusion.12 = f32[512,512]{0,1:T(8,128)S(1)} fusion(f32[512,385]{1,0:T(8,128)S(1)} %copy-done.4, f32[770,1024]{1,0:T(8,128)S(1)} %fusion), kind=kOutput, calls=%fused_computation.23 | convolution fusion | flops 605749760 | bytes 3702784 | tf_op jit(solution)/shard_map/dot_general | solution.py:31
  53.3 0.1 copy-done.6
  53.4 1.1 %convolution_add_fusion = f32[512,512]{0,1:T(8,128)S(1)} fusion(f32[512,512]{0,1:T(8,128)S(1)} %fusion.12, f32[512,383]{1,0:T(8,128)S(1)} %copy-done.6, f32[385,512]{1,0:T(8,128)S(1)} %get-tuple-element.13, f32[385,512]{1,0:T(8,128)S(1)} %get-tuple-element.12), kind=kOutput, calls=%fused_computation.11 | convolution fusion | flops 602865152 | bytes 4456448 | tf_op jit(solution)/shard_map/dot_general | solution.py:31
  54.5 24.1 %all_to_all.9 = f32[16,32,512]{2,1,0:T(8,128)S(1)} all-to-all(f32[16,32,512]{2,1,0:T(8,128)S(1)} %bitcast.52), channel_id=1, replica_groups=mesh['tile'=8,'orient'=16] {'orient'}, dimensions={0} | all-to-all | bytes 2097152 | tf_op jit(solution)/shard_map/all_to_all | solution.py:155
  78.6 0.7 maximum_bitcast_fusion.1
  79.3 0.7 maximum_bitcast_fusion
  80.0 0.8 fusion.18
  (26 shorter events, 0.3 us)
Async XLA Ops:
  0.6 8.5 %copy-start = (f32[512,512]{1,0:T(8,128)S(1)}, f32[512,512]{1,0:T(8,128)}, u32[]{:S(2)}) copy-start(f32[512,512]{1,0:T(8,128)} %param.10) | copy-start | bytes 3145732
  0.6 10.7 %copy-start.8 = (f32[1,32,256]{2,1,0:T(8,128)S(1)}, f32[1,32,256]{2,1,0:T(8,128)}, u32[]{:S(2)}) copy-start(f32[1,32,256]{2,1,0:T(8,128)} %param.11) | copy-start | bytes 98308
  0.7 25.3 %copy-start.9 = (f32[4]{0:T(128)S(1)}, f32[4]{0:T(128)}, u32[]{:S(2)}) copy-start(f32[4]{0:T(128)} %param.12) | copy-start | bytes 52
  2.6 29.3 %copy-start.5 = (f32[768,256]{1,0:T(8,128)S(1)}, f32[768,256]{1,0:T(8,128)}, u32[]{:S(2)}) copy-start(f32[768,256]{1,0:T(8,128)} %constant.69.clone) | copy-start | bytes 2359300
  2.6 31.9 %collective-permute-start = (f32[128,512]{1,0:T(8,128)}, f32[128,512]{1,0:T(8,128)S(1)}, u32[]{:S(2)}, u32[]{:S(2)}) collective-permute-start(f32[128,512]{1,0:T(8,128)} %get-tuple-element.18), channel_id=1, source_target_pairs={{0,16},{16,32},{32,48},{48,64},{64,80},{80,96},{96,112},{1,17},{17... | collective-permute-start | bytes 786440 | tf_op jit(solution)/shard_map/ppermute | solution.py:24
  7.2 27.2 %collective-permute-start.1 = (f32[128,512]{1,0:T(8,128)}, f32[128,512]{1,0:T(8,128)S(1)}, u32[]{:S(2)}, u32[]{:S(2)}) collective-permute-start(f32[128,512]{1,0:T(8,128)} %get-tuple-element.19), channel_id=1, source_target_pairs={{16,0},{32,16},{48,32},{64,48},{80,64},{96,80},{112,96},{17,1},{33... | collective-permute-start | bytes 786440 | tf_op jit(solution)/shard_map/ppermute | solution.py:25
  25.2 7.6 %copy-start.7 = (f32[256,768]{1,0:T(8,128)S(1)}, f32[256,768]{1,0:T(8,128)}, u32[]{:S(2)}) copy-start(f32[256,768]{1,0:T(8,128)} %constant.71.clone) | copy-start | bytes 2359300
  34.5 1.7 %copy-start.2 = (f32[768,768]{1,0:T(8,128)S(1)}, f32[768,768]{1,0:T(8,128)}, u32[]{:S(2)}) copy-start(f32[768,768]{1,0:T(8,128)} %constant.68.clone) | copy-start | bytes 7077892
  36.2 4.0 %copy-start.3 = (f32[512,768]{1,0:T(8,128)S(1)}, f32[512,768]{1,0:T(8,128)}, u32[]{:S(2)}) copy-start(f32[512,768]{1,0:T(8,128)} %constant.70.clone) | copy-start | bytes 4718596
  45.2 1.9 %copy-start.1 = (f32[768,1024]{1,0:T(8,128)S(1)}, f32[768,1024]{1,0:T(8,128)}, u32[]{:S(2)}) copy-start(f32[768,1024]{1,0:T(8,128)} %constant.72.clone) | copy-start | bytes 9437188
  51.1 1.2 %copy-start.4 = (f32[512,385]{1,0:T(8,128)S(1)}, f32[512,385]{1,0:T(8,128)}, u32[]{:S(2)}) copy-start(f32[512,385]{1,0:T(8,128)} %constant.88) | copy-start | bytes 2365444
  52.3 1.1 %copy-start.6 = (f32[512,383]{1,0:T(8,128)S(1)}, f32[512,383]{1,0:T(8,128)}, u32[]{:S(2)}) copy-start(f32[512,383]{1,0:T(8,128)} %constant.89) | copy-start | bytes 2353156

commit v10 on v8

--- a/solution.py
+++ b/solution.py
@@ -144,16 +144,21 @@
     pieces = lax.all_to_all(scores, "orient", 0, 0, tiled=True).reshape(
         orient_count, share_rows, tile_width
     )
-    top = pieces[0]
-    second = jnp.full_like(top, -jnp.inf)
-    total = pieces[0]
-    squares = pieces[0] * pieces[0]
-    for k in range(1, orient_count):
-        value = pieces[k]
-        second = jnp.maximum(second, jnp.minimum(top, value))
-        top = jnp.maximum(top, value)
-        total = total + value
-        squares = squares + value * value
+    def merge(former, latter):
+        return (
+            jnp.maximum(former[0], latter[0]),
+            jnp.maximum(jnp.minimum(former[0], latter[0]), jnp.maximum(former[1], latter[1])),
+            former[2] + latter[2],
+            former[3] + latter[3],
+        )
+
+    lowest = jnp.float32(-jnp.inf)
+    top, second, total, squares = lax.reduce(
+        (pieces, jnp.full_like(pieces, lowest), pieces, pieces * pieces),
+        (lowest, lowest, jnp.float32(0.0), jnp.float32(0.0)),
+        merge,
+        (0,),
+    )
     mean_map = total / orient_count
     variance = squares / orient_count - mean_map * mean_map
     return (top, second, mean_map, variance)

time: 79.6 us -> 78.9 us (level)
    max x2 -> x0, other arithmetic: 1.44 us -> none  [the longest x1 0.73 us: per_device(): second = jnp.maximum(second, jnp.minimum(top, value))]
    another operation x0 -> x1, other arithmetic: none -> 0.92 us  [per_device(): lax.reduce((pieces, jnp.full_like(pieces, lowest), pieces, pieces * piece...]
where the time goes in v10:
time: 78.9 us; the launch traced here: 78.4 us
  blocking collectives  38 us (48%)
  matrix products  14.7 us (19%)
  other arithmetic  9.95 us (13%)
  starting transfers between devices  6.55 us (8%)
  local copies, waits for them, and re-layouts  5.55 us (7%)
  between operations  3.58 us (5%)
    all_to_all x1, blocking collectives, per_device(): lax.all_to_all(scores, 'orient', 0, 0, tiled=True)  24.1 us
    dot_general x7, matrix products, product(): jnp.dot(former, latter, precision=mode, preferred_element_type=jnp.float32)  14.7 us
    all_gather x1, blocking collectives, per_device(): everything = lax.all_gather(payload, 'tile')  13.9 us
    ppermute x1, starting transfers between devices, padded(): before = lax.ppermute(last, axis, up)  4.63 us
    mul x2, other arithmetic, multiply(): (spec_real * template_real + spec_imag * template_imag) * weight  3.63 us
    unnamed x20, local copies, waits for them, and re-layouts  3.25 us
    slice x1, local copies, waits for them, and re-layouts, padded(): last = lax.slice_in_dim(shard, length - width, length, axis=dim)  1.94 us
    ppermute x1, starting transfers between devices, padded(): after = lax.ppermute(initial, axis, down)  1.92 us
  transfers between devices with their start and end apart: 2, of which 0 were waited for; matrix products, arithmetic and copies ran while one was open for 9% of the time, Pallas kernels for 0%

profile of v10, /device:TPU:1, one launch (start us, length us, event | category | flops | bytes accessed | tf_op | source)
XLA Modules:
  0.0 78.4 jit_solution(10685035437256458193)
XLA Ops:
  0.6 0.0 copy-start
  0.6 0.0 copy-start.8
  0.7 0.0 copy-start.9
  0.7 1.9 %fusion.35 = (f32[128,512]{1,0:T(8,128)}, f32[128,512]{1,0:T(8,128)}) fusion(f32[512,512]{1,0:T(8,128)} %param.10), kind=kLoop, calls=%fused_computation.76 | loop fusion | bytes 1048576 | tf_op jit(solution)/shard_map/slice | solution.py:22
  2.6 0.0 copy-start.5
  2.6 4.6 %collective-permute-start = (f32[128,512]{1,0:T(8,128)}, f32[128,512]{1,0:T(8,128)S(1)}, u32[]{:S(2)}, u32[]{:S(2)}) collective-permute-start(f32[128,512]{1,0:T(8,128)} %get-tuple-element.26), channel_id=1, source_target_pairs={{0,16},{16,32},{32,48},{48,64},{64,80},{80,96},{96,112},{1,17},{17... | collective-permute-start | bytes 786440 | tf_op jit(solution)/shard_map/ppermute | solution.py:24
  7.2 1.9 %collective-permute-start.1 = (f32[128,512]{1,0:T(8,128)}, f32[128,512]{1,0:T(8,128)S(1)}, u32[]{:S(2)}, u32[]{:S(2)}) collective-permute-start(f32[128,512]{1,0:T(8,128)} %get-tuple-element.27), channel_id=1, source_target_pairs={{16,0},{32,16},{48,32},{64,48},{80,64},{96,80},{112,96},{17,1},{33... | collective-permute-start | bytes 786440 | tf_op jit(solution)/shard_map/ppermute | solution.py:25
  9.2 0.0 copy-done
  9.2 0.9 %fusion.33 = (f32[]{:T(128)}, f32[]{:T(128)}) fusion(f32[512,512]{1,0:T(8,128)S(1)} %copy-done), kind=kLoop, calls=%fused_computation.74 | loop fusion | flops 786430 | bytes 1048584 | tf_op jit(solution)/shard_map/reduce_sum | solution.py:68
  10.1 1.3 %compare_select_fusion.2 = f32[1,256]{1,0:T(1,128)S(1)} fusion(f32[]{:T(128)} %get-tuple-element.13, f32[]{:T(128)} %get-tuple-element.12), kind=kLoop, calls=%fused_computation.63 | loop fusion | flops 512 | bytes 1032 | tf_op jit(solution)/shard_map/jit(_where)/select_n | solution.py:68
  11.4 0.0 copy-done.8
  11.4 0.0 copy-start.7
  11.4 13.9 %all-gather.1 = f32[8,33,256]{2,1,0:T(8,128)S(1)} all-gather(f32[1,33,256]{2,1,0:T(8,128)S(1)} %maximum_bitcast_fusion), channel_id=2, replica_groups=mesh['tile'=8,'orient'=16] {'tile'}, dimensions={0}, use_global_device_ids=true | all-gather | bytes 304128 | tf_op jit(solution)/shard_map/all_gather | solution.py:70
  25.3 0.7 slice_reduce_fusion
  26.6 0.0 copy-done.9
  26.6 0.6 fusion.31
  28.6 0.7 multiply_reduce_fusion.2
  30.0 0.0 copy-done.5
  30.1 0.9 %fusion.38 = f32[256,768]{1,0:T(8,128)S(1)} fusion(f32[256,256]{1,0:T(8,128)S(1)} %bitcast.25, f32[768,256]{1,0:T(8,128)S(1)} %copy-done.5), kind=kOutput, calls=%fused_computation.79 | convolution fusion | flops 301989888 | bytes 1835008 | tf_op jit(solution)/shard_map/dot_general | solution.py:31
  30.9 0.0 copy-done.7
  30.9 1.3 %fusion.39 = f32[768,768]{1,0:T(8,128)S(1)} fusion(f32[256,768]{1,0:T(8,128)S(1)} %fusion.38, f32[256,768]{1,0:T(8,128)S(1)} %copy-done.7), kind=kOutput, calls=%fused_computation.80 | convolution fusion | flops 905969664 | bytes 3932160 | tf_op jit(solution)/shard_map/dot_general | solution.py:31
  32.3 0.1 slice.131
  32.3 0.2 add_negate_fusion
  32.6 0.0 collective-permute-done
  32.6 0.0 collective-permute-done.1
  32.6 0.0 copy-start.2
  32.6 0.2 fusion.9
  32.8 1.4 %copy-done.2 = f32[768,768]{1,0:T(8,128)S(1)} copy-done((f32[768,768]{1,0:T(8,128)S(1)}, f32[768,768]{1,0:T(8,128)}, u32[]{:S(2)}) %copy-start.2) | copy-done | bytes 2359320
  34.3 0.0 copy-start.3
  34.3 4.0 %fusion.36 = f32[512,768]{1,0:T(8,128)S(1)} fusion(f32[768,512]{1,0:T(8,128)S(1)} %fusion.9, f32[768,768]{1,0:T(8,128)S(1)} %copy-done.2), kind=kOutput, calls=%fused_computation.77 | convolution fusion | flops 1811939328 | bytes 5505024 | tf_op jit(solution)/shard_map/dot_general | solution.py:31
  38.3 0.0 copy-done.3
  38.3 2.5 %fusion.37 = f32[768,768]{1,0:T(8,128)S(1)} fusion(f32[512,768]{1,0:T(8,128)S(1)} %fusion.36, f32[512,768]{1,0:T(8,128)S(1)} %copy-done.3), kind=kOutput, calls=%fused_computation.78 | convolution fusion | flops 1811939328 | bytes 5505024 | tf_op jit(solution)/shard_map/dot_general | solution.py:31
  40.8 0.1 slice.128
  40.9 2.4 %add_multiply_fusion.1 = (f32[385,383]{1,0:T(8,128)S(1)}, f32[385,383]{1,0:T(8,128)S(1)}, f32[385,383]{1,0:T(8,128)S(1)}, f32[385,383]{1,0:T(8,128)S(1)}, f32[385,383]{1,0:T(8,128)S(1)}, /*index=5*/f32[385,383]{1,0:T(8,128)S(1)}) fusion(f32[385,768]{1,0:T(8,128)S(1)} %add_negate_fusion, f32[768,768]{1,0:T(8,128)S(1)} %fusion.37, f32[768,768]{1,0:T(8,128)S(1)} %fusion.39, ...), kind=kLoop, calls=%fused_computation.37 | loop fusion | flops 2359280 | bytes 8841172 | tf_op jit(solution)/shard_map/mul | solution.py:125
  43.3 0.0 copy-start.1
  43.3 1.2 %add_multiply_fusion = (f32[385,385]{1,0:T(8,128)S(1)}, f32[385,385]{1,0:T(8,128)S(1)}) fusion(f32[385,768]{1,0:T(8,128)S(1)} %add_negate_fusion, f32[385,383]{1,0:T(8,128)S(1)} %get-tuple-element.24, f32[768,768]{1,0:T(8,128)S(1)} %fusion.37, f32[385,383]{1,0:T(8,128)S(1)} %get-tuple-element.25, f32[768,768]{1,0:T(8,128)S(1)} %fusion.39, ...), kind=kLoop, calls=%fused_computation.29 | loop fusion | flops 2371600 | bytes 7676932 | tf_op jit(solution)/shard_map/mul | solution.py:125
  44.5 0.7 copy-done.1
  45.2 4.0 %fusion = f32[770,1024]{1,0:T(8,128)S(1)} fusion(f32[768,1024]{1,0:T(8,128)S(1)} %copy-done.1, f32[385,383]{1,0:T(8,128)S(1)} %get-tuple-element.19, f32[385,385]{1,0:T(8,128)S(1)} %get-tuple-element.17, f32[385,383]{1,0:T(8,128)S(1)} %get-tuple-element.18, f32[385,385]{1,0:T(8,128)S(1)} %get-tuple-element.16), kind=kOutput, calls=%fused_computation | convolution fusion | flops 3635089920 | bytes 8665088 | tf_op jit(solution)/shard_map/dot_general | solution.py:31
  49.2 0.0 copy-start.4
  49.2 0.2 fusion.34
  49.4 1.0 %copy-done.4 = f32[512,385]{1,0:T(8,128)S(1)} copy-done((f32[512,385]{1,0:T(8,128)S(1)}, f32[512,385]{1,0:T(8,128)}, u32[]{:S(2)}) %copy-start.4) | copy-done | bytes 788504
  50.4 0.0 copy-start.6
  50.4 1.0 %fusion.12 = f32[512,512]{0,1:T(8,128)S(1)} fusion(f32[512,385]{1,0:T(8,128)S(1)} %copy-done.4, f32[770,1024]{1,0:T(8,128)S(1)} %fusion), kind=kOutput, calls=%fused_computation.24 | convolution fusion | flops 605749760 | bytes 3702784 | tf_op jit(solution)/shard_map/dot_general | solution.py:31
  51.5 0.1 copy-done.6
  51.5 1.1 %convolution_add_fusion = f32[512,512]{0,1:T(8,128)S(1)} fusion(f32[512,512]{0,1:T(8,128)S(1)} %fusion.12, f32[512,383]{1,0:T(8,128)S(1)} %copy-done.6, f32[385,512]{1,0:T(8,128)S(1)} %get-tuple-element.21, f32[385,512]{1,0:T(8,128)S(1)} %get-tuple-element.20), kind=kOutput, calls=%fused_computation.12 | convolution fusion | flops 602865152 | bytes 4456448 | tf_op jit(solution)/shard_map/dot_general | solution.py:31
  52.6 24.1 %all_to_all.9 = f32[16,32,512]{2,1,0:T(8,128)S(1)} all-to-all(f32[16,32,512]{2,1,0:T(8,128)S(1)} %bitcast.24), channel_id=1, replica_groups=mesh['tile'=8,'orient'=16] {'orient'}, dimensions={0} | all-to-all | bytes 2097152 | tf_op jit(solution)/shard_map/all_to_all | solution.py:144
  76.8 0.9 %multiply_reduce_fusion = (f32[32,512]{1,0:T(8,128)}, f32[32,512]{1,0:T(8,128)}, f32[32,512]{1,0:T(8,128)S(1)}, f32[32,512]{1,0:T(8,128)S(1)}) fusion(f32[16,32,512]{2,1,0:T(8,128)S(1)} %all_to_all.9), kind=kLoop, calls=%fused_computation.11 | loop fusion | flops 1736704 | bytes 1310720 | tf_op jit(solution)/shard_map/reduce | solution.py:156
  77.7 0.7 multiply_subtract_fusion
  (9 shorter events, 0.2 us)
Async XLA Ops:
  0.6 8.5 %copy-start = (f32[512,512]{1,0:T(8,128)S(1)}, f32[512,512]{1,0:T(8,128)}, u32[]{:S(2)}) copy-start(f32[512,512]{1,0:T(8,128)} %param.10) | copy-start | bytes 3145732
  0.6 10.7 %copy-start.8 = (f32[1,32,256]{2,1,0:T(8,128)S(1)}, f32[1,32,256]{2,1,0:T(8,128)}, u32[]{:S(2)}) copy-start(f32[1,32,256]{2,1,0:T(8,128)} %param.11) | copy-start | bytes 98308
  0.7 25.9 %copy-start.9 = (f32[4]{0:T(128)S(1)}, f32[4]{0:T(128)}, u32[]{:S(2)}) copy-start(f32[4]{0:T(128)} %param.12) | copy-start | bytes 52
  2.6 27.4 %copy-start.5 = (f32[768,256]{1,0:T(8,128)S(1)}, f32[768,256]{1,0:T(8,128)}, u32[]{:S(2)}) copy-start(f32[768,256]{1,0:T(8,128)} %constant.71.clone) | copy-start | bytes 2359300
  2.6 30.0 %collective-permute-start = (f32[128,512]{1,0:T(8,128)}, f32[128,512]{1,0:T(8,128)S(1)}, u32[]{:S(2)}, u32[]{:S(2)}) collective-permute-start(f32[128,512]{1,0:T(8,128)} %get-tuple-element.26), channel_id=1, source_target_pairs={{0,16},{16,32},{32,48},{48,64},{64,80},{80,96},{96,112},{1,17},{17... | collective-permute-start | bytes 786440 | tf_op jit(solution)/shard_map/ppermute | solution.py:24
  7.2 25.4 %collective-permute-start.1 = (f32[128,512]{1,0:T(8,128)}, f32[128,512]{1,0:T(8,128)S(1)}, u32[]{:S(2)}, u32[]{:S(2)}) collective-permute-start(f32[128,512]{1,0:T(8,128)} %get-tuple-element.27), channel_id=1, source_target_pairs={{16,0},{32,16},{48,32},{64,48},{80,64},{96,80},{112,96},{17,1},{33... | collective-permute-start | bytes 786440 | tf_op jit(solution)/shard_map/ppermute | solution.py:25
  11.4 19.5 %copy-start.7 = (f32[256,768]{1,0:T(8,128)S(1)}, f32[256,768]{1,0:T(8,128)}, u32[]{:S(2)}) copy-start(f32[256,768]{1,0:T(8,128)} %constant.73.clone) | copy-start | bytes 2359300
  32.6 1.7 %copy-start.2 = (f32[768,768]{1,0:T(8,128)S(1)}, f32[768,768]{1,0:T(8,128)}, u32[]{:S(2)}) copy-start(f32[768,768]{1,0:T(8,128)} %constant.70.clone) | copy-start | bytes 7077892
  34.3 4.0 %copy-start.3 = (f32[512,768]{1,0:T(8,128)S(1)}, f32[512,768]{1,0:T(8,128)}, u32[]{:S(2)}) copy-start(f32[512,768]{1,0:T(8,128)} %constant.72.clone) | copy-start | bytes 4718596
  43.3 1.9 %copy-start.1 = (f32[768,1024]{1,0:T(8,128)S(1)}, f32[768,1024]{1,0:T(8,128)}, u32[]{:S(2)}) copy-start(f32[768,1024]{1,0:T(8,128)} %constant.74.clone) | copy-start | bytes 9437188
  49.2 1.2 %copy-start.4 = (f32[512,385]{1,0:T(8,128)S(1)}, f32[512,385]{1,0:T(8,128)}, u32[]{:S(2)}) copy-start(f32[512,385]{1,0:T(8,128)} %constant.90) | copy-start | bytes 2365444
  50.4 1.1 %copy-start.6 = (f32[512,383]{1,0:T(8,128)S(1)}, f32[512,383]{1,0:T(8,128)}, u32[]{:S(2)}) copy-start(f32[512,383]{1,0:T(8,128)} %constant.91) | copy-start | bytes 2353156

commit v11 on v10

--- a/solution.py
+++ b/solution.py
@@ -83,8 +83,17 @@
     extent = gathered.shape[0]
     left, left_t, right_w, right_t, back, final = tables(tile_width, margin, extent)
 
-    centred = gathered - jnp.mean(gathered)
-    root_mean = jnp.sqrt(jnp.mean(centred * centred) + 1e-06)
+    tpl_count = float(gathered.shape[0] * gathered.shape[1])
+    ones = jnp.ones((gathered.shape[1], gathered.shape[1]), jnp.float32)
+
+    def lane_total(rows):
+        return jnp.dot(
+            jnp.sum(rows, axis=0, keepdims=True), ones,
+            precision=lax.Precision.HIGHEST, preferred_element_type=jnp.float32,
+        )
+
+    centred = gathered - lane_total(gathered) / tpl_count
+    root_mean = jnp.sqrt(lane_total(centred * centred) / tpl_count + 1e-06)
     normed = centred / (root_mean * TPL)
 
     edge_rows, edge_cols = ((1, 1), (0, 0)), ((0, 0), (1, 1))

time: 78.9 us -> 76.6 us (0.971)
  between operations: 3.58 us -> 2.31 us
  other arithmetic: 9.95 us -> 8.79 us
    reduce_sum x2, other arithmetic: 1.33 us -> 0.14 us  [lane_total(): jnp.sum(rows, axis=0, keepdims=True)]
  transfers between devices with their start and end apart: 2 -> 2, of which waited for: 0 -> 0; matrix products, arithmetic and copies ran while one was open for 9% -> 8% of each run, Pallas kernels for 0% -> 0%
where the time goes in v11:
time: 76.6 us; the launch traced here: 76.1 us
  blocking collectives  37.8 us (49%)
  matrix products  15 us (20%)
  other arithmetic  8.79 us (11%)
  starting transfers between devices  6.55 us (9%)
  local copies, waits for them, and re-layouts  5.54 us (7%)
  between operations  2.31 us (3%)
    all_to_all x1, blocking collectives, per_device(): lax.all_to_all(scores, 'orient', 0, 0, tiled=True)  24.1 us
    dot_general x7, matrix products, product(): jnp.dot(former, latter, precision=mode, preferred_element_type=jnp.float32)  14.7 us
    all_gather x1, blocking collectives, per_device(): everything = lax.all_gather(payload, 'tile')  13.7 us
    ppermute x1, starting transfers between devices, padded(): before = lax.ppermute(last, axis, up)  4.63 us
    mul x2, other arithmetic, multiply(): (spec_real * template_real + spec_imag * template_imag) * weight  3.64 us
    unnamed x20, local copies, waits for them, and re-layouts  3.25 us
    slice x1, local copies, waits for them, and re-layouts, padded(): last = lax.slice_in_dim(shard, length - width, length, axis=dim)  1.94 us
    ppermute x1, starting transfers between devices, padded(): after = lax.ppermute(initial, axis, down)  1.92 us
  transfers between devices with their start and end apart: 2, of which 0 were waited for; matrix products, arithmetic and copies ran while one was open for 8% of the time, Pallas kernels for 0%

profile of v11, /device:TPU:1, one launch (start us, length us, event | category | flops | bytes accessed | tf_op | source)
XLA Modules:
  0.0 76.1 jit_solution(5125167061180338456)
XLA Ops:
  0.6 0.0 copy-start
  0.6 0.0 copy-start.8
  0.7 0.0 copy-start.9
  0.7 1.9 %fusion.41 = (f32[128,512]{1,0:T(8,128)}, f32[128,512]{1,0:T(8,128)}) fusion(f32[512,512]{1,0:T(8,128)} %param.10), kind=kLoop, calls=%fused_computation.84 | loop fusion | bytes 1048576 | tf_op jit(solution)/shard_map/slice | solution.py:22
  2.6 0.0 copy-start.5
  2.6 4.6 %collective-permute-start = (f32[128,512]{1,0:T(8,128)}, f32[128,512]{1,0:T(8,128)S(1)}, u32[]{:S(2)}, u32[]{:S(2)}) collective-permute-start(f32[128,512]{1,0:T(8,128)} %get-tuple-element.26), channel_id=1, source_target_pairs={{0,16},{16,32},{32,48},{48,64},{64,80},{80,96},{96,112},{1,17},{17... | collective-permute-start | bytes 786440 | tf_op jit(solution)/shard_map/ppermute | solution.py:24
  7.2 1.9 %collective-permute-start.1 = (f32[128,512]{1,0:T(8,128)}, f32[128,512]{1,0:T(8,128)S(1)}, u32[]{:S(2)}, u32[]{:S(2)}) collective-permute-start(f32[128,512]{1,0:T(8,128)} %get-tuple-element.27), channel_id=1, source_target_pairs={{16,0},{32,16},{48,32},{64,48},{80,64},{96,80},{112,96},{17,1},{33... | collective-permute-start | bytes 786440 | tf_op jit(solution)/shard_map/ppermute | solution.py:25
  9.2 0.0 copy-done
  9.2 0.9 %fusion.39 = (f32[]{:T(128)}, f32[]{:T(128)}) fusion(f32[512,512]{1,0:T(8,128)S(1)} %copy-done), kind=kLoop, calls=%fused_computation.82 | loop fusion | flops 786430 | bytes 1048584 | tf_op jit(solution)/shard_map/reduce_sum | solution.py:68
  10.1 1.3 %compare_select_fusion.2 = f32[1,256]{1,0:T(1,128)S(1)} fusion(f32[]{:T(128)} %get-tuple-element.13, f32[]{:T(128)} %get-tuple-element.12), kind=kLoop, calls=%fused_computation.66 | loop fusion | flops 512 | bytes 1032 | tf_op jit(solution)/shard_map/jit(_where)/select_n | solution.py:68
  11.4 0.0 copy-done.8
  11.4 13.7 %all-gather.1 = f32[8,33,256]{2,1,0:T(8,128)S(1)} all-gather(f32[1,33,256]{2,1,0:T(8,128)S(1)} %maximum_bitcast_fusion), channel_id=2, replica_groups=mesh['tile'=8,'orient'=16] {'tile'}, dimensions={0}, use_global_device_ids=true | all-gather | bytes 304128 | tf_op jit(solution)/shard_map/all_gather | solution.py:70
  25.2 0.0 copy-start.7
  25.9 0.0 copy-done.9
  25.9 0.6 fusion.35
  27.3 0.2 fusion.20
  27.5 0.1 multiply_reduce_fusion.2
  27.6 0.2 fusion.18
  27.7 0.1 fusion.17
  27.8 0.0 copy-done.5
  27.8 0.9 %fusion.44 = f32[256,768]{1,0:T(8,128)S(1)} fusion(f32[256,256]{1,0:T(8,128)S(1)} %fusion.17, f32[768,256]{1,0:T(8,128)S(1)} %copy-done.5), kind=kOutput, calls=%fused_computation.87 | convolution fusion | flops 301989888 | bytes 1835008 | tf_op jit(solution)/shard_map/dot_general | solution.py:31
  28.7 0.0 copy-done.7
  28.7 1.3 %fusion.45 = f32[768,768]{1,0:T(8,128)S(1)} fusion(f32[256,768]{1,0:T(8,128)S(1)} %fusion.44, f32[256,768]{1,0:T(8,128)S(1)} %copy-done.7), kind=kOutput, calls=%fused_computation.88 | convolution fusion | flops 905969664 | bytes 3932160 | tf_op jit(solution)/shard_map/dot_general | solution.py:31
  30.0 0.1 slice.131
  30.1 0.2 add_negate_fusion
  30.3 0.0 collective-permute-done
  30.4 0.0 collective-permute-done.1
  30.4 0.0 copy-start.2
  30.4 0.2 fusion.9
  30.6 1.4 %copy-done.2 = f32[768,768]{1,0:T(8,128)S(1)} copy-done((f32[768,768]{1,0:T(8,128)S(1)}, f32[768,768]{1,0:T(8,128)}, u32[]{:S(2)}) %copy-start.2) | copy-done | bytes 2359320
  32.0 0.0 copy-start.3
  32.0 4.0 %fusion.42 = f32[512,768]{1,0:T(8,128)S(1)} fusion(f32[768,512]{1,0:T(8,128)S(1)} %fusion.9, f32[768,768]{1,0:T(8,128)S(1)} %copy-done.2), kind=kOutput, calls=%fused_computation.85 | convolution fusion | flops 1811939328 | bytes 5505024 | tf_op jit(solution)/shard_map/dot_general | solution.py:31
  36.1 0.0 copy-done.3
  36.1 2.5 %fusion.43 = f32[768,768]{1,0:T(8,128)S(1)} fusion(f32[512,768]{1,0:T(8,128)S(1)} %fusion.42, f32[512,768]{1,0:T(8,128)S(1)} %copy-done.3), kind=kOutput, calls=%fused_computation.86 | convolution fusion | flops 1811939328 | bytes 5505024 | tf_op jit(solution)/shard_map/dot_general | solution.py:31
  38.5 0.1 slice.128
  38.6 2.4 %add_multiply_fusion.1 = (f32[385,383]{1,0:T(8,128)S(1)}, f32[385,383]{1,0:T(8,128)S(1)}, f32[385,383]{1,0:T(8,128)S(1)}, f32[385,383]{1,0:T(8,128)S(1)}, f32[385,383]{1,0:T(8,128)S(1)}, /*index=5*/f32[385,383]{1,0:T(8,128)S(1)}) fusion(f32[385,768]{1,0:T(8,128)S(1)} %add_negate_fusion, f32[768,768]{1,0:T(8,128)S(1)} %fusion.43, f32[768,768]{1,0:T(8,128)S(1)} %fusion.45, ...), kind=kLoop, calls=%fused_computation.37 | loop fusion | flops 2359280 | bytes 8841172 | tf_op jit(solution)/shard_map/mul | solution.py:134
  41.1 0.0 copy-start.1
  41.1 1.2 %add_multiply_fusion = (f32[385,385]{1,0:T(8,128)S(1)}, f32[385,385]{1,0:T(8,128)S(1)}) fusion(f32[385,768]{1,0:T(8,128)S(1)} %add_negate_fusion, f32[385,383]{1,0:T(8,128)S(1)} %get-tuple-element.24, f32[768,768]{1,0:T(8,128)S(1)} %fusion.43, f32[385,383]{1,0:T(8,128)S(1)} %get-tuple-element.25, f32[768,768]{1,0:T(8,128)S(1)} %fusion.45, ...), kind=kLoop, calls=%fused_computation.29 | loop fusion | flops 2371600 | bytes 7676932 | tf_op jit(solution)/shard_map/mul | solution.py:134
  42.3 0.7 copy-done.1
  42.9 4.0 %fusion = f32[770,1024]{1,0:T(8,128)S(1)} fusion(f32[768,1024]{1,0:T(8,128)S(1)} %copy-done.1, f32[385,383]{1,0:T(8,128)S(1)} %get-tuple-element.19, f32[385,385]{1,0:T(8,128)S(1)} %get-tuple-element.17, f32[385,383]{1,0:T(8,128)S(1)} %get-tuple-element.18, f32[385,385]{1,0:T(8,128)S(1)} %get-tuple-element.16), kind=kOutput, calls=%fused_computation | convolution fusion | flops 3635089920 | bytes 8665088 | tf_op jit(solution)/shard_map/dot_general | solution.py:31
  46.9 0.0 copy-start.4
  46.9 0.2 fusion.40
  47.1 1.0 %copy-done.4 = f32[512,385]{1,0:T(8,128)S(1)} copy-done((f32[512,385]{1,0:T(8,128)S(1)}, f32[512,385]{1,0:T(8,128)}, u32[]{:S(2)}) %copy-start.4) | copy-done | bytes 788504
  48.2 0.0 copy-start.6
  48.2 1.0 %fusion.12 = f32[512,512]{0,1:T(8,128)S(1)} fusion(f32[512,385]{1,0:T(8,128)S(1)} %copy-done.4, f32[770,1024]{1,0:T(8,128)S(1)} %fusion), kind=kOutput, calls=%fused_computation.24 | convolution fusion | flops 605749760 | bytes 3702784 | tf_op jit(solution)/shard_map/dot_general | solution.py:31
  49.2 0.1 copy-done.6
  49.3 1.1 %convolution_add_fusion = f32[512,512]{0,1:T(8,128)S(1)} fusion(f32[512,512]{0,1:T(8,128)S(1)} %fusion.12, f32[512,383]{1,0:T(8,128)S(1)} %copy-done.6, f32[385,512]{1,0:T(8,128)S(1)} %get-tuple-element.21, f32[385,512]{1,0:T(8,128)S(1)} %get-tuple-element.20), kind=kOutput, calls=%fused_computation.12 | convolution fusion | flops 602865152 | bytes 4456448 | tf_op jit(solution)/shard_map/dot_general | solution.py:31
  50.4 24.1 %all_to_all.9 = f32[16,32,512]{2,1,0:T(8,128)S(1)} all-to-all(f32[16,32,512]{2,1,0:T(8,128)S(1)} %bitcast.33), channel_id=1, replica_groups=mesh['tile'=8,'orient'=16] {'orient'}, dimensions={0} | all-to-all | bytes 2097152 | tf_op jit(solution)/shard_map/all_to_all | solution.py:153
  74.5 0.9 %multiply_reduce_fusion = (f32[32,512]{1,0:T(8,128)}, f32[32,512]{1,0:T(8,128)}, f32[32,512]{1,0:T(8,128)S(1)}, f32[32,512]{1,0:T(8,128)S(1)}) fusion(f32[16,32,512]{2,1,0:T(8,128)S(1)} %all_to_all.9), kind=kLoop, calls=%fused_computation.11 | loop fusion | flops 1736704 | bytes 1310720 | tf_op jit(solution)/shard_map/reduce | solution.py:165
  75.4 0.7 multiply_subtract_fusion
  (11 shorter events, 0.2 us)
Async XLA Ops:
  0.6 8.5 %copy-start = (f32[512,512]{1,0:T(8,128)S(1)}, f32[512,512]{1,0:T(8,128)}, u32[]{:S(2)}) copy-start(f32[512,512]{1,0:T(8,128)} %param.10) | copy-start | bytes 3145732
  0.6 10.7 %copy-start.8 = (f32[1,32,256]{2,1,0:T(8,128)S(1)}, f32[1,32,256]{2,1,0:T(8,128)}, u32[]{:S(2)}) copy-start(f32[1,32,256]{2,1,0:T(8,128)} %param.11) | copy-start | bytes 98308
  0.7 25.3 %copy-start.9 = (f32[4]{0:T(128)S(1)}, f32[4]{0:T(128)}, u32[]{:S(2)}) copy-start(f32[4]{0:T(128)} %param.12) | copy-start | bytes 52
  2.6 25.2 %copy-start.5 = (f32[768,256]{1,0:T(8,128)S(1)}, f32[768,256]{1,0:T(8,128)}, u32[]{:S(2)}) copy-start(f32[768,256]{1,0:T(8,128)} %constant.73.clone) | copy-start | bytes 2359300
  2.6 27.7 %collective-permute-start = (f32[128,512]{1,0:T(8,128)}, f32[128,512]{1,0:T(8,128)S(1)}, u32[]{:S(2)}, u32[]{:S(2)}) collective-permute-start(f32[128,512]{1,0:T(8,128)} %get-tuple-element.26), channel_id=1, source_target_pairs={{0,16},{16,32},{32,48},{48,64},{64,80},{80,96},{96,112},{1,17},{17... | collective-permute-start | bytes 786440 | tf_op jit(solution)/shard_map/ppermute | solution.py:24
  7.2 23.1 %collective-permute-start.1 = (f32[128,512]{1,0:T(8,128)}, f32[128,512]{1,0:T(8,128)S(1)}, u32[]{:S(2)}, u32[]{:S(2)}) collective-permute-start(f32[128,512]{1,0:T(8,128)} %get-tuple-element.27), channel_id=1, source_target_pairs={{16,0},{32,16},{48,32},{64,48},{80,64},{96,80},{112,96},{17,1},{33... | collective-permute-start | bytes 786440 | tf_op jit(solution)/shard_map/ppermute | solution.py:25
  25.2 3.5 %copy-start.7 = (f32[256,768]{1,0:T(8,128)S(1)}, f32[256,768]{1,0:T(8,128)}, u32[]{:S(2)}) copy-start(f32[256,768]{1,0:T(8,128)} %constant.75.clone) | copy-start | bytes 2359300
  30.4 1.7 %copy-start.2 = (f32[768,768]{1,0:T(8,128)S(1)}, f32[768,768]{1,0:T(8,128)}, u32[]{:S(2)}) copy-start(f32[768,768]{1,0:T(8,128)} %constant.72.clone) | copy-start | bytes 7077892
  32.0 4.0 %copy-start.3 = (f32[512,768]{1,0:T(8,128)S(1)}, f32[512,768]{1,0:T(8,128)}, u32[]{:S(2)}) copy-start(f32[512,768]{1,0:T(8,128)} %constant.74.clone) | copy-start | bytes 4718596
  41.1 1.9 %copy-start.1 = (f32[768,1024]{1,0:T(8,128)S(1)}, f32[768,1024]{1,0:T(8,128)}, u32[]{:S(2)}) copy-start(f32[768,1024]{1,0:T(8,128)} %constant.76.clone) | copy-start | bytes 9437188
  46.9 1.2 %copy-start.4 = (f32[512,385]{1,0:T(8,128)S(1)}, f32[512,385]{1,0:T(8,128)}, u32[]{:S(2)}) copy-start(f32[512,385]{1,0:T(8,128)} %constant.92) | copy-start | bytes 2365444
  48.2 1.1 %copy-start.6 = (f32[512,383]{1,0:T(8,128)S(1)}, f32[512,383]{1,0:T(8,128)}, u32[]{:S(2)}) copy-start(f32[512,383]{1,0:T(8,128)} %constant.93) | copy-start | bytes 2353156

commit v12 on v10

--- a/solution.py
+++ b/solution.py
@@ -63,17 +63,26 @@
     pixel_count = float(tile_rows * tile_width * tile_count)
     own_rows, tpl_width = templates.shape[1], templates.shape[2]
     halo = padded(micrograph, (("tile", 0),), margin)
-    lane = lax.broadcasted_iota(jnp.int32, (1, tpl_width), 1)
-    half = tpl_width // 2
-    stats_row = jnp.where(lane < half, jnp.sum(micrograph), jnp.sum(micrograph * micrograph))
-    payload = jnp.concatenate([templates[0], stats_row], axis=0)
+    def lane_fold(columns):
+        return sum(columns[i:i + tpl_width] for i in range(0, tile_width, tpl_width))[None, :]
+
+    sum_row = lane_fold(jnp.sum(micrograph, axis=0))
+    square_row = lane_fold(jnp.sum(micrograph * micrograph, axis=0))
+    payload = jnp.concatenate([templates[0], sum_row, square_row], axis=0)
     everything = lax.all_gather(payload, "tile")
-    totals = jnp.sum(everything[:, own_rows, :], axis=0)
     gathered = everything[:, :own_rows].reshape(tile_count * own_rows, tpl_width)
-    centre = totals[:half] / pixel_count
-    spread = jnp.sqrt(totals[half:] / pixel_count - centre * centre + 1e-05)
-    reps = tile_width // half
-    centre, spread = jnp.tile(centre, reps)[None, :], jnp.tile(spread, reps)[None, :]
+    ones = jnp.ones((tpl_width, tpl_width), jnp.float32)
+
+    def lane_total(rows):
+        return jnp.dot(
+            jnp.sum(rows, axis=0, keepdims=True), ones,
+            precision=lax.Precision.HIGHEST, preferred_element_type=jnp.float32,
+        )
+
+    centre = lane_total(everything[:, own_rows]) / pixel_count
+    spread = jnp.sqrt(lane_total(everything[:, own_rows + 1]) / pixel_count - centre * centre + 1e-05)
+    reps = tile_width // tpl_width
+    centre, spread = jnp.tile(centre, (1, reps)), jnp.tile(spread, (1, reps))
     tile_index = lax.axis_index("tile")
     row_ids = lax.broadcasted_iota(jnp.int32, (n, 1), 0)
     valid = ((row_ids >= margin) | (tile_index > 0)) & (
@@ -83,8 +92,9 @@
     extent = gathered.shape[0]
     left, left_t, right_w, right_t, back, final = tables(tile_width, margin, extent)
 
-    centred = gathered - jnp.mean(gathered)
-    root_mean = jnp.sqrt(jnp.mean(centred * centred) + 1e-06)
+    tpl_count = float(gathered.shape[0] * gathered.shape[1])
+    centred = gathered - lane_total(gathered) / tpl_count
+    root_mean = jnp.sqrt(lane_total(centred * centred) / tpl_count + 1e-06)
     normed = centred / (root_mean * TPL)
 
     edge_rows, edge_cols = ((1, 1), (0, 0)), ((0, 0), (1, 1))

time: 78.9 us -> 74.4 us (0.943)
  other arithmetic: 9.95 us -> 6.79 us
  between operations: 3.58 us -> 2.28 us
    reduce_sum x4, other arithmetic: 2.23 us -> 0.33 us  [the longest x3 0.17 us: lane_total(): jnp.sum(rows, axis=0, keepdims=True)]
    select_n x1 -> x0, other arithmetic: 1.29 us -> none  [per_device(): jnp.where(lane < half, jnp.sum(micrograph), jnp.sum(micrograph * microgra...]
    unnamed x20 -> x24, local copies, waits for them, and re-layouts: 3.25 us -> 3.26 us
  transfers between devices with their start and end apart: 2 -> 2, of which waited for: 0 -> 0; matrix products, arithmetic and copies ran while one was open for 9% -> 6% of each run, Pallas kernels for 0% -> 0%
where the time goes in v12:
time: 74.4 us; the launch traced here: 73.9 us
  blocking collectives  38.2 us (51%)
  matrix products  15.4 us (21%)
  other arithmetic  6.79 us (9%)
  starting transfers between devices  6.43 us (9%)
  local copies, waits for them, and re-layouts  4.77 us (6%)
  between operations  2.28 us (3%)
    all_to_all x1, blocking collectives, per_device(): lax.all_to_all(scores, 'orient', 0, 0, tiled=True)  24.1 us
    dot_general x7, matrix products, product(): jnp.dot(former, latter, precision=mode, preferred_element_type=jnp.float32)  14.7 us
    all_gather x1, blocking collectives, per_device(): everything = lax.all_gather(payload, 'tile')  14 us
    ppermute x1, starting transfers between devices, padded(): before = lax.ppermute(last, axis, up)  4.51 us
    mul x2, other arithmetic, multiply(): (spec_real * template_real + spec_imag * template_imag) * weight  3.64 us
    unnamed x24, local copies, waits for them, and re-layouts  3.26 us
    ppermute x1, starting transfers between devices, padded(): after = lax.ppermute(initial, axis, down)  1.92 us
  transfers between devices with their start and end apart: 2, of which 0 were waited for; matrix products, arithmetic and copies ran while one was open for 6% of the time, Pallas kernels for 0%

profile of v12, /device:TPU:1, one launch (start us, length us, event | category | flops | bytes accessed | tf_op | source)
XLA Modules:
  0.0 73.9 jit_solution(4030641473447322487)
XLA Ops:
  0.6 0.0 copy-start
  0.6 0.0 copy-start.8
  0.7 0.0 copy-start.9
  0.7 1.1 %fusion.47 = (f32[128,512]{1,0:T(8,128)S(1)}, f32[128,512]{1,0:T(8,128)S(1)}) fusion(f32[512,512]{1,0:T(8,128)} %param.10), kind=kLoop, calls=%fused_computation.92 | loop fusion | bytes 1048576 | tf_op jit(solution)/shard_map/slice | solution.py:22
  1.8 4.5 %collective-permute-start = (f32[128,512]{1,0:T(8,128)S(1)}, f32[128,512]{1,0:T(8,128)S(1)}, u32[]{:S(2)}, u32[]{:S(2)}) collective-permute-start(f32[128,512]{1,0:T(8,128)S(1)} %get-tuple-element.28), channel_id=1, source_target_pairs={{0,16},{16,32},{32,48},{48,64},{64,80},{80,96},{96,112},{1,17},{17... | collective-permute-start | bytes 786440 | tf_op jit(solution)/shard_map/ppermute | solution.py:24
  6.3 1.9 %collective-permute-start.1 = (f32[128,512]{1,0:T(8,128)S(1)}, f32[128,512]{1,0:T(8,128)S(1)}, u32[]{:S(2)}, u32[]{:S(2)}) collective-permute-start(f32[128,512]{1,0:T(8,128)S(1)} %get-tuple-element.29), channel_id=1, source_target_pairs={{16,0},{32,16},{48,32},{64,48},{80,64},{96,80},{112,96},{17,1},{33... | collective-permute-start | bytes 786440 | tf_op jit(solution)/shard_map/ppermute | solution.py:25
  8.3 0.0 copy-done
  8.3 0.0 copy-start.5
  8.3 0.2 fusion.45
  8.5 0.0 copy-done.8
  8.5 14.0 %all-gather.1 = f32[8,34,256]{2,1,0:T(8,128)S(1)} all-gather(f32[1,34,256]{2,1,0:T(8,128)S(1)} %maximum_bitcast_fusion), channel_id=2, replica_groups=mesh['tile'=8,'orient'=16] {'tile'}, dimensions={0}, use_global_device_ids=true | all-gather | bytes 313344 | tf_op jit(solution)/shard_map/all_gather | solution.py:72
  23.3 0.0 copy-done.9
  23.3 0.6 fusion.39
  24.6 0.0 copy-start.7
  24.6 0.2 fusion.20
  24.8 0.1 multiply_reduce_fusion.2
  24.9 0.2 fusion.18
  25.1 0.2 fusion.24
  25.3 0.2 fusion.22
  25.5 0.0 copy-done.5
  25.6 0.9 %fusion.50 = f32[256,768]{1,0:T(8,128)S(1)} fusion(f32[256,256]{1,0:T(8,128)S(1)} %fusion.17, f32[768,256]{1,0:T(8,128)S(1)} %copy-done.5), kind=kOutput, calls=%fused_computation.95 | convolution fusion | flops 301989888 | bytes 1835008 | tf_op jit(solution)/shard_map/dot_general | solution.py:31
  26.4 0.0 copy-done.7
  26.4 1.3 %fusion.51 = f32[768,768]{1,0:T(8,128)S(1)} fusion(f32[256,768]{1,0:T(8,128)S(1)} %fusion.50, f32[256,768]{1,0:T(8,128)S(1)} %copy-done.7), kind=kOutput, calls=%fused_computation.96 | convolution fusion | flops 905969664 | bytes 3932160 | tf_op jit(solution)/shard_map/dot_general | solution.py:31
  27.8 0.1 slice.144
  27.9 0.2 add_negate_fusion
  28.1 0.0 collective-permute-done
  28.1 0.0 collective-permute-done.1
  28.1 0.0 copy-start.2
  28.1 0.2 fusion.9
  28.4 1.4 %copy-done.2 = f32[768,768]{1,0:T(8,128)S(1)} copy-done((f32[768,768]{1,0:T(8,128)S(1)}, f32[768,768]{1,0:T(8,128)}, u32[]{:S(2)}) %copy-start.2) | copy-done | bytes 2359320
  29.8 0.0 copy-start.3
  29.8 4.0 %fusion.48 = f32[512,768]{1,0:T(8,128)S(1)} fusion(f32[768,512]{1,0:T(8,128)S(1)} %fusion.9, f32[768,768]{1,0:T(8,128)S(1)} %copy-done.2), kind=kOutput, calls=%fused_computation.93 | convolution fusion | flops 1811939328 | bytes 5505024 | tf_op jit(solution)/shard_map/dot_general | solution.py:31
  33.8 0.0 copy-done.3
  33.8 2.5 %fusion.49 = f32[768,768]{1,0:T(8,128)S(1)} fusion(f32[512,768]{1,0:T(8,128)S(1)} %fusion.48, f32[512,768]{1,0:T(8,128)S(1)} %copy-done.3), kind=kOutput, calls=%fused_computation.94 | convolution fusion | flops 1811939328 | bytes 5505024 | tf_op jit(solution)/shard_map/dot_general | solution.py:31
  36.3 0.1 slice.141
  36.4 2.4 %add_multiply_fusion.1 = (f32[385,383]{1,0:T(8,128)S(1)}, f32[385,383]{1,0:T(8,128)S(1)}, f32[385,383]{1,0:T(8,128)S(1)}, f32[385,383]{1,0:T(8,128)S(1)}, f32[385,383]{1,0:T(8,128)S(1)}, /*index=5*/f32[385,383]{1,0:T(8,128)S(1)}) fusion(f32[385,768]{1,0:T(8,128)S(1)} %add_negate_fusion, f32[768,768]{1,0:T(8,128)S(1)} %fusion.49, f32[768,768]{1,0:T(8,128)S(1)} %fusion.51, ...), kind=kLoop, calls=%fused_computation.37 | loop fusion | flops 2359280 | bytes 8841172 | tf_op jit(solution)/shard_map/mul | solution.py:135
  38.8 0.0 copy-start.1
  38.8 1.2 %add_multiply_fusion = (f32[385,385]{1,0:T(8,128)S(1)}, f32[385,385]{1,0:T(8,128)S(1)}) fusion(f32[385,768]{1,0:T(8,128)S(1)} %add_negate_fusion, f32[385,383]{1,0:T(8,128)S(1)} %get-tuple-element.26, f32[768,768]{1,0:T(8,128)S(1)} %fusion.49, f32[385,383]{1,0:T(8,128)S(1)} %get-tuple-element.27, f32[768,768]{1,0:T(8,128)S(1)} %fusion.51, ...), kind=kLoop, calls=%fused_computation.29 | loop fusion | flops 2371600 | bytes 7676932 | tf_op jit(solution)/shard_map/mul | solution.py:135
  40.0 0.7 copy-done.1
  40.7 4.0 %fusion = f32[770,1024]{1,0:T(8,128)S(1)} fusion(f32[768,1024]{1,0:T(8,128)S(1)} %copy-done.1, f32[385,383]{1,0:T(8,128)S(1)} %get-tuple-element.21, f32[385,385]{1,0:T(8,128)S(1)} %get-tuple-element.19, f32[385,383]{1,0:T(8,128)S(1)} %get-tuple-element.20, f32[385,385]{1,0:T(8,128)S(1)} %get-tuple-element.18), kind=kOutput, calls=%fused_computation | convolution fusion | flops 3635089920 | bytes 8665088 | tf_op jit(solution)/shard_map/dot_general | solution.py:31
  44.7 0.0 copy-start.4
  44.7 0.2 fusion.46
  44.9 1.0 %copy-done.4 = f32[512,385]{1,0:T(8,128)S(1)} copy-done((f32[512,385]{1,0:T(8,128)S(1)}, f32[512,385]{1,0:T(8,128)}, u32[]{:S(2)}) %copy-start.4) | copy-done | bytes 788504
  45.9 0.0 copy-start.6
  45.9 1.0 %fusion.12 = f32[512,512]{0,1:T(8,128)S(1)} fusion(f32[512,385]{1,0:T(8,128)S(1)} %copy-done.4, f32[770,1024]{1,0:T(8,128)S(1)} %fusion), kind=kOutput, calls=%fused_computation.24 | convolution fusion | flops 605749760 | bytes 3702784 | tf_op jit(solution)/shard_map/dot_general | solution.py:31
  47.0 0.1 copy-done.6
  47.1 1.1 %convolution_add_fusion = f32[512,512]{0,1:T(8,128)S(1)} fusion(f32[512,512]{0,1:T(8,128)S(1)} %fusion.12, f32[512,383]{1,0:T(8,128)S(1)} %copy-done.6, f32[385,512]{1,0:T(8,128)S(1)} %get-tuple-element.23, f32[385,512]{1,0:T(8,128)S(1)} %get-tuple-element.22), kind=kOutput, calls=%fused_computation.12 | convolution fusion | flops 602865152 | bytes 4456448 | tf_op jit(solution)/shard_map/dot_general | solution.py:31
  48.2 24.1 %all_to_all.9 = f32[16,32,512]{2,1,0:T(8,128)S(1)} all-to-all(f32[16,32,512]{2,1,0:T(8,128)S(1)} %bitcast.43), channel_id=1, replica_groups=mesh['tile'=8,'orient'=16] {'orient'}, dimensions={0} | all-to-all | bytes 2097152 | tf_op jit(solution)/shard_map/all_to_all | solution.py:154
  72.3 0.9 %multiply_reduce_fusion = (f32[32,512]{1,0:T(8,128)}, f32[32,512]{1,0:T(8,128)}, f32[32,512]{1,0:T(8,128)S(1)}, f32[32,512]{1,0:T(8,128)S(1)}) fusion(f32[16,32,512]{2,1,0:T(8,128)S(1)} %all_to_all.9), kind=kLoop, calls=%fused_computation.11 | loop fusion | flops 1736704 | bytes 1310720 | tf_op jit(solution)/shard_map/reduce | solution.py:166
  73.2 0.7 multiply_subtract_fusion
  (16 shorter events, 0.3 us)
Async XLA Ops:
  0.6 7.6 %copy-start = (f32[512,512]{1,0:T(8,128)S(1)}, f32[512,512]{1,0:T(8,128)}, u32[]{:S(2)}) copy-start(f32[512,512]{1,0:T(8,128)} %param.10) | copy-start | bytes 3145732
  0.6 7.8 %copy-start.8 = (f32[1,32,256]{2,1,0:T(8,128)S(1)}, f32[1,32,256]{2,1,0:T(8,128)}, u32[]{:S(2)}) copy-start(f32[1,32,256]{2,1,0:T(8,128)} %param.11) | copy-start | bytes 98308
  0.7 22.6 %copy-start.9 = (f32[4]{0:T(128)S(1)}, f32[4]{0:T(128)}, u32[]{:S(2)}) copy-start(f32[4]{0:T(128)} %param.12) | copy-start | bytes 52
  1.8 26.3 %collective-permute-start = (f32[128,512]{1,0:T(8,128)S(1)}, f32[128,512]{1,0:T(8,128)S(1)}, u32[]{:S(2)}, u32[]{:S(2)}) collective-permute-start(f32[128,512]{1,0:T(8,128)S(1)} %get-tuple-element.28), channel_id=1, source_target_pairs={{0,16},{16,32},{32,48},{48,64},{64,80},{80,96},{96,112},{1,17},{17... | collective-permute-start | bytes 786440 | tf_op jit(solution)/shard_map/ppermute | solution.py:24
  6.3 21.8 %collective-permute-start.1 = (f32[128,512]{1,0:T(8,128)S(1)}, f32[128,512]{1,0:T(8,128)S(1)}, u32[]{:S(2)}, u32[]{:S(2)}) collective-permute-start(f32[128,512]{1,0:T(8,128)S(1)} %get-tuple-element.29), channel_id=1, source_target_pairs={{16,0},{32,16},{48,32},{64,48},{80,64},{96,80},{112,96},{17,1},{33... | collective-permute-start | bytes 786440 | tf_op jit(solution)/shard_map/ppermute | solution.py:25
  8.3 17.3 %copy-start.5 = (f32[768,256]{1,0:T(8,128)S(1)}, f32[768,256]{1,0:T(8,128)}, u32[]{:S(2)}) copy-start(f32[768,256]{1,0:T(8,128)} %constant.72.clone) | copy-start | bytes 2359300
  24.6 1.8 %copy-start.7 = (f32[256,768]{1,0:T(8,128)S(1)}, f32[256,768]{1,0:T(8,128)}, u32[]{:S(2)}) copy-start(f32[256,768]{1,0:T(8,128)} %constant.74.clone) | copy-start | bytes 2359300
  28.1 1.7 %copy-start.2 = (f32[768,768]{1,0:T(8,128)S(1)}, f32[768,768]{1,0:T(8,128)}, u32[]{:S(2)}) copy-start(f32[768,768]{1,0:T(8,128)} %constant.71.clone) | copy-start | bytes 7077892
  29.8 4.0 %copy-start.3 = (f32[512,768]{1,0:T(8,128)S(1)}, f32[512,768]{1,0:T(8,128)}, u32[]{:S(2)}) copy-start(f32[512,768]{1,0:T(8,128)} %constant.73.clone) | copy-start | bytes 4718596
  38.8 1.9 %copy-start.1 = (f32[768,1024]{1,0:T(8,128)S(1)}, f32[768,1024]{1,0:T(8,128)}, u32[]{:S(2)}) copy-start(f32[768,1024]{1,0:T(8,128)} %constant.75.clone) | copy-start | bytes 9437188
  44.7 1.2 %copy-start.4 = (f32[512,385]{1,0:T(8,128)S(1)}, f32[512,385]{1,0:T(8,128)}, u32[]{:S(2)}) copy-start(f32[512,385]{1,0:T(8,128)} %constant.91) | copy-start | bytes 2365444
  45.9 1.1 %copy-start.6 = (f32[512,383]{1,0:T(8,128)S(1)}, f32[512,383]{1,0:T(8,128)}, u32[]{:S(2)}) copy-start(f32[512,383]{1,0:T(8,128)} %constant.92) | copy-start | bytes 2353156

commit v13 on v12

--- a/solution.py
+++ b/solution.py
@@ -62,7 +62,6 @@
     tile_count = lax.axis_size("tile")
     pixel_count = float(tile_rows * tile_width * tile_count)
     own_rows, tpl_width = templates.shape[1], templates.shape[2]
-    halo = padded(micrograph, (("tile", 0),), margin)
     def lane_fold(columns):
         return sum(columns[i:i + tpl_width] for i in range(0, tile_width, tpl_width))[None, :]
 
@@ -70,6 +69,8 @@
     square_row = lane_fold(jnp.sum(micrograph * micrograph, axis=0))
     payload = jnp.concatenate([templates[0], sum_row, square_row], axis=0)
     everything = lax.all_gather(payload, "tile")
+    micrograph_after, everything = lax.optimization_barrier((micrograph, everything))
+    halo = padded(micrograph_after, (("tile", 0),), margin)
     gathered = everything[:, :own_rows].reshape(tile_count * own_rows, tpl_width)
     ones = jnp.ones((tpl_width, tpl_width), jnp.float32)
 

time: 74.4 us -> 74.7 us (level)
  other arithmetic: 6.79 us -> 8.94 us
  starting transfers between devices: 6.43 us -> 4.8 us
  local copies, waits for them, and re-layouts: 4.77 us -> 3.66 us
  blocking collectives: 38.2 us -> 39.1 us
    ppermute x1, starting transfers between devices: 4.51 us -> 2.88 us  [padded(): before = lax.ppermute(last, axis, up)]
    reduce_sum x1, other arithmetic: 0.16 us -> 1.47 us  [per_device(): sum_row = lane_fold(jnp.sum(micrograph, axis=0))]
    slice x1, local copies, waits for them, and re-layouts: 1.15 us -> 0.03 us  [padded(): last = lax.slice_in_dim(shard, length - width, length, axis=dim)]
    unnamed x1, other arithmetic: 0.01 us -> 0.84 us
    unnamed x24 -> x22, local copies, waits for them, and re-layouts: 3.26 us -> 3.27 us
  transfers between devices with their start and end apart: 2 -> 2, of which waited for: 0 -> 1; matrix products, arithmetic and copies ran while one was open for 6% -> 6% of each run, Pallas kernels for 0% -> 0%
where the time goes in v13:
time: 74.7 us; the launch traced here: 74.3 us
  blocking collectives  39.1 us (52%)
  matrix products  15.4 us (21%)
  other arithmetic  8.94 us (12%)
  starting transfers between devices  4.8 us (6%)
  local copies, waits for them, and re-layouts  3.66 us (5%)
  between operations  2.23 us (3%)
    all_to_all x1, blocking collectives, per_device(): lax.all_to_all(scores, 'orient', 0, 0, tiled=True)  24.6 us
    dot_general x7, matrix products, product(): jnp.dot(former, latter, precision=mode, preferred_element_type=jnp.float32)  14.7 us
    all_gather x1, blocking collectives, per_device(): everything = lax.all_gather(payload, 'tile')  14.6 us
    mul x2, other arithmetic, multiply(): (spec_real * template_real + spec_imag * template_imag) * weight  3.64 us
    unnamed x22, local copies, waits for them, and re-layouts  3.27 us
    ppermute x1, starting transfers between devices, padded(): before = lax.ppermute(last, axis, up)  2.88 us
    ppermute x1, starting transfers between devices, padded(): after = lax.ppermute(initial, axis, down)  1.92 us
  transfers between devices with their start and end apart: 2, of which 1 were waited for; matrix products, arithmetic and copies ran while one was open for 6% of the time, Pallas kernels for 0%

profile of v13, /device:TPU:1, one launch (start us, length us, event | category | flops | bytes accessed | tf_op | source)
XLA Modules:
  0.0 74.3 jit_solution(14049888348381313554)
XLA Ops:
  0.6 0.0 copy-start
  0.6 0.0 copy-start.8
  0.7 1.5 %fusion.45 = (f32[512]{0:T(512)S(1)}, f32[512]{0:T(512)S(1)}) fusion(f32[512,512]{1,0:T(8,128)} %param.10), kind=kLoop, calls=%fused_computation.90 | loop fusion | flops 785408 | bytes 1052672 | tf_op jit(solution)/shard_map/reduce_sum | solution.py:68
  2.1 0.0 copy-start.5
  2.1 0.8 %maximum_bitcast_fusion = f32[1,34,256]{2,1,0:T(8,128)S(1)} fusion(f32[1,256]{1,0:T(1,128)S(1)} %bitcast.47, f32[1,256]{1,0:T(1,128)S(1)} %bitcast.48, f32[32,256]{1,0:T(8,128)} %bitcast.44), kind=kLoop, calls=%fused_computation.50 | loop fusion | flops 17408 | bytes 69632
  3.0 14.6 %all-gather.1 = f32[8,34,256]{2,1,0:T(8,128)S(1)} all-gather(f32[1,34,256]{2,1,0:T(8,128)S(1)} %maximum_bitcast_fusion), channel_id=2, replica_groups=mesh['tile'=8,'orient'=16] {'tile'}, dimensions={0}, use_global_device_ids=true | all-gather | bytes 313344 | tf_op jit(solution)/shard_map/all_gather | solution.py:71
  17.6 0.0 copy-done
  17.6 2.9 %collective-permute-start = (f32[128,512]{1,0:T(8,128)S(1)}, f32[128,512]{1,0:T(8,128)S(1)}, u32[]{:S(2)}, u32[]{:S(2)}) collective-permute-start(f32[128,512]{1,0:T(8,128)S(1)} %get-tuple-element.32), channel_id=1, source_target_pairs={{0,16},{16,32},{32,48},{48,64},{64,80},{80,96},{96,112},{1,17},{17... | collective-permute-start | bytes 786440 | tf_op jit(solution)/shard_map/ppermute | solution.py:24
  20.5 1.9 %collective-permute-start.1 = (f32[128,512]{1,0:T(8,128)S(1)}, f32[128,512]{1,0:T(8,128)S(1)}, u32[]{:S(2)}, u32[]{:S(2)}) collective-permute-start(f32[128,512]{1,0:T(8,128)S(1)} %get-tuple-element.33), channel_id=1, source_target_pairs={{16,0},{32,16},{48,32},{64,48},{80,64},{96,80},{112,96},{17,1},{33... | collective-permute-start | bytes 786440 | tf_op jit(solution)/shard_map/ppermute | solution.py:25
  23.2 0.0 copy-done.8
  23.2 0.6 fusion.39
  24.5 0.0 copy-start.7
  24.5 0.2 fusion.20
  24.7 0.1 multiply_reduce_fusion.2
  24.8 0.2 fusion.18
  25.0 0.2 fusion.24
  25.2 0.2 fusion.22
  25.5 0.0 copy-done.5
  25.5 0.9 %fusion.50 = f32[256,768]{1,0:T(8,128)S(1)} fusion(f32[256,256]{1,0:T(8,128)S(1)} %fusion.17, f32[768,256]{1,0:T(8,128)S(1)} %copy-done.5), kind=kOutput, calls=%fused_computation.95 | convolution fusion | flops 301989888 | bytes 1835008 | tf_op jit(solution)/shard_map/dot_general | solution.py:31
  26.3 0.0 copy-done.7
  26.3 1.3 %fusion.51 = f32[768,768]{1,0:T(8,128)S(1)} fusion(f32[256,768]{1,0:T(8,128)S(1)} %fusion.50, f32[256,768]{1,0:T(8,128)S(1)} %copy-done.7), kind=kOutput, calls=%fused_computation.96 | convolution fusion | flops 905969664 | bytes 3932160 | tf_op jit(solution)/shard_map/dot_general | solution.py:31
  27.7 0.1 slice.141
  27.8 0.2 add_negate_fusion
  28.0 0.0 collective-permute-done
  28.0 0.2 collective-permute-done.1
  28.2 0.0 copy-start.2
  28.2 0.2 fusion.9
  28.4 1.5 %copy-done.2 = f32[768,768]{1,0:T(8,128)S(1)} copy-done((f32[768,768]{1,0:T(8,128)S(1)}, f32[768,768]{1,0:T(8,128)}, u32[]{:S(2)}) %copy-start.2) | copy-done | bytes 2359320
  29.8 0.0 copy-start.3
  29.8 4.0 %fusion.48 = f32[512,768]{1,0:T(8,128)S(1)} fusion(f32[768,512]{1,0:T(8,128)S(1)} %fusion.9, f32[768,768]{1,0:T(8,128)S(1)} %copy-done.2), kind=kOutput, calls=%fused_computation.93 | convolution fusion | flops 1811939328 | bytes 5505024 | tf_op jit(solution)/shard_map/dot_general | solution.py:31
  33.9 0.0 copy-done.3
  33.9 2.5 %fusion.49 = f32[768,768]{1,0:T(8,128)S(1)} fusion(f32[512,768]{1,0:T(8,128)S(1)} %fusion.48, f32[512,768]{1,0:T(8,128)S(1)} %copy-done.3), kind=kOutput, calls=%fused_computation.94 | convolution fusion | flops 1811939328 | bytes 5505024 | tf_op jit(solution)/shard_map/dot_general | solution.py:31
  36.3 0.1 slice.139
  36.4 2.4 %add_multiply_fusion.1 = (f32[385,383]{1,0:T(8,128)S(1)}, f32[385,383]{1,0:T(8,128)S(1)}, f32[385,383]{1,0:T(8,128)S(1)}, f32[385,383]{1,0:T(8,128)S(1)}, f32[385,383]{1,0:T(8,128)S(1)}, /*index=5*/f32[385,383]{1,0:T(8,128)S(1)}) fusion(f32[385,768]{1,0:T(8,128)S(1)} %add_negate_fusion, f32[768,768]{1,0:T(8,128)S(1)} %fusion.49, f32[768,768]{1,0:T(8,128)S(1)} %fusion.51, ...), kind=kLoop, calls=%fused_computation.37 | loop fusion | flops 2359280 | bytes 8841172 | tf_op jit(solution)/shard_map/mul | solution.py:136
  38.9 0.0 copy-start.1
  38.9 1.2 %add_multiply_fusion = (f32[385,385]{1,0:T(8,128)S(1)}, f32[385,385]{1,0:T(8,128)S(1)}) fusion(f32[385,768]{1,0:T(8,128)S(1)} %add_negate_fusion, f32[385,383]{1,0:T(8,128)S(1)} %get-tuple-element.30, f32[768,768]{1,0:T(8,128)S(1)} %fusion.49, f32[385,383]{1,0:T(8,128)S(1)} %get-tuple-element.31, f32[768,768]{1,0:T(8,128)S(1)} %fusion.51, ...), kind=kLoop, calls=%fused_computation.29 | loop fusion | flops 2371600 | bytes 7676932 | tf_op jit(solution)/shard_map/mul | solution.py:136
  40.1 0.7 copy-done.1
  40.8 4.0 %fusion = f32[770,1024]{1,0:T(8,128)S(1)} fusion(f32[768,1024]{1,0:T(8,128)S(1)} %copy-done.1, f32[385,383]{1,0:T(8,128)S(1)} %get-tuple-element.25, f32[385,385]{1,0:T(8,128)S(1)} %get-tuple-element.23, f32[385,383]{1,0:T(8,128)S(1)} %get-tuple-element.24, f32[385,385]{1,0:T(8,128)S(1)} %get-tuple-element.22), kind=kOutput, calls=%fused_computation | convolution fusion | flops 3635089920 | bytes 8665088 | tf_op jit(solution)/shard_map/dot_general | solution.py:31
  44.7 0.0 copy-start.4
  44.8 0.2 fusion.46
  45.0 1.0 %copy-done.4 = f32[512,385]{1,0:T(8,128)S(1)} copy-done((f32[512,385]{1,0:T(8,128)S(1)}, f32[512,385]{1,0:T(8,128)}, u32[]{:S(2)}) %copy-start.4) | copy-done | bytes 788504
  46.0 0.0 copy-start.6
  46.0 1.0 %fusion.12 = f32[512,512]{0,1:T(8,128)S(1)} fusion(f32[512,385]{1,0:T(8,128)S(1)} %copy-done.4, f32[770,1024]{1,0:T(8,128)S(1)} %fusion), kind=kOutput, calls=%fused_computation.24 | convolution fusion | flops 605749760 | bytes 3702784 | tf_op jit(solution)/shard_map/dot_general | solution.py:31
  47.0 0.1 copy-done.6
  47.1 1.1 %convolution_add_fusion = f32[512,512]{0,1:T(8,128)S(1)} fusion(f32[512,512]{0,1:T(8,128)S(1)} %fusion.12, f32[512,383]{1,0:T(8,128)S(1)} %copy-done.6, f32[385,512]{1,0:T(8,128)S(1)} %get-tuple-element.27, f32[385,512]{1,0:T(8,128)S(1)} %get-tuple-element.26), kind=kOutput, calls=%fused_computation.12 | convolution fusion | flops 602865152 | bytes 4456448 | tf_op jit(solution)/shard_map/dot_general | solution.py:31
  48.2 24.6 %all_to_all.9 = f32[16,32,512]{2,1,0:T(8,128)S(1)} all-to-all(f32[16,32,512]{2,1,0:T(8,128)S(1)} %bitcast.43), channel_id=1, replica_groups=mesh['tile'=8,'orient'=16] {'orient'}, dimensions={0} | all-to-all | bytes 2097152 | tf_op jit(solution)/shard_map/all_to_all | solution.py:155
  72.8 0.9 %multiply_reduce_fusion = (f32[32,512]{1,0:T(8,128)}, f32[32,512]{1,0:T(8,128)}, f32[32,512]{1,0:T(8,128)S(1)}, f32[32,512]{1,0:T(8,128)S(1)}) fusion(f32[16,32,512]{2,1,0:T(8,128)S(1)} %all_to_all.9), kind=kLoop, calls=%fused_computation.11 | loop fusion | flops 1736704 | bytes 1310720 | tf_op jit(solution)/shard_map/reduce | solution.py:167
  73.7 0.7 multiply_subtract_fusion
  (16 shorter events, 0.3 us)
Async XLA Ops:
  0.6 16.9 %copy-start = (f32[512,512]{1,0:T(8,128)S(1)}, f32[512,512]{1,0:T(8,128)}, u32[]{:S(2)}) copy-start(f32[512,512]{1,0:T(8,128)} %param.10) | copy-start | bytes 3145732
  0.6 22.5 %copy-start.8 = (f32[4]{0:T(128)S(1)}, f32[4]{0:T(128)}, u32[]{:S(2)}) copy-start(f32[4]{0:T(128)} %param.12) | copy-start | bytes 52
  2.1 23.3 %copy-start.5 = (f32[768,256]{1,0:T(8,128)S(1)}, f32[768,256]{1,0:T(8,128)}, u32[]{:S(2)}) copy-start(f32[768,256]{1,0:T(8,128)} %constant.72.clone) | copy-start | bytes 2359300
  17.6 10.4 %collective-permute-start = (f32[128,512]{1,0:T(8,128)S(1)}, f32[128,512]{1,0:T(8,128)S(1)}, u32[]{:S(2)}, u32[]{:S(2)}) collective-permute-start(f32[128,512]{1,0:T(8,128)S(1)} %get-tuple-element.32), channel_id=1, source_target_pairs={{0,16},{16,32},{32,48},{48,64},{64,80},{80,96},{96,112},{1,17},{17... | collective-permute-start | bytes 786440 | tf_op jit(solution)/shard_map/ppermute | solution.py:24
  20.5 7.7 %collective-permute-start.1 = (f32[128,512]{1,0:T(8,128)S(1)}, f32[128,512]{1,0:T(8,128)S(1)}, u32[]{:S(2)}, u32[]{:S(2)}) collective-permute-start(f32[128,512]{1,0:T(8,128)S(1)} %get-tuple-element.33), channel_id=1, source_target_pairs={{16,0},{32,16},{48,32},{64,48},{80,64},{96,80},{112,96},{17,1},{33... | collective-permute-start | bytes 786440 | tf_op jit(solution)/shard_map/ppermute | solution.py:25
  24.5 1.8 %copy-start.7 = (f32[256,768]{1,0:T(8,128)S(1)}, f32[256,768]{1,0:T(8,128)}, u32[]{:S(2)}) copy-start(f32[256,768]{1,0:T(8,128)} %constant.74.clone) | copy-start | bytes 2359300
  28.2 1.7 %copy-start.2 = (f32[768,768]{1,0:T(8,128)S(1)}, f32[768,768]{1,0:T(8,128)}, u32[]{:S(2)}) copy-start(f32[768,768]{1,0:T(8,128)} %constant.71.clone) | copy-start | bytes 7077892
  29.8 4.0 %copy-start.3 = (f32[512,768]{1,0:T(8,128)S(1)}, f32[512,768]{1,0:T(8,128)}, u32[]{:S(2)}) copy-start(f32[512,768]{1,0:T(8,128)} %constant.73.clone) | copy-start | bytes 4718596
  38.9 1.9 %copy-start.1 = (f32[768,1024]{1,0:T(8,128)S(1)}, f32[768,1024]{1,0:T(8,128)}, u32[]{:S(2)}) copy-start(f32[768,1024]{1,0:T(8,128)} %constant.75.clone) | copy-start | bytes 9437188
  44.7 1.2 %copy-start.4 = (f32[512,385]{1,0:T(8,128)S(1)}, f32[512,385]{1,0:T(8,128)}, u32[]{:S(2)}) copy-start(f32[512,385]{1,0:T(8,128)} %constant.91) | copy-start | bytes 2365444
  46.0 1.1 %copy-start.6 = (f32[512,383]{1,0:T(8,128)S(1)}, f32[512,383]{1,0:T(8,128)}, u32[]{:S(2)}) copy-start(f32[512,383]{1,0:T(8,128)} %constant.92) | copy-start | bytes 2353156

commit v14 on v12

--- a/solution.py
+++ b/solution.py
@@ -142,18 +142,26 @@
         [jnp.concatenate([real_d, real_m], axis=1), jnp.concatenate([imag_d, imag_m], axis=1)],
         axis=0,
     )
-    inner = product(lhs, back)
-    pr_c, pr_s = inner[:h, :tile_width], inner[:h, tile_width:]
-    pi_c, pi_s = inner[h:, :tile_width], inner[h:, tile_width:]
-    back_real = pr_c - pi_s
-    back_imag = pr_s + pi_c
-    scores = product(final, jnp.concatenate([back_real, back_imag[1:h - 1]], axis=0))
-
     orient_count = lax.axis_size("orient")
     share_rows = tile_rows // orient_count
-    pieces = lax.all_to_all(scores, "orient", 0, 0, tiled=True).reshape(
-        orient_count, share_rows, tile_width
-    )
+    half_cols = tile_width // 2
+    received = []
+    for part in range(2):
+        cols = slice(part * half_cols, (part + 1) * half_cols)
+        back_part = jnp.concatenate(
+            [back[:, cols], back[:, tile_width + part * half_cols:tile_width + (part + 1) * half_cols]],
+            axis=1,
+        )
+        inner = product(lhs, back_part)
+        pr_c, pr_s = inner[:h, :half_cols], inner[:h, half_cols:]
+        pi_c, pi_s = inner[h:, :half_cols], inner[h:, half_cols:]
+        back_real = pr_c - pi_s
+        back_imag = pr_s + pi_c
+        scores = product(final, jnp.concatenate([back_real, back_imag[1:h - 1]], axis=0))
+        scores, lhs = lax.optimization_barrier((scores, lhs))
+        received.append(lax.all_to_all(scores, "orient", 0, 0, tiled=True))
+    pieces = jnp.concatenate(received, axis=1).reshape(orient_count, share_rows, tile_width)
+
     def merge(former, latter):
         return (
             jnp.maximum(former[0], latter[0]),

time: 74.4 us -> 85.3 us (1.15); the launches traced: 73.9 us -> 83.7 us
  blocking collectives: 38.2 us -> 14 us
  waiting for transfers between devices: 0.01 us -> 13.4 us
  starting transfers between devices: 6.43 us -> 17.8 us
  local copies, waits for them, and re-layouts: 4.77 us -> 9.27 us
  matrix products: 15.4 us -> 19.6 us
    all_to_all x1 -> x0, blocking collectives: 24.1 us -> none  [per_device(): lax.all_to_all(scores, 'orient', 0, 0, tiled=True)]
    all_to_all x0 -> x2, waiting for transfers between devices: none -> 13.4 us  [per_device(): received.append(lax.all_to_all(scores, 'orient', 0, 0, tiled=True))]
    all_to_all x0 -> x2, starting transfers between devices: none -> 11.4 us  [per_device(): received.append(lax.all_to_all(scores, 'orient', 0, 0, tiled=True))]
    dot_general x7 -> x10, matrix products: 14.7 us -> 18.9 us  [product(): jnp.dot(former, latter, precision=mode, preferred_element_type=jnp.float32)]
    optimization_barrier x0 -> x2, local copies, waits for them, and re-layouts: none -> 3.05 us  [per_device(): scores, lhs = lax.optimization_barrier((scores, lhs))]
    unnamed x24 -> x27, local copies, waits for them, and re-layouts: 3.26 us -> 4.75 us
  transfers between devices with their start and end apart: 2 -> 4, of which waited for: 0 -> 2; matrix products, arithmetic and copies ran while one was open for 6% -> 14% of each run, Pallas kernels for 0% -> 0%
where the time goes in v14:
time: 85.3 us; the launch traced here: 83.7 us
  matrix products  19.6 us (23%)
  starting transfers between devices  17.8 us (21%)
  blocking collectives  14 us (16%)
  waiting for transfers between devices  13.4 us (16%)
  local copies, waits for them, and re-layouts  9.27 us (11%)
  other arithmetic  7.21 us (8%)
  between operations  2.38 us (3%)
    dot_general x10, matrix products, product(): jnp.dot(former, latter, precision=mode, preferred_element_type=jnp.float32)  18.9 us
    all_gather x1, blocking collectives, per_device(): everything = lax.all_gather(payload, 'tile')  14 us
    all_to_all x2, waiting for transfers between devices, per_device(): received.append(lax.all_to_all(scores, 'orient', 0, 0, tiled=True))  13.4 us
    all_to_all x2, starting transfers between devices, per_device(): received.append(lax.all_to_all(scores, 'orient', 0, 0, tiled=True))  11.4 us
    unnamed x27, local copies, waits for them, and re-layouts  4.75 us
    ppermute x1, starting transfers between devices, padded(): before = lax.ppermute(last, axis, up)  4.51 us
    mul x2, other arithmetic, multiply(): (spec_real * template_real + spec_imag * template_imag) * weight  3.64 us
    optimization_barrier x2, local copies, waits for them, and re-layouts, per_device(): scores, lhs = lax.optimization_barrier((scores, lhs))  3.05 us
  transfers between devices with their start and end apart: 4, of which 2 were waited for; matrix products, arithmetic and copies ran while one was open for 14% of the time, Pallas kernels for 0%

profile of v14, /device:TPU:1, one launch (start us, length us, event | category | flops | bytes accessed | tf_op | source)
XLA Modules:
  0.0 83.7 jit_solution(13014164666853147751)
XLA Ops:
  0.6 0.0 copy-start
  0.6 0.0 copy-start.9
  0.7 0.0 copy-start.10
  0.7 1.1 %fusion.44 = (f32[128,512]{1,0:T(8,128)S(1)}, f32[128,512]{1,0:T(8,128)S(1)}) fusion(f32[512,512]{1,0:T(8,128)} %param.10), kind=kLoop, calls=%fused_computation.95 | loop fusion | bytes 1048576 | tf_op jit(solution)/shard_map/slice | solution.py:22
  1.8 4.5 %collective-permute-start = (f32[128,512]{1,0:T(8,128)S(1)}, f32[128,512]{1,0:T(8,128)S(1)}, u32[]{:S(2)}, u32[]{:S(2)}) collective-permute-start(f32[128,512]{1,0:T(8,128)S(1)} %get-tuple-element.36), channel_id=1, source_target_pairs={{0,16},{16,32},{32,48},{48,64},{64,80},{80,96},{96,112},{1,17},{17... | collective-permute-start | bytes 786440 | tf_op jit(solution)/shard_map/ppermute | solution.py:24
  6.3 1.9 %collective-permute-start.1 = (f32[128,512]{1,0:T(8,128)S(1)}, f32[128,512]{1,0:T(8,128)S(1)}, u32[]{:S(2)}, u32[]{:S(2)}) collective-permute-start(f32[128,512]{1,0:T(8,128)S(1)} %get-tuple-element.37), channel_id=1, source_target_pairs={{16,0},{32,16},{48,32},{64,48},{80,64},{96,80},{112,96},{17,1},{33... | collective-permute-start | bytes 786440 | tf_op jit(solution)/shard_map/ppermute | solution.py:25
  8.3 0.0 copy-done
  8.3 0.0 copy-start.7
  8.3 0.2 fusion.41
  8.5 0.0 copy-done.9
  8.5 14.0 %all-gather.1 = f32[8,34,256]{2,1,0:T(8,128)S(1)} all-gather(f32[1,34,256]{2,1,0:T(8,128)S(1)} %maximum_bitcast_fusion), channel_id=2, replica_groups=mesh['tile'=8,'orient'=16] {'tile'}, dimensions={0}, use_global_device_ids=true | all-gather | bytes 313344 | tf_op jit(solution)/shard_map/all_gather | solution.py:72
  23.3 0.0 copy-done.10
  23.3 0.6 fusion.36
  24.6 0.0 copy-start.8
  24.6 0.2 fusion.17
  24.8 0.1 multiply_reduce_fusion.2
  24.9 0.2 fusion.15
  25.1 0.2 fusion.21
  25.3 0.2 fusion.19
  25.5 0.0 copy-done.7
  25.6 0.9 %fusion.47 = f32[256,768]{1,0:T(8,128)S(1)} fusion(f32[256,256]{1,0:T(8,128)S(1)} %fusion.14, f32[768,256]{1,0:T(8,128)S(1)} %copy-done.7), kind=kOutput, calls=%fused_computation.98 | convolution fusion | flops 301989888 | bytes 1835008 | tf_op jit(solution)/shard_map/dot_general | solution.py:31
  26.4 0.0 copy-done.8
  26.4 1.3 %fusion.48 = f32[768,768]{1,0:T(8,128)S(1)} fusion(f32[256,768]{1,0:T(8,128)S(1)} %fusion.47, f32[256,768]{1,0:T(8,128)S(1)} %copy-done.8), kind=kOutput, calls=%fused_computation.99 | convolution fusion | flops 905969664 | bytes 3932160 | tf_op jit(solution)/shard_map/dot_general | solution.py:31
  27.8 0.1 slice.182
  27.9 0.2 add_negate_fusion
  28.1 0.0 collective-permute-done
  28.1 0.0 collective-permute-done.1
  28.1 0.0 copy-start.4
  28.1 0.2 fusion.1
  28.4 1.4 %copy-done.4 = f32[768,768]{1,0:T(8,128)S(1)} copy-done((f32[768,768]{1,0:T(8,128)S(1)}, f32[768,768]{1,0:T(8,128)}, u32[]{:S(2)}) %copy-start.4) | copy-done | bytes 2359320
  29.8 0.0 copy-start.6
  29.8 4.0 %fusion.45 = f32[512,768]{1,0:T(8,128)S(1)} fusion(f32[768,512]{1,0:T(8,128)S(1)} %fusion.1, f32[768,768]{1,0:T(8,128)S(1)} %copy-done.4), kind=kOutput, calls=%fused_computation.96 | convolution fusion | flops 1811939328 | bytes 5505024 | tf_op jit(solution)/shard_map/dot_general | solution.py:31
  33.8 0.0 copy-done.6
  33.8 2.5 %fusion.46 = f32[768,768]{1,0:T(8,128)S(1)} fusion(f32[512,768]{1,0:T(8,128)S(1)} %fusion.45, f32[512,768]{1,0:T(8,128)S(1)} %copy-done.6), kind=kOutput, calls=%fused_computation.97 | convolution fusion | flops 1811939328 | bytes 5505024 | tf_op jit(solution)/shard_map/dot_general | solution.py:31
  36.3 0.1 slice.179
  36.4 2.4 %add_multiply_fusion.1 = (f32[385,383]{1,0:T(8,128)S(1)}, f32[385,383]{1,0:T(8,128)S(1)}, f32[385,383]{1,0:T(8,128)S(1)}, f32[385,383]{1,0:T(8,128)S(1)}, f32[385,383]{1,0:T(8,128)S(1)}, /*index=5*/f32[385,383]{1,0:T(8,128)S(1)}) fusion(f32[385,768]{1,0:T(8,128)S(1)} %add_negate_fusion, f32[768,768]{1,0:T(8,128)S(1)} %fusion.46, f32[768,768]{1,0:T(8,128)S(1)} %fusion.48, ...), kind=kLoop, calls=%fused_computation.28 | loop fusion | flops 2359280 | bytes 8841172 | tf_op jit(solution)/shard_map/mul | solution.py:135
  38.8 1.2 %add_multiply_fusion = (f32[385,385]{1,0:T(8,128)S(1)}, f32[385,385]{1,0:T(8,128)S(1)}) fusion(f32[385,768]{1,0:T(8,128)S(1)} %add_negate_fusion, f32[385,383]{1,0:T(8,128)S(1)} %get-tuple-element.34, f32[768,768]{1,0:T(8,128)S(1)} %fusion.46, f32[385,383]{1,0:T(8,128)S(1)} %get-tuple-element.35, f32[768,768]{1,0:T(8,128)S(1)} %fusion.48, ...), kind=kLoop, calls=%fused_computation.22 | loop fusion | flops 2371600 | bytes 7676932 | tf_op jit(solution)/shard_map/mul | solution.py:135
  40.0 0.0 copy-start.5
  40.0 0.4 maximum_maximum_fusion
  40.4 1.0 %copy-done.5 = f32[768,512]{1,0:T(8,128)S(1)} copy-done((f32[768,512]{1,0:T(8,128)S(1)}, f32[768,512]{1,0:T(8,128)}, u32[]{:S(2)}) %copy-start.5) | copy-done | bytes 1572888
  41.4 2.0 %fusion.49 = f32[770,512]{1,0:T(8,128)S(1)} fusion(f32[770,768]{1,0:T(8,128)S(1)} %maximum_maximum_fusion, f32[768,512]{1,0:T(8,128)S(1)} %copy-done.5), kind=kOutput, calls=%fused_computation.100 | convolution fusion | flops 1816657920 | bytes 5515264 | tf_op jit(solution)/shard_map/dot_general | solution.py:31
  43.5 0.0 copy-start.1
  43.5 0.0 copy-start.2
  43.5 0.1 fusion.43
  43.6 1.1 %copy-done.1 = f32[512,385]{1,0:T(8,128)S(1)} copy-done((f32[512,385]{1,0:T(8,128)S(1)}, f32[512,385]{1,0:T(8,128)}, u32[]{:S(2)}) %copy-start.1) | copy-done | bytes 788504
  44.7 1.1 %fusion.10 = f32[256,512]{1,0:T(8,128)S(1)} fusion(f32[512,385]{1,0:T(8,128)S(1)} %copy-done.1, f32[770,512]{1,0:T(8,128)S(1)} %fusion.49), kind=kOutput, calls=%fused_computation.33 | convolution fusion | flops 302874880 | bytes 2375680 | tf_op jit(solution)/shard_map/dot_general | solution.py:31
  45.8 0.0 copy-done.2
  45.8 1.7 %fusion.2 = f32[512,256]{0,1:T(8,128)} fusion(f32[256,512]{1,0:T(8,128)S(1)} %fusion.10, f32[512,383]{1,0:T(8,128)S(1)} %copy-done.2, f32[385,256]{1,0:T(8,128)S(1)} %get-tuple-element.33, f32[385,256]{1,0:T(8,128)S(1)} %get-tuple-element.32), kind=kOutput, calls=%fused_computation.7 | convolution fusion | flops 301432576 | bytes 2621440 | tf_op jit(solution)/shard_map/dot_general | solution.py:31
  47.5 2.0 %copy.16 = f32[512,256]{1,0:T(8,128)} copy(f32[512,256]{0,1:T(8,128)} %fusion.2) | data formatting | bytes 1048576 | tf_op jit(solution)/shard_map/optimization_barrier | solution.py:161
  49.6 7.8 %all-to-all-start = ((f32[16,32,256]{2,1,0:T(8,128)}), f32[16,32,256]{2,1,0:T(8,128)}, u32[]{:S(2)}, u32[]{:S(2)}) async-start(f32[16,32,256]{2,1,0:T(8,128)} %bitcast.51), calls=%async_computation | async-start | bytes 1048576 | tf_op jit(solution)/shard_map/all_to_all | solution.py:162
  57.4 3.5 %fusion.50 = f32[770,512]{1,0:T(8,128)S(1)} fusion(f32[770,768]{1,0:T(8,128)S(1)} %maximum_maximum_fusion, f32[768,512]{1,0:T(8,128)} %constant.98), kind=kOutput, calls=%fused_computation.101 | convolution fusion | flops 1816657920 | bytes 5515264 | tf_op jit(solution)/shard_map/dot_general | solution.py:31
  60.9 0.0 copy-start.3
  60.9 1.1 %fusion.8 = f32[256,512]{1,0:T(8,128)S(1)} fusion(f32[512,385]{1,0:T(8,128)S(1)} %copy-done.1, f32[770,512]{1,0:T(8,128)S(1)} %fusion.50), kind=kOutput, calls=%fused_computation.30 | convolution fusion | flops 302874880 | bytes 2375680 | tf_op jit(solution)/shard_map/dot_general | solution.py:31
  62.0 0.1 fusion.42
  62.0 0.0 copy-done.3
  62.0 0.9 %fusion.3 = f32[512,256]{0,1:T(8,128)S(1)} fusion(f32[256,512]{1,0:T(8,128)S(1)} %fusion.8, f32[512,383]{1,0:T(8,128)S(1)} %copy-done.3, f32[385,256]{1,0:T(8,128)S(1)} %get-tuple-element.31, f32[385,256]{1,0:T(8,128)S(1)} %get-tuple-element.30), kind=kOutput, calls=%fused_computation.8 | convolution fusion | flops 301432576 | bytes 2621440 | tf_op jit(solution)/shard_map/dot_general | solution.py:31
  62.9 1.0 %copy.17 = f32[512,256]{1,0:T(8,128)} copy(f32[512,256]{0,1:T(8,128)S(1)} %fusion.3) | data formatting | bytes 1048576 | tf_op jit(solution)/shard_map/optimization_barrier | solution.py:161
  64.0 4.4 %all-to-all-done = f32[16,32,256]{2,1,0:T(8,128)} async-done(((f32[16,32,256]{2,1,0:T(8,128)}), f32[16,32,256]{2,1,0:T(8,128)}, u32[]{:S(2)}, u32[]{:S(2)}) %all-to-all-start) | async-done | bytes 524320 | tf_op jit(solution)/shard_map/all_to_all | solution.py:162
  68.4 3.6 %all-to-all-start.1 = ((f32[16,32,256]{2,1,0:T(8,128)}), f32[16,32,256]{2,1,0:T(8,128)S(1)}, u32[]{:S(2)}, u32[]{:S(2)}) async-start(f32[16,32,256]{2,1,0:T(8,128)} %bitcast.17), calls=%async_computation.1 | async-start | bytes 1048576 | tf_op jit(solution)/shard_map/all_to_all | solution.py:162
  71.9 1.1 %constant_dynamic-update-slice_fusion.1 = f32[16,32,512]{2,1,0:T(8,128)S(1)} fusion(f32[16,32,256]{2,1,0:T(8,128)} %all-to-all-done), kind=kLoop, calls=%fused_computation.58 | loop fusion | bytes 1048576
  73.0 9.0 %all-to-all-done.1 = f32[16,32,256]{2,1,0:T(8,128)S(1)} async-done(((f32[16,32,256]{2,1,0:T(8,128)}), f32[16,32,256]{2,1,0:T(8,128)S(1)}, u32[]{:S(2)}, u32[]{:S(2)}) %all-to-all-start.1) | async-done | bytes 524320 | tf_op jit(solution)/shard_map/all_to_all | solution.py:162
  82.0 0.1 constant_dynamic-update-slice_fusion
  82.1 0.9 %multiply_reduce_fusion = (f32[32,512]{1,0:T(8,128)}, f32[32,512]{1,0:T(8,128)}, f32[32,512]{1,0:T(8,128)S(1)}, f32[32,512]{1,0:T(8,128)S(1)}) fusion(f32[16,32,512]{2,1,0:T(8,128)S(1)} %constant_dynamic-update-slice_fusion), kind=kLoop, calls=%fused_computation.4 | loop fusion | flops 1736704 | bytes 1310720 | tf_op jit(solution)/shard_map/reduce | solution.py:174
  83.0 0.7 multiply_subtract_fusion
  (16 shorter events, 0.3 us)
Async XLA Ops:
  0.6 7.6 %copy-start = (f32[512,512]{1,0:T(8,128)S(1)}, f32[512,512]{1,0:T(8,128)}, u32[]{:S(2)}) copy-start(f32[512,512]{1,0:T(8,128)} %param.10) | copy-start | bytes 3145732
  0.6 7.8 %copy-start.9 = (f32[1,32,256]{2,1,0:T(8,128)S(1)}, f32[1,32,256]{2,1,0:T(8,128)}, u32[]{:S(2)}) copy-start(f32[1,32,256]{2,1,0:T(8,128)} %param.11) | copy-start | bytes 98308
  0.7 22.6 %copy-start.10 = (f32[4]{0:T(128)S(1)}, f32[4]{0:T(128)}, u32[]{:S(2)}) copy-start(f32[4]{0:T(128)} %param.12) | copy-start | bytes 52
  1.8 26.3 %collective-permute-start = (f32[128,512]{1,0:T(8,128)S(1)}, f32[128,512]{1,0:T(8,128)S(1)}, u32[]{:S(2)}, u32[]{:S(2)}) collective-permute-start(f32[128,512]{1,0:T(8,128)S(1)} %get-tuple-element.36), channel_id=1, source_target_pairs={{0,16},{16,32},{32,48},{48,64},{64,80},{80,96},{96,112},{1,17},{17... | collective-permute-start | bytes 786440 | tf_op jit(solution)/shard_map/ppermute | solution.py:24
  6.3 21.8 %collective-permute-start.1 = (f32[128,512]{1,0:T(8,128)S(1)}, f32[128,512]{1,0:T(8,128)S(1)}, u32[]{:S(2)}, u32[]{:S(2)}) collective-permute-start(f32[128,512]{1,0:T(8,128)S(1)} %get-tuple-element.37), channel_id=1, source_target_pairs={{16,0},{32,16},{48,32},{64,48},{80,64},{96,80},{112,96},{17,1},{33... | collective-permute-start | bytes 786440 | tf_op jit(solution)/shard_map/ppermute | solution.py:25
  8.3 17.3 %copy-start.7 = (f32[768,256]{1,0:T(8,128)S(1)}, f32[768,256]{1,0:T(8,128)}, u32[]{:S(2)}) copy-start(f32[768,256]{1,0:T(8,128)} %constant.72.clone) | copy-start | bytes 2359300
  24.6 1.8 %copy-start.8 = (f32[256,768]{1,0:T(8,128)S(1)}, f32[256,768]{1,0:T(8,128)}, u32[]{:S(2)}) copy-start(f32[256,768]{1,0:T(8,128)} %constant.74.clone) | copy-start | bytes 2359300
  28.1 1.7 %copy-start.4 = (f32[768,768]{1,0:T(8,128)S(1)}, f32[768,768]{1,0:T(8,128)}, u32[]{:S(2)}) copy-start(f32[768,768]{1,0:T(8,128)} %constant.71.clone) | copy-start | bytes 7077892
  29.8 4.0 %copy-start.6 = (f32[512,768]{1,0:T(8,128)S(1)}, f32[512,768]{1,0:T(8,128)}, u32[]{:S(2)}) copy-start(f32[512,768]{1,0:T(8,128)} %constant.73.clone) | copy-start | bytes 4718596
  40.0 1.4 %copy-start.5 = (f32[768,512]{1,0:T(8,128)S(1)}, f32[768,512]{1,0:T(8,128)}, u32[]{:S(2)}) copy-start(f32[768,512]{1,0:T(8,128)} %constant.93) | copy-start | bytes 4718596
  43.5 1.2 %copy-start.1 = (f32[512,385]{1,0:T(8,128)S(1)}, f32[512,385]{1,0:T(8,128)}, u32[]{:S(2)}) copy-start(f32[512,385]{1,0:T(8,128)} %constant.94) | copy-start | bytes 2365444
  43.5 2.3 %copy-start.2 = (f32[512,383]{1,0:T(8,128)S(1)}, f32[512,383]{1,0:T(8,128)}, u32[]{:S(2)}) copy-start(f32[512,383]{1,0:T(8,128)} %constant.95) | copy-start | bytes 2353156
  49.6 18.8 %all-to-all-start = ((f32[16,32,256]{2,1,0:T(8,128)}), f32[16,32,256]{2,1,0:T(8,128)}, u32[]{:S(2)}, u32[]{:S(2)}) async-start(f32[16,32,256]{2,1,0:T(8,128)} %bitcast.51), calls=%async_computation | async-start | bytes 1048576 | tf_op jit(solution)/shard_map/all_to_all | solution.py:162
  60.9 1.2 %copy-start.3 = (f32[512,383]{1,0:T(8,128)S(1)}, f32[512,383]{1,0:T(8,128)}, u32[]{:S(2)}) copy-start(f32[512,383]{1,0:T(8,128)} %constant.95) | copy-start | bytes 2353156
  68.4 13.7 %all-to-all-start.1 = ((f32[16,32,256]{2,1,0:T(8,128)}), f32[16,32,256]{2,1,0:T(8,128)S(1)}, u32[]{:S(2)}, u32[]{:S(2)}) async-start(f32[16,32,256]{2,1,0:T(8,128)} %bitcast.17), calls=%async_computation.1 | async-start | bytes 1048576 | tf_op jit(solution)/shard_map/all_to_all | solution.py:162

commit v15 on v12

--- a/solution.py
+++ b/solution.py
@@ -88,7 +88,7 @@
     valid = ((row_ids >= margin) | (tile_index > 0)) & (
         (row_ids < margin + tile_rows) | (tile_index < tile_count - 1)
     )
-    rows_ext = lax.optimization_barrier(jnp.where(valid, (halo - centre) / spread, 0.0))
+    rows_ext = jnp.where(valid, (halo - centre) / spread, 0.0)
     extent = gathered.shape[0]
     left, left_t, right_w, right_t, back, final = tables(tile_width, margin, extent)
 

time: 74.4 us -> 74.2 us (level)
  no operation moved by 1% of the time
where the time goes in v15:
time: 74.2 us; the launch traced here: 73.6 us
  blocking collectives  38.1 us (51%)
  matrix products  15.6 us (21%)
  other arithmetic  6.58 us (9%)
  starting transfers between devices  6.43 us (9%)
  local copies, waits for them, and re-layouts  4.63 us (6%)
  between operations  2.28 us (3%)
    all_to_all x1, blocking collectives, per_device(): lax.all_to_all(scores, 'orient', 0, 0, tiled=True)  24.1 us
    dot_general x7, matrix products, product(): jnp.dot(former, latter, precision=mode, preferred_element_type=jnp.float32)  14.9 us
    all_gather x1, blocking collectives, per_device(): everything = lax.all_gather(payload, 'tile')  14 us
    ppermute x1, starting transfers between devices, padded(): before = lax.ppermute(last, axis, up)  4.51 us
    mul x2, other arithmetic, multiply(): (spec_real * template_real + spec_imag * template_imag) * weight  3.64 us
    unnamed x24, local copies, waits for them, and re-layouts  3.13 us
    ppermute x1, starting transfers between devices, padded(): after = lax.ppermute(initial, axis, down)  1.92 us
  transfers between devices with their start and end apart: 2, of which 0 were waited for; matrix products, arithmetic and copies ran while one was open for 6% of the time, Pallas kernels for 0%

profile of v15, /device:TPU:1, one launch (start us, length us, event | category | flops | bytes accessed | tf_op | source)
XLA Modules:
  0.0 73.6 jit_solution(6057008738632021435)
XLA Ops:
  0.6 0.0 copy-start.1
  0.6 0.0 copy-start.7
  0.7 0.0 copy-start.8
  0.7 1.1 %fusion.55 = (f32[128,512]{1,0:T(8,128)S(1)}, f32[128,512]{1,0:T(8,128)S(1)}) fusion(f32[512,512]{1,0:T(8,128)} %param.10), kind=kLoop, calls=%fused_computation.99 | loop fusion | bytes 1048576 | tf_op jit(solution)/shard_map/slice | solution.py:22
  1.8 4.5 %collective-permute-start = (f32[128,512]{1,0:T(8,128)S(1)}, f32[128,512]{1,0:T(8,128)S(1)}, u32[]{:S(2)}, u32[]{:S(2)}) collective-permute-start(f32[128,512]{1,0:T(8,128)S(1)} %get-tuple-element.28), channel_id=1, source_target_pairs={{0,16},{16,32},{32,48},{48,64},{64,80},{80,96},{96,112},{1,17},{17... | collective-permute-start | bytes 786440 | tf_op jit(solution)/shard_map/ppermute | solution.py:24
  6.3 1.9 %collective-permute-start.1 = (f32[128,512]{1,0:T(8,128)S(1)}, f32[128,512]{1,0:T(8,128)S(1)}, u32[]{:S(2)}, u32[]{:S(2)}) collective-permute-start(f32[128,512]{1,0:T(8,128)S(1)} %get-tuple-element.29), channel_id=1, source_target_pairs={{16,0},{32,16},{48,32},{64,48},{80,64},{96,80},{112,96},{17,1},{33... | collective-permute-start | bytes 786440 | tf_op jit(solution)/shard_map/ppermute | solution.py:25
  8.3 0.0 copy-done.1
  8.3 0.0 copy-start.4
  8.3 0.2 fusion.53
  8.5 0.0 copy-done.7
  8.5 14.0 %all-gather.1 = f32[8,34,256]{2,1,0:T(8,128)S(1)} all-gather(f32[1,34,256]{2,1,0:T(8,128)S(1)} %maximum_bitcast_fusion), channel_id=2, replica_groups=mesh['tile'=8,'orient'=16] {'tile'}, dimensions={0}, use_global_device_ids=true | all-gather | bytes 313344 | tf_op jit(solution)/shard_map/all_gather | solution.py:72
  23.3 0.0 copy-done.8
  23.3 0.6 fusion.45
  24.6 0.0 copy-start.6
  24.6 0.2 fusion.26
  24.8 0.1 multiply_reduce_fusion.2
  24.9 0.2 fusion.24
  25.1 0.2 fusion.30
  25.3 0.2 fusion.28
  25.5 0.0 copy-done.4
  25.6 0.9 %fusion.57 = f32[256,768]{1,0:T(8,128)S(1)} fusion(f32[256,256]{1,0:T(8,128)S(1)} %fusion.23, f32[768,256]{1,0:T(8,128)S(1)} %copy-done.4), kind=kOutput, calls=%fused_computation.101 | convolution fusion | flops 301989888 | bytes 1835008 | tf_op jit(solution)/shard_map/dot_general | solution.py:31
  26.4 0.0 copy-done.6
  26.4 1.3 %fusion.58 = f32[768,768]{1,0:T(8,128)S(1)} fusion(f32[256,768]{1,0:T(8,128)S(1)} %fusion.57, f32[256,768]{1,0:T(8,128)S(1)} %copy-done.6), kind=kOutput, calls=%fused_computation.102 | convolution fusion | flops 905969664 | bytes 3932160 | tf_op jit(solution)/shard_map/dot_general | solution.py:31
  27.8 0.0 copy-start.9
  27.8 0.1 slice.144
  27.9 0.2 add_negate_fusion
  28.1 0.0 collective-permute-done
  28.1 0.0 collective-permute-done.1
  28.1 1.3 %copy-done.9 = f32[768,768]{1,0:T(8,128)S(1)} copy-done((f32[768,768]{1,0:T(8,128)S(1)}, f32[768,768]{1,0:T(8,128)}, u32[]{:S(2)}) %copy-start.9) | copy-done | bytes 2359320
  29.4 0.0 copy-start.2
  29.4 4.1 %fusion.10 = f32[512,768]{1,0:T(8,128)S(1)} fusion(f32[768,768]{1,0:T(8,128)S(1)} %copy-done.9, f32[128,512]{1,0:T(8,128)S(1)} %collective-permute-done.1, f32[512,512]{1,0:T(8,128)S(1)} %copy-done.1, f32[128,512]{1,0:T(8,128)S(1)} %collective-permute-done, f32[512]{0:T(512)S(1)} %bitcast.47, f32[512]{0:T(512)S(1)} %bitcast.46, pred[768]{0:T(1024)(128)(4,1)S(1)} %fusion.41), kind=kOutput, calls=%fused_computation.12 | convolution fusion | flops 1813905408 | bytes 5509888 | tf_op jit(solution)/shard_map/dot_general | solution.py:31
  33.6 0.0 copy-done.2
  33.6 2.5 %fusion.56 = f32[768,768]{1,0:T(8,128)S(1)} fusion(f32[512,768]{1,0:T(8,128)S(1)} %fusion.10, f32[512,768]{1,0:T(8,128)S(1)} %copy-done.2), kind=kOutput, calls=%fused_computation.100 | convolution fusion | flops 1811939328 | bytes 5505024 | tf_op jit(solution)/shard_map/dot_general | solution.py:31
  36.1 0.1 slice.141
  36.2 2.4 %add_multiply_fusion.1 = (f32[385,383]{1,0:T(8,128)S(1)}, f32[385,383]{1,0:T(8,128)S(1)}, f32[385,383]{1,0:T(8,128)S(1)}, f32[385,383]{1,0:T(8,128)S(1)}, f32[385,383]{1,0:T(8,128)S(1)}, /*index=5*/f32[385,383]{1,0:T(8,128)S(1)}) fusion(f32[385,768]{1,0:T(8,128)S(1)} %add_negate_fusion, f32[768,768]{1,0:T(8,128)S(1)} %fusion.56, f32[768,768]{1,0:T(8,128)S(1)} %fusion.58, ...), kind=kLoop, calls=%fused_computation.42 | loop fusion | flops 2359280 | bytes 8841172 | tf_op jit(solution)/shard_map/mul | solution.py:135
  38.6 0.0 copy-start
  38.6 1.2 %add_multiply_fusion = (f32[385,385]{1,0:T(8,128)S(1)}, f32[385,385]{1,0:T(8,128)S(1)}) fusion(f32[385,768]{1,0:T(8,128)S(1)} %add_negate_fusion, f32[385,383]{1,0:T(8,128)S(1)} %get-tuple-element.26, f32[768,768]{1,0:T(8,128)S(1)} %fusion.56, f32[385,383]{1,0:T(8,128)S(1)} %get-tuple-element.27, f32[768,768]{1,0:T(8,128)S(1)} %fusion.58, ...), kind=kLoop, calls=%fused_computation.30 | loop fusion | flops 2371600 | bytes 7676932 | tf_op jit(solution)/shard_map/mul | solution.py:135
  39.8 0.7 copy-done
  40.5 4.0 %fusion = f32[770,1024]{1,0:T(8,128)S(1)} fusion(f32[768,1024]{1,0:T(8,128)S(1)} %copy-done, f32[385,383]{1,0:T(8,128)S(1)} %get-tuple-element.21, f32[385,385]{1,0:T(8,128)S(1)} %get-tuple-element.19, f32[385,383]{1,0:T(8,128)S(1)} %get-tuple-element.20, f32[385,385]{1,0:T(8,128)S(1)} %get-tuple-element.18), kind=kOutput, calls=%fused_computation | convolution fusion | flops 3635089920 | bytes 8665088 | tf_op jit(solution)/shard_map/dot_general | solution.py:31
  44.5 0.0 copy-start.3
  44.5 0.2 fusion.54
  44.7 1.0 %copy-done.3 = f32[512,385]{1,0:T(8,128)S(1)} copy-done((f32[512,385]{1,0:T(8,128)S(1)}, f32[512,385]{1,0:T(8,128)}, u32[]{:S(2)}) %copy-start.3) | copy-done | bytes 788504
  45.7 0.0 copy-start.5
  45.7 1.0 %fusion.14 = f32[512,512]{0,1:T(8,128)S(1)} fusion(f32[512,385]{1,0:T(8,128)S(1)} %copy-done.3, f32[770,1024]{1,0:T(8,128)S(1)} %fusion), kind=kOutput, calls=%fused_computation.25 | convolution fusion | flops 605749760 | bytes 3702784 | tf_op jit(solution)/shard_map/dot_general | solution.py:31
  46.8 0.1 copy-done.5
  46.9 1.1 %convolution_add_fusion = f32[512,512]{0,1:T(8,128)S(1)} fusion(f32[512,512]{0,1:T(8,128)S(1)} %fusion.14, f32[512,383]{1,0:T(8,128)S(1)} %copy-done.5, f32[385,512]{1,0:T(8,128)S(1)} %get-tuple-element.23, f32[385,512]{1,0:T(8,128)S(1)} %get-tuple-element.22), kind=kOutput, calls=%fused_computation.13 | convolution fusion | flops 602865152 | bytes 4456448 | tf_op jit(solution)/shard_map/dot_general | solution.py:31
  47.9 24.1 %all_to_all.9 = f32[16,32,512]{2,1,0:T(8,128)S(1)} all-to-all(f32[16,32,512]{2,1,0:T(8,128)S(1)} %bitcast.42), channel_id=1, replica_groups=mesh['tile'=8,'orient'=16] {'orient'}, dimensions={0} | all-to-all | bytes 2097152 | tf_op jit(solution)/shard_map/all_to_all | solution.py:154
  72.0 0.9 %multiply_reduce_fusion = (f32[32,512]{1,0:T(8,128)}, f32[32,512]{1,0:T(8,128)}, f32[32,512]{1,0:T(8,128)S(1)}, f32[32,512]{1,0:T(8,128)S(1)}) fusion(f32[16,32,512]{2,1,0:T(8,128)S(1)} %all_to_all.9), kind=kLoop, calls=%fused_computation.11 | loop fusion | flops 1736704 | bytes 1310720 | tf_op jit(solution)/shard_map/reduce | solution.py:166
  73.0 0.7 multiply_subtract_fusion
  (16 shorter events, 0.3 us)
Async XLA Ops:
  0.6 7.6 %copy-start.1 = (f32[512,512]{1,0:T(8,128)S(1)}, f32[512,512]{1,0:T(8,128)}, u32[]{:S(2)}) copy-start(f32[512,512]{1,0:T(8,128)} %param.10) | copy-start | bytes 3145732
  0.6 7.8 %copy-start.7 = (f32[1,32,256]{2,1,0:T(8,128)S(1)}, f32[1,32,256]{2,1,0:T(8,128)}, u32[]{:S(2)}) copy-start(f32[1,32,256]{2,1,0:T(8,128)} %param.11) | copy-start | bytes 98308
  0.7 22.6 %copy-start.8 = (f32[4]{0:T(128)S(1)}, f32[4]{0:T(128)}, u32[]{:S(2)}) copy-start(f32[4]{0:T(128)} %param.12) | copy-start | bytes 52
  1.8 26.3 %collective-permute-start = (f32[128,512]{1,0:T(8,128)S(1)}, f32[128,512]{1,0:T(8,128)S(1)}, u32[]{:S(2)}, u32[]{:S(2)}) collective-permute-start(f32[128,512]{1,0:T(8,128)S(1)} %get-tuple-element.28), channel_id=1, source_target_pairs={{0,16},{16,32},{32,48},{48,64},{64,80},{80,96},{96,112},{1,17},{17... | collective-permute-start | bytes 786440 | tf_op jit(solution)/shard_map/ppermute | solution.py:24
  6.3 21.8 %collective-permute-start.1 = (f32[128,512]{1,0:T(8,128)S(1)}, f32[128,512]{1,0:T(8,128)S(1)}, u32[]{:S(2)}, u32[]{:S(2)}) collective-permute-start(f32[128,512]{1,0:T(8,128)S(1)} %get-tuple-element.29), channel_id=1, source_target_pairs={{16,0},{32,16},{48,32},{64,48},{80,64},{96,80},{112,96},{17,1},{33... | collective-permute-start | bytes 786440 | tf_op jit(solution)/shard_map/ppermute | solution.py:25
  8.3 17.3 %copy-start.4 = (f32[768,256]{1,0:T(8,128)S(1)}, f32[768,256]{1,0:T(8,128)}, u32[]{:S(2)}) copy-start(f32[768,256]{1,0:T(8,128)} %constant.72.clone) | copy-start | bytes 2359300
  24.6 1.8 %copy-start.6 = (f32[256,768]{1,0:T(8,128)S(1)}, f32[256,768]{1,0:T(8,128)}, u32[]{:S(2)}) copy-start(f32[256,768]{1,0:T(8,128)} %constant.74.clone) | copy-start | bytes 2359300
  27.8 1.7 %copy-start.9 = (f32[768,768]{1,0:T(8,128)S(1)}, f32[768,768]{1,0:T(8,128)}, u32[]{:S(2)}) copy-start(f32[768,768]{1,0:T(8,128)} %constant.71.clone) | copy-start | bytes 7077892
  29.4 4.2 %copy-start.2 = (f32[512,768]{1,0:T(8,128)S(1)}, f32[512,768]{1,0:T(8,128)}, u32[]{:S(2)}) copy-start(f32[512,768]{1,0:T(8,128)} %constant.73.clone) | copy-start | bytes 4718596
  38.6 1.9 %copy-start = (f32[768,1024]{1,0:T(8,128)S(1)}, f32[768,1024]{1,0:T(8,128)}, u32[]{:S(2)}) copy-start(f32[768,1024]{1,0:T(8,128)} %constant.75.clone) | copy-start | bytes 9437188
  44.5 1.2 %copy-start.3 = (f32[512,385]{1,0:T(8,128)S(1)}, f32[512,385]{1,0:T(8,128)}, u32[]{:S(2)}) copy-start(f32[512,385]{1,0:T(8,128)} %constant.91) | copy-start | bytes 2365444
  45.7 1.1 %copy-start.5 = (f32[512,383]{1,0:T(8,128)S(1)}, f32[512,383]{1,0:T(8,128)}, u32[]{:S(2)}) copy-start(f32[512,383]{1,0:T(8,128)} %constant.92) | copy-start | bytes 2353156

commit v16 on v15

--- a/solution.py
+++ b/solution.py
@@ -117,11 +117,15 @@
         jnp.where(positions < n // 2, positions, positions - n).astype(jnp.float32) / n
     )
     packed_freq = jnp.where(positions < h, positions, positions - (h - 1)).astype(jnp.float32) / n
-    group_ids = lax.iota(jnp.int32, defocus_values.shape[0])
-    defocus = jnp.sum(jnp.where(group_ids == defocus_group[0], defocus_values, 0.0))
-    scale = math.pi * WAVELENGTH * defocus
-    row_phase = scale * signed_freq[:h, None] ** 2
-    col_phase = scale * packed_freq[None, :] ** 2
+    groups = defocus_values.shape[0]
+    group = defocus_group[0]
+    pick_cols = lax.broadcasted_iota(jnp.int32, (groups, n), 0) == group
+    defocus_cols = jnp.sum(jnp.where(pick_cols, defocus_values[:, None], 0.0), axis=0)[None, :]
+    pick_rows = lax.broadcasted_iota(jnp.int32, (h, groups), 1) == group
+    defocus_rows = jnp.sum(jnp.where(pick_rows, defocus_values[None, :], 0.0), axis=1)[:, None]
+    phase_unit = math.pi * WAVELENGTH
+    row_phase = phase_unit * defocus_rows * signed_freq[:h, None] ** 2
+    col_phase = phase_unit * defocus_cols * packed_freq[None, :] ** 2
     sin_r, cos_r = jnp.sin(row_phase), jnp.cos(row_phase)
     sin_c, cos_c = jnp.sin(col_phase), jnp.cos(col_phase)
     weight_sin = math.sqrt(1.0 - AMPLITUDE * AMPLITUDE)

time: 74.2 us -> 74.2 us (level)
  other arithmetic: 6.58 us -> 7.46 us
    reduce_sum x1 -> x2, other arithmetic: 0.6 us -> 1.48 us  [the longest x1 0.74 us: per_device(): jnp.sum(jnp.where(pick_rows, defocus_values[None, :], 0.0), axis=1)[:, None]]
    unnamed x24 -> x22, local copies, waits for them, and re-layouts: 3.13 us -> 3.12 us
  transfers between devices with their start and end apart: 2 -> 2, of which waited for: 0 -> 0; matrix products, arithmetic and copies ran while one was open for 6% -> 7% of each run, Pallas kernels for 0% -> 0%
where the time goes in v16:
time: 74.2 us; the launch traced here: 73.6 us
  blocking collectives  37.9 us (51%)
  matrix products  15.6 us (21%)
  other arithmetic  7.46 us (10%)
  starting transfers between devices  6.43 us (9%)
  local copies, waits for them, and re-layouts  4.63 us (6%)
  between operations  1.61 us (2%)
    all_to_all x1, blocking collectives, per_device(): lax.all_to_all(scores, 'orient', 0, 0, tiled=True)  24.1 us
    dot_general x7, matrix products, product(): jnp.dot(former, latter, precision=mode, preferred_element_type=jnp.float32)  14.9 us
    all_gather x1, blocking collectives, per_device(): everything = lax.all_gather(payload, 'tile')  13.9 us
    ppermute x1, starting transfers between devices, padded(): before = lax.ppermute(last, axis, up)  4.51 us
    mul x2, other arithmetic, multiply(): (spec_real * template_real + spec_imag * template_imag) * weight  3.63 us
    unnamed x22, local copies, waits for them, and re-layouts  3.12 us
    ppermute x1, starting transfers between devices, padded(): after = lax.ppermute(initial, axis, down)  1.92 us
  transfers between devices with their start and end apart: 2, of which 0 were waited for; matrix products, arithmetic and copies ran while one was open for 7% of the time, Pallas kernels for 0%

profile of v16, /device:TPU:1, one launch (start us, length us, event | category | flops | bytes accessed | tf_op | source)
XLA Modules:
  0.0 73.6 jit_solution(13917226136726889983)
XLA Ops:
  0.6 0.0 copy-start.1
  0.6 0.0 copy-start.7
  0.7 1.2 %fusion.54 = (f32[128,512]{1,0:T(8,128)S(1)}, f32[128,512]{1,0:T(8,128)S(1)}) fusion(f32[512,512]{1,0:T(8,128)} %param.10), kind=kLoop, calls=%fused_computation.100 | loop fusion | bytes 1048576 | tf_op jit(solution)/shard_map/slice | solution.py:22
  1.8 4.5 %collective-permute-start = (f32[128,512]{1,0:T(8,128)S(1)}, f32[128,512]{1,0:T(8,128)S(1)}, u32[]{:S(2)}, u32[]{:S(2)}) collective-permute-start(f32[128,512]{1,0:T(8,128)S(1)} %get-tuple-element.28), channel_id=1, source_target_pairs={{0,16},{16,32},{32,48},{48,64},{64,80},{80,96},{96,112},{1,17},{17... | collective-permute-start | bytes 786440 | tf_op jit(solution)/shard_map/ppermute | solution.py:24
  6.3 1.9 %collective-permute-start.1 = (f32[128,512]{1,0:T(8,128)S(1)}, f32[128,512]{1,0:T(8,128)S(1)}, u32[]{:S(2)}, u32[]{:S(2)}) collective-permute-start(f32[128,512]{1,0:T(8,128)S(1)} %get-tuple-element.29), channel_id=1, source_target_pairs={{16,0},{32,16},{48,32},{64,48},{80,64},{96,80},{112,96},{17,1},{33... | collective-permute-start | bytes 786440 | tf_op jit(solution)/shard_map/ppermute | solution.py:25
  8.9 0.7 %select_reduce_fusion.1 = f32[385]{0:T(512)S(1)} fusion(f32[4]{0:T(128)} %param.12, pred[4]{0:T(512)(128)(4,1)S(1)} %iota_compare_fusion.2), kind=kLoop, calls=%fused_computation.62 | loop fusion | flops 2695 | bytes 1560 | tf_op jit(solution)/shard_map/reduce_sum | solution.py:125
  9.7 0.7 %select_reduce_fusion = f32[768]{0:T(1024)S(1)} fusion(f32[4]{0:T(128)} %param.12, pred[4]{0:T(512)(128)(4,1)S(1)} %iota_compare_fusion.2), kind=kLoop, calls=%fused_computation.57 | loop fusion | flops 5376 | bytes 3092 | tf_op jit(solution)/shard_map/reduce_sum | solution.py:123
  10.4 0.0 copy-done.1
  10.4 0.0 copy-start.4
  10.4 0.2 fusion.52
  10.6 0.0 copy-done.7
  10.6 13.9 %all-gather.1 = f32[8,34,256]{2,1,0:T(8,128)S(1)} all-gather(f32[1,34,256]{2,1,0:T(8,128)S(1)} %maximum_bitcast_fusion), channel_id=2, replica_groups=mesh['tile'=8,'orient'=16] {'tile'}, dimensions={0}, use_global_device_ids=true | all-gather | bytes 313344 | tf_op jit(solution)/shard_map/all_gather | solution.py:72
  24.6 0.2 fusion.26
  24.8 0.0 copy-start.6
  24.8 0.1 multiply_reduce_fusion.2
  24.9 0.2 fusion.24
  25.1 0.2 fusion.30
  25.3 0.2 fusion.28
  25.6 0.0 copy-done.4
  25.6 0.9 %fusion.56 = f32[256,768]{1,0:T(8,128)S(1)} fusion(f32[256,256]{1,0:T(8,128)S(1)} %fusion.23, f32[768,256]{1,0:T(8,128)S(1)} %copy-done.4), kind=kOutput, calls=%fused_computation.102 | convolution fusion | flops 301989888 | bytes 1835008 | tf_op jit(solution)/shard_map/dot_general | solution.py:31
  26.5 0.0 copy-done.6
  26.5 1.3 %fusion.57 = f32[768,768]{1,0:T(8,128)S(1)} fusion(f32[256,768]{1,0:T(8,128)S(1)} %fusion.56, f32[256,768]{1,0:T(8,128)S(1)} %copy-done.6), kind=kOutput, calls=%fused_computation.103 | convolution fusion | flops 905969664 | bytes 3932160 | tf_op jit(solution)/shard_map/dot_general | solution.py:31
  27.8 0.0 copy-start.8
  27.8 0.1 slice.144
  27.9 0.2 add_negate_fusion
  28.1 0.0 collective-permute-done
  28.2 0.0 collective-permute-done.1
  28.2 1.3 %copy-done.8 = f32[768,768]{1,0:T(8,128)S(1)} copy-done((f32[768,768]{1,0:T(8,128)S(1)}, f32[768,768]{1,0:T(8,128)}, u32[]{:S(2)}) %copy-start.8) | copy-done | bytes 2359320
  29.5 0.0 copy-start.2
  29.5 4.1 %fusion.10 = f32[512,768]{1,0:T(8,128)S(1)} fusion(f32[768,768]{1,0:T(8,128)S(1)} %copy-done.8, f32[128,512]{1,0:T(8,128)S(1)} %collective-permute-done.1, f32[512,512]{1,0:T(8,128)S(1)} %copy-done.1, f32[128,512]{1,0:T(8,128)S(1)} %collective-permute-done, f32[512]{0:T(512)S(1)} %bitcast.47, f32[512]{0:T(512)S(1)} %bitcast.46, pred[768]{0:T(1024)(128)(4,1)S(1)} %fusion.39), kind=kOutput, calls=%fused_computation.12 | convolution fusion | flops 1813905408 | bytes 5509888 | tf_op jit(solution)/shard_map/dot_general | solution.py:31
  33.6 0.0 copy-done.2
  33.6 2.5 %fusion.55 = f32[768,768]{1,0:T(8,128)S(1)} fusion(f32[512,768]{1,0:T(8,128)S(1)} %fusion.10, f32[512,768]{1,0:T(8,128)S(1)} %copy-done.2), kind=kOutput, calls=%fused_computation.101 | convolution fusion | flops 1811939328 | bytes 5505024 | tf_op jit(solution)/shard_map/dot_general | solution.py:31
  36.1 0.1 slice.141
  36.2 2.4 %add_multiply_fusion.1 = (f32[385,383]{1,0:T(8,128)S(1)}, f32[385,383]{1,0:T(8,128)S(1)}, f32[385,383]{1,0:T(8,128)S(1)}, f32[385,383]{1,0:T(8,128)S(1)}, f32[385,383]{1,0:T(8,128)S(1)}, /*index=5*/f32[385,383]{1,0:T(8,128)S(1)}) fusion(f32[385,768]{1,0:T(8,128)S(1)} %add_negate_fusion, f32[768,768]{1,0:T(8,128)S(1)} %fusion.55, f32[768,768]{1,0:T(8,128)S(1)} %fusion.57, ...), kind=kLoop, calls=%fused_computation.42 | loop fusion | flops 2359280 | bytes 8841172 | tf_op jit(solution)/shard_map/mul | solution.py:139
  38.6 0.0 copy-start
  38.7 1.2 %add_multiply_fusion = (f32[385,385]{1,0:T(8,128)S(1)}, f32[385,385]{1,0:T(8,128)S(1)}) fusion(f32[385,768]{1,0:T(8,128)S(1)} %add_negate_fusion, f32[385,383]{1,0:T(8,128)S(1)} %get-tuple-element.26, f32[768,768]{1,0:T(8,128)S(1)} %fusion.55, f32[385,383]{1,0:T(8,128)S(1)} %get-tuple-element.27, f32[768,768]{1,0:T(8,128)S(1)} %fusion.57, ...), kind=kLoop, calls=%fused_computation.30 | loop fusion | flops 2371600 | bytes 7676932 | tf_op jit(solution)/shard_map/mul | solution.py:139
  39.9 0.7 copy-done
  40.5 4.0 %fusion = f32[770,1024]{1,0:T(8,128)S(1)} fusion(f32[768,1024]{1,0:T(8,128)S(1)} %copy-done, f32[385,383]{1,0:T(8,128)S(1)} %get-tuple-element.21, f32[385,385]{1,0:T(8,128)S(1)} %get-tuple-element.19, f32[385,383]{1,0:T(8,128)S(1)} %get-tuple-element.20, f32[385,385]{1,0:T(8,128)S(1)} %get-tuple-element.18), kind=kOutput, calls=%fused_computation | convolution fusion | flops 3635089920 | bytes 8665088 | tf_op jit(solution)/shard_map/dot_general | solution.py:31
  44.5 0.0 copy-start.3
  44.5 0.2 fusion.53
  44.7 1.0 %copy-done.3 = f32[512,385]{1,0:T(8,128)S(1)} copy-done((f32[512,385]{1,0:T(8,128)S(1)}, f32[512,385]{1,0:T(8,128)}, u32[]{:S(2)}) %copy-start.3) | copy-done | bytes 788504
  45.7 0.0 copy-start.5
  45.7 1.0 %fusion.14 = f32[512,512]{0,1:T(8,128)S(1)} fusion(f32[512,385]{1,0:T(8,128)S(1)} %copy-done.3, f32[770,1024]{1,0:T(8,128)S(1)} %fusion), kind=kOutput, calls=%fused_computation.25 | convolution fusion | flops 605749760 | bytes 3702784 | tf_op jit(solution)/shard_map/dot_general | solution.py:31
  46.8 0.1 copy-done.5
  46.9 1.1 %convolution_add_fusion = f32[512,512]{0,1:T(8,128)S(1)} fusion(f32[512,512]{0,1:T(8,128)S(1)} %fusion.14, f32[512,383]{1,0:T(8,128)S(1)} %copy-done.5, f32[385,512]{1,0:T(8,128)S(1)} %get-tuple-element.23, f32[385,512]{1,0:T(8,128)S(1)} %get-tuple-element.22), kind=kOutput, calls=%fused_computation.13 | convolution fusion | flops 602865152 | bytes 4456448 | tf_op jit(solution)/shard_map/dot_general | solution.py:31
  48.0 24.1 %all_to_all.9 = f32[16,32,512]{2,1,0:T(8,128)S(1)} all-to-all(f32[16,32,512]{2,1,0:T(8,128)S(1)} %bitcast.42), channel_id=1, replica_groups=mesh['tile'=8,'orient'=16] {'orient'}, dimensions={0} | all-to-all | bytes 2097152 | tf_op jit(solution)/shard_map/all_to_all | solution.py:158
  72.0 0.9 %multiply_reduce_fusion = (f32[32,512]{1,0:T(8,128)}, f32[32,512]{1,0:T(8,128)}, f32[32,512]{1,0:T(8,128)S(1)}, f32[32,512]{1,0:T(8,128)S(1)}) fusion(f32[16,32,512]{2,1,0:T(8,128)S(1)} %all_to_all.9), kind=kLoop, calls=%fused_computation.11 | loop fusion | flops 1736704 | bytes 1310720 | tf_op jit(solution)/shard_map/reduce | solution.py:170
  73.0 0.7 multiply_subtract_fusion
  (17 shorter events, 0.3 us)
Async XLA Ops:
  0.6 9.8 %copy-start.1 = (f32[512,512]{1,0:T(8,128)S(1)}, f32[512,512]{1,0:T(8,128)}, u32[]{:S(2)}) copy-start(f32[512,512]{1,0:T(8,128)} %param.10) | copy-start | bytes 3145732
  0.6 10.0 %copy-start.7 = (f32[1,32,256]{2,1,0:T(8,128)S(1)}, f32[1,32,256]{2,1,0:T(8,128)}, u32[]{:S(2)}) copy-start(f32[1,32,256]{2,1,0:T(8,128)} %param.11) | copy-start | bytes 98308
  1.8 26.3 %collective-permute-start = (f32[128,512]{1,0:T(8,128)S(1)}, f32[128,512]{1,0:T(8,128)S(1)}, u32[]{:S(2)}, u32[]{:S(2)}) collective-permute-start(f32[128,512]{1,0:T(8,128)S(1)} %get-tuple-element.28), channel_id=1, source_target_pairs={{0,16},{16,32},{32,48},{48,64},{64,80},{80,96},{96,112},{1,17},{17... | collective-permute-start | bytes 786440 | tf_op jit(solution)/shard_map/ppermute | solution.py:24
  6.3 21.8 %collective-permute-start.1 = (f32[128,512]{1,0:T(8,128)S(1)}, f32[128,512]{1,0:T(8,128)S(1)}, u32[]{:S(2)}, u32[]{:S(2)}) collective-permute-start(f32[128,512]{1,0:T(8,128)S(1)} %get-tuple-element.29), channel_id=1, source_target_pairs={{16,0},{32,16},{48,32},{64,48},{80,64},{96,80},{112,96},{17,1},{33... | collective-permute-start | bytes 786440 | tf_op jit(solution)/shard_map/ppermute | solution.py:25
  10.4 15.2 %copy-start.4 = (f32[768,256]{1,0:T(8,128)S(1)}, f32[768,256]{1,0:T(8,128)}, u32[]{:S(2)}) copy-start(f32[768,256]{1,0:T(8,128)} %constant.73.clone) | copy-start | bytes 2359300
  24.8 1.7 %copy-start.6 = (f32[256,768]{1,0:T(8,128)S(1)}, f32[256,768]{1,0:T(8,128)}, u32[]{:S(2)}) copy-start(f32[256,768]{1,0:T(8,128)} %constant.75.clone) | copy-start | bytes 2359300
  27.8 1.7 %copy-start.8 = (f32[768,768]{1,0:T(8,128)S(1)}, f32[768,768]{1,0:T(8,128)}, u32[]{:S(2)}) copy-start(f32[768,768]{1,0:T(8,128)} %constant.72.clone) | copy-start | bytes 7077892
  29.5 4.2 %copy-start.2 = (f32[512,768]{1,0:T(8,128)S(1)}, f32[512,768]{1,0:T(8,128)}, u32[]{:S(2)}) copy-start(f32[512,768]{1,0:T(8,128)} %constant.74.clone) | copy-start | bytes 4718596
  38.6 1.9 %copy-start = (f32[768,1024]{1,0:T(8,128)S(1)}, f32[768,1024]{1,0:T(8,128)}, u32[]{:S(2)}) copy-start(f32[768,1024]{1,0:T(8,128)} %constant.76.clone) | copy-start | bytes 9437188
  44.5 1.2 %copy-start.3 = (f32[512,385]{1,0:T(8,128)S(1)}, f32[512,385]{1,0:T(8,128)}, u32[]{:S(2)}) copy-start(f32[512,385]{1,0:T(8,128)} %constant.92) | copy-start | bytes 2365444
  45.7 1.1 %copy-start.5 = (f32[512,383]{1,0:T(8,128)S(1)}, f32[512,383]{1,0:T(8,128)}, u32[]{:S(2)}) copy-start(f32[512,383]{1,0:T(8,128)} %constant.93) | copy-start | bytes 2353156

commit v17 on v16

--- a/solution.py
+++ b/solution.py
@@ -70,6 +70,9 @@
     square_row = lane_fold(jnp.sum(micrograph * micrograph, axis=0))
     payload = jnp.concatenate([templates[0], sum_row, square_row], axis=0)
     everything = lax.all_gather(payload, "tile")
+    defocus_values, defocus_group, everything = lax.optimization_barrier(
+        (defocus_values, defocus_group, everything)
+    )
     gathered = everything[:, :own_rows].reshape(tile_count * own_rows, tpl_width)
     ones = jnp.ones((tpl_width, tpl_width), jnp.float32)
 

time: 74.2 us -> 72.9 us (0.982)
  other arithmetic: 7.46 us -> 6.15 us
    unnamed x22 -> x24, local copies, waits for them, and re-layouts: 3.12 us -> 3.13 us
  transfers between devices with their start and end apart: 2 -> 2, of which waited for: 0 -> 0; matrix products, arithmetic and copies ran while one was open for 7% -> 5% of each run, Pallas kernels for 0% -> 0%
where the time goes in v17:
time: 72.9 us; the launch traced here: 72.4 us
  blocking collectives  37.9 us (52%)
  matrix products  15.6 us (21%)
  starting transfers between devices  6.43 us (9%)
  other arithmetic  6.15 us (8%)
  local copies, waits for them, and re-layouts  4.63 us (6%)
  between operations  1.7 us (2%)
    all_to_all x1, blocking collectives, per_device(): lax.all_to_all(scores, 'orient', 0, 0, tiled=True)  24.1 us
    dot_general x7, matrix products, product(): jnp.dot(former, latter, precision=mode, preferred_element_type=jnp.float32)  14.9 us
    all_gather x1, blocking collectives, per_device(): everything = lax.all_gather(payload, 'tile')  13.7 us
    ppermute x1, starting transfers between devices, padded(): before = lax.ppermute(last, axis, up)  4.51 us
    mul x2, other arithmetic, multiply(): (spec_real * template_real + spec_imag * template_imag) * weight  3.63 us
    unnamed x24, local copies, waits for them, and re-layouts  3.13 us
    ppermute x1, starting transfers between devices, padded(): after = lax.ppermute(initial, axis, down)  1.92 us
  transfers between devices with their start and end apart: 2, of which 0 were waited for; matrix products, arithmetic and copies ran while one was open for 5% of the time, Pallas kernels for 0%

profile of v17, /device:TPU:1, one launch (start us, length us, event | category | flops | bytes accessed | tf_op | source)
XLA Modules:
  0.0 72.4 jit_solution(5715470540114097281)
XLA Ops:
  0.6 0.0 copy-start.1
  0.6 0.0 copy-start.7
  0.7 0.0 copy-start.8
  0.7 1.1 %fusion.54 = (f32[128,512]{1,0:T(8,128)S(1)}, f32[128,512]{1,0:T(8,128)S(1)}) fusion(f32[512,512]{1,0:T(8,128)} %param.10), kind=kLoop, calls=%fused_computation.100 | loop fusion | bytes 1048576 | tf_op jit(solution)/shard_map/slice | solution.py:22
  1.8 4.5 %collective-permute-start = (f32[128,512]{1,0:T(8,128)S(1)}, f32[128,512]{1,0:T(8,128)S(1)}, u32[]{:S(2)}, u32[]{:S(2)}) collective-permute-start(f32[128,512]{1,0:T(8,128)S(1)} %get-tuple-element.34), channel_id=1, source_target_pairs={{0,16},{16,32},{32,48},{48,64},{64,80},{80,96},{96,112},{1,17},{17... | collective-permute-start | bytes 786440 | tf_op jit(solution)/shard_map/ppermute | solution.py:24
  6.3 1.9 %collective-permute-start.1 = (f32[128,512]{1,0:T(8,128)S(1)}, f32[128,512]{1,0:T(8,128)S(1)}, u32[]{:S(2)}, u32[]{:S(2)}) collective-permute-start(f32[128,512]{1,0:T(8,128)S(1)} %get-tuple-element.35), channel_id=1, source_target_pairs={{16,0},{32,16},{48,32},{64,48},{80,64},{96,80},{112,96},{17,1},{33... | collective-permute-start | bytes 786440 | tf_op jit(solution)/shard_map/ppermute | solution.py:25
  8.3 0.0 copy-done.1
  8.3 0.0 copy-start.4
  8.3 0.2 fusion.52
  9.2 0.0 copy-done.7
  9.2 13.7 %all-gather.1 = f32[8,34,256]{2,1,0:T(8,128)S(1)} all-gather(f32[1,34,256]{2,1,0:T(8,128)S(1)} %maximum_bitcast_fusion), channel_id=2, replica_groups=mesh['tile'=8,'orient'=16] {'tile'}, dimensions={0}, use_global_device_ids=true | all-gather | bytes 313344 | tf_op jit(solution)/shard_map/all_gather | solution.py:72
  23.0 0.0 copy-done.8
  23.0 0.1 select_reduce_fusion.1
  23.1 0.1 select_reduce_fusion
  23.2 0.2 fusion.26
  23.4 0.0 copy-start.6
  23.4 0.1 multiply_reduce_fusion.2
  23.5 0.2 fusion.24
  23.7 0.2 fusion.30
  23.9 0.2 fusion.28
  24.2 0.0 copy-done.4
  24.2 0.9 %fusion.56 = f32[256,768]{1,0:T(8,128)S(1)} fusion(f32[256,256]{1,0:T(8,128)S(1)} %fusion.23, f32[768,256]{1,0:T(8,128)S(1)} %copy-done.4), kind=kOutput, calls=%fused_computation.102 | convolution fusion | flops 301989888 | bytes 1835008 | tf_op jit(solution)/shard_map/dot_general | solution.py:31
  25.1 0.0 copy-done.6
  25.1 1.3 %fusion.57 = f32[768,768]{1,0:T(8,128)S(1)} fusion(f32[256,768]{1,0:T(8,128)S(1)} %fusion.56, f32[256,768]{1,0:T(8,128)S(1)} %copy-done.6), kind=kOutput, calls=%fused_computation.103 | convolution fusion | flops 905969664 | bytes 3932160 | tf_op jit(solution)/shard_map/dot_general | solution.py:31
  26.5 0.0 copy-start.9
  26.5 0.1 slice.141
  26.6 0.2 add_negate_fusion
  26.8 0.0 collective-permute-done
  26.8 0.0 collective-permute-done.1
  26.8 1.3 %copy-done.9 = f32[768,768]{1,0:T(8,128)S(1)} copy-done((f32[768,768]{1,0:T(8,128)S(1)}, f32[768,768]{1,0:T(8,128)}, u32[]{:S(2)}) %copy-start.9) | copy-done | bytes 2359320
  28.1 0.0 copy-start.2
  28.1 4.1 %fusion.10 = f32[512,768]{1,0:T(8,128)S(1)} fusion(f32[768,768]{1,0:T(8,128)S(1)} %copy-done.9, f32[128,512]{1,0:T(8,128)S(1)} %collective-permute-done.1, f32[512,512]{1,0:T(8,128)S(1)} %copy-done.1, f32[128,512]{1,0:T(8,128)S(1)} %collective-permute-done, f32[512]{0:T(512)S(1)} %bitcast.47, f32[512]{0:T(512)S(1)} %bitcast.46, pred[768]{0:T(1024)(128)(4,1)S(1)} %fusion.39), kind=kOutput, calls=%fused_computation.12 | convolution fusion | flops 1813905408 | bytes 5509888 | tf_op jit(solution)/shard_map/dot_general | solution.py:31
  32.3 0.0 copy-done.2
  32.3 2.5 %fusion.55 = f32[768,768]{1,0:T(8,128)S(1)} fusion(f32[512,768]{1,0:T(8,128)S(1)} %fusion.10, f32[512,768]{1,0:T(8,128)S(1)} %copy-done.2), kind=kOutput, calls=%fused_computation.101 | convolution fusion | flops 1811939328 | bytes 5505024 | tf_op jit(solution)/shard_map/dot_general | solution.py:31
  34.8 0.1 slice.139
  34.9 2.4 %add_multiply_fusion.1 = (f32[385,383]{1,0:T(8,128)S(1)}, f32[385,383]{1,0:T(8,128)S(1)}, f32[385,383]{1,0:T(8,128)S(1)}, f32[385,383]{1,0:T(8,128)S(1)}, f32[385,383]{1,0:T(8,128)S(1)}, /*index=5*/f32[385,383]{1,0:T(8,128)S(1)}) fusion(f32[385,768]{1,0:T(8,128)S(1)} %add_negate_fusion, f32[768,768]{1,0:T(8,128)S(1)} %fusion.55, f32[768,768]{1,0:T(8,128)S(1)} %fusion.57, ...), kind=kLoop, calls=%fused_computation.42 | loop fusion | flops 2359280 | bytes 8841172 | tf_op jit(solution)/shard_map/mul | solution.py:142
  37.3 0.0 copy-start
  37.3 1.2 %add_multiply_fusion = (f32[385,385]{1,0:T(8,128)S(1)}, f32[385,385]{1,0:T(8,128)S(1)}) fusion(f32[385,768]{1,0:T(8,128)S(1)} %add_negate_fusion, f32[385,383]{1,0:T(8,128)S(1)} %get-tuple-element.32, f32[768,768]{1,0:T(8,128)S(1)} %fusion.55, f32[385,383]{1,0:T(8,128)S(1)} %get-tuple-element.33, f32[768,768]{1,0:T(8,128)S(1)} %fusion.57, ...), kind=kLoop, calls=%fused_computation.30 | loop fusion | flops 2371600 | bytes 7676932 | tf_op jit(solution)/shard_map/mul | solution.py:142
  38.5 0.7 copy-done
  39.2 4.0 %fusion = f32[770,1024]{1,0:T(8,128)S(1)} fusion(f32[768,1024]{1,0:T(8,128)S(1)} %copy-done, f32[385,383]{1,0:T(8,128)S(1)} %get-tuple-element.27, f32[385,385]{1,0:T(8,128)S(1)} %get-tuple-element.25, f32[385,383]{1,0:T(8,128)S(1)} %get-tuple-element.26, f32[385,385]{1,0:T(8,128)S(1)} %get-tuple-element.24), kind=kOutput, calls=%fused_computation | convolution fusion | flops 3635089920 | bytes 8665088 | tf_op jit(solution)/shard_map/dot_general | solution.py:31
  43.2 0.0 copy-start.3
  43.2 0.2 fusion.53
  43.4 1.0 %copy-done.3 = f32[512,385]{1,0:T(8,128)S(1)} copy-done((f32[512,385]{1,0:T(8,128)S(1)}, f32[512,385]{1,0:T(8,128)}, u32[]{:S(2)}) %copy-start.3) | copy-done | bytes 788504
  44.4 0.0 copy-start.5
  44.4 1.0 %fusion.14 = f32[512,512]{0,1:T(8,128)S(1)} fusion(f32[512,385]{1,0:T(8,128)S(1)} %copy-done.3, f32[770,1024]{1,0:T(8,128)S(1)} %fusion), kind=kOutput, calls=%fused_computation.25 | convolution fusion | flops 605749760 | bytes 3702784 | tf_op jit(solution)/shard_map/dot_general | solution.py:31
  45.5 0.1 copy-done.5
  45.5 1.1 %convolution_add_fusion = f32[512,512]{0,1:T(8,128)S(1)} fusion(f32[512,512]{0,1:T(8,128)S(1)} %fusion.14, f32[512,383]{1,0:T(8,128)S(1)} %copy-done.5, f32[385,512]{1,0:T(8,128)S(1)} %get-tuple-element.29, f32[385,512]{1,0:T(8,128)S(1)} %get-tuple-element.28), kind=kOutput, calls=%fused_computation.13 | convolution fusion | flops 602865152 | bytes 4456448 | tf_op jit(solution)/shard_map/dot_general | solution.py:31
  46.6 24.1 %all_to_all.9 = f32[16,32,512]{2,1,0:T(8,128)S(1)} all-to-all(f32[16,32,512]{2,1,0:T(8,128)S(1)} %bitcast.42), channel_id=1, replica_groups=mesh['tile'=8,'orient'=16] {'orient'}, dimensions={0} | all-to-all | bytes 2097152 | tf_op jit(solution)/shard_map/all_to_all | solution.py:161
  70.8 0.9 %multiply_reduce_fusion = (f32[32,512]{1,0:T(8,128)}, f32[32,512]{1,0:T(8,128)}, f32[32,512]{1,0:T(8,128)S(1)}, f32[32,512]{1,0:T(8,128)S(1)}) fusion(f32[16,32,512]{2,1,0:T(8,128)S(1)} %all_to_all.9), kind=kLoop, calls=%fused_computation.11 | loop fusion | flops 1736704 | bytes 1310720 | tf_op jit(solution)/shard_map/reduce | solution.py:173
  71.7 0.7 multiply_subtract_fusion
  (17 shorter events, 0.3 us)
Async XLA Ops:
  0.6 7.6 %copy-start.1 = (f32[512,512]{1,0:T(8,128)S(1)}, f32[512,512]{1,0:T(8,128)}, u32[]{:S(2)}) copy-start(f32[512,512]{1,0:T(8,128)} %param.10) | copy-start | bytes 3145732
  0.6 8.6 %copy-start.7 = (f32[1,32,256]{2,1,0:T(8,128)S(1)}, f32[1,32,256]{2,1,0:T(8,128)}, u32[]{:S(2)}) copy-start(f32[1,32,256]{2,1,0:T(8,128)} %param.11) | copy-start | bytes 98308
  0.7 22.4 %copy-start.8 = (f32[4]{0:T(128)S(1)}, f32[4]{0:T(128)}, u32[]{:S(2)}) copy-start(f32[4]{0:T(128)} %param.12) | copy-start | bytes 52
  1.8 25.0 %collective-permute-start = (f32[128,512]{1,0:T(8,128)S(1)}, f32[128,512]{1,0:T(8,128)S(1)}, u32[]{:S(2)}, u32[]{:S(2)}) collective-permute-start(f32[128,512]{1,0:T(8,128)S(1)} %get-tuple-element.34), channel_id=1, source_target_pairs={{0,16},{16,32},{32,48},{48,64},{64,80},{80,96},{96,112},{1,17},{17... | collective-permute-start | bytes 786440 | tf_op jit(solution)/shard_map/ppermute | solution.py:24
  6.3 20.5 %collective-permute-start.1 = (f32[128,512]{1,0:T(8,128)S(1)}, f32[128,512]{1,0:T(8,128)S(1)}, u32[]{:S(2)}, u32[]{:S(2)}) collective-permute-start(f32[128,512]{1,0:T(8,128)S(1)} %get-tuple-element.35), channel_id=1, source_target_pairs={{16,0},{32,16},{48,32},{64,48},{80,64},{96,80},{112,96},{17,1},{33... | collective-permute-start | bytes 786440 | tf_op jit(solution)/shard_map/ppermute | solution.py:25
  8.3 15.9 %copy-start.4 = (f32[768,256]{1,0:T(8,128)S(1)}, f32[768,256]{1,0:T(8,128)}, u32[]{:S(2)}) copy-start(f32[768,256]{1,0:T(8,128)} %constant.73.clone) | copy-start | bytes 2359300
  23.4 1.7 %copy-start.6 = (f32[256,768]{1,0:T(8,128)S(1)}, f32[256,768]{1,0:T(8,128)}, u32[]{:S(2)}) copy-start(f32[256,768]{1,0:T(8,128)} %constant.75.clone) | copy-start | bytes 2359300
  26.5 1.7 %copy-start.9 = (f32[768,768]{1,0:T(8,128)S(1)}, f32[768,768]{1,0:T(8,128)}, u32[]{:S(2)}) copy-start(f32[768,768]{1,0:T(8,128)} %constant.72.clone) | copy-start | bytes 7077892
  28.1 4.2 %copy-start.2 = (f32[512,768]{1,0:T(8,128)S(1)}, f32[512,768]{1,0:T(8,128)}, u32[]{:S(2)}) copy-start(f32[512,768]{1,0:T(8,128)} %constant.74.clone) | copy-start | bytes 4718596
  37.3 1.9 %copy-start = (f32[768,1024]{1,0:T(8,128)S(1)}, f32[768,1024]{1,0:T(8,128)}, u32[]{:S(2)}) copy-start(f32[768,1024]{1,0:T(8,128)} %constant.76.clone) | copy-start | bytes 9437188
  43.2 1.2 %copy-start.3 = (f32[512,385]{1,0:T(8,128)S(1)}, f32[512,385]{1,0:T(8,128)}, u32[]{:S(2)}) copy-start(f32[512,385]{1,0:T(8,128)} %constant.92) | copy-start | bytes 2365444
  44.4 1.1 %copy-start.5 = (f32[512,383]{1,0:T(8,128)S(1)}, f32[512,383]{1,0:T(8,128)}, u32[]{:S(2)}) copy-start(f32[512,383]{1,0:T(8,128)} %constant.93) | copy-start | bytes 2353156

commit v18 on v17

--- a/solution.py
+++ b/solution.py
@@ -154,7 +154,10 @@
     pi_c, pi_s = inner[h:, :tile_width], inner[h:, tile_width:]
     back_real = pr_c - pi_s
     back_imag = pr_s + pi_c
-    scores = product(final, jnp.concatenate([back_real, back_imag[1:h - 1]], axis=0))
+    split = h - 1
+    slot = lax.broadcasted_iota(jnp.int32, (split, 1), 0) == 0
+    tail = jnp.where(slot, back_real[split:], jnp.pad(back_imag[1:split], ((1, 0), (0, 0))))
+    scores = product(final, jnp.concatenate([back_real[:split], tail], axis=0))
 
     orient_count = lax.axis_size("orient")
     share_rows = tile_rows // orient_count

time: 72.9 us -> 75.1 us (1.030)
  matrix products: 15.6 us -> 16.7 us
    dot_general x7, matrix products: 14.9 us -> 16 us  [product(): jnp.dot(former, latter, precision=mode, preferred_element_type=jnp.float32)]
where the time goes in v18:
time: 75.1 us; the launch traced here: 74.6 us
  blocking collectives  37.9 us (50%)
  matrix products  16.7 us (22%)
  other arithmetic  6.71 us (9%)
  starting transfers between devices  6.56 us (9%)
  local copies, waits for them, and re-layouts  4.99 us (7%)
  between operations  1.66 us (2%)
    all_to_all x1, blocking collectives, per_device(): lax.all_to_all(scores, 'orient', 0, 0, tiled=True)  24.1 us
    dot_general x7, matrix products, product(): jnp.dot(former, latter, precision=mode, preferred_element_type=jnp.float32)  16 us
    all_gather x1, blocking collectives, per_device(): everything = lax.all_gather(payload, 'tile')  13.8 us
    ppermute x1, starting transfers between devices, padded(): before = lax.ppermute(last, axis, up)  4.51 us
    unnamed x24, local copies, waits for them, and re-layouts  3.68 us
    mul x2, other arithmetic, multiply(): (spec_real * template_real + spec_imag * template_imag) * weight  3.64 us
    ppermute x1, starting transfers between devices, padded(): after = lax.ppermute(initial, axis, down)  2.05 us
  transfers between devices with their start and end apart: 2, of which 0 were waited for; matrix products, arithmetic and copies ran while one was open for 5% of the time, Pallas kernels for 0%

profile of v18, /device:TPU:1, one launch (start us, length us, event | category | flops | bytes accessed | tf_op | source)
XLA Modules:
  0.0 74.6 jit_solution(9755514002810883550)
XLA Ops:
  0.6 0.0 copy-start.1
  0.6 0.0 copy-start.7
  0.7 0.0 copy-start.8
  0.7 1.1 %fusion.58 = (f32[128,512]{1,0:T(8,128)S(1)}, f32[128,512]{1,0:T(8,128)S(1)}) fusion(f32[512,512]{1,0:T(8,128)} %param.10), kind=kLoop, calls=%fused_computation.105 | loop fusion | bytes 1048576 | tf_op jit(solution)/shard_map/slice | solution.py:22
  1.8 4.5 %collective-permute-start = (f32[128,512]{1,0:T(8,128)S(1)}, f32[128,512]{1,0:T(8,128)}, u32[]{:S(2)}, u32[]{:S(2)}) collective-permute-start(f32[128,512]{1,0:T(8,128)S(1)} %get-tuple-element.35), channel_id=1, source_target_pairs={{0,16},{16,32},{32,48},{48,64},{64,80},{80,96},{96,112},{1,17},{17... | collective-permute-start | bytes 786440 | tf_op jit(solution)/shard_map/ppermute | solution.py:24
  6.3 0.0 copy-start.4
  6.3 2.1 %collective-permute-start.1 = (f32[128,512]{1,0:T(8,128)S(1)}, f32[128,512]{1,0:T(8,128)}, u32[]{:S(2)}, u32[]{:S(2)}) collective-permute-start(f32[128,512]{1,0:T(8,128)S(1)} %get-tuple-element.36), channel_id=1, source_target_pairs={{16,0},{32,16},{48,32},{64,48},{80,64},{96,80},{112,96},{17,1},{33... | collective-permute-start | bytes 786440 | tf_op jit(solution)/shard_map/ppermute | solution.py:25
  8.4 0.0 copy-done.1
  8.4 0.2 fusion.56
  8.6 0.0 copy-done.7
  8.6 13.8 %all-gather.1 = f32[8,34,256]{2,1,0:T(8,128)S(1)} all-gather(f32[1,34,256]{2,1,0:T(8,128)S(1)} %maximum_bitcast_fusion), channel_id=2, replica_groups=mesh['tile'=8,'orient'=16] {'tile'}, dimensions={0}, use_global_device_ids=true | all-gather | bytes 313344 | tf_op jit(solution)/shard_map/all_gather | solution.py:72
  23.2 0.0 copy-done.8
  23.2 0.1 select_reduce_fusion
  23.3 0.1 select_reduce_fusion.1
  23.4 0.2 fusion.29
  23.6 0.0 copy-start.6
  23.6 0.1 multiply_reduce_fusion.2
  23.6 0.2 fusion.27
  23.8 0.2 fusion.33
  24.0 0.2 fusion.31
  24.4 0.0 copy-done.4
  24.4 0.9 %fusion.60 = f32[256,768]{1,0:T(8,128)S(1)} fusion(f32[256,256]{1,0:T(8,128)S(1)} %fusion.26, f32[768,256]{1,0:T(8,128)S(1)} %copy-done.4), kind=kOutput, calls=%fused_computation.107 | convolution fusion | flops 301989888 | bytes 1835008 | tf_op jit(solution)/shard_map/dot_general | solution.py:31
  25.2 0.0 copy-done.6
  25.2 1.3 %fusion.61 = f32[768,768]{1,0:T(8,128)S(1)} fusion(f32[256,768]{1,0:T(8,128)S(1)} %fusion.60, f32[256,768]{1,0:T(8,128)S(1)} %copy-done.6), kind=kOutput, calls=%fused_computation.108 | convolution fusion | flops 905969664 | bytes 3932160 | tf_op jit(solution)/shard_map/dot_general | solution.py:31
  26.6 0.0 copy-start.9
  26.6 0.1 slice.149
  26.7 0.2 add_negate_fusion
  27.0 0.0 collective-permute-done
  27.0 0.0 collective-permute-done.1
  27.0 1.3 %copy-done.9 = f32[768,768]{1,0:T(8,128)S(1)} copy-done((f32[768,768]{1,0:T(8,128)S(1)}, f32[768,768]{1,0:T(8,128)}, u32[]{:S(2)}) %copy-start.9) | copy-done | bytes 2359320
  28.3 0.0 copy-start.2
  28.3 5.3 %fusion.10 = f32[512,768]{1,0:T(8,128)S(1)} fusion(f32[768,768]{1,0:T(8,128)S(1)} %copy-done.9, f32[128,512]{1,0:T(8,128)} %collective-permute-done.1, f32[512,512]{1,0:T(8,128)S(1)} %copy-done.1, f32[128,512]{1,0:T(8,128)} %collective-permute-done, f32[512]{0:T(512)S(1)} %bitcast.49, f32[512]{0:T(512)S(1)} %bitcast.48, pred[768]{0:T(1024)(128)(4,1)S(1)} %fusion.42), kind=kOutput, calls=%fused_computation.12 | convolution fusion | flops 1813905408 | bytes 5509888 | tf_op jit(solution)/shard_map/dot_general | solution.py:31
  33.6 0.0 copy-done.2
  33.6 2.5 %fusion.59 = f32[768,768]{1,0:T(8,128)S(1)} fusion(f32[512,768]{1,0:T(8,128)S(1)} %fusion.10, f32[512,768]{1,0:T(8,128)S(1)} %copy-done.2), kind=kOutput, calls=%fused_computation.106 | convolution fusion | flops 1811939328 | bytes 5505024 | tf_op jit(solution)/shard_map/dot_general | solution.py:31
  36.1 0.1 slice.147
  36.2 2.4 %add_multiply_fusion.1 = (f32[385,383]{1,0:T(8,128)S(1)}, f32[385,383]{1,0:T(8,128)S(1)}, f32[385,383]{1,0:T(8,128)S(1)}, f32[385,383]{1,0:T(8,128)S(1)}, f32[385,383]{1,0:T(8,128)S(1)}, /*index=5*/f32[385,383]{1,0:T(8,128)S(1)}) fusion(f32[385,768]{1,0:T(8,128)S(1)} %add_negate_fusion, f32[768,768]{1,0:T(8,128)S(1)} %fusion.59, f32[768,768]{1,0:T(8,128)S(1)} %fusion.61, ...), kind=kLoop, calls=%fused_computation.43 | loop fusion | flops 2359280 | bytes 8841172 | tf_op jit(solution)/shard_map/mul | solution.py:142
  38.6 0.0 copy-start
  38.6 1.2 %add_multiply_fusion = (f32[385,385]{1,0:T(8,128)S(1)}, f32[385,385]{1,0:T(8,128)S(1)}) fusion(f32[385,768]{1,0:T(8,128)S(1)} %add_negate_fusion, f32[385,383]{1,0:T(8,128)S(1)} %get-tuple-element.33, f32[768,768]{1,0:T(8,128)S(1)} %fusion.59, f32[385,383]{1,0:T(8,128)S(1)} %get-tuple-element.34, f32[768,768]{1,0:T(8,128)S(1)} %fusion.61, ...), kind=kLoop, calls=%fused_computation.28 | loop fusion | flops 2371600 | bytes 7676932 | tf_op jit(solution)/shard_map/mul | solution.py:142
  39.8 0.7 copy-done
  40.5 4.0 %fusion = f32[770,1024]{1,0:T(8,128)S(1)} fusion(f32[768,1024]{1,0:T(8,128)S(1)} %copy-done, f32[385,383]{1,0:T(8,128)S(1)} %get-tuple-element.27, f32[385,385]{1,0:T(8,128)S(1)} %get-tuple-element.25, f32[385,383]{1,0:T(8,128)S(1)} %get-tuple-element.26, f32[385,385]{1,0:T(8,128)S(1)} %get-tuple-element.24), kind=kOutput, calls=%fused_computation | convolution fusion | flops 3635089920 | bytes 8665088 | tf_op jit(solution)/shard_map/dot_general | solution.py:31
  44.5 0.0 copy-start.5
  44.5 0.4 fusion.57
  44.9 0.7 copy-done.5
  45.6 1.0 %fusion.14 = f32[512,512]{0,1:T(8,128)S(1)} fusion(f32[512,384]{1,0:T(8,128)S(1)} %copy-done.5, f32[385,512]{1,0:T(8,128)S(1)} %get-tuple-element.29), kind=kOutput, calls=%fused_computation.30 | convolution fusion | flops 603979776 | bytes 2621440 | tf_op jit(solution)/shard_map/dot_general | solution.py:31
  46.6 0.0 copy-start.3
  46.6 0.2 slice_add_fusion
  46.8 0.9 %copy-done.3 = f32[512,384]{1,0:T(8,128)S(1)} copy-done((f32[512,384]{1,0:T(8,128)S(1)}, f32[512,384]{1,0:T(8,128)}, u32[]{:S(2)}) %copy-start.3) | copy-done | bytes 786456
  47.8 1.1 %convolution_add_fusion = f32[512,512]{0,1:T(8,128)S(1)} fusion(f32[512,512]{0,1:T(8,128)S(1)} %fusion.14, f32[512,384]{1,0:T(8,128)S(1)} %copy-done.3, f32[383,512]{1,0:T(8,128)S(1)} %slice_add_fusion, f32[512]{0:T(512)S(1)} %bitcast.45, pred[384]{0:T(512)(128)(4,1)S(1)} %iota_compare_fusion.2), kind=kOutput, calls=%fused_computation.13 | convolution fusion | flops 604438528 | bytes 3670400 | tf_op jit(solution)/shard_map/dot_general | solution.py:31
  48.9 24.1 %all_to_all.9 = f32[16,32,512]{2,1,0:T(8,128)S(1)} all-to-all(f32[16,32,512]{2,1,0:T(8,128)S(1)} %bitcast.43), channel_id=1, replica_groups=mesh['tile'=8,'orient'=16] {'orient'}, dimensions={0} | all-to-all | bytes 2097152 | tf_op jit(solution)/shard_map/all_to_all | solution.py:164
  73.0 0.9 %multiply_reduce_fusion = (f32[32,512]{1,0:T(8,128)}, f32[32,512]{1,0:T(8,128)}, f32[32,512]{1,0:T(8,128)S(1)}, f32[32,512]{1,0:T(8,128)S(1)}) fusion(f32[16,32,512]{2,1,0:T(8,128)S(1)} %all_to_all.9), kind=kLoop, calls=%fused_computation.11 | loop fusion | flops 1736704 | bytes 1310720 | tf_op jit(solution)/shard_map/reduce | solution.py:176
  73.9 0.7 multiply_subtract_fusion
  (19 shorter events, 0.3 us)
Async XLA Ops:
  0.6 7.8 %copy-start.1 = (f32[512,512]{1,0:T(8,128)S(1)}, f32[512,512]{1,0:T(8,128)}, u32[]{:S(2)}) copy-start(f32[512,512]{1,0:T(8,128)} %param.10) | copy-start | bytes 3145732
  0.6 8.0 %copy-start.7 = (f32[1,32,256]{2,1,0:T(8,128)S(1)}, f32[1,32,256]{2,1,0:T(8,128)}, u32[]{:S(2)}) copy-start(f32[1,32,256]{2,1,0:T(8,128)} %param.11) | copy-start | bytes 98308
  0.7 22.5 %copy-start.8 = (f32[4]{0:T(128)S(1)}, f32[4]{0:T(128)}, u32[]{:S(2)}) copy-start(f32[4]{0:T(128)} %param.12) | copy-start | bytes 52
  1.8 25.2 %collective-permute-start = (f32[128,512]{1,0:T(8,128)S(1)}, f32[128,512]{1,0:T(8,128)}, u32[]{:S(2)}, u32[]{:S(2)}) collective-permute-start(f32[128,512]{1,0:T(8,128)S(1)} %get-tuple-element.35), channel_id=1, source_target_pairs={{0,16},{16,32},{32,48},{48,64},{64,80},{80,96},{96,112},{1,17},{17... | collective-permute-start | bytes 786440 | tf_op jit(solution)/shard_map/ppermute | solution.py:24
  6.3 18.0 %copy-start.4 = (f32[768,256]{1,0:T(8,128)S(1)}, f32[768,256]{1,0:T(8,128)}, u32[]{:S(2)}) copy-start(f32[768,256]{1,0:T(8,128)} %constant.74.clone) | copy-start | bytes 2359300
  6.3 20.7 %collective-permute-start.1 = (f32[128,512]{1,0:T(8,128)S(1)}, f32[128,512]{1,0:T(8,128)}, u32[]{:S(2)}, u32[]{:S(2)}) collective-permute-start(f32[128,512]{1,0:T(8,128)S(1)} %get-tuple-element.36), channel_id=1, source_target_pairs={{16,0},{32,16},{48,32},{64,48},{80,64},{96,80},{112,96},{17,1},{33... | collective-permute-start | bytes 786440 | tf_op jit(solution)/shard_map/ppermute | solution.py:25
  23.6 1.7 %copy-start.6 = (f32[256,768]{1,0:T(8,128)S(1)}, f32[256,768]{1,0:T(8,128)}, u32[]{:S(2)}) copy-start(f32[256,768]{1,0:T(8,128)} %constant.76.clone) | copy-start | bytes 2359300
  26.6 1.7 %copy-start.9 = (f32[768,768]{1,0:T(8,128)S(1)}, f32[768,768]{1,0:T(8,128)}, u32[]{:S(2)}) copy-start(f32[768,768]{1,0:T(8,128)} %constant.73.clone) | copy-start | bytes 7077892
  28.3 5.3 %copy-start.2 = (f32[512,768]{1,0:T(8,128)S(1)}, f32[512,768]{1,0:T(8,128)}, u32[]{:S(2)}) copy-start(f32[512,768]{1,0:T(8,128)} %constant.75.clone) | copy-start | bytes 4718596
  38.6 1.9 %copy-start = (f32[768,1024]{1,0:T(8,128)S(1)}, f32[768,1024]{1,0:T(8,128)}, u32[]{:S(2)}) copy-start(f32[768,1024]{1,0:T(8,128)} %constant.77.clone) | copy-start | bytes 9437188
  44.5 1.1 %copy-start.5 = (f32[512,384]{1,0:T(8,128)S(1)}, f32[512,384]{1,0:T(8,128)}, u32[]{:S(2)}) copy-start(f32[512,384]{1,0:T(8,128)} %constant.95) | copy-start | bytes 2359300
  46.6 1.1 %copy-start.3 = (f32[512,384]{1,0:T(8,128)S(1)}, f32[512,384]{1,0:T(8,128)}, u32[]{:S(2)}) copy-start(f32[512,384]{1,0:T(8,128)} %constant.96) | copy-start | bytes 2359300

commit v19 on v17

--- a/solution.py
+++ b/solution.py
@@ -112,7 +112,9 @@
     def mirrored(ga, gb):
         return ga[:, 1:h - 1] + gb[:, h:], ga[:, h:] - gb[:, 1:h - 1]
 
-    window_parts = halves(product(product(left, rows_ext), right_w))
+    window_rows = product(left, rows_ext)
+    window_rows, normed = lax.optimization_barrier((window_rows, normed))
+    window_parts = halves(product(window_rows, right_w))
     template_parts = halves(product(product(left_t, normed), right_t))
 
     positions = lax.iota(jnp.int32, n)

time: 72.9 us -> 70.8 us (0.971)
  matrix products: 15.6 us -> 13.5 us
    dot_general x7, matrix products: 14.9 us -> 12.8 us  [product(): jnp.dot(former, latter, precision=mode, preferred_element_type=jnp.float32)]
  transfers between devices with their start and end apart: 2 -> 2, of which waited for: 0 -> 0; matrix products, arithmetic and copies ran while one was open for 5% -> 2% of each run, Pallas kernels for 0% -> 0%
where the time goes in v19:
time: 70.8 us; the launch traced here: 70.3 us
  blocking collectives  37.8 us (53%)
  matrix products  13.5 us (19%)
  starting transfers between devices  6.43 us (9%)
  other arithmetic  5.98 us (8%)
  local copies, waits for them, and re-layouts  4.88 us (7%)
  between operations  1.62 us (2%)
    all_to_all x1, blocking collectives, per_device(): lax.all_to_all(scores, 'orient', 0, 0, tiled=True)  24.1 us
    all_gather x1, blocking collectives, per_device(): everything = lax.all_gather(payload, 'tile')  13.7 us
    dot_general x7, matrix products, product(): jnp.dot(former, latter, precision=mode, preferred_element_type=jnp.float32)  12.8 us
    ppermute x1, starting transfers between devices, padded(): before = lax.ppermute(last, axis, up)  4.51 us
    mul x2, other arithmetic, multiply(): (spec_real * template_real + spec_imag * template_imag) * weight  3.46 us
    unnamed x24, local copies, waits for them, and re-layouts  3.37 us
    ppermute x1, starting transfers between devices, padded(): after = lax.ppermute(initial, axis, down)  1.92 us
  transfers between devices with their start and end apart: 2, of which 0 were waited for; matrix products, arithmetic and copies ran while one was open for 2% of the time, Pallas kernels for 0%

profile of v19, /device:TPU:1, one launch (start us, length us, event | category | flops | bytes accessed | tf_op | source)
XLA Modules:
  0.0 70.3 jit_solution(4869562302719120832)
XLA Ops:
  0.6 0.0 copy-start.1
  0.6 0.0 copy-start.7
  0.7 0.0 copy-start.8
  0.7 1.1 %fusion.54 = (f32[128,512]{1,0:T(8,128)S(1)}, f32[128,512]{1,0:T(8,128)S(1)}) fusion(f32[512,512]{1,0:T(8,128)} %param.10), kind=kLoop, calls=%fused_computation.100 | loop fusion | bytes 1048576 | tf_op jit(solution)/shard_map/slice | solution.py:22
  1.8 4.5 %collective-permute-start = (f32[128,512]{1,0:T(8,128)S(1)}, f32[128,512]{1,0:T(8,128)S(1)}, u32[]{:S(2)}, u32[]{:S(2)}) collective-permute-start(f32[128,512]{1,0:T(8,128)S(1)} %get-tuple-element.38), channel_id=1, source_target_pairs={{0,16},{16,32},{32,48},{48,64},{64,80},{80,96},{96,112},{1,17},{17... | collective-permute-start | bytes 786440 | tf_op jit(solution)/shard_map/ppermute | solution.py:24
  6.3 1.9 %collective-permute-start.1 = (f32[128,512]{1,0:T(8,128)S(1)}, f32[128,512]{1,0:T(8,128)S(1)}, u32[]{:S(2)}, u32[]{:S(2)}) collective-permute-start(f32[128,512]{1,0:T(8,128)S(1)} %get-tuple-element.39), channel_id=1, source_target_pairs={{16,0},{32,16},{48,32},{64,48},{80,64},{96,80},{112,96},{17,1},{33... | collective-permute-start | bytes 786440 | tf_op jit(solution)/shard_map/ppermute | solution.py:25
  8.3 0.0 copy-done.1
  8.3 0.2 fusion.52
  9.1 0.0 copy-done.7
  9.1 13.7 %all-gather.1 = f32[8,34,256]{2,1,0:T(8,128)S(1)} all-gather(f32[1,34,256]{2,1,0:T(8,128)S(1)} %maximum_bitcast_fusion), channel_id=2, replica_groups=mesh['tile'=8,'orient'=16] {'tile'}, dimensions={0}, use_global_device_ids=true | all-gather | bytes 313344 | tf_op jit(solution)/shard_map/all_gather | solution.py:72
  23.0 0.0 copy-done.8
  23.0 0.1 select_reduce_fusion.1
  23.1 0.1 select_reduce_fusion
  23.1 0.0 copy-start.9
  23.1 0.2 fusion.26
  23.3 0.1 multiply_reduce_fusion.2
  23.4 0.2 fusion.24
  23.6 0.2 fusion.30
  23.8 0.2 fusion.28
  24.2 0.2 add_negate_fusion
  24.4 0.0 collective-permute-done
  24.4 0.0 collective-permute-done.1
  24.5 0.4 copy-done.9
  24.8 0.0 copy-start.2
  24.8 2.2 %fusion.10 = f32[768,512]{1,0:T(8,128)S(1)} fusion(f32[768,768]{1,0:T(8,128)S(1)} %copy-done.9, f32[128,512]{1,0:T(8,128)S(1)} %collective-permute-done.1, f32[512,512]{1,0:T(8,128)S(1)} %copy-done.1, f32[128,512]{1,0:T(8,128)S(1)} %collective-permute-done, f32[512]{0:T(512)S(1)} %bitcast.47, f32[512]{0:T(512)S(1)} %bitcast.46, pred[768]{0:T(1024)(128)(4,1)S(1)} %fusion.39), kind=kOutput, calls=%fused_computation.12 | convolution fusion | flops 1813905408 | bytes 5509888 | tf_op jit(solution)/shard_map/dot_general | solution.py:31
  27.0 0.0 copy-done.2
  27.0 2.2 %fusion.55 = f32[768,768]{1,0:T(8,128)S(1)} fusion(f32[768,512]{1,0:T(8,128)S(1)} %fusion.10, f32[512,768]{1,0:T(8,128)S(1)} %copy-done.2), kind=kOutput, calls=%fused_computation.101 | convolution fusion | flops 1811939328 | bytes 5505024 | tf_op jit(solution)/shard_map/dot_general | solution.py:31
  29.2 0.0 copy-start.4
  29.2 0.0 copy-start.6
  29.2 0.1 slice.139
  29.3 1.0 %copy-done.4 = f32[768,256]{1,0:T(8,128)S(1)} copy-done((f32[768,256]{1,0:T(8,128)S(1)}, f32[768,256]{1,0:T(8,128)}, u32[]{:S(2)}) %copy-start.4) | copy-done | bytes 786456
  30.3 0.8 %fusion.56 = f32[256,768]{1,0:T(8,128)S(1)} fusion(f32[256,256]{1,0:T(8,128)S(1)} %fusion.23, f32[768,256]{1,0:T(8,128)S(1)} %copy-done.4), kind=kOutput, calls=%fused_computation.102 | convolution fusion | flops 301989888 | bytes 1835008 | tf_op jit(solution)/shard_map/dot_general | solution.py:31
  31.2 0.0 copy-done.6
  31.2 1.3 %fusion.57 = f32[768,768]{1,0:T(8,128)S(1)} fusion(f32[256,768]{1,0:T(8,128)S(1)} %fusion.56, f32[256,768]{1,0:T(8,128)S(1)} %copy-done.6), kind=kOutput, calls=%fused_computation.103 | convolution fusion | flops 905969664 | bytes 3932160 | tf_op jit(solution)/shard_map/dot_general | solution.py:31
  32.5 0.1 slice.141
  32.6 2.4 %add_multiply_fusion.1 = (f32[385,383]{1,0:T(8,128)S(1)}, f32[385,383]{1,0:T(8,128)S(1)}, f32[385,383]{1,0:T(8,128)S(1)}, f32[385,383]{1,0:T(8,128)S(1)}, f32[385,383]{1,0:T(8,128)S(1)}, /*index=5*/f32[385,383]{1,0:T(8,128)S(1)}) fusion(f32[385,768]{1,0:T(8,128)S(1)} %add_negate_fusion, f32[768,768]{1,0:T(8,128)S(1)} %fusion.55, f32[768,768]{1,0:T(8,128)S(1)} %fusion.57, ...), kind=kLoop, calls=%fused_computation.42 | loop fusion | flops 2359280 | bytes 8841172 | tf_op jit(solution)/shard_map/mul | solution.py:144
  35.1 0.0 copy-start
  35.1 1.0 %add_multiply_fusion = (f32[385,385]{1,0:T(8,128)S(1)}, f32[385,385]{1,0:T(8,128)S(1)}) fusion(f32[385,768]{1,0:T(8,128)S(1)} %add_negate_fusion, f32[385,383]{1,0:T(8,128)S(1)} %get-tuple-element.36, f32[768,768]{1,0:T(8,128)S(1)} %fusion.55, f32[385,383]{1,0:T(8,128)S(1)} %get-tuple-element.37, f32[768,768]{1,0:T(8,128)S(1)} %fusion.57, ...), kind=kLoop, calls=%fused_computation.30 | loop fusion | flops 2371600 | bytes 7676932 | tf_op jit(solution)/shard_map/mul | solution.py:144
  36.1 0.8 %copy-done = f32[768,1024]{1,0:T(8,128)S(1)} copy-done((f32[768,1024]{1,0:T(8,128)S(1)}, f32[768,1024]{1,0:T(8,128)}, u32[]{:S(2)}) %copy-start) | copy-done | bytes 3145752
  37.0 4.2 %fusion = f32[770,1024]{1,0:T(8,128)S(1)} fusion(f32[768,1024]{1,0:T(8,128)S(1)} %copy-done, f32[385,383]{1,0:T(8,128)S(1)} %get-tuple-element.31, f32[385,385]{1,0:T(8,128)S(1)} %get-tuple-element.29, f32[385,383]{1,0:T(8,128)S(1)} %get-tuple-element.30, f32[385,385]{1,0:T(8,128)S(1)} %get-tuple-element.28), kind=kOutput, calls=%fused_computation | convolution fusion | flops 3635089920 | bytes 8665088 | tf_op jit(solution)/shard_map/dot_general | solution.py:31
  41.1 0.0 copy-start.3
  41.1 0.2 fusion.53
  41.3 1.0 %copy-done.3 = f32[512,385]{1,0:T(8,128)S(1)} copy-done((f32[512,385]{1,0:T(8,128)S(1)}, f32[512,385]{1,0:T(8,128)}, u32[]{:S(2)}) %copy-start.3) | copy-done | bytes 788504
  42.3 0.0 copy-start.5
  42.4 1.0 %fusion.14 = f32[512,512]{0,1:T(8,128)S(1)} fusion(f32[512,385]{1,0:T(8,128)S(1)} %copy-done.3, f32[770,1024]{1,0:T(8,128)S(1)} %fusion), kind=kOutput, calls=%fused_computation.25 | convolution fusion | flops 605749760 | bytes 3702784 | tf_op jit(solution)/shard_map/dot_general | solution.py:31
  43.4 0.1 copy-done.5
  43.5 1.1 %convolution_add_fusion = f32[512,512]{0,1:T(8,128)S(1)} fusion(f32[512,512]{0,1:T(8,128)S(1)} %fusion.14, f32[512,383]{1,0:T(8,128)S(1)} %copy-done.5, f32[385,512]{1,0:T(8,128)S(1)} %get-tuple-element.33, f32[385,512]{1,0:T(8,128)S(1)} %get-tuple-element.32), kind=kOutput, calls=%fused_computation.13 | convolution fusion | flops 602865152 | bytes 4456448 | tf_op jit(solution)/shard_map/dot_general | solution.py:31
  44.6 24.1 %all_to_all.9 = f32[16,32,512]{2,1,0:T(8,128)S(1)} all-to-all(f32[16,32,512]{2,1,0:T(8,128)S(1)} %bitcast.42), channel_id=1, replica_groups=mesh['tile'=8,'orient'=16] {'orient'}, dimensions={0} | all-to-all | bytes 2097152 | tf_op jit(solution)/shard_map/all_to_all | solution.py:163
  68.7 0.9 %multiply_reduce_fusion = (f32[32,512]{1,0:T(8,128)}, f32[32,512]{1,0:T(8,128)}, f32[32,512]{1,0:T(8,128)S(1)}, f32[32,512]{1,0:T(8,128)S(1)}) fusion(f32[16,32,512]{2,1,0:T(8,128)S(1)} %all_to_all.9), kind=kLoop, calls=%fused_computation.11 | loop fusion | flops 1736704 | bytes 1310720 | tf_op jit(solution)/shard_map/reduce | solution.py:175
  69.6 0.7 multiply_subtract_fusion
  (17 shorter events, 0.3 us)
Async XLA Ops:
  0.6 7.6 %copy-start.1 = (f32[512,512]{1,0:T(8,128)S(1)}, f32[512,512]{1,0:T(8,128)}, u32[]{:S(2)}) copy-start(f32[512,512]{1,0:T(8,128)} %param.10) | copy-start | bytes 3145732
  0.6 8.5 %copy-start.7 = (f32[1,32,256]{2,1,0:T(8,128)S(1)}, f32[1,32,256]{2,1,0:T(8,128)}, u32[]{:S(2)}) copy-start(f32[1,32,256]{2,1,0:T(8,128)} %param.11) | copy-start | bytes 98308
  0.7 22.3 %copy-start.8 = (f32[4]{0:T(128)S(1)}, f32[4]{0:T(128)}, u32[]{:S(2)}) copy-start(f32[4]{0:T(128)} %param.12) | copy-start | bytes 52
  1.8 22.6 %collective-permute-start = (f32[128,512]{1,0:T(8,128)S(1)}, f32[128,512]{1,0:T(8,128)S(1)}, u32[]{:S(2)}, u32[]{:S(2)}) collective-permute-start(f32[128,512]{1,0:T(8,128)S(1)} %get-tuple-element.38), channel_id=1, source_target_pairs={{0,16},{16,32},{32,48},{48,64},{64,80},{80,96},{96,112},{1,17},{17... | collective-permute-start | bytes 786440 | tf_op jit(solution)/shard_map/ppermute | solution.py:24
  6.3 18.1 %collective-permute-start.1 = (f32[128,512]{1,0:T(8,128)S(1)}, f32[128,512]{1,0:T(8,128)S(1)}, u32[]{:S(2)}, u32[]{:S(2)}) collective-permute-start(f32[128,512]{1,0:T(8,128)S(1)} %get-tuple-element.39), channel_id=1, source_target_pairs={{16,0},{32,16},{48,32},{64,48},{80,64},{96,80},{112,96},{17,1},{33... | collective-permute-start | bytes 786440 | tf_op jit(solution)/shard_map/ppermute | solution.py:25
  23.1 1.7 %copy-start.9 = (f32[768,768]{1,0:T(8,128)S(1)}, f32[768,768]{1,0:T(8,128)}, u32[]{:S(2)}) copy-start(f32[768,768]{1,0:T(8,128)} %constant.72.clone) | copy-start | bytes 7077892
  24.8 2.2 %copy-start.2 = (f32[512,768]{1,0:T(8,128)S(1)}, f32[512,768]{1,0:T(8,128)}, u32[]{:S(2)}) copy-start(f32[512,768]{1,0:T(8,128)} %constant.74.clone) | copy-start | bytes 4718596
  29.2 1.1 %copy-start.4 = (f32[768,256]{1,0:T(8,128)S(1)}, f32[768,256]{1,0:T(8,128)}, u32[]{:S(2)}) copy-start(f32[768,256]{1,0:T(8,128)} %constant.73.clone) | copy-start | bytes 2359300
  29.2 2.0 %copy-start.6 = (f32[256,768]{1,0:T(8,128)S(1)}, f32[256,768]{1,0:T(8,128)}, u32[]{:S(2)}) copy-start(f32[256,768]{1,0:T(8,128)} %constant.75.clone) | copy-start | bytes 2359300
  35.1 1.9 %copy-start = (f32[768,1024]{1,0:T(8,128)S(1)}, f32[768,1024]{1,0:T(8,128)}, u32[]{:S(2)}) copy-start(f32[768,1024]{1,0:T(8,128)} %constant.76.clone) | copy-start | bytes 9437188
  41.1 1.2 %copy-start.3 = (f32[512,385]{1,0:T(8,128)S(1)}, f32[512,385]{1,0:T(8,128)}, u32[]{:S(2)}) copy-start(f32[512,385]{1,0:T(8,128)} %constant.92) | copy-start | bytes 2365444
  42.3 1.1 %copy-start.5 = (f32[512,383]{1,0:T(8,128)S(1)}, f32[512,383]{1,0:T(8,128)}, u32[]{:S(2)}) copy-start(f32[512,383]{1,0:T(8,128)} %constant.93) | copy-start | bytes 2353156

commit v20 on v19

--- a/solution.py
+++ b/solution.py
@@ -114,8 +114,10 @@
 
     window_rows = product(left, rows_ext)
     window_rows, normed = lax.optimization_barrier((window_rows, normed))
+    template_rows = product(left_t, normed)
+    template_rows, window_rows = lax.optimization_barrier((template_rows, window_rows))
     window_parts = halves(product(window_rows, right_w))
-    template_parts = halves(product(product(left_t, normed), right_t))
+    template_parts = halves(product(template_rows, right_t))
 
     positions = lax.iota(jnp.int32, n)
     signed_freq = (

time: 70.8 us -> 71.2 us (level)
  local copies, waits for them, and re-layouts: 4.88 us -> 5.8 us
    unnamed x24, local copies, waits for them, and re-layouts: 3.37 us -> 4.29 us
where the time goes in v20:
time: 71.2 us; the launch traced here: 70.6 us
  blocking collectives  37.8 us (53%)
  matrix products  13 us (18%)
  starting transfers between devices  6.43 us (9%)
  other arithmetic  5.98 us (8%)
  local copies, waits for them, and re-layouts  5.8 us (8%)
  between operations  1.61 us (2%)
    all_to_all x1, blocking collectives, per_device(): lax.all_to_all(scores, 'orient', 0, 0, tiled=True)  24.1 us
    all_gather x1, blocking collectives, per_device(): everything = lax.all_gather(payload, 'tile')  13.7 us
    dot_general x7, matrix products, product(): jnp.dot(former, latter, precision=mode, preferred_element_type=jnp.float32)  12.3 us
    ppermute x1, starting transfers between devices, padded(): before = lax.ppermute(last, axis, up)  4.51 us
    unnamed x24, local copies, waits for them, and re-layouts  4.29 us
    mul x2, other arithmetic, multiply(): (spec_real * template_real + spec_imag * template_imag) * weight  3.46 us
    ppermute x1, starting transfers between devices, padded(): after = lax.ppermute(initial, axis, down)  1.92 us
  transfers between devices with their start and end apart: 2, of which 0 were waited for; matrix products, arithmetic and copies ran while one was open for 2% of the time, Pallas kernels for 0%

profile of v20, /device:TPU:1, one launch (start us, length us, event | category | flops | bytes accessed | tf_op | source)
XLA Modules:
  0.0 70.6 jit_solution(6044167454109356020)
XLA Ops:
  0.6 0.0 copy-start.1
  0.6 0.0 copy-start.7
  0.7 0.0 copy-start.8
  0.7 1.1 %fusion.54 = (f32[128,512]{1,0:T(8,128)S(1)}, f32[128,512]{1,0:T(8,128)S(1)}) fusion(f32[512,512]{1,0:T(8,128)} %param.10), kind=kLoop, calls=%fused_computation.100 | loop fusion | bytes 1048576 | tf_op jit(solution)/shard_map/slice | solution.py:22
  1.8 4.5 %collective-permute-start = (f32[128,512]{1,0:T(8,128)S(1)}, f32[128,512]{1,0:T(8,128)S(1)}, u32[]{:S(2)}, u32[]{:S(2)}) collective-permute-start(f32[128,512]{1,0:T(8,128)S(1)} %get-tuple-element.42), channel_id=1, source_target_pairs={{0,16},{16,32},{32,48},{48,64},{64,80},{80,96},{96,112},{1,17},{17... | collective-permute-start | bytes 786440 | tf_op jit(solution)/shard_map/ppermute | solution.py:24
  6.3 1.9 %collective-permute-start.1 = (f32[128,512]{1,0:T(8,128)S(1)}, f32[128,512]{1,0:T(8,128)S(1)}, u32[]{:S(2)}, u32[]{:S(2)}) collective-permute-start(f32[128,512]{1,0:T(8,128)S(1)} %get-tuple-element.43), channel_id=1, source_target_pairs={{16,0},{32,16},{48,32},{64,48},{80,64},{96,80},{112,96},{17,1},{33... | collective-permute-start | bytes 786440 | tf_op jit(solution)/shard_map/ppermute | solution.py:25
  8.3 0.0 copy-done.1
  8.3 0.2 fusion.52
  9.1 0.0 copy-done.7
  9.1 13.7 %all-gather.1 = f32[8,34,256]{2,1,0:T(8,128)S(1)} all-gather(f32[1,34,256]{2,1,0:T(8,128)S(1)} %maximum_bitcast_fusion), channel_id=2, replica_groups=mesh['tile'=8,'orient'=16] {'tile'}, dimensions={0}, use_global_device_ids=true | all-gather | bytes 313344 | tf_op jit(solution)/shard_map/all_gather | solution.py:72
  23.0 0.0 copy-done.8
  23.0 0.1 select_reduce_fusion.1
  23.1 0.1 select_reduce_fusion
  23.1 0.0 copy-start.9
  23.1 0.2 fusion.26
  23.3 0.1 multiply_reduce_fusion.2
  23.4 0.2 fusion.24
  23.6 0.2 fusion.30
  23.8 0.2 fusion.28
  24.2 0.2 add_negate_fusion
  24.4 0.0 collective-permute-done
  24.4 0.0 collective-permute-done.1
  24.5 0.4 copy-done.9
  24.8 0.0 copy-start.4
  24.8 2.2 %fusion.10 = f32[768,512]{1,0:T(8,128)S(1)} fusion(f32[768,768]{1,0:T(8,128)S(1)} %copy-done.9, f32[128,512]{1,0:T(8,128)S(1)} %collective-permute-done.1, f32[512,512]{1,0:T(8,128)S(1)} %copy-done.1, f32[128,512]{1,0:T(8,128)S(1)} %collective-permute-done, f32[512]{0:T(512)S(1)} %bitcast.47, f32[512]{0:T(512)S(1)} %bitcast.46, pred[768]{0:T(1024)(128)(4,1)S(1)} %fusion.39), kind=kOutput, calls=%fused_computation.12 | convolution fusion | flops 1813905408 | bytes 5509888 | tf_op jit(solution)/shard_map/dot_general | solution.py:31
  27.0 0.0 copy-done.4
  27.0 0.0 copy-start.2
  27.0 0.5 fusion.55
  27.5 0.9 %copy-done.2 = f32[512,768]{1,0:T(8,128)S(1)} copy-done((f32[512,768]{1,0:T(8,128)S(1)}, f32[512,768]{1,0:T(8,128)}, u32[]{:S(2)}) %copy-start.2) | copy-done | bytes 1572888
  28.4 2.2 %fusion.56 = f32[768,768]{1,0:T(8,128)S(1)} fusion(f32[768,512]{1,0:T(8,128)S(1)} %fusion.10, f32[512,768]{1,0:T(8,128)S(1)} %copy-done.2), kind=kOutput, calls=%fused_computation.102 | convolution fusion | flops 1811939328 | bytes 5505024 | tf_op jit(solution)/shard_map/dot_general | solution.py:31
  30.6 0.0 copy-start.6
  30.6 0.1 slice.139
  30.7 1.0 %copy-done.6 = f32[256,768]{1,0:T(8,128)S(1)} copy-done((f32[256,768]{1,0:T(8,128)S(1)}, f32[256,768]{1,0:T(8,128)}, u32[]{:S(2)}) %copy-start.6) | copy-done | bytes 786456
  31.7 1.1 %fusion.57 = f32[768,768]{1,0:T(8,128)S(1)} fusion(f32[768,256]{1,0:T(8,128)S(1)} %fusion.55, f32[256,768]{1,0:T(8,128)S(1)} %copy-done.6), kind=kOutput, calls=%fused_computation.103 | convolution fusion | flops 905969664 | bytes 3932160 | tf_op jit(solution)/shard_map/dot_general | solution.py:31
  32.9 0.1 slice.141
  33.0 2.4 %add_multiply_fusion.1 = (f32[385,383]{1,0:T(8,128)S(1)}, f32[385,383]{1,0:T(8,128)S(1)}, f32[385,383]{1,0:T(8,128)S(1)}, f32[385,383]{1,0:T(8,128)S(1)}, f32[385,383]{1,0:T(8,128)S(1)}, /*index=5*/f32[385,383]{1,0:T(8,128)S(1)}) fusion(f32[385,768]{1,0:T(8,128)S(1)} %add_negate_fusion, f32[768,768]{1,0:T(8,128)S(1)} %fusion.56, f32[768,768]{1,0:T(8,128)S(1)} %fusion.57, ...), kind=kLoop, calls=%fused_computation.42 | loop fusion | flops 2359280 | bytes 8841172 | tf_op jit(solution)/shard_map/mul | solution.py:146
  35.4 0.0 copy-start
  35.4 1.0 %add_multiply_fusion = (f32[385,385]{1,0:T(8,128)S(1)}, f32[385,385]{1,0:T(8,128)S(1)}) fusion(f32[385,768]{1,0:T(8,128)S(1)} %add_negate_fusion, f32[385,383]{1,0:T(8,128)S(1)} %get-tuple-element.40, f32[768,768]{1,0:T(8,128)S(1)} %fusion.56, f32[385,383]{1,0:T(8,128)S(1)} %get-tuple-element.41, f32[768,768]{1,0:T(8,128)S(1)} %fusion.57, ...), kind=kLoop, calls=%fused_computation.30 | loop fusion | flops 2371600 | bytes 7676932 | tf_op jit(solution)/shard_map/mul | solution.py:146
  36.5 0.8 %copy-done = f32[768,1024]{1,0:T(8,128)S(1)} copy-done((f32[768,1024]{1,0:T(8,128)S(1)}, f32[768,1024]{1,0:T(8,128)}, u32[]{:S(2)}) %copy-start) | copy-done | bytes 3145752
  37.3 4.2 %fusion = f32[770,1024]{1,0:T(8,128)S(1)} fusion(f32[768,1024]{1,0:T(8,128)S(1)} %copy-done, f32[385,383]{1,0:T(8,128)S(1)} %get-tuple-element.35, f32[385,385]{1,0:T(8,128)S(1)} %get-tuple-element.33, f32[385,383]{1,0:T(8,128)S(1)} %get-tuple-element.34, f32[385,385]{1,0:T(8,128)S(1)} %get-tuple-element.32), kind=kOutput, calls=%fused_computation | convolution fusion | flops 3635089920 | bytes 8665088 | tf_op jit(solution)/shard_map/dot_general | solution.py:31
  41.5 0.0 copy-start.3
  41.5 0.2 fusion.53
  41.7 1.0 %copy-done.3 = f32[512,385]{1,0:T(8,128)S(1)} copy-done((f32[512,385]{1,0:T(8,128)S(1)}, f32[512,385]{1,0:T(8,128)}, u32[]{:S(2)}) %copy-start.3) | copy-done | bytes 788504
  42.7 0.0 copy-start.5
  42.7 1.0 %fusion.14 = f32[512,512]{0,1:T(8,128)S(1)} fusion(f32[512,385]{1,0:T(8,128)S(1)} %copy-done.3, f32[770,1024]{1,0:T(8,128)S(1)} %fusion), kind=kOutput, calls=%fused_computation.25 | convolution fusion | flops 605749760 | bytes 3702784 | tf_op jit(solution)/shard_map/dot_general | solution.py:31
  43.8 0.1 copy-done.5
  43.8 1.1 %convolution_add_fusion = f32[512,512]{0,1:T(8,128)S(1)} fusion(f32[512,512]{0,1:T(8,128)S(1)} %fusion.14, f32[512,383]{1,0:T(8,128)S(1)} %copy-done.5, f32[385,512]{1,0:T(8,128)S(1)} %get-tuple-element.37, f32[385,512]{1,0:T(8,128)S(1)} %get-tuple-element.36), kind=kOutput, calls=%fused_computation.13 | convolution fusion | flops 602865152 | bytes 4456448 | tf_op jit(solution)/shard_map/dot_general | solution.py:31
  44.9 24.1 %all_to_all.9 = f32[16,32,512]{2,1,0:T(8,128)S(1)} all-to-all(f32[16,32,512]{2,1,0:T(8,128)S(1)} %bitcast.42), channel_id=1, replica_groups=mesh['tile'=8,'orient'=16] {'orient'}, dimensions={0} | all-to-all | bytes 2097152 | tf_op jit(solution)/shard_map/all_to_all | solution.py:165
  69.0 0.9 %multiply_reduce_fusion = (f32[32,512]{1,0:T(8,128)}, f32[32,512]{1,0:T(8,128)}, f32[32,512]{1,0:T(8,128)S(1)}, f32[32,512]{1,0:T(8,128)S(1)}) fusion(f32[16,32,512]{2,1,0:T(8,128)S(1)} %all_to_all.9), kind=kLoop, calls=%fused_computation.11 | loop fusion | flops 1736704 | bytes 1310720 | tf_op jit(solution)/shard_map/reduce | solution.py:177
  70.0 0.7 multiply_subtract_fusion
  (17 shorter events, 0.3 us)
Async XLA Ops:
  0.6 7.6 %copy-start.1 = (f32[512,512]{1,0:T(8,128)S(1)}, f32[512,512]{1,0:T(8,128)}, u32[]{:S(2)}) copy-start(f32[512,512]{1,0:T(8,128)} %param.10) | copy-start | bytes 3145732
  0.6 8.5 %copy-start.7 = (f32[1,32,256]{2,1,0:T(8,128)S(1)}, f32[1,32,256]{2,1,0:T(8,128)}, u32[]{:S(2)}) copy-start(f32[1,32,256]{2,1,0:T(8,128)} %param.11) | copy-start | bytes 98308
  0.7 22.3 %copy-start.8 = (f32[4]{0:T(128)S(1)}, f32[4]{0:T(128)}, u32[]{:S(2)}) copy-start(f32[4]{0:T(128)} %param.12) | copy-start | bytes 52
  1.8 22.6 %collective-permute-start = (f32[128,512]{1,0:T(8,128)S(1)}, f32[128,512]{1,0:T(8,128)S(1)}, u32[]{:S(2)}, u32[]{:S(2)}) collective-permute-start(f32[128,512]{1,0:T(8,128)S(1)} %get-tuple-element.42), channel_id=1, source_target_pairs={{0,16},{16,32},{32,48},{48,64},{64,80},{80,96},{96,112},{1,17},{17... | collective-permute-start | bytes 786440 | tf_op jit(solution)/shard_map/ppermute | solution.py:24
  6.3 18.1 %collective-permute-start.1 = (f32[128,512]{1,0:T(8,128)S(1)}, f32[128,512]{1,0:T(8,128)S(1)}, u32[]{:S(2)}, u32[]{:S(2)}) collective-permute-start(f32[128,512]{1,0:T(8,128)S(1)} %get-tuple-element.43), channel_id=1, source_target_pairs={{16,0},{32,16},{48,32},{64,48},{80,64},{96,80},{112,96},{17,1},{33... | collective-permute-start | bytes 786440 | tf_op jit(solution)/shard_map/ppermute | solution.py:25
  23.1 1.7 %copy-start.9 = (f32[768,768]{1,0:T(8,128)S(1)}, f32[768,768]{1,0:T(8,128)}, u32[]{:S(2)}) copy-start(f32[768,768]{1,0:T(8,128)} %constant.72.clone) | copy-start | bytes 7077892
  24.8 2.2 %copy-start.4 = (f32[768,256]{1,0:T(8,128)S(1)}, f32[768,256]{1,0:T(8,128)}, u32[]{:S(2)}) copy-start(f32[768,256]{1,0:T(8,128)} %constant.73.clone) | copy-start | bytes 2359300
  27.0 1.4 %copy-start.2 = (f32[512,768]{1,0:T(8,128)S(1)}, f32[512,768]{1,0:T(8,128)}, u32[]{:S(2)}) copy-start(f32[512,768]{1,0:T(8,128)} %constant.74.clone) | copy-start | bytes 4718596
  30.6 1.1 %copy-start.6 = (f32[256,768]{1,0:T(8,128)S(1)}, f32[256,768]{1,0:T(8,128)}, u32[]{:S(2)}) copy-start(f32[256,768]{1,0:T(8,128)} %constant.75.clone) | copy-start | bytes 2359300
  35.4 1.9 %copy-start = (f32[768,1024]{1,0:T(8,128)S(1)}, f32[768,1024]{1,0:T(8,128)}, u32[]{:S(2)}) copy-start(f32[768,1024]{1,0:T(8,128)} %constant.76.clone) | copy-start | bytes 9437188
  41.5 1.2 %copy-start.3 = (f32[512,385]{1,0:T(8,128)S(1)}, f32[512,385]{1,0:T(8,128)}, u32[]{:S(2)}) copy-start(f32[512,385]{1,0:T(8,128)} %constant.92) | copy-start | bytes 2365444
  42.7 1.1 %copy-start.5 = (f32[512,383]{1,0:T(8,128)S(1)}, f32[512,383]{1,0:T(8,128)}, u32[]{:S(2)}) copy-start(f32[512,383]{1,0:T(8,128)} %constant.93) | copy-start | bytes 2353156

commit v21 on v19

--- a/solution.py
+++ b/solution.py
@@ -114,7 +114,11 @@
 
     window_rows = product(left, rows_ext)
     window_rows, normed = lax.optimization_barrier((window_rows, normed))
-    window_parts = halves(product(window_rows, right_w))
+    window_spec = product(window_rows, right_w)
+    defocus_values, defocus_group, window_spec = lax.optimization_barrier(
+        (defocus_values, defocus_group, window_spec)
+    )
+    window_parts = halves(window_spec)
     template_parts = halves(product(product(left_t, normed), right_t))
 
     positions = lax.iota(jnp.int32, n)

time: 70.8 us -> 72.2 us (1.020)
  matrix products: 13.5 us -> 15.5 us
    dot_general x7, matrix products: 12.8 us -> 14.8 us  [product(): jnp.dot(former, latter, precision=mode, preferred_element_type=jnp.float32)]
    unnamed x24 -> x22, local copies, waits for them, and re-layouts: 3.37 us -> 2.74 us
where the time goes in v21:
time: 72.2 us; the launch traced here: 71.7 us
  blocking collectives  37.8 us (52%)
  matrix products  15.5 us (21%)
  starting transfers between devices  6.43 us (9%)
  other arithmetic  6.01 us (8%)
  local copies, waits for them, and re-layouts  4.25 us (6%)
  between operations  1.63 us (2%)
    all_to_all x1, blocking collectives, per_device(): lax.all_to_all(scores, 'orient', 0, 0, tiled=True)  24.1 us
    dot_general x7, matrix products, product(): jnp.dot(former, latter, precision=mode, preferred_element_type=jnp.float32)  14.8 us
    all_gather x1, blocking collectives, per_device(): everything = lax.all_gather(payload, 'tile')  13.7 us
    ppermute x1, starting transfers between devices, padded(): before = lax.ppermute(last, axis, up)  4.51 us
    mul x2, other arithmetic, multiply(): (spec_real * template_real + spec_imag * template_imag) * weight  3.48 us
    unnamed x22, local copies, waits for them, and re-layouts  2.74 us
    ppermute x1, starting transfers between devices, padded(): after = lax.ppermute(initial, axis, down)  1.92 us
  transfers between devices with their start and end apart: 2, of which 0 were waited for; matrix products, arithmetic and copies ran while one was open for 2% of the time, Pallas kernels for 0%

profile of v21, /device:TPU:1, one launch (start us, length us, event | category | flops | bytes accessed | tf_op | source)
XLA Modules:
  0.0 71.7 jit_solution(8051734918722602531)
XLA Ops:
  0.6 0.0 copy-start.1
  0.6 0.0 copy-start.7
  0.7 1.2 %fusion.54 = (f32[128,512]{1,0:T(8,128)S(1)}, f32[128,512]{1,0:T(8,128)S(1)}) fusion(f32[512,512]{1,0:T(8,128)} %param.10), kind=kLoop, calls=%fused_computation.100 | loop fusion | bytes 1048576 | tf_op jit(solution)/shard_map/slice | solution.py:22
  1.8 4.5 %collective-permute-start = (f32[128,512]{1,0:T(8,128)S(1)}, f32[128,512]{1,0:T(8,128)S(1)}, u32[]{:S(2)}, u32[]{:S(2)}) collective-permute-start(f32[128,512]{1,0:T(8,128)S(1)} %get-tuple-element.44), channel_id=1, source_target_pairs={{0,16},{16,32},{32,48},{48,64},{64,80},{80,96},{96,112},{1,17},{17... | collective-permute-start | bytes 786440 | tf_op jit(solution)/shard_map/ppermute | solution.py:24
  6.3 1.9 %collective-permute-start.1 = (f32[128,512]{1,0:T(8,128)S(1)}, f32[128,512]{1,0:T(8,128)S(1)}, u32[]{:S(2)}, u32[]{:S(2)}) collective-permute-start(f32[128,512]{1,0:T(8,128)S(1)} %get-tuple-element.45), channel_id=1, source_target_pairs={{16,0},{32,16},{48,32},{64,48},{80,64},{96,80},{112,96},{17,1},{33... | collective-permute-start | bytes 786440 | tf_op jit(solution)/shard_map/ppermute | solution.py:25
  8.3 0.0 copy-done.1
  8.3 0.2 fusion.52
  9.1 0.0 copy-done.7
  9.1 13.7 %all-gather.1 = f32[8,34,256]{2,1,0:T(8,128)S(1)} all-gather(f32[1,34,256]{2,1,0:T(8,128)S(1)} %maximum_bitcast_fusion), channel_id=2, replica_groups=mesh['tile'=8,'orient'=16] {'tile'}, dimensions={0}, use_global_device_ids=true | all-gather | bytes 313344 | tf_op jit(solution)/shard_map/all_gather | solution.py:72
  22.9 0.2 fusion.26
  23.1 0.1 multiply_reduce_fusion.2
  23.2 0.2 fusion.24
  23.4 0.2 fusion.30
  23.6 0.2 fusion.28
  23.9 0.0 collective-permute-done
  23.9 0.0 collective-permute-done.1
  23.9 0.0 copy-start.2
  23.9 4.0 %fusion.10 = f32[768,512]{1,0:T(8,128)S(1)} fusion(f32[768,768]{1,0:T(8,128)} %constant.72.clone, f32[128,512]{1,0:T(8,128)S(1)} %collective-permute-done.1, f32[512,512]{1,0:T(8,128)S(1)} %copy-done.1, f32[128,512]{1,0:T(8,128)S(1)} %collective-permute-done, f32[512]{0:T(512)S(1)} %bitcast.47, f32[512]{0:T(512)S(1)} %bitcast.46, pred[768]{0:T(1024)(128)(4,1)S(1)} %fusion.39), kind=kOutput, calls=%fused_computation.12 | convolution fusion | flops 1813905408 | bytes 5509888 | tf_op jit(solution)/shard_map/dot_general | solution.py:31
  27.9 0.0 copy-done.2
  27.9 0.0 copy-start.8
  27.9 2.2 %fusion.55 = f32[768,768]{1,0:T(8,128)S(1)} fusion(f32[768,512]{1,0:T(8,128)S(1)} %fusion.10, f32[512,768]{1,0:T(8,128)S(1)} %copy-done.2), kind=kOutput, calls=%fused_computation.101 | convolution fusion | flops 1811939328 | bytes 5505024 | tf_op jit(solution)/shard_map/dot_general | solution.py:31
  30.1 0.0 copy-done.8
  30.1 0.0 copy-start.4
  30.1 0.1 select_reduce_fusion.1
  30.2 0.1 select_reduce_fusion
  30.3 0.1 multiply_subtract_fusion.1
  30.4 0.0 copy-start.6
  30.4 0.1 slice.115
  30.5 0.8 %copy-done.4 = f32[768,256]{1,0:T(8,128)S(1)} copy-done((f32[768,256]{1,0:T(8,128)S(1)}, f32[768,256]{1,0:T(8,128)}, u32[]{:S(2)}) %copy-start.4) | copy-done | bytes 786456
  31.3 0.8 %fusion.56 = f32[256,768]{1,0:T(8,128)S(1)} fusion(f32[256,256]{1,0:T(8,128)S(1)} %fusion.23, f32[768,256]{1,0:T(8,128)S(1)} %copy-done.4), kind=kOutput, calls=%fused_computation.102 | convolution fusion | flops 301989888 | bytes 1835008 | tf_op jit(solution)/shard_map/dot_general | solution.py:31
  32.1 0.0 copy-done.6
  32.1 1.3 %fusion.57 = f32[768,768]{1,0:T(8,128)S(1)} fusion(f32[256,768]{1,0:T(8,128)S(1)} %fusion.56, f32[256,768]{1,0:T(8,128)S(1)} %copy-done.6), kind=kOutput, calls=%fused_computation.103 | convolution fusion | flops 905969664 | bytes 3932160 | tf_op jit(solution)/shard_map/dot_general | solution.py:31
  33.5 0.1 slice.139
  33.6 0.2 add_negate_fusion
  33.8 2.4 %add_multiply_fusion.1 = (f32[385,383]{1,0:T(8,128)S(1)}, f32[385,383]{1,0:T(8,128)S(1)}, f32[385,383]{1,0:T(8,128)S(1)}, f32[385,383]{1,0:T(8,128)S(1)}, f32[385,383]{1,0:T(8,128)S(1)}, /*index=5*/f32[385,383]{1,0:T(8,128)S(1)}) fusion(f32[385,768]{1,0:T(8,128)S(1)} %add_negate_fusion, f32[768,768]{1,0:T(8,128)S(1)} %fusion.55, f32[768,768]{1,0:T(8,128)S(1)} %fusion.57, ...), kind=kLoop, calls=%fused_computation.41 | loop fusion | flops 2359280 | bytes 8841172 | tf_op jit(solution)/shard_map/mul | solution.py:148
  36.3 0.0 copy-start
  36.3 1.0 %add_multiply_fusion = (f32[385,385]{1,0:T(8,128)S(1)}, f32[385,385]{1,0:T(8,128)S(1)}) fusion(f32[385,768]{1,0:T(8,128)S(1)} %add_negate_fusion, f32[385,383]{1,0:T(8,128)S(1)} %get-tuple-element.42, f32[768,768]{1,0:T(8,128)S(1)} %fusion.55, f32[385,383]{1,0:T(8,128)S(1)} %get-tuple-element.43, f32[768,768]{1,0:T(8,128)S(1)} %fusion.57, ...), kind=kLoop, calls=%fused_computation.29 | loop fusion | flops 2371600 | bytes 7676932 | tf_op jit(solution)/shard_map/mul | solution.py:148
  37.3 0.8 %copy-done = f32[768,1024]{1,0:T(8,128)S(1)} copy-done((f32[768,1024]{1,0:T(8,128)S(1)}, f32[768,1024]{1,0:T(8,128)}, u32[]{:S(2)}) %copy-start) | copy-done | bytes 3145752
  38.2 4.3 %fusion = f32[770,1024]{1,0:T(8,128)S(1)} fusion(f32[768,1024]{1,0:T(8,128)S(1)} %copy-done, f32[385,383]{1,0:T(8,128)S(1)} %get-tuple-element.37, f32[385,385]{1,0:T(8,128)S(1)} %get-tuple-element.35, f32[385,383]{1,0:T(8,128)S(1)} %get-tuple-element.36, f32[385,385]{1,0:T(8,128)S(1)} %get-tuple-element.34), kind=kOutput, calls=%fused_computation | convolution fusion | flops 3635089920 | bytes 8665088 | tf_op jit(solution)/shard_map/dot_general | solution.py:31
  42.5 0.0 copy-start.3
  42.5 0.2 fusion.53
  42.7 1.0 %copy-done.3 = f32[512,385]{1,0:T(8,128)S(1)} copy-done((f32[512,385]{1,0:T(8,128)S(1)}, f32[512,385]{1,0:T(8,128)}, u32[]{:S(2)}) %copy-start.3) | copy-done | bytes 788504
  43.7 0.0 copy-start.5
  43.7 1.1 %fusion.14 = f32[512,512]{0,1:T(8,128)S(1)} fusion(f32[512,385]{1,0:T(8,128)S(1)} %copy-done.3, f32[770,1024]{1,0:T(8,128)S(1)} %fusion), kind=kOutput, calls=%fused_computation.25 | convolution fusion | flops 605749760 | bytes 3702784 | tf_op jit(solution)/shard_map/dot_general | solution.py:31
  44.8 0.1 copy-done.5
  44.9 1.1 %convolution_add_fusion = f32[512,512]{0,1:T(8,128)S(1)} fusion(f32[512,512]{0,1:T(8,128)S(1)} %fusion.14, f32[512,383]{1,0:T(8,128)S(1)} %copy-done.5, f32[385,512]{1,0:T(8,128)S(1)} %get-tuple-element.39, f32[385,512]{1,0:T(8,128)S(1)} %get-tuple-element.38), kind=kOutput, calls=%fused_computation.13 | convolution fusion | flops 602865152 | bytes 4456448 | tf_op jit(solution)/shard_map/dot_general | solution.py:31
  46.0 24.1 %all_to_all.9 = f32[16,32,512]{2,1,0:T(8,128)S(1)} all-to-all(f32[16,32,512]{2,1,0:T(8,128)S(1)} %bitcast.42), channel_id=1, replica_groups=mesh['tile'=8,'orient'=16] {'orient'}, dimensions={0} | all-to-all | bytes 2097152 | tf_op jit(solution)/shard_map/all_to_all | solution.py:167
  70.1 0.9 %multiply_reduce_fusion = (f32[32,512]{1,0:T(8,128)}, f32[32,512]{1,0:T(8,128)}, f32[32,512]{1,0:T(8,128)S(1)}, f32[32,512]{1,0:T(8,128)S(1)}) fusion(f32[16,32,512]{2,1,0:T(8,128)S(1)} %all_to_all.9), kind=kLoop, calls=%fused_computation.11 | loop fusion | flops 1736704 | bytes 1310720 | tf_op jit(solution)/shard_map/reduce | solution.py:179
  71.0 0.7 multiply_subtract_fusion
  (16 shorter events, 0.2 us)
Async XLA Ops:
  0.6 7.6 %copy-start.1 = (f32[512,512]{1,0:T(8,128)S(1)}, f32[512,512]{1,0:T(8,128)}, u32[]{:S(2)}) copy-start(f32[512,512]{1,0:T(8,128)} %param.10) | copy-start | bytes 3145732
  0.6 8.5 %copy-start.7 = (f32[1,32,256]{2,1,0:T(8,128)S(1)}, f32[1,32,256]{2,1,0:T(8,128)}, u32[]{:S(2)}) copy-start(f32[1,32,256]{2,1,0:T(8,128)} %param.11) | copy-start | bytes 98308
  1.8 22.1 %collective-permute-start = (f32[128,512]{1,0:T(8,128)S(1)}, f32[128,512]{1,0:T(8,128)S(1)}, u32[]{:S(2)}, u32[]{:S(2)}) collective-permute-start(f32[128,512]{1,0:T(8,128)S(1)} %get-tuple-element.44), channel_id=1, source_target_pairs={{0,16},{16,32},{32,48},{48,64},{64,80},{80,96},{96,112},{1,17},{17... | collective-permute-start | bytes 786440 | tf_op jit(solution)/shard_map/ppermute | solution.py:24
  6.3 17.6 %collective-permute-start.1 = (f32[128,512]{1,0:T(8,128)S(1)}, f32[128,512]{1,0:T(8,128)S(1)}, u32[]{:S(2)}, u32[]{:S(2)}) collective-permute-start(f32[128,512]{1,0:T(8,128)S(1)} %get-tuple-element.45), channel_id=1, source_target_pairs={{16,0},{32,16},{48,32},{64,48},{80,64},{96,80},{112,96},{17,1},{33... | collective-permute-start | bytes 786440 | tf_op jit(solution)/shard_map/ppermute | solution.py:25
  23.9 4.0 %copy-start.2 = (f32[512,768]{1,0:T(8,128)S(1)}, f32[512,768]{1,0:T(8,128)}, u32[]{:S(2)}) copy-start(f32[512,768]{1,0:T(8,128)} %constant.74.clone) | copy-start | bytes 4718596
  27.9 2.2 %copy-start.8 = (f32[4]{0:T(128)S(1)}, f32[4]{0:T(128)}, u32[]{:S(2)}) copy-start(f32[4]{0:T(128)} %param.12) | copy-start | bytes 52
  30.1 1.1 %copy-start.4 = (f32[768,256]{1,0:T(8,128)S(1)}, f32[768,256]{1,0:T(8,128)}, u32[]{:S(2)}) copy-start(f32[768,256]{1,0:T(8,128)} %constant.73.clone) | copy-start | bytes 2359300
  30.4 1.8 %copy-start.6 = (f32[256,768]{1,0:T(8,128)S(1)}, f32[256,768]{1,0:T(8,128)}, u32[]{:S(2)}) copy-start(f32[256,768]{1,0:T(8,128)} %constant.75.clone) | copy-start | bytes 2359300
  36.3 1.9 %copy-start = (f32[768,1024]{1,0:T(8,128)S(1)}, f32[768,1024]{1,0:T(8,128)}, u32[]{:S(2)}) copy-start(f32[768,1024]{1,0:T(8,128)} %constant.76.clone) | copy-start | bytes 9437188
  42.5 1.2 %copy-start.3 = (f32[512,385]{1,0:T(8,128)S(1)}, f32[512,385]{1,0:T(8,128)}, u32[]{:S(2)}) copy-start(f32[512,385]{1,0:T(8,128)} %constant.92) | copy-start | bytes 2365444
  43.7 1.1 %copy-start.5 = (f32[512,383]{1,0:T(8,128)S(1)}, f32[512,383]{1,0:T(8,128)}, u32[]{:S(2)}) copy-start(f32[512,383]{1,0:T(8,128)} %constant.93) | copy-start | bytes 2353156

commit v22 on v19

--- a/solution.py
+++ b/solution.py
@@ -115,6 +115,7 @@
     window_rows = product(left, rows_ext)
     window_rows, normed = lax.optimization_barrier((window_rows, normed))
     window_parts = halves(product(window_rows, right_w))
+    left_t = lax.dynamic_slice_in_dim(left, jnp.minimum(tile_index, 0), extent, axis=1)
     template_parts = halves(product(product(left_t, normed), right_t))
 
     positions = lax.iota(jnp.int32, n)

time: 70.8 us -> 72.4 us (1.023)
  matrix products: 13.5 us -> 16.5 us
  local copies, waits for them, and re-layouts: 4.88 us -> 3.46 us
    dot_general x7, matrix products: 12.8 us -> 15.8 us  [product(): jnp.dot(former, latter, precision=mode, preferred_element_type=jnp.float32)]
    unnamed x24 -> x20, local copies, waits for them, and re-layouts: 3.37 us -> 1.99 us
where the time goes in v22:
time: 72.4 us; the launch traced here: 71.8 us
  blocking collectives  37.8 us (52%)
  matrix products  16.5 us (23%)
  starting transfers between devices  6.43 us (9%)
  other arithmetic  6.02 us (8%)
  local copies, waits for them, and re-layouts  3.46 us (5%)
  between operations  1.62 us (2%)
    all_to_all x1, blocking collectives, per_device(): lax.all_to_all(scores, 'orient', 0, 0, tiled=True)  24.1 us
    dot_general x7, matrix products, product(): jnp.dot(former, latter, precision=mode, preferred_element_type=jnp.float32)  15.8 us
    all_gather x1, blocking collectives, per_device(): everything = lax.all_gather(payload, 'tile')  13.7 us
    ppermute x1, starting transfers between devices, padded(): before = lax.ppermute(last, axis, up)  4.51 us
    mul x2, other arithmetic, multiply(): (spec_real * template_real + spec_imag * template_imag) * weight  3.5 us
    unnamed x20, local copies, waits for them, and re-layouts  1.99 us
    ppermute x1, starting transfers between devices, padded(): after = lax.ppermute(initial, axis, down)  1.92 us
  transfers between devices with their start and end apart: 2, of which 0 were waited for; matrix products, arithmetic and copies ran while one was open for 2% of the time, Pallas kernels for 0%

profile of v22, /device:TPU:1, one launch (start us, length us, event | category | flops | bytes accessed | tf_op | source)
XLA Modules:
  0.0 71.8 jit_solution(8362214089997277133)
XLA Ops:
  0.6 0.0 copy-start.1
  0.6 0.0 copy-start.6
  0.7 0.0 copy-start.7
  0.7 1.1 %fusion.57 = (f32[128,512]{1,0:T(8,128)S(1)}, f32[128,512]{1,0:T(8,128)S(1)}) fusion(f32[512,512]{1,0:T(8,128)} %param.9), kind=kLoop, calls=%fused_computation.103 | loop fusion | bytes 1048576 | tf_op jit(solution)/shard_map/slice | solution.py:22
  1.8 4.5 %collective-permute-start = (f32[128,512]{1,0:T(8,128)S(1)}, f32[128,512]{1,0:T(8,128)S(1)}, u32[]{:S(2)}, u32[]{:S(2)}) collective-permute-start(f32[128,512]{1,0:T(8,128)S(1)} %get-tuple-element.38), channel_id=1, source_target_pairs={{0,16},{16,32},{32,48},{48,64},{64,80},{80,96},{96,112},{1,17},{17... | collective-permute-start | bytes 786440 | tf_op jit(solution)/shard_map/ppermute | solution.py:24
  6.3 1.9 %collective-permute-start.1 = (f32[128,512]{1,0:T(8,128)S(1)}, f32[128,512]{1,0:T(8,128)S(1)}, u32[]{:S(2)}, u32[]{:S(2)}) collective-permute-start(f32[128,512]{1,0:T(8,128)S(1)} %get-tuple-element.39), channel_id=1, source_target_pairs={{16,0},{32,16},{48,32},{64,48},{80,64},{96,80},{112,96},{17,1},{33... | collective-permute-start | bytes 786440 | tf_op jit(solution)/shard_map/ppermute | solution.py:25
  8.3 0.0 copy-done.1
  8.3 0.2 fusion.55
  9.1 0.0 copy-done.6
  9.1 13.7 %all-gather.1 = f32[8,34,256]{2,1,0:T(8,128)S(1)} all-gather(f32[1,34,256]{2,1,0:T(8,128)S(1)} %maximum_bitcast_fusion), channel_id=2, replica_groups=mesh['tile'=8,'orient'=16] {'tile'}, dimensions={0}, use_global_device_ids=true | all-gather | bytes 313344 | tf_op jit(solution)/shard_map/all_gather | solution.py:72
  23.0 0.0 copy-done.7
  23.0 0.1 select_reduce_fusion.1
  23.1 0.1 select_reduce_fusion
  23.1 0.2 fusion.28
  23.3 0.1 multiply_reduce_fusion.2
  23.4 0.2 fusion.26
  23.6 0.2 fusion.32
  23.8 0.2 fusion.30
  24.2 0.2 add_negate_fusion
  24.4 0.0 collective-permute-done
  24.4 0.0 collective-permute-done.1
  24.4 0.0 copy-start.2
  24.5 4.0 %fusion.10 = f32[768,512]{1,0:T(8,128)S(1)} fusion(f32[768,768]{1,0:T(8,128)} %constant.72.clone, f32[128,512]{1,0:T(8,128)S(1)} %collective-permute-done.1, f32[512,512]{1,0:T(8,128)S(1)} %copy-done.1, f32[128,512]{1,0:T(8,128)S(1)} %collective-permute-done, f32[512]{0:T(512)S(1)} %bitcast.46, f32[512]{0:T(512)S(1)} %bitcast.45, pred[768]{0:T(1024)(128)(4,1)S(1)} %fusion.41), kind=kOutput, calls=%fused_computation.12 | convolution fusion | flops 1813905408 | bytes 5509888 | tf_op jit(solution)/shard_map/dot_general | solution.py:31
  28.4 0.0 copy-done.2
  28.5 2.2 %fusion.58 = f32[768,768]{1,0:T(8,128)S(1)} fusion(f32[768,512]{1,0:T(8,128)S(1)} %fusion.10, f32[512,768]{1,0:T(8,128)S(1)} %copy-done.2), kind=kOutput, calls=%fused_computation.104 | convolution fusion | flops 1811939328 | bytes 5505024 | tf_op jit(solution)/shard_map/dot_general | solution.py:31
  30.6 0.0 copy-start.5
  30.7 0.1 slice.139
  30.7 1.9 %fusion.17 = f32[768,256]{1,0:T(8,128)S(1)} fusion(f32[256,256]{1,0:T(8,128)S(1)} %fusion.25, f32[768,768]{1,0:T(8,128)} %constant.72.clone, s32[]{:T(128)S(6)} %select_n.30), kind=kOutput, calls=%fused_computation.33 | convolution fusion | flops 301989888 | bytes 1835012 | tf_op jit(solution)/shard_map/dot_general | solution.py:31
  32.7 0.0 copy-done.5
  32.7 1.2 %fusion.59 = f32[768,768]{1,0:T(8,128)S(1)} fusion(f32[768,256]{1,0:T(8,128)S(1)} %fusion.17, f32[256,768]{1,0:T(8,128)S(1)} %copy-done.5), kind=kOutput, calls=%fused_computation.105 | convolution fusion | flops 905969664 | bytes 3932160 | tf_op jit(solution)/shard_map/dot_general | solution.py:31
  33.9 0.1 slice.141
  33.9 2.5 %add_multiply_fusion.1 = (f32[385,383]{1,0:T(8,128)S(1)}, f32[385,383]{1,0:T(8,128)S(1)}, f32[385,383]{1,0:T(8,128)S(1)}, f32[385,383]{1,0:T(8,128)S(1)}, f32[385,383]{1,0:T(8,128)S(1)}, /*index=5*/f32[385,383]{1,0:T(8,128)S(1)}) fusion(f32[385,768]{1,0:T(8,128)S(1)} %add_negate_fusion, f32[768,768]{1,0:T(8,128)S(1)} %fusion.58, f32[768,768]{1,0:T(8,128)S(1)} %fusion.59, ...), kind=kLoop, calls=%fused_computation.44 | loop fusion | flops 2359280 | bytes 8841172 | tf_op jit(solution)/shard_map/mul | solution.py:145
  36.4 0.0 copy-start
  36.4 1.0 %add_multiply_fusion = (f32[385,385]{1,0:T(8,128)S(1)}, f32[385,385]{1,0:T(8,128)S(1)}) fusion(f32[385,768]{1,0:T(8,128)S(1)} %add_negate_fusion, f32[385,383]{1,0:T(8,128)S(1)} %get-tuple-element.36, f32[768,768]{1,0:T(8,128)S(1)} %fusion.58, f32[385,383]{1,0:T(8,128)S(1)} %get-tuple-element.37, f32[768,768]{1,0:T(8,128)S(1)} %fusion.59, ...), kind=kLoop, calls=%fused_computation.30 | loop fusion | flops 2371600 | bytes 7676932 | tf_op jit(solution)/shard_map/mul | solution.py:145
  37.5 0.8 %copy-done = f32[768,1024]{1,0:T(8,128)S(1)} copy-done((f32[768,1024]{1,0:T(8,128)S(1)}, f32[768,1024]{1,0:T(8,128)}, u32[]{:S(2)}) %copy-start) | copy-done | bytes 3145752
  38.3 4.3 %fusion = f32[770,1024]{1,0:T(8,128)S(1)} fusion(f32[768,1024]{1,0:T(8,128)S(1)} %copy-done, f32[385,383]{1,0:T(8,128)S(1)} %get-tuple-element.31, f32[385,385]{1,0:T(8,128)S(1)} %get-tuple-element.29, f32[385,383]{1,0:T(8,128)S(1)} %get-tuple-element.30, f32[385,385]{1,0:T(8,128)S(1)} %get-tuple-element.28), kind=kOutput, calls=%fused_computation | convolution fusion | flops 3635089920 | bytes 8665088 | tf_op jit(solution)/shard_map/dot_general | solution.py:31
  42.7 0.0 copy-start.3
  42.7 0.2 fusion.56
  42.8 1.0 %copy-done.3 = f32[512,385]{1,0:T(8,128)S(1)} copy-done((f32[512,385]{1,0:T(8,128)S(1)}, f32[512,385]{1,0:T(8,128)}, u32[]{:S(2)}) %copy-start.3) | copy-done | bytes 788504
  43.9 0.0 copy-start.4
  43.9 1.1 %fusion.14 = f32[512,512]{0,1:T(8,128)S(1)} fusion(f32[512,385]{1,0:T(8,128)S(1)} %copy-done.3, f32[770,1024]{1,0:T(8,128)S(1)} %fusion), kind=kOutput, calls=%fused_computation.25 | convolution fusion | flops 605749760 | bytes 3702784 | tf_op jit(solution)/shard_map/dot_general | solution.py:31
  45.0 0.1 copy-done.4
  45.0 1.1 %convolution_add_fusion = f32[512,512]{0,1:T(8,128)S(1)} fusion(f32[512,512]{0,1:T(8,128)S(1)} %fusion.14, f32[512,383]{1,0:T(8,128)S(1)} %copy-done.4, f32[385,512]{1,0:T(8,128)S(1)} %get-tuple-element.33, f32[385,512]{1,0:T(8,128)S(1)} %get-tuple-element.32), kind=kOutput, calls=%fused_computation.13 | convolution fusion | flops 602865152 | bytes 4456448 | tf_op jit(solution)/shard_map/dot_general | solution.py:31
  46.2 24.1 %all_to_all.9 = f32[16,32,512]{2,1,0:T(8,128)S(1)} all-to-all(f32[16,32,512]{2,1,0:T(8,128)S(1)} %bitcast.41), channel_id=1, replica_groups=mesh['tile'=8,'orient'=16] {'orient'}, dimensions={0} | all-to-all | bytes 2097152 | tf_op jit(solution)/shard_map/all_to_all | solution.py:164
  70.3 0.9 %multiply_reduce_fusion = (f32[32,512]{1,0:T(8,128)}, f32[32,512]{1,0:T(8,128)}, f32[32,512]{1,0:T(8,128)S(1)}, f32[32,512]{1,0:T(8,128)S(1)}) fusion(f32[16,32,512]{2,1,0:T(8,128)S(1)} %all_to_all.9), kind=kLoop, calls=%fused_computation.11 | loop fusion | flops 1736704 | bytes 1310720 | tf_op jit(solution)/shard_map/reduce | solution.py:176
  71.2 0.7 multiply_subtract_fusion
  (17 shorter events, 0.3 us)
Async XLA Ops:
  0.6 7.6 %copy-start.1 = (f32[512,512]{1,0:T(8,128)S(1)}, f32[512,512]{1,0:T(8,128)}, u32[]{:S(2)}) copy-start(f32[512,512]{1,0:T(8,128)} %param.9) | copy-start | bytes 3145732
  0.6 8.5 %copy-start.6 = (f32[1,32,256]{2,1,0:T(8,128)S(1)}, f32[1,32,256]{2,1,0:T(8,128)}, u32[]{:S(2)}) copy-start(f32[1,32,256]{2,1,0:T(8,128)} %param.10) | copy-start | bytes 98308
  0.7 22.3 %copy-start.7 = (f32[4]{0:T(128)S(1)}, f32[4]{0:T(128)}, u32[]{:S(2)}) copy-start(f32[4]{0:T(128)} %param.11) | copy-start | bytes 52
  1.8 22.6 %collective-permute-start = (f32[128,512]{1,0:T(8,128)S(1)}, f32[128,512]{1,0:T(8,128)S(1)}, u32[]{:S(2)}, u32[]{:S(2)}) collective-permute-start(f32[128,512]{1,0:T(8,128)S(1)} %get-tuple-element.38), channel_id=1, source_target_pairs={{0,16},{16,32},{32,48},{48,64},{64,80},{80,96},{96,112},{1,17},{17... | collective-permute-start | bytes 786440 | tf_op jit(solution)/shard_map/ppermute | solution.py:24
  6.3 18.1 %collective-permute-start.1 = (f32[128,512]{1,0:T(8,128)S(1)}, f32[128,512]{1,0:T(8,128)S(1)}, u32[]{:S(2)}, u32[]{:S(2)}) collective-permute-start(f32[128,512]{1,0:T(8,128)S(1)} %get-tuple-element.39), channel_id=1, source_target_pairs={{16,0},{32,16},{48,32},{64,48},{80,64},{96,80},{112,96},{17,1},{33... | collective-permute-start | bytes 786440 | tf_op jit(solution)/shard_map/ppermute | solution.py:25
  24.4 4.0 %copy-start.2 = (f32[512,768]{1,0:T(8,128)S(1)}, f32[512,768]{1,0:T(8,128)}, u32[]{:S(2)}) copy-start(f32[512,768]{1,0:T(8,128)} %constant.73.clone) | copy-start | bytes 4718596
  30.6 2.0 %copy-start.5 = (f32[256,768]{1,0:T(8,128)S(1)}, f32[256,768]{1,0:T(8,128)}, u32[]{:S(2)}) copy-start(f32[256,768]{1,0:T(8,128)} %constant.74.clone) | copy-start | bytes 2359300
  36.4 1.9 %copy-start = (f32[768,1024]{1,0:T(8,128)S(1)}, f32[768,1024]{1,0:T(8,128)}, u32[]{:S(2)}) copy-start(f32[768,1024]{1,0:T(8,128)} %constant.75.clone) | copy-start | bytes 9437188
  42.7 1.2 %copy-start.3 = (f32[512,385]{1,0:T(8,128)S(1)}, f32[512,385]{1,0:T(8,128)}, u32[]{:S(2)}) copy-start(f32[512,385]{1,0:T(8,128)} %constant.91) | copy-start | bytes 2365444
  43.9 1.1 %copy-start.4 = (f32[512,383]{1,0:T(8,128)S(1)}, f32[512,383]{1,0:T(8,128)}, u32[]{:S(2)}) copy-start(f32[512,383]{1,0:T(8,128)} %constant.92) | copy-start | bytes 2353156

commit v23 on v19

--- a/solution.py
+++ b/solution.py
@@ -115,7 +115,8 @@
     window_rows = product(left, rows_ext)
     window_rows, normed = lax.optimization_barrier((window_rows, normed))
     window_parts = halves(product(window_rows, right_w))
-    template_parts = halves(product(product(left_t, normed), right_t))
+    normed_rows = jnp.pad(normed, ((0, n - extent), (0, 0)))
+    template_parts = halves(product(product(left, normed_rows), right_t))
 
     positions = lax.iota(jnp.int32, n)
     signed_freq = (

time: 70.8 us -> 74.8 us (1.056)
  matrix products: 13.5 us -> 15.1 us
  local copies, waits for them, and re-layouts: 4.88 us -> 6.14 us
  other arithmetic: 5.98 us -> 6.97 us
    dot_general x7, matrix products: 12.8 us -> 14.4 us  [product(): jnp.dot(former, latter, precision=mode, preferred_element_type=jnp.float32)]
    reduce_sum x3, other arithmetic: 0.17 us -> 1.11 us  [lane_total(): jnp.sum(rows, axis=0, keepdims=True)]
    slice x1, local copies, waits for them, and re-layouts: 1.15 us -> 1.95 us  [padded(): last = lax.slice_in_dim(shard, length - width, length, axis=dim)]
  transfers between devices with their start and end apart: 2 -> 2, of which waited for: 0 -> 0; matrix products, arithmetic and copies ran while one was open for 2% -> 3% of each run, Pallas kernels for 0% -> 0%
where the time goes in v23:
time: 74.8 us; the launch traced here: 74.2 us
  blocking collectives  38 us (51%)
  matrix products  15.1 us (20%)
  other arithmetic  6.97 us (9%)
  starting transfers between devices  6.42 us (9%)
  local copies, waits for them, and re-layouts  6.14 us (8%)
  between operations  1.61 us (2%)
    all_to_all x1, blocking collectives, per_device(): lax.all_to_all(scores, 'orient', 0, 0, tiled=True)  24.1 us
    dot_general x7, matrix products, product(): jnp.dot(former, latter, precision=mode, preferred_element_type=jnp.float32)  14.4 us
    all_gather x1, blocking collectives, per_device(): everything = lax.all_gather(payload, 'tile')  13.9 us
    ppermute x1, starting transfers between devices, padded(): before = lax.ppermute(last, axis, up)  4.5 us
    unnamed x24, local copies, waits for them, and re-layouts  3.86 us
    mul x2, other arithmetic, multiply(): (spec_real * template_real + spec_imag * template_imag) * weight  3.5 us
    slice x1, local copies, waits for them, and re-layouts, padded(): last = lax.slice_in_dim(shard, length - width, length, axis=dim)  1.95 us
    ppermute x1, starting transfers between devices, padded(): after = lax.ppermute(initial, axis, down)  1.92 us
  transfers between devices with their start and end apart: 2, of which 0 were waited for; matrix products, arithmetic and copies ran while one was open for 3% of the time, Pallas kernels for 0%

profile of v23, /device:TPU:1, one launch (start us, length us, event | category | flops | bytes accessed | tf_op | source)
XLA Modules:
  0.0 74.2 jit_solution(466487811138204377)
XLA Ops:
  0.6 0.0 copy-start.1
  0.6 0.0 copy-start.8
  0.7 0.0 copy-start.9
  0.7 1.9 %fusion.57 = (f32[128,512]{1,0:T(8,128)}, f32[128,512]{1,0:T(8,128)}) fusion(f32[512,512]{1,0:T(8,128)} %param.9), kind=kLoop, calls=%fused_computation.103 | loop fusion | bytes 1048576 | tf_op jit(solution)/shard_map/slice | solution.py:22
  2.6 4.5 %collective-permute-start = (f32[128,512]{1,0:T(8,128)}, f32[128,512]{1,0:T(8,128)}, u32[]{:S(2)}, u32[]{:S(2)}) collective-permute-start(f32[128,512]{1,0:T(8,128)} %get-tuple-element.38), channel_id=1, source_target_pairs={{0,16},{16,32},{32,48},{48,64},{64,80},{80,96},{96,112},{1,17},{17... | collective-permute-start | bytes 786440 | tf_op jit(solution)/shard_map/ppermute | solution.py:24
  7.1 1.9 %collective-permute-start.1 = (f32[128,512]{1,0:T(8,128)}, f32[128,512]{1,0:T(8,128)}, u32[]{:S(2)}, u32[]{:S(2)}) collective-permute-start(f32[128,512]{1,0:T(8,128)} %get-tuple-element.39), channel_id=1, source_target_pairs={{16,0},{32,16},{48,32},{64,48},{80,64},{96,80},{112,96},{17,1},{33... | collective-permute-start | bytes 786440 | tf_op jit(solution)/shard_map/ppermute | solution.py:25
  9.1 0.0 copy-done.1
  9.1 0.2 fusion.55
  9.9 0.0 copy-done.8
  9.9 0.0 copy-start.2
  9.9 13.9 %all-gather.1 = f32[8,34,256]{2,1,0:T(8,128)S(1)} all-gather(f32[1,34,256]{2,1,0:T(8,128)S(1)} %maximum_bitcast_fusion), channel_id=2, replica_groups=mesh['tile'=8,'orient'=16] {'tile'}, dimensions={0}, use_global_device_ids=true | all-gather | bytes 313344 | tf_op jit(solution)/shard_map/all_gather | solution.py:72
  23.8 0.0 copy-start.3
  23.8 0.7 copy-done.3
  24.5 0.0 copy-done.9
  24.6 0.1 select_reduce_fusion.1
  24.6 0.1 select_reduce_fusion
  24.7 0.2 fusion.28
  24.9 1.0 %multiply_reduce_fusion.2 = (f32[256]{0:T(256)S(1)}, f32[8,32,256]{2,1,0:T(8,128)S(1)}) fusion(f32[256]{0:T(256)S(1)} %broadcast_multiply_fusion.1, f32[8,34,256]{2,1,0:T(8,128)} %copy-done.3), kind=kLoop, calls=%fused_computation.47 | loop fusion | flops 196352 | bytes 526336 | tf_op jit(solution)/shard_map/reduce_sum | solution.py:81
  25.9 0.2 fusion.26
  26.1 0.2 fusion.32
  26.3 0.2 fusion.30
  26.7 0.2 add_negate_fusion
  27.0 0.0 collective-permute-done
  27.0 0.0 collective-permute-done.1
  27.0 0.0 copy-done.2
  27.0 3.2 %fusion.10 = f32[768,512]{1,0:T(8,128)S(1)} fusion(f32[768,768]{1,0:T(8,128)S(1)} %copy-done.2, f32[128,512]{1,0:T(8,128)} %collective-permute-done.1, f32[512,512]{1,0:T(8,128)S(1)} %copy-done.1, f32[128,512]{1,0:T(8,128)} %collective-permute-done, f32[512]{0:T(512)S(1)} %bitcast.46, f32[512]{0:T(512)S(1)} %bitcast.45, pred[768]{0:T(1024)(128)(4,1)S(1)} %fusion.41), kind=kOutput, calls=%fused_computation.12 | convolution fusion | flops 1813905408 | bytes 5509888 | tf_op jit(solution)/shard_map/dot_general | solution.py:31
  30.2 0.0 copy-start.4
  30.2 1.2 %fusion.17 = f32[256,768]{1,0:T(8,128)S(1)} fusion(f32[768,768]{1,0:T(8,128)S(1)} %copy-done.2, f32[256,256]{1,0:T(8,128)S(1)} %fusion.25), kind=kOutput, calls=%fused_computation.33 | convolution fusion | flops 905969664 | bytes 3407872 | tf_op jit(solution)/shard_map/dot_general | solution.py:31
  31.4 0.2 copy-done.4
  31.6 2.2 %fusion.58 = f32[768,768]{1,0:T(8,128)S(1)} fusion(f32[768,512]{1,0:T(8,128)S(1)} %fusion.10, f32[512,768]{1,0:T(8,128)S(1)} %copy-done.4), kind=kOutput, calls=%fused_computation.104 | convolution fusion | flops 1811939328 | bytes 5505024 | tf_op jit(solution)/shard_map/dot_general | solution.py:31
  33.8 0.0 copy-start.7
  33.8 0.1 slice.139
  33.9 1.0 %copy-done.7 = f32[256,768]{1,0:T(8,128)S(1)} copy-done((f32[256,768]{1,0:T(8,128)S(1)}, f32[256,768]{1,0:T(8,128)}, u32[]{:S(2)}) %copy-start.7) | copy-done | bytes 786456
  34.9 1.3 %fusion.59 = f32[768,768]{1,0:T(8,128)S(1)} fusion(f32[256,768]{1,0:T(8,128)S(1)} %fusion.17, f32[256,768]{1,0:T(8,128)S(1)} %copy-done.7), kind=kOutput, calls=%fused_computation.105 | convolution fusion | flops 905969664 | bytes 3932160 | tf_op jit(solution)/shard_map/dot_general | solution.py:31
  36.3 0.1 slice.141
  36.4 2.5 %add_multiply_fusion.1 = (f32[385,383]{1,0:T(8,128)S(1)}, f32[385,383]{1,0:T(8,128)S(1)}, f32[385,383]{1,0:T(8,128)S(1)}, f32[385,383]{1,0:T(8,128)S(1)}, f32[385,383]{1,0:T(8,128)S(1)}, /*index=5*/f32[385,383]{1,0:T(8,128)S(1)}) fusion(f32[385,768]{1,0:T(8,128)S(1)} %add_negate_fusion, f32[768,768]{1,0:T(8,128)S(1)} %fusion.58, f32[768,768]{1,0:T(8,128)S(1)} %fusion.59, ...), kind=kLoop, calls=%fused_computation.44 | loop fusion | flops 2359280 | bytes 8841172 | tf_op jit(solution)/shard_map/mul | solution.py:145
  38.8 0.0 copy-start
  38.8 1.0 %add_multiply_fusion = (f32[385,385]{1,0:T(8,128)S(1)}, f32[385,385]{1,0:T(8,128)S(1)}) fusion(f32[385,768]{1,0:T(8,128)S(1)} %add_negate_fusion, f32[385,383]{1,0:T(8,128)S(1)} %get-tuple-element.36, f32[768,768]{1,0:T(8,128)S(1)} %fusion.58, f32[385,383]{1,0:T(8,128)S(1)} %get-tuple-element.37, f32[768,768]{1,0:T(8,128)S(1)} %fusion.59, ...), kind=kLoop, calls=%fused_computation.30 | loop fusion | flops 2371600 | bytes 7676932 | tf_op jit(solution)/shard_map/mul | solution.py:145
  39.9 0.8 %copy-done = f32[768,1024]{1,0:T(8,128)S(1)} copy-done((f32[768,1024]{1,0:T(8,128)S(1)}, f32[768,1024]{1,0:T(8,128)}, u32[]{:S(2)}) %copy-start) | copy-done | bytes 3145752
  40.7 4.3 %fusion = f32[770,1024]{1,0:T(8,128)S(1)} fusion(f32[768,1024]{1,0:T(8,128)S(1)} %copy-done, f32[385,383]{1,0:T(8,128)S(1)} %get-tuple-element.31, f32[385,385]{1,0:T(8,128)S(1)} %get-tuple-element.29, f32[385,383]{1,0:T(8,128)S(1)} %get-tuple-element.30, f32[385,385]{1,0:T(8,128)S(1)} %get-tuple-element.28), kind=kOutput, calls=%fused_computation | convolution fusion | flops 3635089920 | bytes 8665088 | tf_op jit(solution)/shard_map/dot_general | solution.py:31
  45.1 0.0 copy-start.5
  45.1 0.2 fusion.56
  45.3 1.0 %copy-done.5 = f32[512,385]{1,0:T(8,128)S(1)} copy-done((f32[512,385]{1,0:T(8,128)S(1)}, f32[512,385]{1,0:T(8,128)}, u32[]{:S(2)}) %copy-start.5) | copy-done | bytes 788504
  46.3 0.0 copy-start.6
  46.3 1.1 %fusion.14 = f32[512,512]{0,1:T(8,128)S(1)} fusion(f32[512,385]{1,0:T(8,128)S(1)} %copy-done.5, f32[770,1024]{1,0:T(8,128)S(1)} %fusion), kind=kOutput, calls=%fused_computation.25 | convolution fusion | flops 605749760 | bytes 3702784 | tf_op jit(solution)/shard_map/dot_general | solution.py:31
  47.4 0.1 copy-done.6
  47.4 1.1 %convolution_add_fusion = f32[512,512]{0,1:T(8,128)S(1)} fusion(f32[512,512]{0,1:T(8,128)S(1)} %fusion.14, f32[512,383]{1,0:T(8,128)S(1)} %copy-done.6, f32[385,512]{1,0:T(8,128)S(1)} %get-tuple-element.33, f32[385,512]{1,0:T(8,128)S(1)} %get-tuple-element.32), kind=kOutput, calls=%fused_computation.13 | convolution fusion | flops 602865152 | bytes 4456448 | tf_op jit(solution)/shard_map/dot_general | solution.py:31
  48.5 24.1 %all_to_all.9 = f32[16,32,512]{2,1,0:T(8,128)S(1)} all-to-all(f32[16,32,512]{2,1,0:T(8,128)S(1)} %bitcast.41), channel_id=1, replica_groups=mesh['tile'=8,'orient'=16] {'orient'}, dimensions={0} | all-to-all | bytes 2097152 | tf_op jit(solution)/shard_map/all_to_all | solution.py:164
  72.6 0.9 %multiply_reduce_fusion = (f32[32,512]{1,0:T(8,128)}, f32[32,512]{1,0:T(8,128)}, f32[32,512]{1,0:T(8,128)S(1)}, f32[32,512]{1,0:T(8,128)S(1)}) fusion(f32[16,32,512]{2,1,0:T(8,128)S(1)} %all_to_all.9), kind=kLoop, calls=%fused_computation.11 | loop fusion | flops 1736704 | bytes 1310720 | tf_op jit(solution)/shard_map/reduce | solution.py:176
  73.6 0.7 multiply_subtract_fusion
  (17 shorter events, 0.3 us)
Async XLA Ops:
  0.6 8.4 %copy-start.1 = (f32[512,512]{1,0:T(8,128)S(1)}, f32[512,512]{1,0:T(8,128)}, u32[]{:S(2)}) copy-start(f32[512,512]{1,0:T(8,128)} %param.9) | copy-start | bytes 3145732
  0.6 9.3 %copy-start.8 = (f32[1,32,256]{2,1,0:T(8,128)S(1)}, f32[1,32,256]{2,1,0:T(8,128)}, u32[]{:S(2)}) copy-start(f32[1,32,256]{2,1,0:T(8,128)} %param.10) | copy-start | bytes 98308
  0.7 23.9 %copy-start.9 = (f32[4]{0:T(128)S(1)}, f32[4]{0:T(128)}, u32[]{:S(2)}) copy-start(f32[4]{0:T(128)} %param.11) | copy-start | bytes 52
  2.6 24.4 %collective-permute-start = (f32[128,512]{1,0:T(8,128)}, f32[128,512]{1,0:T(8,128)}, u32[]{:S(2)}, u32[]{:S(2)}) collective-permute-start(f32[128,512]{1,0:T(8,128)} %get-tuple-element.38), channel_id=1, source_target_pairs={{0,16},{16,32},{32,48},{48,64},{64,80},{80,96},{96,112},{1,17},{17... | collective-permute-start | bytes 786440 | tf_op jit(solution)/shard_map/ppermute | solution.py:24
  7.1 19.9 %collective-permute-start.1 = (f32[128,512]{1,0:T(8,128)}, f32[128,512]{1,0:T(8,128)}, u32[]{:S(2)}, u32[]{:S(2)}) collective-permute-start(f32[128,512]{1,0:T(8,128)} %get-tuple-element.39), channel_id=1, source_target_pairs={{16,0},{32,16},{48,32},{64,48},{80,64},{96,80},{112,96},{17,1},{33... | collective-permute-start | bytes 786440 | tf_op jit(solution)/shard_map/ppermute | solution.py:25
  9.9 17.1 %copy-start.2 = (f32[768,768]{1,0:T(8,128)S(1)}, f32[768,768]{1,0:T(8,128)}, u32[]{:S(2)}) copy-start(f32[768,768]{1,0:T(8,128)} %constant.70.clone) | copy-start | bytes 7077892
  23.8 0.7 copy-start.3
  30.2 1.4 %copy-start.4 = (f32[512,768]{1,0:T(8,128)S(1)}, f32[512,768]{1,0:T(8,128)}, u32[]{:S(2)}) copy-start(f32[512,768]{1,0:T(8,128)} %constant.71.clone) | copy-start | bytes 4718596
  33.8 1.1 %copy-start.7 = (f32[256,768]{1,0:T(8,128)S(1)}, f32[256,768]{1,0:T(8,128)}, u32[]{:S(2)}) copy-start(f32[256,768]{1,0:T(8,128)} %constant.72.clone) | copy-start | bytes 2359300
  38.8 1.9 %copy-start = (f32[768,1024]{1,0:T(8,128)S(1)}, f32[768,1024]{1,0:T(8,128)}, u32[]{:S(2)}) copy-start(f32[768,1024]{1,0:T(8,128)} %constant.73.clone) | copy-start | bytes 9437188
  45.1 1.2 %copy-start.5 = (f32[512,385]{1,0:T(8,128)S(1)}, f32[512,385]{1,0:T(8,128)}, u32[]{:S(2)}) copy-start(f32[512,385]{1,0:T(8,128)} %constant.91) | copy-start | bytes 2365444
  46.3 1.1 %copy-start.6 = (f32[512,383]{1,0:T(8,128)S(1)}, f32[512,383]{1,0:T(8,128)}, u32[]{:S(2)}) copy-start(f32[512,383]{1,0:T(8,128)} %constant.92) | copy-start | bytes 2353156
